TPU v7x, 512 devices: a whole 4x8x8 slice. The times are simulated.
512 devices in a mesh: expert: 32 (over z_lo, y, core), mp: 16 (over x, z_hi).
Axes of the slice: x: 4, y: 8, z: 8 (z_hi: 4, z_lo: 2; z = z_hi * 2 + z_lo), core: 2. Of those that a mesh axis runs over, the one named last changes fastest.
Arguments:
- tokens: bfloat16 [24576, 2048], P('expert', 'mp'), may hold values from -270 to 270
- norm_gain: float32 [2048], replicated, may hold values from 0.1 to 1.9
- router_weight: bfloat16 [2048, 32], replicated, may hold values from -0.125 to 0.125
- gate_proj: bfloat16 [32, 2048, 5120], P('expert', None, 'mp'), may hold values from -0.125 to 0.125
- up_proj: bfloat16 [32, 2048, 5120], P('expert', None, 'mp'), may hold values from -0.125 to 0.125
- down_proj: bfloat16 [32, 5120, 2048], P('expert', 'mp'), may hold values from -0.125 to 0.125
- expert_ids: int32 [24576], P('expert'), may hold values from 0 to 31, as said below
- slots: int32 [24576], P('expert'), may hold values from 0 to 31
- capacity: int32 [32], replicated, may hold values from 16 to 32, as said below
Outputs:
- expert_update: bfloat16 [24576, 2048], P('expert', 'mp')
Inputs may be any that keep to these rules, and one draw needn't show every extreme that they name: `expert_ids`: within the 768 rows of one group no two rows name the same expert and slot; one expert, drawn from the seed, is named with every slot 0 to 31 in every group. The expert that every group fills has capacity 32.
All inputs are finite; a program needn't handle non-finite values.
Results may differ from a plain program's by a relative error of at most 0.015.
Values may be sent and summed in bfloat16 or wider, within the bound.
No kernel may reach another device: no remote copies, remote signals or barrier semaphores. Data moves between devices by JAX's collectives and lax.ppermute only.
A program may use at most 64 MiB of HBM per device.

v0:
```python
import jax
import jax.numpy as jnp
from jax import lax
from jax.sharding import PartitionSpec as P

norm_eps = 1e-06


def shards(
    tokens, norm_gain, router_weight, gate_proj, up_proj, down_proj, expert_ids, slots, capacity
):
    tok_rows, shard_width = tokens.shape
    model_width = norm_gain.shape[0]
    experts = router_weight.shape[1]
    slot_count = 4 * tok_rows // (3 * experts)
    onehot = expert_ids[:, None] == jnp.arange(experts, dtype=jnp.int32)[None, :]
    cap_token = jnp.sum(jnp.where(onehot, capacity[None, :], 0), axis=1)
    kept_rows = slots < cap_token
    target = expert_ids * slot_count + slots
    owner = (
        jnp.zeros((experts * slot_count,), jnp.int32)
        .at[target]
        .set(jnp.arange(tok_rows, dtype=jnp.int32))
    )
    live_slot = jnp.zeros((experts * slot_count,), jnp.bool_).at[target].set(kept_rows)
    whole = lax.all_gather(tokens, "mp", axis=1, tiled=True)
    features = whole.astype(jnp.float32)
    mean_square = jnp.mean(features * features, axis=1, keepdims=True)
    normed = (features * lax.rsqrt(mean_square + norm_eps) * norm_gain).astype(jnp.bfloat16)
    logits = jnp.dot(normed, router_weight, preferred_element_type=jnp.float32)
    picked = jnp.sum(jnp.where(onehot, logits, 0.0), axis=1)
    taken = jnp.take(normed, owner, axis=0)
    masked = jnp.where(live_slot[:, None], taken, jnp.zeros_like(taken))
    received = lax.all_to_all(
        masked.reshape(experts, slot_count, normed.shape[1]),
        "expert",
        split_axis=0,
        concat_axis=0,
        tiled=True,
    )
    flat_rows = received.reshape(-1, model_width)
    pre_gate = jnp.dot(flat_rows, gate_proj[0], preferred_element_type=jnp.float32)
    pre_up = jnp.dot(flat_rows, up_proj[0], preferred_element_type=jnp.float32)
    gate_prob = jax.nn.sigmoid(picked)
    hidden = (jax.nn.gelu(pre_gate, approximate=True) * pre_up).astype(jnp.bfloat16)
    out_weight = down_proj[0]
    summed = lax.psum_scatter(
        lax.dot_general(
            out_weight, hidden, (((0,), (1,)), ((), ())), preferred_element_type=jnp.float32
        ).astype(jnp.bfloat16),
        "mp",
        scatter_dimension=0,
        tiled=True,
    ).astype(jnp.float32)
    expert_out = summed.T.astype(jnp.bfloat16).reshape(-1, slot_count, summed.shape[0])
    returned = lax.all_to_all(expert_out, "expert", split_axis=0, concat_axis=0, tiled=True)
    returned_rows = jnp.take(returned.reshape(experts * slot_count, shard_width), target, axis=0)
    update = jnp.where(
        kept_rows[:, None], gate_prob[:, None] * returned_rows.astype(jnp.float32), 0.0
    )
    return update.astype(jnp.bfloat16)


def solution(mesh):
    in_specs = (
        P("expert", "mp"),
        P(),
        P(),
        P("expert", None, "mp"),
        P("expert", None, "mp"),
        P("expert", "mp", None),
        P("expert"),
        P("expert"),
        P(),
    )
    out_specs = P("expert", "mp")
    return jax.shard_map(shards, mesh=mesh, in_specs=in_specs, out_specs=out_specs, check_vma=False)
```

profile of v0, /device:TPU:6, one launch (start us, length us, event | category | flops | bytes accessed | tf_op | source)
XLA Modules:
  0.0 362.8 jit_solution(12922910694898019356)
XLA Ops:
  6.5 0.7 all-gather.2.cloned.1.call-update
  7.3 0.8 select_reduce_fusion
  8.1 0.7 compare_and_fusion.1
  8.8 3.4 scatter_custom_fusion
  12.2 0.1 broadcast_in_dim.90
  12.3 3.4 scatter_custom_fusion.1
  15.8 78.4 %all-gather.2.cloned.1.call-done = bf16[768,2048]{1,0:T(8,128)(2,1)} async-done(((bf16[768,128]{1,0:T(8,128)(2,1)}), bf16[768,2048]{1,0:T(8,128)(2,1)}) %all-gather.2.cloned.1.call-update) | async-done | bytes 3145744 | tf_op jit(solution)/shard_map/all_gather | solution.py:26
  94.1 2.7 fusion
  96.9 0.1 copy-done.1
  97.0 2.5 fusion.2
  99.5 11.1 %gather_fusion = bf16[1024,2048]{1,0:T(8,128)(2,1)} fusion(bf16[768,2048]{1,0:T(8,128)(2,1)} %fusion.2, s32[1024]{0:T(1024)S(1)} %fusion.22), kind=kCustom, calls=%fused_computation | custom fusion | bytes 8392704 | tf_op jit(solution)/shard_map/jit(_take)/gather | solution.py:32
  110.6 2.6 select_select_fusion
  113.2 102.8 %all_to_all.10 = bf16[32,32,2048]{2,1,0:T(8,128)(2,1)S(1)} all-to-all(bf16[32,32,2048]{2,1,0:T(8,128)(2,1)S(1)} %select_select_fusion), channel_id=1, replica_groups=mesh['expert'=32,'mp'=16] {'expert'}, dimensions={0} | all-to-all | bytes 8388608 | tf_op jit(solution)/shard_map/all_to_all | solution.py:34
  216.1 2.0 copy-done.2
  218.0 2.6 fusion.13
  220.7 8.4 %convert_bitcast_fusion = bf16[2048,1024]{0,1:T(8,128)(2,1)} fusion(bf16[1,320,2048]{2,1,0:T(8,128)(2,1)S(1)} %copy-done, bf16[1024,2048]{1,0:T(8,128)(2,1)} %bitcast.29, f32[1024,320]{0,1:T(8,128)} %fusion.13, bf16[1,2048,320]{1,2,0:T(8,128)(2,1)S(1)} %copy-done.7), kind=kOutput, calls=%fused_computation.9 | convolution fusion | flops 2689728512 | bytes 12320768 | tf_op jit(solution)/shard_map/dot_general | solution.py:48
  229.1 6.4 %copy.10 = bf16[2048,1024]{1,0:T(8,128)(2,1)} copy(bf16[2048,1024]{0,1:T(8,128)(2,1)} %convert_bitcast_fusion) | data formatting | bytes 8388608
  235.5 95.1 %reduce-scatter.4.cloned.1.call-done = bf16[128,1024]{1,0:T(8,128)(2,1)} async-done(((bf16[2048,1024]{1,0:T(8,128)(2,1)}), bf16[128,1024]{1,0:T(8,128)(2,1)}) %reduce-scatter.4.cloned.1.call-update) | async-done | bytes 262160
  330.7 1.8 copy.11
  332.5 7.3 %all-to-all-start.1 = ((bf16[32,32,128]{2,1,0:T(8,128)(2,1)}), bf16[32,32,128]{2,1,0:T(8,128)(2,1)S(1)}, u32[]{:S(2)}, u32[]{:S(2)}) async-start(bf16[32,32,128]{2,1,0:T(8,128)(2,1)} %bitcast.7), calls=%async_computation.1 | async-start | bytes 524288 | tf_op jit(solution)/shard_map/all_to_all | solution.py:56
  339.8 2.9 fusion.15
  342.8 10.2 %all-to-all-done.1 = bf16[32,32,128]{2,1,0:T(8,128)(2,1)S(1)} async-done(((bf16[32,32,128]{2,1,0:T(8,128)(2,1)}), bf16[32,32,128]{2,1,0:T(8,128)(2,1)S(1)}, u32[]{:S(2)}, u32[]{:S(2)}) %all-to-all-start.1) | async-done | bytes 262176 | tf_op jit(solution)/shard_map/all_to_all | solution.py:56
  353.0 1.9 gather_fusion.1
  354.9 1.1 select_convert_fusion
  (24 shorter events, 0.2 us)
Async XLA Ops:
  6.5 214.1 %copy-start = (bf16[1,320,2048]{2,1,0:T(8,128)(2,1)S(1)}, bf16[1,320,2048]{2,1,0:T(8,128)(2,1)}, u32[]{:S(2)}) copy-start(bf16[1,320,2048]{2,1,0:T(8,128)(2,1)} %param.14) | copy-start | bytes 3932164
  6.5 90.3 %copy-start.5 = (f32[2048]{0:T(1024)S(1)}, f32[2048]{0:T(1024)}, u32[]{:S(2)}) copy-start(f32[2048]{0:T(1024)} %param.10) | copy-start | bytes 24580
  6.5 87.6 %all-gather.2.cloned.1.call-start = ((), (), s32[]{:S(2)}) async-start(), calls=%async_computation.3 | async-start | bytes 3342336 | tf_op jit(solution)/shard_map/all_gather | solution.py:26
  7.3 323.4 %reduce-scatter.4.cloned.1.call-start = ((), (), s32[]{:S(2)}) async-start(), calls=%async_computation.4 | async-start | bytes 4456448
  94.1 2.8 copy-start.1
  113.2 104.8 %copy-start.6 = (bf16[1,2048,320]{1,2,0:T(8,128)(2,1)S(1)}, bf16[1,2048,320]{1,2,0:T(8,128)(2,1)}, u32[]{:S(2)}) copy-start(bf16[1,2048,320]{1,2,0:T(8,128)(2,1)} %param.12) | copy-start | bytes 3932164
  216.1 2.0 copy-start.2
  218.0 2.7 copy-start.7
  235.5 104.3 %copy-start.3 = (s32[768]{0:T(1024)S(1)}, s32[768]{0:T(1024)}, u32[]{:S(2)}) copy-start(s32[768]{0:T(1024)} %param.15) | copy-start | bytes 9220
  235.5 104.3 %copy-start.4 = (bf16[2048,32]{0,1:T(8,128)(2,1)S(1)}, bf16[2048,32]{0,1:T(8,128)(2,1)}, u32[]{:S(2)}) copy-start(bf16[2048,32]{0,1:T(8,128)(2,1)} %param.11) | copy-start | bytes 393220
  332.5 20.5 %all-to-all-start.1 = ((bf16[32,32,128]{2,1,0:T(8,128)(2,1)}), bf16[32,32,128]{2,1,0:T(8,128)(2,1)S(1)}, u32[]{:S(2)}, u32[]{:S(2)}) async-start(bf16[32,32,128]{2,1,0:T(8,128)(2,1)} %bitcast.7), calls=%async_computation.1 | async-start | bytes 524288 | tf_op jit(solution)/shard_map/all_to_all | solution.py:56
Sparse Core Ops, SparseCore 0:
  10.3 83.7 all-gather.1
  235.7 94.9 reduce-scatter.3
where the time goes:
time: 364 us; the launch traced here: 363 us
  waiting for transfers between devices  184 us (51%)
  blocking collectives  103 us (28%)
  local copies, waits for them, and re-layouts  30.2 us (8%)
  matrix products  14 us (4%)
  between operations  13.5 us (4%)
  other arithmetic  10.4 us (3%)
  starting transfers between devices  7.39 us (2%)
    all_to_all x1, blocking collectives, shards(): lax.all_to_all(masked.reshape(experts, slot_count, normed.shape[1]), 'exp...  103 us
    unnamed x3, waiting for transfers between devices  95.9 us
    all_gather x1, waiting for transfers between devices, shards(): whole = lax.all_gather(tokens, 'mp', axis=1, tiled=True)  78.4 us
    gather x1, local copies, waits for them, and re-layouts, shards(): taken = jnp.take(normed, owner, axis=0)  11.1 us
    unnamed x18, local copies, waits for them, and re-layouts  10.3 us
    all_to_all x1, waiting for transfers between devices, shards(): lax.all_to_all(expert_out, 'expert', split_axis=0, concat_axis=0, tiled=T...  10.2 us
    dot_general x1, matrix products, shards(): lax.dot_general(out_weight, hidden, (((0,), (1,)), ((), ())), preferred_e...  8.42 us
    all_to_all x1, starting transfers between devices, shards(): lax.all_to_all(expert_out, 'expert', split_axis=0, concat_axis=0, tiled=T...  7.35 us
  transfers between devices with their start and end apart: 3, of which 3 were waited for; matrix products, arithmetic and copies ran while one was open for 3% of the time, Pallas kernels for 0%

commit v1 on v0

v1 whole, which is shorter than its diff:
```python
import jax
import jax.numpy as jnp
from jax import lax
from jax.sharding import PartitionSpec as P

norm_eps = 1e-06


def shards(
    tokens, norm_gain, router_weight, gate_proj, up_proj, down_proj, expert_ids, slots, capacity
):
    tok_rows, shard_width = tokens.shape
    model_width = norm_gain.shape[0]
    experts = router_weight.shape[1]
    n_mp = model_width // shard_width
    slot_count = 4 * tok_rows // (3 * experts)
    cells = experts * slot_count
    me = lax.axis_index("expert")

    onehot = expert_ids[:, None] == jnp.arange(experts, dtype=jnp.int32)[None, :]
    cap_token = jnp.sum(jnp.where(onehot, capacity[None, :], 0), axis=1)
    kept_rows = slots < cap_token
    target = expert_ids * slot_count + slots
    route = (
        (target[:, None] == jnp.arange(cells, dtype=jnp.int32)[None, :]) & kept_rows[:, None]
    ).astype(jnp.bfloat16)

    masked = lax.dot_general(
        route, tokens, (((0,), (0,)), ((), ())), preferred_element_type=jnp.float32
    ).astype(jnp.bfloat16)
    received = lax.all_to_all(
        masked.reshape(experts, slot_count, shard_width),
        "expert",
        split_axis=0,
        concat_axis=0,
        tiled=True,
    ).reshape(cells, shard_width)
    whole = lax.all_gather(received, "mp", axis=0, tiled=False)

    features = whole.astype(jnp.float32)
    mean_square = jnp.sum(features * features, axis=(0, 2)) / model_width
    scale = lax.rsqrt(mean_square + norm_eps)
    gain = norm_gain.reshape(n_mp, 1, shard_width)
    normed = (features * scale[None, :, None] * gain).astype(jnp.bfloat16)

    logits = lax.dot_general(
        normed,
        router_weight.reshape(n_mp, shard_width, experts),
        (((0, 2), (0, 1)), ((), ())),
        preferred_element_type=jnp.float32,
    )
    picked = jnp.sum(
        jnp.where(jnp.arange(experts, dtype=jnp.int32)[None, :] == me, logits, 0.0), axis=1
    )
    gate_prob = jax.nn.sigmoid(picked)

    ff_local = gate_proj.shape[2]
    w_gate = gate_proj[0].reshape(n_mp, shard_width, ff_local)
    w_up = up_proj[0].reshape(n_mp, shard_width, ff_local)
    dims = (((0, 2), (0, 1)), ((), ()))
    pre_gate = lax.dot_general(normed, w_gate, dims, preferred_element_type=jnp.float32)
    pre_up = lax.dot_general(normed, w_up, dims, preferred_element_type=jnp.float32)
    hidden = (jax.nn.gelu(pre_gate, approximate=True) * pre_up).astype(jnp.bfloat16)
    block_out = jnp.dot(hidden, down_proj[0], preferred_element_type=jnp.float32).astype(
        jnp.bfloat16
    )
    summed = lax.psum_scatter(block_out, "mp", scatter_dimension=1, tiled=True)
    gated = (gate_prob[:, None] * summed.astype(jnp.float32)).astype(jnp.bfloat16)

    returned = lax.all_to_all(
        gated.reshape(experts, slot_count, shard_width),
        "expert",
        split_axis=0,
        concat_axis=0,
        tiled=True,
    ).reshape(cells, shard_width)
    update = jnp.dot(route, returned, preferred_element_type=jnp.float32)
    return update.astype(jnp.bfloat16)


def solution(mesh):
    in_specs = (
        P("expert", "mp"),
        P(),
        P(),
        P("expert", None, "mp"),
        P("expert", None, "mp"),
        P("expert", "mp", None),
        P("expert"),
        P("expert"),
        P(),
    )
    out_specs = P("expert", "mp")
    return jax.shard_map(shards, mesh=mesh, in_specs=in_specs, out_specs=out_specs, check_vma=False)
```

time: 364 us -> 268 us (0.74)
  blocking collectives: 103 us -> 42.5 us
  local copies, waits for them, and re-layouts: 30.2 us -> 10.4 us
  waiting for transfers between devices: 184 us -> 175 us
  starting transfers between devices: 7.39 us -> 0.04 us
  matrix products: 14 us -> 19.1 us
  other arithmetic: 10.4 us -> 5.79 us
    all_to_all x1 -> x2, blocking collectives: 103 us -> 42.5 us  [the longest x1 22.4 us: shards(): lax.all_to_all(masked.reshape(experts, slot_count, shard_width), 'expert'...]
    gather x2 -> x0, local copies, waits for them, and re-layouts: 13 us -> none  [the longest x1 11.1 us: shards(): taken = jnp.take(normed, owner, axis=0)]
    all_to_all x1 -> x0, waiting for transfers between devices: 10.2 us -> none  [shards(): lax.all_to_all(expert_out, 'expert', split_axis=0, concat_axis=0, tiled=T...]
    all_to_all x1 -> x0, starting transfers between devices: 7.35 us -> none  [shards(): lax.all_to_all(expert_out, 'expert', split_axis=0, concat_axis=0, tiled=T...]
    scatter x2 -> x0, local copies, waits for them, and re-layouts: 6.75 us -> none  [the longest x1 3.38 us: shards(): jnp.zeros((experts * slot_count,), jnp.bool_).at[target].set(kept_rows)]
    dot_general x3 -> x5, matrix products: 14 us -> 19.1 us  [the longest x1 7.75 us: shards(): jnp.dot(hidden, down_proj[0], preferred_element_type=jnp.float32)]
    unnamed x18 -> x16, local copies, waits for them, and re-layouts: 10.3 us -> 10.4 us
  transfers between devices with their start and end apart: 3 -> 2, of which waited for: 3 -> 2; matrix products, arithmetic and copies ran while one was open for 3% -> 2% of each run, Pallas kernels for 0% -> 0%
where the time goes in v1:
time: 268 us; the launch traced here: 266 us
  waiting for transfers between devices  175 us (65%)
  blocking collectives  42.5 us (16%)
  matrix products  19.1 us (7%)
  between operations  13.5 us (5%)
  local copies, waits for them, and re-layouts  10.4 us (4%)
  other arithmetic  5.79 us (2%)
    unnamed x3, waiting for transfers between devices  93.8 us
    all_gather x1, waiting for transfers between devices, shards(): whole = lax.all_gather(received, 'mp', axis=0, tiled=False)  80.9 us
    all_to_all x1, blocking collectives, shards(): lax.all_to_all(masked.reshape(experts, slot_count, shard_width), 'expert'...  22.4 us
    all_to_all x1, blocking collectives, shards(): lax.all_to_all(gated.reshape(experts, slot_count, shard_width), 'expert',...  20.1 us
    unnamed x16, local copies, waits for them, and re-layouts  10.4 us
    dot_general x1, matrix products, shards(): jnp.dot(hidden, down_proj[0], preferred_element_type=jnp.float32)  7.75 us
  transfers between devices with their start and end apart: 2, of which 2 were waited for; matrix products, arithmetic and copies ran while one was open for 2% of the time, Pallas kernels for 0%

profile of v1, /device:TPU:6, one launch (start us, length us, event | category | flops | bytes accessed | tf_op | source)
XLA Modules:
  0.0 265.9 jit_solution(7734337664534413390)
XLA Ops:
  6.5 0.9 multiply_add_fusion
  7.4 0.8 select_reduce_fusion
  8.2 0.7 lt.3
  8.9 2.1 fusion.24
  11.0 22.4 %all_to_all.10 = bf16[32,32,128]{2,1,0:T(8,128)(2,1)} all-to-all(bf16[32,32,128]{2,1,0:T(8,128)(2,1)S(1)} %bitcast.54), channel_id=1, replica_groups=mesh['expert'=32,'mp'=16] {'expert'}, dimensions={0} | all-to-all | bytes 524288 | tf_op jit(solution)/shard_map/all_to_all | solution.py:31
  33.4 0.0 all-gather.2.cloned.1.call-update
  33.4 0.0 reduce-scatter.4.cloned.1.call-start
  33.5 1.4 copy.20
  34.9 0.1 copy-done.3
  35.0 0.3 copy.21
  35.3 80.9 %all-gather.2.cloned.1.call-done = bf16[16,1024,128]{2,1,0:T(8,128)(2,1)} async-done(((bf16[1,1024,128]{2,1,0:T(8,128)(2,1)}), bf16[16,1024,128]{2,1,0:T(8,128)(2,1)}) %all-gather.2.cloned.1.call-update) | async-done | bytes 4194320 | tf_op jit(solution)/shard_map/all_gather | solution.py:38
  116.2 3.2 %fusion = f32[1024]{0:T(1024)S(1)} fusion(bf16[16,1024,128]{2,1,0:T(8,128)(2,1)} %all-gather.2.cloned.1.call-done), kind=kLoop, calls=%fused_computation.2 | loop fusion | flops 6290432 | bytes 4198400 | tf_op jit(solution)/shard_map/reduce_sum | solution.py:41
  119.4 0.2 copy-done.1
  119.6 4.1 %convolution_bitcast_fusion.1 = f32[1024,320]{0,1:T(8,128)} fusion(bf16[16,128,320]{1,0,2:T(8,128)(2,1)} %bitcast.49, bf16[16,1024,128]{2,1,0:T(8,128)(2,1)S(1)} %copy-done.1, f32[16,128]{1,0:T(8,128)S(1)} %bitcast.55, f32[1024]{0:T(1024)S(1)} %add_rsqrt_fusion), kind=kOutput, calls=%fused_computation.17 | convolution fusion | flops 1350565888 | bytes 6828032 | tf_op jit(solution)/shard_map/dot_general | solution.py:61
  123.8 7.8 %convolution_convert_fusion = bf16[1024,2048]{1,0:T(8,128)(2,1)} fusion(bf16[1,320,2048]{2,1,0:T(8,128)(2,1)S(1)} %copy-done, f32[1024,320]{0,1:T(8,128)} %convolution_bitcast_fusion.1, bf16[16,128,320]{1,0,2:T(8,128)(2,1)S(1)} %bitcast.48, bf16[16,1024,128]{2,1,0:T(8,128)(2,1)} %all-gather.2.cloned.1.call-done, f32[16,128]{1,0:T(8,128)S(1)} %bitcast.56, ...), kind=kOutput, calls=%fused_computation.5 | convolution fusion | flops 2698117120 | bytes 12333056 | tf_op jit(solution)/shard_map/dot_general | solution.py:64
  131.5 6.4 %copy.17 = bf16[1024,2048]{0,1:T(8,128)(2,1)} copy(bf16[1024,2048]{1,0:T(8,128)(2,1)} %convolution_convert_fusion) | data formatting | bytes 8388608
  137.9 0.0 reduce-scatter.4.cloned.1.call-update
  138.0 0.9 copy-done.4
  138.8 3.6 %fusion.31 = f32[1024]{0:T(1024)S(1)} fusion(pred[32]{0:T(512)(128)(4,1)S(1)} %iota_compare_fusion.2, bf16[16,1024,128]{2,1,0:T(8,128)(2,1)} %all-gather.2.cloned.1.call-done, f32[16,128]{1,0:T(8,128)S(1)} %bitcast.57, f32[1024]{0:T(1024)S(1)} %add_rsqrt_fusion, bf16[2048,32]{0,1:T(8,128)(2,1)S(1)} %copy-done.4), kind=kOutput, calls=%fused_computation.33 | convolution fusion | flops 142670848 | bytes 4341792 | tf_op jit(solution)/shard_map/dot_general | solution.py:46
  142.5 93.7 %reduce-scatter.4.cloned.1.call-done = bf16[128,1024]{1,0:T(8,128)(2,1)} async-done(((bf16[2048,1024]{1,0:T(8,128)(2,1)}), bf16[128,1024]{1,0:T(8,128)(2,1)}) %reduce-scatter.4.cloned.1.call-update) | async-done | bytes 262160
  236.2 1.1 copy.18
  237.3 0.2 multiply_convert_fusion
  237.6 20.1 %all_to_all.11 = bf16[32,32,128]{2,1,0:T(8,128)(2,1)S(1)} all-to-all(bf16[32,32,128]{2,1,0:T(8,128)(2,1)S(1)} %bitcast.51), channel_id=1, replica_groups=mesh['expert'=32,'mp'=16] {'expert'}, dimensions={0} | all-to-all | bytes 524288 | tf_op jit(solution)/shard_map/all_to_all | solution.py:70
  257.7 1.5 fusion.27
  (13 shorter events, 0.0 us)
Async XLA Ops:
  6.5 117.2 %copy-start = (bf16[1,320,2048]{2,1,0:T(8,128)(2,1)S(1)}, bf16[1,320,2048]{2,1,0:T(8,128)(2,1)}, u32[]{:S(2)}) copy-start(bf16[1,320,2048]{2,1,0:T(8,128)(2,1)} %param.14) | copy-start | bytes 3932164
  6.5 27.0 %copy-start.2 = (bf16[1,2048,320]{1,2,0:T(8,128)(2,1)S(1)}, bf16[1,2048,320]{1,2,0:T(8,128)(2,1)}, u32[]{:S(2)}) copy-start(bf16[1,2048,320]{1,2,0:T(8,128)(2,1)} %param.12) | copy-start | bytes 3932164
  6.5 109.6 %all-gather.2.cloned.1.call-start = ((), (), s32[]{:S(2)}) async-start(), calls=%async_computation.3 | async-start | bytes 4456448 | tf_op jit(solution)/shard_map/all_gather | solution.py:38
  33.4 202.8 %reduce-scatter.4.cloned.1.call-start = ((), (), s32[]{:S(2)}) async-start(), calls=%async_computation.4 | async-start | bytes 4456448
  33.5 1.5 copy-start.3
  35.0 84.5 %copy-start.5 = (f32[2048]{0:T(1024)S(1)}, f32[2048]{0:T(1024)}, u32[]{:S(2)}) copy-start(f32[2048]{0:T(1024)} %param.10) | copy-start | bytes 24580
  116.2 3.4 %copy-start.1 = (bf16[16,1024,128]{2,1,0:T(8,128)(2,1)S(1)}, bf16[16,1024,128]{2,1,0:T(8,128)(2,1)}, u32[]{:S(2)}) copy-start(bf16[16,1024,128]{2,1,0:T(8,128)(2,1)} %all-gather.2.cloned.1.call-done) | copy-start | bytes 12582916
  137.9 0.9 copy-start.4
Sparse Core Ops, SparseCore 0:
  33.6 82.5 all-gather.1
  138.1 98.0 reduce-scatter.3

commit v2 on v1

--- a/solution.py
+++ b/solution.py
@@ -1,7 +1,7 @@
 import jax
 import jax.numpy as jnp
 from jax import lax
-from jax.sharding import PartitionSpec as P
+from jax.sharding import Mesh, PartitionSpec as P
 
 norm_eps = 1e-06
 
@@ -35,7 +35,8 @@
         concat_axis=0,
         tiled=True,
     ).reshape(cells, shard_width)
-    whole = lax.all_gather(received, "mp", axis=0, tiled=False)
+    part = lax.all_gather(received, "mz", axis=0, tiled=False)
+    whole = lax.all_gather(part, "mx", axis=0, tiled=False).reshape(n_mp, cells, shard_width)
 
     features = whole.astype(jnp.float32)
     mean_square = jnp.sum(features * features, axis=(0, 2)) / model_width
@@ -64,7 +65,8 @@
     block_out = jnp.dot(hidden, down_proj[0], preferred_element_type=jnp.float32).astype(
         jnp.bfloat16
     )
-    summed = lax.psum_scatter(block_out, "mp", scatter_dimension=1, tiled=True)
+    half = lax.psum_scatter(block_out, "mx", scatter_dimension=1, tiled=True)
+    summed = lax.psum_scatter(half, "mz", scatter_dimension=1, tiled=True)
     gated = (gate_prob[:, None] * summed.astype(jnp.float32)).astype(jnp.bfloat16)
 
     returned = lax.all_to_all(
@@ -79,16 +81,20 @@
 
 
 def solution(mesh):
+    n_expert, n_mp = mesh.devices.shape
+    n_x = len({device.coords[0] for device in mesh.devices[0]})
+    split = Mesh(mesh.devices.reshape(n_expert, n_x, n_mp // n_x), ("expert", "mx", "mz"))
+    mp = ("mx", "mz")
     in_specs = (
-        P("expert", "mp"),
+        P("expert", mp),
         P(),
         P(),
-        P("expert", None, "mp"),
-        P("expert", None, "mp"),
-        P("expert", "mp", None),
+        P("expert", None, mp),
+        P("expert", None, mp),
+        P("expert", mp, None),
         P("expert"),
         P("expert"),
         P(),
     )
-    out_specs = P("expert", "mp")
-    return jax.shard_map(shards, mesh=mesh, in_specs=in_specs, out_specs=out_specs, check_vma=False)
+    out_specs = P("expert", mp)
+    return jax.shard_map(shards, mesh=split, in_specs=in_specs, out_specs=out_specs, check_vma=False)

time: 268 us -> 263 us (0.981)
  local copies, waits for them, and re-layouts: 10.4 us -> 5.41 us
    unnamed x3 -> x5, waiting for transfers between devices: 93.8 us -> 35.5 us
    reduce_scatter x0 -> x1, waiting for transfers between devices: none -> 52.6 us  [shards(): half = lax.psum_scatter(block_out, 'mx', scatter_dimension=1, tiled=True)]
    all_gather x1 -> x2, waiting for transfers between devices: 80.9 us -> 87.2 us  [the longest x1 51.5 us: shards(): lax.all_gather(part, 'mx', axis=0, tiled=False)]
    unnamed x16 -> x20, local copies, waits for them, and re-layouts: 10.4 us -> 5.41 us
  transfers between devices with their start and end apart: 2 -> 4, of which waited for: 2 -> 4; matrix products, arithmetic and copies ran while one was open for 2% -> 2% of each run, Pallas kernels for 0% -> 0%
where the time goes in v2:
time: 263 us
  waiting for transfers between devices  175 us (67%)
  blocking collectives  43.5 us (17%)
  matrix products  18.2 us (7%)
  between operations  13.3 us (5%)
  other arithmetic  7.12 us (3%)
  local copies, waits for them, and re-layouts  5.41 us (2%)
    reduce_scatter x1, waiting for transfers between devices, shards(): half = lax.psum_scatter(block_out, 'mx', scatter_dimension=1, tiled=True)  52.6 us
    all_gather x1, waiting for transfers between devices, shards(): lax.all_gather(part, 'mx', axis=0, tiled=False)  51.5 us
    all_gather x1, waiting for transfers between devices, shards(): part = lax.all_gather(received, 'mz', axis=0, tiled=False)  35.7 us
    unnamed x5, waiting for transfers between devices  35.5 us
    all_to_all x1, blocking collectives, shards(): lax.all_to_all(masked.reshape(experts, slot_count, shard_width), 'expert'...  22.5 us
    all_to_all x1, blocking collectives, shards(): lax.all_to_all(gated.reshape(experts, slot_count, shard_width), 'expert',...  21 us
    dot_general x1, matrix products, shards(): jnp.dot(hidden, down_proj[0], preferred_element_type=jnp.float32)  8.39 us
    unnamed x20, local copies, waits for them, and re-layouts  5.41 us
  transfers between devices with their start and end apart: 4, of which 4 were waited for; matrix products, arithmetic and copies ran while one was open for 2% of the time, Pallas kernels for 0%

profile of v2, /device:TPU:6, one launch (start us, length us, event | category | flops | bytes accessed | tf_op | source)
XLA Modules:
  0.0 262.8 jit_solution(10527546903721437285)
XLA Ops:
  6.5 0.9 select_reduce_fusion
  7.4 0.7 multiply_add_fusion
  8.1 0.7 lt.3
  8.8 2.1 fusion.24
  11.0 22.5 %all_to_all.10 = bf16[32,32,128]{2,1,0:T(8,128)(2,1)} all-to-all(bf16[32,32,128]{2,1,0:T(8,128)(2,1)S(1)} %bitcast.65), channel_id=1, replica_groups=mesh['expert'=32,'mx'=4,'mz'=4] {'expert'}, dimensions={0} | all-to-all | bytes 524288 | tf_op jit(solution)/shard_map/all_to_all | solution.py:31
  33.6 35.7 %all-gather.4.cloned.1.call-done = bf16[4,1024,128]{2,1,0:T(8,128)(2,1)} async-done(((bf16[1,1024,128]{2,1,0:T(8,128)(2,1)}), bf16[4,1024,128]{2,1,0:T(8,128)(2,1)}) %all-gather.4.cloned.1.call-update) | async-done | bytes 1048592 | tf_op jit(solution)/shard_map/all_gather | solution.py:38
  69.4 1.4 copy.20
  70.7 0.1 copy-done.4
  70.9 0.3 copy.21
  71.2 51.5 %all-gather.6.cloned.1.call-done = bf16[16,1024,128]{2,1,0:T(8,128)(2,1)} async-done(((bf16[4,1024,128]{2,1,0:T(8,128)(2,1)}), bf16[16,1024,128]{2,1,0:T(8,128)(2,1)}) %all-gather.6.cloned.1.call-update) | async-done | bytes 4194320 | tf_op jit(solution)/shard_map/all_gather | solution.py:39
  122.6 3.2 %fusion = f32[1024]{0:T(1024)S(1)} fusion(bf16[4,4,1024,128]{3,2,1,0:T(8,128)(2,1)} %bitcast.55), kind=kLoop, calls=%fused_computation.2 | loop fusion | flops 6290432 | bytes 4198400 | tf_op jit(solution)/shard_map/reduce_sum | solution.py:42
  125.9 0.2 copy-done.2
  126.1 1.4 fusion.2
  127.5 2.7 %convolution_bitcast_fusion.1 = f32[1024,320]{0,1:T(8,128)} fusion(bf16[16,1024,128]{2,1,0:T(8,128)(2,1)S(1)} %bitcast.52, bf16[16,128,320]{1,0,2:T(8,128)(2,1)S(1)} %bitcast.60), kind=kOutput, calls=%fused_computation.17 | convolution fusion | flops 1342177280 | bytes 6815744 | tf_op jit(solution)/shard_map/dot_general | solution.py:62
  130.2 8.4 %convolution_convert_fusion = bf16[1024,2048]{1,0:T(8,128)(2,1)} fusion(bf16[1,320,2048]{2,1,0:T(8,128)(2,1)S(1)} %copy-done, bf16[16,1024,128]{2,1,0:T(8,128)(2,1)} %bitcast.53, f32[1024,320]{0,1:T(8,128)} %convolution_bitcast_fusion.1, bf16[16,128,320]{1,0,2:T(8,128)(2,1)S(1)} %bitcast.59), kind=kOutput, calls=%fused_computation.5 | convolution fusion | flops 2689728512 | bytes 12320768 | tf_op jit(solution)/shard_map/dot_general | solution.py:65
  138.6 0.0 reduce-scatter.7.cloned.1.call-start
  138.7 52.6 %reduce-scatter.5.cloned.1.call-done = bf16[1024,512]{1,0:T(8,128)(2,1)} async-done(((bf16[1024,2048]{1,0:T(8,128)(2,1)}), bf16[1024,512]{1,0:T(8,128)(2,1)}) %reduce-scatter.5.cloned.1.call-update) | async-done | bytes 1048592 | tf_op jit(solution)/shard_map/reduce_scatter | solution.py:68
  191.2 2.3 copy.17
  193.6 3.5 %fusion.31 = f32[1024]{0:T(1024)S(1)} fusion(bf16[16,1024,128]{2,1,0:T(8,128)(2,1)} %bitcast.54, pred[32]{0:T(512)(128)(4,1)S(1)} %iota_compare_fusion.2, bf16[2048,32]{0,1:T(8,128)(2,1)S(1)} %copy-done.6), kind=kOutput, calls=%fused_computation.33 | convolution fusion | flops 134282240 | bytes 4329504 | tf_op jit(solution)/shard_map/dot_general | solution.py:47
  197.1 35.4 %reduce-scatter.7.cloned.1.call-done = bf16[128,1024]{1,0:T(8,128)(2,1)} async-done(((bf16[512,1024]{1,0:T(8,128)(2,1)}), bf16[128,1024]{1,0:T(8,128)(2,1)}) %reduce-scatter.7.cloned.1.call-update) | async-done | bytes 262160
  232.5 1.1 copy.18
  233.6 0.2 multiply_convert_fusion
  233.9 21.0 %all_to_all.11 = bf16[32,32,128]{2,1,0:T(8,128)(2,1)S(1)} all-to-all(bf16[32,32,128]{2,1,0:T(8,128)(2,1)S(1)} %bitcast.62), channel_id=1, replica_groups=mesh['expert'=32,'mx'=4,'mz'=4] {'expert'}, dimensions={0} | all-to-all | bytes 524288 | tf_op jit(solution)/shard_map/all_to_all | solution.py:72
  254.9 1.5 fusion.27
  (24 shorter events, 0.2 us)
Async XLA Ops:
  6.5 123.7 %copy-start = (bf16[1,320,2048]{2,1,0:T(8,128)(2,1)S(1)}, bf16[1,320,2048]{2,1,0:T(8,128)(2,1)}, u32[]{:S(2)}) copy-start(bf16[1,320,2048]{2,1,0:T(8,128)(2,1)} %param.14) | copy-start | bytes 3932164
  6.5 62.8 %all-gather.4.cloned.1.call-start = ((), (), s32[]{:S(2)}) async-start(), calls=%async_computation.4 | async-start | bytes 1310720 | tf_op jit(solution)/shard_map/all_gather | solution.py:38
  11.0 58.4 %copy-start.3 = (bf16[1,2048,320]{1,2,0:T(8,128)(2,1)S(1)}, bf16[1,2048,320]{1,2,0:T(8,128)(2,1)}, u32[]{:S(2)}) copy-start(bf16[1,2048,320]{1,2,0:T(8,128)(2,1)} %param.12) | copy-start | bytes 3932164
  33.5 89.1 %all-gather.6.cloned.1.call-start = ((), (), s32[]{:S(2)}) async-start(), calls=%async_computation.6 | async-start | bytes 5242880 | tf_op jit(solution)/shard_map/all_gather | solution.py:39
  69.3 121.9 %reduce-scatter.5.cloned.1.call-start = ((), (), s32[]{:S(2)}) async-start(), calls=%async_computation.5 | async-start | bytes 5242880 | tf_op jit(solution)/shard_map/reduce_scatter | solution.py:68
  69.4 1.5 copy-start.4
  122.6 3.4 %copy-start.2 = (bf16[16,1024,128]{2,1,0:T(8,128)(2,1)S(1)}, bf16[16,1024,128]{2,1,0:T(8,128)(2,1)}, u32[]{:S(2)}) copy-start(bf16[16,1024,128]{2,1,0:T(8,128)(2,1)} %all-gather.6.cloned.1.call-done) | copy-start | bytes 12582916
  122.6 3.4 %copy-start.7 = (f32[2048]{0:T(1024)S(1)}, f32[2048]{0:T(1024)}, u32[]{:S(2)}) copy-start(f32[2048]{0:T(1024)} %param.10) | copy-start | bytes 24580
  126.1 1.4 copy-start.5
  127.5 2.7 %copy-start.1 = (bf16[4,4,1024,128]{3,2,1,0:T(8,128)(2,1)}, bf16[4,4,1024,128]{3,2,1,0:T(8,128)(2,1)S(1)}, u32[]{:S(2)}) copy-start(bf16[4,4,1024,128]{3,2,1,0:T(8,128)(2,1)S(1)} %fusion.2) | copy-start | bytes 12582916
  138.6 54.9 %copy-start.6 = (bf16[2048,32]{0,1:T(8,128)(2,1)S(1)}, bf16[2048,32]{0,1:T(8,128)(2,1)}, u32[]{:S(2)}) copy-start(bf16[2048,32]{0,1:T(8,128)(2,1)} %param.11) | copy-start | bytes 393220
  138.6 93.9 %reduce-scatter.7.cloned.1.call-start = ((), (), s32[]{:S(2)}) async-start(), calls=%async_computation.7 | async-start | bytes 1310720
Sparse Core Ops, SparseCore 0:
  33.7 35.5 all-gather.3
  71.4 51.1 all-gather.5
  138.7 52.4 reduce-scatter.4
  194.2 38.2 reduce-scatter.6

commit v3 on v2

--- a/solution.py
+++ b/solution.py
@@ -4,6 +4,53 @@
 from jax.sharding import Mesh, PartitionSpec as P
 
 norm_eps = 1e-06
+
+
+def shift(value, axis, n, step):
+    return lax.ppermute(value, axis, [(i, (i + step) % n) for i in range(n)])
+
+
+def ring_gather(block, axis, n):
+    if n == 1:
+        return block[None]
+    me = lax.axis_index(axis)
+    half = block.shape[0] // 2
+    pieces = [None] * n
+    pieces[0] = block
+    rightward = leftward = block
+    for step in range(1, (n + 1) // 2):
+        rightward = shift(rightward, axis, n, 1)
+        leftward = shift(leftward, axis, n, -1)
+        pieces[n - step] = rightward
+        pieces[step] = leftward
+    if n % 2 == 0:
+        first = shift(rightward[:half], axis, n, 1)
+        second = shift(leftward[half:], axis, n, -1)
+        pieces[n // 2] = jnp.concatenate([first, second], axis=0)
+    return jnp.roll(jnp.stack(pieces), me, axis=0)
+
+
+def ring_reduce_scatter(parts, axis, n):
+    if n == 1:
+        return parts[:, 0].astype(jnp.float32)
+    me = lax.axis_index(axis)
+    half = parts.shape[0] // 2
+
+    def term(dest, lower):
+        rows = parts[:half] if lower else parts[half:]
+        return lax.dynamic_index_in_dim(rows, dest % n, axis=1, keepdims=False)
+
+    results = []
+    for lower, direction in ((True, 1), (False, -1)):
+        carried = term(me - direction, lower)
+        for step in range(1, n):
+            arrived = shift(carried, axis, n, direction)
+            total = arrived.astype(jnp.float32) + term(
+                me - direction * (step + 1), lower
+            ).astype(jnp.float32)
+            carried = total.astype(parts.dtype) if step < n - 1 else total
+        results.append(carried)
+    return jnp.concatenate(results, axis=0)
 
 
 def shards(
@@ -35,8 +82,10 @@
         concat_axis=0,
         tiled=True,
     ).reshape(cells, shard_width)
-    part = lax.all_gather(received, "mz", axis=0, tiled=False)
-    whole = lax.all_gather(part, "mx", axis=0, tiled=False).reshape(n_mp, cells, shard_width)
+    n_z = lax.psum(1, "mz")
+    n_x = n_mp // n_z
+    part = ring_gather(received, "mz", n_z)
+    whole = ring_gather(part, "mx", n_x).reshape(n_mp, cells, shard_width)
 
     features = whole.astype(jnp.float32)
     mean_square = jnp.sum(features * features, axis=(0, 2)) / model_width
@@ -65,8 +114,10 @@
     block_out = jnp.dot(hidden, down_proj[0], preferred_element_type=jnp.float32).astype(
         jnp.bfloat16
     )
-    half = lax.psum_scatter(block_out, "mx", scatter_dimension=1, tiled=True)
-    summed = lax.psum_scatter(half, "mz", scatter_dimension=1, tiled=True)
+    across_x = ring_reduce_scatter(block_out.reshape(cells, n_x, -1), "mx", n_x)
+    summed = ring_reduce_scatter(
+        across_x.astype(jnp.bfloat16).reshape(cells, n_z, shard_width), "mz", n_z
+    ).astype(jnp.bfloat16)
     gated = (gate_prob[:, None] * summed.astype(jnp.float32)).astype(jnp.bfloat16)
 
     returned = lax.all_to_all(

time: 263 us -> 260 us (0.989)
  waiting for transfers between devices: 175 us -> 62.7 us
  starting transfers between devices: 0.12 us -> 71.3 us
  local copies, waits for them, and re-layouts: 5.41 us -> 39.7 us
  other arithmetic: 7.12 us -> 22.3 us
  between operations: 13.3 us -> 0.94 us
    all_gather x2 -> x0, waiting for transfers between devices: 87.2 us -> none  [the longest x1 51.5 us: shards(): lax.all_gather(part, 'mx', axis=0, tiled=False)]
    ppermute x0 -> x20, starting transfers between devices: none -> 71.3 us  [shift(): return lax.ppermute(value, axis, [(i, (i + step) % n) for i in range(n)])]
    ppermute x0 -> x20, waiting for transfers between devices: none -> 62.7 us  [shift(): return lax.ppermute(value, axis, [(i, (i + step) % n) for i in range(n)])]
    reduce_scatter x1 -> x0, waiting for transfers between devices: 52.6 us -> none  [shards(): half = lax.psum_scatter(block_out, 'mx', scatter_dimension=1, tiled=True)]
    unnamed x5 -> x0, waiting for transfers between devices: 35.5 us -> none
    slice x0 -> x9, local copies, waits for them, and re-layouts: none -> 13.5 us  [the longest x5 11.8 us: term(): rows = parts[:half] if lower else parts[half:]]
    dynamic_slice x0 -> x5, local copies, waits for them, and re-layouts: none -> 12.8 us  [term(): return lax.dynamic_index_in_dim(rows, dest % n, axis=1, keepdims=False)]
    unnamed x20 -> x64, local copies, waits for them, and re-layouts: 5.41 us -> 12.2 us
  transfers between devices with their start and end apart: 4 -> 20, of which waited for: 4 -> 14; matrix products, arithmetic and copies ran while one was open for 2% -> 11% of each run, Pallas kernels for 0% -> 0%
where the time goes in v3:
time: 260 us; the launch traced here: 258 us
  starting transfers between devices  71.3 us (27%)
  waiting for transfers between devices  62.7 us (24%)
  blocking collectives  45.5 us (18%)
  local copies, waits for them, and re-layouts  39.7 us (15%)
  other arithmetic  22.3 us (9%)
  matrix products  16 us (6%)
    ppermute x20, starting transfers between devices, shift(): return lax.ppermute(value, axis, [(i, (i + step) % n) for i in range(n)])  71.3 us
    ppermute x20, waiting for transfers between devices, shift(): return lax.ppermute(value, axis, [(i, (i + step) % n) for i in range(n)])  62.7 us
    all_to_all x1, blocking collectives, shards(): lax.all_to_all(gated.reshape(experts, slot_count, shard_width), 'expert',...  23.2 us
    all_to_all x1, blocking collectives, shards(): lax.all_to_all(masked.reshape(experts, slot_count, shard_width), 'expert'...  22.3 us
    dynamic_slice x5, local copies, waits for them, and re-layouts, term(): return lax.dynamic_index_in_dim(rows, dest % n, axis=1, keepdims=False)  12.8 us
    unnamed x64, local copies, waits for them, and re-layouts  12.2 us
    slice x5, local copies, waits for them, and re-layouts, term(): rows = parts[:half] if lower else parts[half:]  11.8 us
    dot_general x1, matrix products, shards(): jnp.dot(hidden, down_proj[0], preferred_element_type=jnp.float32)  8.44 us
  transfers between devices with their start and end apart: 20, of which 14 were waited for; matrix products, arithmetic and copies ran while one was open for 11% of the time, Pallas kernels for 0%

profile of v3, /device:TPU:6, one launch (start us, length us, event | category | flops | bytes accessed | tf_op | source)
XLA Modules:
  0.0 258.5 jit_solution(17537472587066873233)
XLA Ops:
  4.5 22.3 %all_to_all.10 = bf16[32,32,128]{2,1,0:T(8,128)(2,1)S(1)} all-to-all(bf16[32,32,128]{2,1,0:T(8,128)(2,1)S(1)} %bitcast.159), channel_id=1, replica_groups=mesh['expert'=32,'mx'=4,'mz'=4] {'expert'}, dimensions={0} | all-to-all | bytes 524288 | tf_op jit(solution)/shard_map/all_to_all | solution.py:78
  26.7 6.1 %collective-permute-start.1 = (bf16[1024,128]{1,0:T(8,128)(2,1)S(1)}, bf16[1024,128]{1,0:T(8,128)(2,1)S(1)}, u32[]{:S(2)}, u32[]{:S(2)}) collective-permute-start(bf16[1024,128]{1,0:T(8,128)(2,1)S(1)} %bitcast.148), channel_id=1, source_target_pairs={{0,1},{1,2},{2,3},{3,0},{4,5},{5,6},{6,7},{7,4},{8,9},{9,10},{10,1... | collective-permute-start | bytes 786440 | tf_op jit(solution)/shard_map/ppermute | solution.py:10
  32.8 5.9 %collective-permute-start = (bf16[1024,128]{1,0:T(8,128)(2,1)S(1)}, bf16[1024,128]{1,0:T(8,128)(2,1)S(1)}, u32[]{:S(2)}, u32[]{:S(2)}) collective-permute-start(bf16[1024,128]{1,0:T(8,128)(2,1)S(1)} %bitcast.149), channel_id=1, source_target_pairs={{0,3},{1,0},{2,1},{3,2},{4,7},{5,4},{6,5},{7,6},{8,11},{9,8},{10,9... | collective-permute-start | bytes 786440 | tf_op jit(solution)/shard_map/ppermute | solution.py:10
  38.8 9.2 %collective-permute-done.1 = bf16[1024,128]{1,0:T(8,128)(2,1)S(1)} collective-permute-done((bf16[1024,128]{1,0:T(8,128)(2,1)S(1)}, bf16[1024,128]{1,0:T(8,128)(2,1)S(1)}, u32[]{:S(2)}, u32[]{:S(2)}) %collective-permute-start.1) | collective-permute-done | bytes 262176 | tf_op jit(solution)/shard_map/ppermute | solution.py:10
  49.9 6.0 %collective-permute-start.3 = (bf16[512,128]{1,0:T(8,128)(2,1)S(1)}, bf16[512,128]{1,0:T(8,128)(2,1)S(1)}, u32[]{:S(2)}, u32[]{:S(2)}) collective-permute-start(bf16[512,128]{1,0:T(8,128)(2,1)S(1)} %slice.61), channel_id=1, source_target_pairs={{0,3},{1,0},{2,1},{3,2},{4,7},{5,4},{6,5},{7,6},{8,11},{9,8},{10,9... | collective-permute-start | bytes 393224 | tf_op jit(solution)/shard_map/ppermute | solution.py:10
  63.3 3.5 %collective-permute-start.4 = (bf16[4,1024,128]{2,1,0:T(8,128)(2,1)S(1)}, bf16[4,1024,128]{2,1,0:T(8,128)(2,1)S(1)}, u32[]{:S(2)}, u32[]{:S(2)}) collective-permute-start(bf16[4,1024,128]{2,1,0:T(8,128)(2,1)S(1)} %get-tuple-element.6), channel_id=1, source_target_pairs={{0,12},{4,0},{8,4},{12,8},{1,13},{5,1},{9,5},{13,9},{2,14},{6,2},{... | collective-permute-start | bytes 3145736 | tf_op jit(solution)/shard_map/ppermute | solution.py:10
  66.8 20.4 %collective-permute-done.5 = bf16[4,1024,128]{2,1,0:T(8,128)(2,1)S(1)} collective-permute-done((bf16[4,1024,128]{2,1,0:T(8,128)(2,1)S(1)}, bf16[4,1024,128]{2,1,0:T(8,128)(2,1)S(1)}, u32[]{:S(2)}, u32[]{:S(2)}) %collective-permute-start.5) | collective-permute-done | bytes 1048608 | tf_op jit(solution)/shard_map/ppermute | solution.py:10
  88.0 3.6 %collective-permute-start.6 = (bf16[2,1024,128]{2,1,0:T(8,128)(2,1)}, bf16[2,1024,128]{2,1,0:T(8,128)(2,1)}, u32[]{:S(2)}, u32[]{:S(2)}) collective-permute-start(bf16[2,1024,128]{2,1,0:T(8,128)(2,1)} %slice.62), channel_id=1, source_target_pairs={{0,4},{4,8},{8,12},{12,0},{1,5},{5,9},{9,13},{13,1},{2,6},{6,10},{... | collective-permute-start | bytes 1572872 | tf_op jit(solution)/shard_map/ppermute | solution.py:10
  102.5 5.4 %collective-permute-done.7 = bf16[2,1024,128]{2,1,0:T(8,128)(2,1)} collective-permute-done((bf16[2,1024,128]{2,1,0:T(8,128)(2,1)}, bf16[2,1024,128]{2,1,0:T(8,128)(2,1)}, u32[]{:S(2)}, u32[]{:S(2)}) %collective-permute-start.7) | collective-permute-done | bytes 524320 | tf_op jit(solution)/shard_map/ppermute | solution.py:10
  119.8 3.8 %fusion.2 = bf16[4,4,1024,128]{3,2,1,0:T(8,128)(2,1)S(1)} fusion(f32[4,4,128]{2,1,0:T(4,128)S(1)} %bitcast.162, f32[1024]{0:T(1024)S(1)} %add_rsqrt_fusion, bf16[8,4,1024,128]{3,2,1,0:T(8,128)(2,1)} %bitcast_dynamic-update-slice_fusion.1, s32[]{:T(128)S(6)} %select_n.151), kind=kLoop, calls=%fused_computation.4 | loop fusion | flops 8388608 | bytes 8400900 | tf_op jit(solution)/shard_map/convert_element_type | solution.py:94
  126.3 8.4 %convolution_convert_fusion = bf16[1024,2048]{1,0:T(8,128)(2,1)} fusion(bf16[1,320,2048]{2,1,0:T(8,128)(2,1)S(1)} %copy-done, bf16[16,1024,128]{2,1,0:T(8,128)(2,1)} %bitcast.146, f32[1024,320]{0,1:T(8,128)} %convolution_bitcast_fusion.1, bf16[16,128,320]{1,0,2:T(8,128)(2,1)S(1)} %bitcast.155), kind=kOutput, calls=%fused_computation.5 | convolution fusion | flops 2689728512 | bytes 12320768 | tf_op jit(solution)/shard_map/dot_general | solution.py:114
  134.7 4.9 %fusion.61 = (bf16[512,2048]{1,0:T(8,128)(2,1)}, bf16[512,2048]{1,0:T(8,128)(2,1)}) fusion(bf16[1024,2048]{1,0:T(8,128)(2,1)} %convolution_convert_fusion), kind=kLoop, calls=%fused_computation.124 | loop fusion | bytes 8388608 | tf_op jit(solution)/shard_map/slice | solution.py:40
  142.9 5.4 %constant_dynamic-slice_fusion.12 = (bf16[512,1,512]{2,1,0:T(2,128)(2,1)}, bf16[512,1,512]{2,1,0:T(2,128)(2,1)}, bf16[512,1,512]{2,1,0:T(2,128)(2,1)}, bf16[512,1,512]{2,1,0:T(2,128)(2,1)S(1)}) fusion(bf16[512,4,512]{2,1,0:T(4,128)(2,1)S(1)} %slice.53, s32[]{:T(128)S(6)} %select_n.160, s32[]{:T(128)S(6)} %select_n.158, s32[]{:T(128)S(6)} %select_n.156, ...), kind=kLoop, calls=%fused_computation.111 | loop fusion | bytes 4194320 | tf_op jit(solution)/shard_map/jit(dynamic_index_in_dim)/dynamic_slice | solution.py:41
  154.7 5.4 %constant_dynamic-slice_fusion.4 = (bf16[512,1,512]{2,1,0:T(2,128)(2,1)}, bf16[512,1,512]{2,1,0:T(2,128)(2,1)}, bf16[512,1,512]{2,1,0:T(2,128)(2,1)}, bf16[512,1,512]{2,1,0:T(2,128)(2,1)S(1)}) fusion(bf16[512,4,512]{2,1,0:T(4,128)(2,1)S(1)} %slice.57, s32[]{:T(128)S(6)} %select_n.176, s32[]{:T(128)S(6)} %select_n.174, s32[]{:T(128)S(6)} %select_n.172, ...), kind=kLoop, calls=%fused_computation.103 | loop fusion | bytes 4194320 | tf_op jit(solution)/shard_map/jit(dynamic_index_in_dim)/dynamic_slice | solution.py:41
  161.1 3.9 %collective-permute-start.14 = (bf16[512,512]{1,0:T(8,128)(2,1)}, bf16[512,512]{1,0:T(8,128)(2,1)}, u32[]{:S(2)}, u32[]{:S(2)}) collective-permute-start(bf16[512,512]{1,0:T(8,128)(2,1)} %bitcast.140), channel_id=1, source_target_pairs={{0,12},{4,0},{8,4},{12,8},{1,13},{5,1},{9,5},{13,9},{2,14},{6,2},{... | collective-permute-start | bytes 1572872 | tf_op jit(solution)/shard_map/ppermute | solution.py:10
  170.4 5.1 %collective-permute-done.14 = bf16[512,512]{1,0:T(8,128)(2,1)} collective-permute-done((bf16[512,512]{1,0:T(8,128)(2,1)}, bf16[512,512]{1,0:T(8,128)(2,1)}, u32[]{:S(2)}, u32[]{:S(2)}) %collective-permute-start.14) | collective-permute-done | bytes 524320 | tf_op jit(solution)/shard_map/ppermute | solution.py:10
  181.1 4.8 %collective-permute-start.10 = (bf16[512,512]{1,0:T(8,128)(2,1)S(1)}, bf16[512,512]{1,0:T(8,128)(2,1)S(1)}, u32[]{:S(2)}, u32[]{:S(2)}) collective-permute-start(bf16[512,512]{1,0:T(8,128)(2,1)S(1)} %fusion.36), channel_id=1, source_target_pairs={{0,4},{4,8},{8,12},{12,0},{1,5},{5,9},{9,13},{13,1},{2,6},{6,10},{... | collective-permute-start | bytes 1572872 | tf_op jit(solution)/shard_map/ppermute | solution.py:10
  195.5 4.2 %collective-permute-start.11 = (bf16[512,128]{1,0:T(8,128)(2,1)S(1)}, bf16[512,128]{1,0:T(8,128)(2,1)}, u32[]{:S(2)}, u32[]{:S(2)}) collective-permute-start(bf16[512,128]{1,0:T(8,128)(2,1)S(1)} %bitcast.160), channel_id=1, source_target_pairs={{0,1},{1,2},{2,3},{3,0},{4,5},{5,6},{6,7},{7,4},{8,9},{9,10},{10,1... | collective-permute-start | bytes 393224 | tf_op jit(solution)/shard_map/ppermute | solution.py:10
  199.7 4.2 %collective-permute-done.16 = bf16[512,512]{1,0:T(8,128)(2,1)} collective-permute-done((bf16[512,512]{1,0:T(8,128)(2,1)}, bf16[512,512]{1,0:T(8,128)(2,1)}, u32[]{:S(2)}, u32[]{:S(2)}) %collective-permute-start.16) | collective-permute-done | bytes 524320 | tf_op jit(solution)/shard_map/ppermute | solution.py:10
  208.8 4.8 %collective-permute-start.12 = (bf16[512,128]{1,0:T(8,128)(2,1)S(1)}, bf16[512,128]{1,0:T(8,128)(2,1)S(1)}, u32[]{:S(2)}, u32[]{:S(2)}) collective-permute-start(bf16[512,128]{1,0:T(8,128)(2,1)S(1)} %fusion.52), channel_id=1, source_target_pairs={{0,1},{1,2},{2,3},{3,0},{4,5},{5,6},{6,7},{7,4},{8,9},{9,10},{10,1... | collective-permute-start | bytes 393224 | tf_op jit(solution)/shard_map/ppermute | solution.py:10
  216.8 3.5 %collective-permute-done.12 = bf16[512,128]{1,0:T(8,128)(2,1)S(1)} collective-permute-done((bf16[512,128]{1,0:T(8,128)(2,1)S(1)}, bf16[512,128]{1,0:T(8,128)(2,1)S(1)}, u32[]{:S(2)}, u32[]{:S(2)}) %collective-permute-start.12) | collective-permute-done | bytes 131104 | tf_op jit(solution)/shard_map/ppermute | solution.py:10
  224.2 4.1 %collective-permute-start.19 = (bf16[512,128]{1,0:T(8,128)(2,1)S(1)}, bf16[512,128]{1,0:T(8,128)(2,1)S(1)}, u32[]{:S(2)}, u32[]{:S(2)}) collective-permute-start(bf16[512,128]{1,0:T(8,128)(2,1)S(1)} %fusion.48), channel_id=1, source_target_pairs={{0,3},{1,0},{2,1},{3,2},{4,7},{5,4},{6,5},{7,6},{8,11},{9,8},{10,9... | collective-permute-start | bytes 393224 | tf_op jit(solution)/shard_map/ppermute | solution.py:10
  229.5 4.0 %collective-permute-done.19 = bf16[512,128]{1,0:T(8,128)(2,1)S(1)} collective-permute-done((bf16[512,128]{1,0:T(8,128)(2,1)S(1)}, bf16[512,128]{1,0:T(8,128)(2,1)S(1)}, u32[]{:S(2)}, u32[]{:S(2)}) %collective-permute-start.19) | collective-permute-done | bytes 131104 | tf_op jit(solution)/shard_map/ppermute | solution.py:10
  233.8 23.2 %all_to_all.11 = bf16[32,32,128]{2,1,0:T(8,128)(2,1)S(1)} all-to-all(bf16[32,32,128]{2,1,0:T(8,128)(2,1)S(1)} %fusion.46), channel_id=1, replica_groups=mesh['expert'=32,'mx'=4,'mz'=4] {'expert'}, dimensions={0} | all-to-all | bytes 524288 | tf_op jit(solution)/shard_map/all_to_all | solution.py:123
  (130 shorter events, 85.6 us)
Async XLA Ops:
  0.0 126.3 %copy-start = (bf16[1,320,2048]{2,1,0:T(8,128)(2,1)S(1)}, bf16[1,320,2048]{2,1,0:T(8,128)(2,1)}, u32[]{:S(2)}) copy-start(bf16[1,320,2048]{2,1,0:T(8,128)(2,1)} %param.14) | copy-start | bytes 3932164
  26.7 21.2 %collective-permute-start.1 = (bf16[1024,128]{1,0:T(8,128)(2,1)S(1)}, bf16[1024,128]{1,0:T(8,128)(2,1)S(1)}, u32[]{:S(2)}, u32[]{:S(2)}) collective-permute-start(bf16[1024,128]{1,0:T(8,128)(2,1)S(1)} %bitcast.148), channel_id=1, source_target_pairs={{0,1},{1,2},{2,3},{3,0},{4,5},{5,6},{6,7},{7,4},{8,9},{9,10},{10,1... | collective-permute-start | bytes 786440 | tf_op jit(solution)/shard_map/ppermute | solution.py:10
  32.8 17.1 %collective-permute-start = (bf16[1024,128]{1,0:T(8,128)(2,1)S(1)}, bf16[1024,128]{1,0:T(8,128)(2,1)S(1)}, u32[]{:S(2)}, u32[]{:S(2)}) collective-permute-start(bf16[1024,128]{1,0:T(8,128)(2,1)S(1)} %bitcast.149), channel_id=1, source_target_pairs={{0,3},{1,0},{2,1},{3,2},{4,7},{5,4},{6,5},{7,6},{8,11},{9,8},{10,9... | collective-permute-start | bytes 786440 | tf_op jit(solution)/shard_map/ppermute | solution.py:10
  48.0 9.0 %collective-permute-start.2 = (bf16[512,128]{1,0:T(8,128)(2,1)S(1)}, bf16[512,128]{1,0:T(8,128)(2,1)S(1)}, u32[]{:S(2)}, u32[]{:S(2)}) collective-permute-start(bf16[512,128]{1,0:T(8,128)(2,1)S(1)} %slice.60), channel_id=1, source_target_pairs={{0,1},{1,2},{2,3},{3,0},{4,5},{5,6},{6,7},{7,4},{8,9},{9,10},{10,1... | collective-permute-start | bytes 393224 | tf_op jit(solution)/shard_map/ppermute | solution.py:10
  49.9 9.5 %collective-permute-start.3 = (bf16[512,128]{1,0:T(8,128)(2,1)S(1)}, bf16[512,128]{1,0:T(8,128)(2,1)S(1)}, u32[]{:S(2)}, u32[]{:S(2)}) collective-permute-start(bf16[512,128]{1,0:T(8,128)(2,1)S(1)} %slice.61), channel_id=1, source_target_pairs={{0,3},{1,0},{2,1},{3,2},{4,7},{5,4},{6,5},{7,6},{8,11},{9,8},{10,9... | collective-permute-start | bytes 393224 | tf_op jit(solution)/shard_map/ppermute | solution.py:10
  60.9 30.7 %copy-start.9 = (bf16[4,1024,128]{2,1,0:T(8,128)(2,1)}, bf16[4,1024,128]{2,1,0:T(8,128)(2,1)S(1)}, u32[]{:S(2)}) copy-start(bf16[4,1024,128]{2,1,0:T(8,128)(2,1)S(1)} %get-tuple-element.6) | copy-start | bytes 3145732
  60.9 26.3 %collective-permute-start.5 = (bf16[4,1024,128]{2,1,0:T(8,128)(2,1)S(1)}, bf16[4,1024,128]{2,1,0:T(8,128)(2,1)S(1)}, u32[]{:S(2)}, u32[]{:S(2)}) collective-permute-start(bf16[4,1024,128]{2,1,0:T(8,128)(2,1)S(1)} %get-tuple-element.6), channel_id=1, source_target_pairs={{0,4},{4,8},{8,12},{12,0},{1,5},{5,9},{9,13},{13,1},{2,6},{6,10},{... | collective-permute-start | bytes 3145736 | tf_op jit(solution)/shard_map/ppermute | solution.py:10
  63.3 28.3 %collective-permute-start.4 = (bf16[4,1024,128]{2,1,0:T(8,128)(2,1)S(1)}, bf16[4,1024,128]{2,1,0:T(8,128)(2,1)S(1)}, u32[]{:S(2)}, u32[]{:S(2)}) collective-permute-start(bf16[4,1024,128]{2,1,0:T(8,128)(2,1)S(1)} %get-tuple-element.6), channel_id=1, source_target_pairs={{0,12},{4,0},{8,4},{12,8},{1,13},{5,1},{9,5},{13,9},{2,14},{6,2},{... | collective-permute-start | bytes 3145736 | tf_op jit(solution)/shard_map/ppermute | solution.py:10
  88.0 14.4 %collective-permute-start.6 = (bf16[2,1024,128]{2,1,0:T(8,128)(2,1)}, bf16[2,1024,128]{2,1,0:T(8,128)(2,1)}, u32[]{:S(2)}, u32[]{:S(2)}) collective-permute-start(bf16[2,1024,128]{2,1,0:T(8,128)(2,1)} %slice.62), channel_id=1, source_target_pairs={{0,4},{4,8},{8,12},{12,0},{1,5},{5,9},{9,13},{13,1},{2,6},{6,10},{... | collective-permute-start | bytes 1572872 | tf_op jit(solution)/shard_map/ppermute | solution.py:10
  92.5 15.4 %collective-permute-start.7 = (bf16[2,1024,128]{2,1,0:T(8,128)(2,1)}, bf16[2,1024,128]{2,1,0:T(8,128)(2,1)}, u32[]{:S(2)}, u32[]{:S(2)}) collective-permute-start(bf16[2,1024,128]{2,1,0:T(8,128)(2,1)} %slice.63), channel_id=1, source_target_pairs={{0,12},{4,0},{8,4},{12,8},{1,13},{5,1},{9,5},{13,9},{2,14},{6,2},{... | collective-permute-start | bytes 1572872 | tf_op jit(solution)/shard_map/ppermute | solution.py:10
  149.2 15.8 %collective-permute-start.8 = (bf16[512,512]{1,0:T(8,128)(2,1)}, bf16[512,512]{1,0:T(8,128)(2,1)}, u32[]{:S(2)}, u32[]{:S(2)}) collective-permute-start(bf16[512,512]{1,0:T(8,128)(2,1)} %bitcast.141), channel_id=1, source_target_pairs={{0,4},{4,8},{8,12},{12,0},{1,5},{5,9},{9,13},{13,1},{2,6},{6,10},{... | collective-permute-start | bytes 1572872 | tf_op jit(solution)/shard_map/ppermute | solution.py:10
  161.1 14.4 %collective-permute-start.14 = (bf16[512,512]{1,0:T(8,128)(2,1)}, bf16[512,512]{1,0:T(8,128)(2,1)}, u32[]{:S(2)}, u32[]{:S(2)}) collective-permute-start(bf16[512,512]{1,0:T(8,128)(2,1)} %bitcast.140), channel_id=1, source_target_pairs={{0,12},{4,0},{8,4},{12,8},{1,13},{5,1},{9,5},{13,9},{2,14},{6,2},{... | collective-permute-start | bytes 1572872 | tf_op jit(solution)/shard_map/ppermute | solution.py:10
  167.1 12.7 %collective-permute-start.9 = (bf16[512,512]{1,0:T(8,128)(2,1)}, bf16[512,512]{1,0:T(8,128)(2,1)}, u32[]{:S(2)}, u32[]{:S(2)}) collective-permute-start(bf16[512,512]{1,0:T(8,128)(2,1)} %fusion.37), channel_id=1, source_target_pairs={{0,4},{4,8},{8,12},{12,0},{1,5},{5,9},{9,13},{13,1},{2,6},{6,10},{... | collective-permute-start | bytes 1572872 | tf_op jit(solution)/shard_map/ppermute | solution.py:10
  176.9 13.3 %collective-permute-start.15 = (bf16[512,512]{1,0:T(8,128)(2,1)S(1)}, bf16[512,512]{1,0:T(8,128)(2,1)S(1)}, u32[]{:S(2)}, u32[]{:S(2)}) collective-permute-start(bf16[512,512]{1,0:T(8,128)(2,1)S(1)} %fusion.34), channel_id=1, source_target_pairs={{0,12},{4,0},{8,4},{12,8},{1,13},{5,1},{9,5},{13,9},{2,14},{6,2},{... | collective-permute-start | bytes 1572872 | tf_op jit(solution)/shard_map/ppermute | solution.py:10
  181.1 12.2 %collective-permute-start.10 = (bf16[512,512]{1,0:T(8,128)(2,1)S(1)}, bf16[512,512]{1,0:T(8,128)(2,1)S(1)}, u32[]{:S(2)}, u32[]{:S(2)}) collective-permute-start(bf16[512,512]{1,0:T(8,128)(2,1)S(1)} %fusion.36), channel_id=1, source_target_pairs={{0,4},{4,8},{8,12},{12,0},{1,5},{5,9},{9,13},{13,1},{2,6},{6,10},{... | collective-permute-start | bytes 1572872 | tf_op jit(solution)/shard_map/ppermute | solution.py:10
  191.2 12.6 %collective-permute-start.16 = (bf16[512,512]{1,0:T(8,128)(2,1)}, bf16[512,512]{1,0:T(8,128)(2,1)}, u32[]{:S(2)}, u32[]{:S(2)}) collective-permute-start(bf16[512,512]{1,0:T(8,128)(2,1)} %fusion.33), channel_id=1, source_target_pairs={{0,12},{4,0},{8,4},{12,8},{1,13},{5,1},{9,5},{13,9},{2,14},{6,2},{... | collective-permute-start | bytes 1572872 | tf_op jit(solution)/shard_map/ppermute | solution.py:10
  195.5 12.3 %collective-permute-start.11 = (bf16[512,128]{1,0:T(8,128)(2,1)S(1)}, bf16[512,128]{1,0:T(8,128)(2,1)}, u32[]{:S(2)}, u32[]{:S(2)}) collective-permute-start(bf16[512,128]{1,0:T(8,128)(2,1)S(1)} %bitcast.160), channel_id=1, source_target_pairs={{0,1},{1,2},{2,3},{3,0},{4,5},{5,6},{6,7},{7,4},{8,9},{9,10},{10,1... | collective-permute-start | bytes 393224 | tf_op jit(solution)/shard_map/ppermute | solution.py:10
  205.5 8.1 %collective-permute-start.17 = (bf16[512,128]{1,0:T(8,128)(2,1)S(1)}, bf16[512,128]{1,0:T(8,128)(2,1)S(1)}, u32[]{:S(2)}, u32[]{:S(2)}) collective-permute-start(bf16[512,128]{1,0:T(8,128)(2,1)S(1)} %bitcast.161), channel_id=1, source_target_pairs={{0,3},{1,0},{2,1},{3,2},{4,7},{5,4},{6,5},{7,6},{8,11},{9,8},{10,9... | collective-permute-start | bytes 393224 | tf_op jit(solution)/shard_map/ppermute | solution.py:10
  207.8 49.2 %copy-start.20 = (s32[768]{0:T(1024)S(1)}, s32[768]{0:T(1024)}, u32[]{:S(2)}) copy-start(s32[768]{0:T(1024)} %copy-done.19) | copy-start | bytes 9220
  207.8 49.2 %copy-start.22 = (pred[768]{0:T(1024)(128)(4,1)S(1)}, pred[768]{0:T(1024)(128)(4,1)}, u32[]{:S(2)}) copy-start(pred[768]{0:T(1024)(128)(4,1)} %copy-done.21) | copy-start | bytes 2308
  208.8 11.5 %collective-permute-start.12 = (bf16[512,128]{1,0:T(8,128)(2,1)S(1)}, bf16[512,128]{1,0:T(8,128)(2,1)S(1)}, u32[]{:S(2)}, u32[]{:S(2)}) collective-permute-start(bf16[512,128]{1,0:T(8,128)(2,1)S(1)} %fusion.52), channel_id=1, source_target_pairs={{0,1},{1,2},{2,3},{3,0},{4,5},{5,6},{6,7},{7,4},{8,9},{9,10},{10,1... | collective-permute-start | bytes 393224 | tf_op jit(solution)/shard_map/ppermute | solution.py:10
  213.7 10.5 %collective-permute-start.18 = (bf16[512,128]{1,0:T(8,128)(2,1)S(1)}, bf16[512,128]{1,0:T(8,128)(2,1)S(1)}, u32[]{:S(2)}, u32[]{:S(2)}) collective-permute-start(bf16[512,128]{1,0:T(8,128)(2,1)S(1)} %fusion.49), channel_id=1, source_target_pairs={{0,3},{1,0},{2,1},{3,2},{4,7},{5,4},{6,5},{7,6},{8,11},{9,8},{10,9... | collective-permute-start | bytes 393224 | tf_op jit(solution)/shard_map/ppermute | solution.py:10
  220.3 9.1 %collective-permute-start.13 = (bf16[512,128]{1,0:T(8,128)(2,1)S(1)}, bf16[512,128]{1,0:T(8,128)(2,1)S(1)}, u32[]{:S(2)}, u32[]{:S(2)}) collective-permute-start(bf16[512,128]{1,0:T(8,128)(2,1)S(1)} %fusion.51), channel_id=1, source_target_pairs={{0,1},{1,2},{2,3},{3,0},{4,5},{5,6},{6,7},{7,4},{8,9},{9,10},{10,1... | collective-permute-start | bytes 393224 | tf_op jit(solution)/shard_map/ppermute | solution.py:10
  224.2 9.3 %collective-permute-start.19 = (bf16[512,128]{1,0:T(8,128)(2,1)S(1)}, bf16[512,128]{1,0:T(8,128)(2,1)S(1)}, u32[]{:S(2)}, u32[]{:S(2)}) collective-permute-start(bf16[512,128]{1,0:T(8,128)(2,1)S(1)} %fusion.48), channel_id=1, source_target_pairs={{0,3},{1,0},{2,1},{3,2},{4,7},{5,4},{6,5},{7,6},{8,11},{9,8},{10,9... | collective-permute-start | bytes 393224 | tf_op jit(solution)/shard_map/ppermute | solution.py:10
  (19 other events, 220.9 us)

commit v4 on v3

--- a/solution.py
+++ b/solution.py
@@ -13,7 +13,6 @@
 def ring_gather(block, axis, n):
     if n == 1:
         return block[None]
-    me = lax.axis_index(axis)
     half = block.shape[0] // 2
     pieces = [None] * n
     pieces[0] = block
@@ -27,27 +26,26 @@
         first = shift(rightward[:half], axis, n, 1)
         second = shift(leftward[half:], axis, n, -1)
         pieces[n // 2] = jnp.concatenate([first, second], axis=0)
-    return jnp.roll(jnp.stack(pieces), me, axis=0)
+    return jnp.stack(pieces)
 
 
 def ring_reduce_scatter(parts, axis, n):
     if n == 1:
         return parts[:, 0].astype(jnp.float32)
-    me = lax.axis_index(axis)
     half = parts.shape[0] // 2
 
-    def term(dest, lower):
+    def term(offset, lower):
         rows = parts[:half] if lower else parts[half:]
-        return lax.dynamic_index_in_dim(rows, dest % n, axis=1, keepdims=False)
+        return rows[:, offset % n]
 
     results = []
     for lower, direction in ((True, 1), (False, -1)):
-        carried = term(me - direction, lower)
+        carried = term(-direction, lower)
         for step in range(1, n):
             arrived = shift(carried, axis, n, direction)
-            total = arrived.astype(jnp.float32) + term(
-                me - direction * (step + 1), lower
-            ).astype(jnp.float32)
+            total = arrived.astype(jnp.float32) + term(-direction * (step + 1), lower).astype(
+                jnp.float32
+            )
             carried = total.astype(parts.dtype) if step < n - 1 else total
         results.append(carried)
     return jnp.concatenate(results, axis=0)
@@ -84,18 +82,25 @@
     ).reshape(cells, shard_width)
     n_z = lax.psum(1, "mz")
     n_x = n_mp // n_z
+    at_x, at_z = lax.axis_index("mx"), lax.axis_index("mz")
+
+    def relative(blocks, axes):
+        return jnp.roll(blocks, (-at_x, -at_z), axis=axes)
+
     part = ring_gather(received, "mz", n_z)
     whole = ring_gather(part, "mx", n_x).reshape(n_mp, cells, shard_width)
 
     features = whole.astype(jnp.float32)
     mean_square = jnp.sum(features * features, axis=(0, 2)) / model_width
     scale = lax.rsqrt(mean_square + norm_eps)
-    gain = norm_gain.reshape(n_mp, 1, shard_width)
+    gain = relative(norm_gain.reshape(n_x, n_z, shard_width), (0, 1)).reshape(n_mp, 1, shard_width)
     normed = (features * scale[None, :, None] * gain).astype(jnp.bfloat16)
 
     logits = lax.dot_general(
         normed,
-        router_weight.reshape(n_mp, shard_width, experts),
+        relative(router_weight.reshape(n_x, n_z, shard_width, experts), (0, 1)).reshape(
+            n_mp, shard_width, experts
+        ),
         (((0, 2), (0, 1)), ((), ())),
         preferred_element_type=jnp.float32,
     )
@@ -105,15 +110,18 @@
     gate_prob = jax.nn.sigmoid(picked)
 
     ff_local = gate_proj.shape[2]
-    w_gate = gate_proj[0].reshape(n_mp, shard_width, ff_local)
-    w_up = up_proj[0].reshape(n_mp, shard_width, ff_local)
+    w_gate = relative(gate_proj[0].reshape(n_x, n_z, shard_width, ff_local), (0, 1))
+    w_up = relative(up_proj[0].reshape(n_x, n_z, shard_width, ff_local), (0, 1))
+    w_gate = w_gate.reshape(n_mp, shard_width, ff_local)
+    w_up = w_up.reshape(n_mp, shard_width, ff_local)
+    w_down = relative(down_proj[0].reshape(ff_local, n_x, n_z, shard_width), (1, 2))
     dims = (((0, 2), (0, 1)), ((), ()))
     pre_gate = lax.dot_general(normed, w_gate, dims, preferred_element_type=jnp.float32)
     pre_up = lax.dot_general(normed, w_up, dims, preferred_element_type=jnp.float32)
     hidden = (jax.nn.gelu(pre_gate, approximate=True) * pre_up).astype(jnp.bfloat16)
-    block_out = jnp.dot(hidden, down_proj[0], preferred_element_type=jnp.float32).astype(
-        jnp.bfloat16
-    )
+    block_out = jnp.dot(
+        hidden, w_down.reshape(ff_local, model_width), preferred_element_type=jnp.float32
+    ).astype(jnp.bfloat16)
     across_x = ring_reduce_scatter(block_out.reshape(cells, n_x, -1), "mx", n_x)
     summed = ring_reduce_scatter(
         across_x.astype(jnp.bfloat16).reshape(cells, n_z, shard_width), "mz", n_z

time: 260 us -> 256 us (0.985); the launches traced: 258 us -> 251 us
  waiting for transfers between devices: 62.7 us -> 33.8 us
  other arithmetic: 22.3 us -> 41.6 us
  starting transfers between devices: 71.3 us -> 77.7 us
  blocking collectives: 45.5 us -> 42.3 us
    ppermute x20, waiting for transfers between devices: 62.7 us -> 33.8 us  [shift(): return lax.ppermute(value, axis, [(i, (i + step) % n) for i in range(n)])]
    another operation x0 -> x5, local copies, waits for them, and re-layouts: none -> 17.7 us  [the longest x2 6.85 us: shards(): gate_proj[0].reshape(n_x, n_z, shard_width, ff_local)]
    slice x0 -> x3, other arithmetic: none -> 13.7 us  [term(): return rows[:, offset % n]]
    dynamic_slice x5 -> x0, local copies, waits for them, and re-layouts: 12.8 us -> none  [term(): return lax.dynamic_index_in_dim(rows, dest % n, axis=1, keepdims=False)]
    concatenate x0 -> x6, other arithmetic: none -> 10.2 us  [relative(): return jnp.roll(blocks, (-at_x, -at_z), axis=axes)]
    unnamed x64 -> x24, local copies, waits for them, and re-layouts: 12.2 us -> 2.04 us
    ppermute x20, starting transfers between devices: 71.3 us -> 77.7 us  [shift(): return lax.ppermute(value, axis, [(i, (i + step) % n) for i in range(n)])]
    unnamed x4 -> x0, other arithmetic: 4.56 us -> none
  transfers between devices with their start and end apart: 20 -> 20, of which waited for: 14 -> 12; matrix products, arithmetic and copies ran while one was open for 11% -> 21% of each run, Pallas kernels for 0% -> 0%
where the time goes in v4:
time: 256 us; the launch traced here: 251 us
  starting transfers between devices  77.7 us (30%)
  blocking collectives  42.3 us (17%)
  other arithmetic  41.6 us (16%)
  local copies, waits for them, and re-layouts  39.8 us (16%)
  waiting for transfers between devices  33.8 us (13%)
  matrix products  15.1 us (6%)
    ppermute x20, starting transfers between devices, shift(): return lax.ppermute(value, axis, [(i, (i + step) % n) for i in range(n)])  77.7 us
    ppermute x20, waiting for transfers between devices, shift(): return lax.ppermute(value, axis, [(i, (i + step) % n) for i in range(n)])  33.8 us
    all_to_all x1, blocking collectives, shards(): lax.all_to_all(masked.reshape(experts, slot_count, shard_width), 'expert'...  22.3 us
    all_to_all x1, blocking collectives, shards(): lax.all_to_all(gated.reshape(experts, slot_count, shard_width), 'expert',...  20 us
    slice x3, other arithmetic, term(): return rows[:, offset % n]  13.7 us
    slice x5, local copies, waits for them, and re-layouts, term(): rows = parts[:half] if lower else parts[half:]  12.9 us
    concatenate x6, other arithmetic, relative(): return jnp.roll(blocks, (-at_x, -at_z), axis=axes)  10.2 us
    dot_general x1, matrix products, shards(): jnp.dot(hidden, w_down.reshape(ff_local, model_width), preferred_element_...  8.44 us
  transfers between devices with their start and end apart: 20, of which 12 were waited for; matrix products, arithmetic and copies ran while one was open for 21% of the time, Pallas kernels for 0%

profile of v4, /device:TPU:6, one launch (start us, length us, event | category | flops | bytes accessed | tf_op | source)
XLA Modules:
  0.0 250.8 jit_solution(4274629470312240624)
XLA Ops:
  3.5 22.3 %all_to_all.10 = bf16[32,32,128]{2,1,0:T(8,128)(2,1)S(1)} all-to-all(bf16[32,32,128]{2,1,0:T(8,128)(2,1)S(1)} %bitcast.132), channel_id=1, replica_groups=mesh['expert'=32,'mx'=4,'mz'=4] {'expert'}, dimensions={0} | all-to-all | bytes 524288 | tf_op jit(solution)/shard_map/all_to_all | solution.py:76
  25.7 6.1 %collective-permute-start.1 = (bf16[1024,128]{1,0:T(8,128)(2,1)S(1)}, bf16[1024,128]{1,0:T(8,128)(2,1)S(1)}, u32[]{:S(2)}, u32[]{:S(2)}) collective-permute-start(bf16[1024,128]{1,0:T(8,128)(2,1)S(1)} %bitcast.123), channel_id=1, source_target_pairs={{0,1},{1,2},{2,3},{3,0},{4,5},{5,6},{6,7},{7,4},{8,9},{9,10},{10,1... | collective-permute-start | bytes 786440 | tf_op jit(solution)/shard_map/ppermute | solution.py:10
  31.8 5.9 %collective-permute-start = (bf16[1024,128]{1,0:T(8,128)(2,1)S(1)}, bf16[1024,128]{1,0:T(8,128)(2,1)S(1)}, u32[]{:S(2)}, u32[]{:S(2)}) collective-permute-start(bf16[1024,128]{1,0:T(8,128)(2,1)S(1)} %bitcast.124), channel_id=1, source_target_pairs={{0,3},{1,0},{2,1},{3,2},{4,7},{5,4},{6,5},{7,6},{8,11},{9,8},{10,9... | collective-permute-start | bytes 786440 | tf_op jit(solution)/shard_map/ppermute | solution.py:10
  37.7 9.2 %collective-permute-done.1 = bf16[1024,128]{1,0:T(8,128)(2,1)S(1)} collective-permute-done((bf16[1024,128]{1,0:T(8,128)(2,1)S(1)}, bf16[1024,128]{1,0:T(8,128)(2,1)S(1)}, u32[]{:S(2)}, u32[]{:S(2)}) %collective-permute-start.1) | collective-permute-done | bytes 262176 | tf_op jit(solution)/shard_map/ppermute | solution.py:10
  48.9 6.0 %collective-permute-start.3 = (bf16[512,128]{1,0:T(8,128)(2,1)S(1)}, bf16[512,128]{1,0:T(8,128)(2,1)S(1)}, u32[]{:S(2)}, u32[]{:S(2)}) collective-permute-start(bf16[512,128]{1,0:T(8,128)(2,1)S(1)} %slice.125), channel_id=1, source_target_pairs={{0,3},{1,0},{2,1},{3,2},{4,7},{5,4},{6,5},{7,6},{8,11},{9,8},{10,9... | collective-permute-start | bytes 393224 | tf_op jit(solution)/shard_map/ppermute | solution.py:10
  62.3 4.3 %collective-permute-start.5 = (bf16[4,1024,128]{2,1,0:T(8,128)(2,1)}, bf16[4,1024,128]{2,1,0:T(8,128)(2,1)S(1)}, u32[]{:S(2)}, u32[]{:S(2)}) collective-permute-start(bf16[4,1024,128]{2,1,0:T(8,128)(2,1)} %get-tuple-element.17), channel_id=1, source_target_pairs={{0,4},{4,8},{8,12},{12,0},{1,5},{5,9},{9,13},{13,1},{2,6},{6,10},{... | collective-permute-start | bytes 3145736 | tf_op jit(solution)/shard_map/ppermute | solution.py:10
  66.7 4.1 %reshape_squeeze.9 = bf16[4,4,128,320]{2,1,0,3:T(4,128)(2,1)} reshape(bf16[1,2048,320]{1,2,0:T(8,128)(2,1)} %param.14) | data formatting | bytes 2621440 | tf_op jit(solution)/shard_map/reshape;squeeze | solution.py:113
  73.5 4.1 %reshape_squeeze.10 = bf16[4,4,128,320]{2,1,0,3:T(4,128)(2,1)} reshape(bf16[1,2048,320]{1,2,0:T(8,128)(2,1)} %param.15) | data formatting | bytes 2621440 | tf_op jit(solution)/shard_map/reshape;squeeze | solution.py:114
  80.3 4.1 %reshape_squeeze.11 = bf16[320,4,4,128]{3,2,1,0:T(4,128)(2,1)} reshape(bf16[1,320,2048]{2,1,0:T(8,128)(2,1)} %param.16) | data formatting | bytes 2621440 | tf_op jit(solution)/shard_map/reshape;squeeze | solution.py:117
  91.0 5.3 %collective-permute-start.6 = (bf16[2,1024,128]{2,1,0:T(8,128)(2,1)}, bf16[2,1024,128]{2,1,0:T(8,128)(2,1)}, u32[]{:S(2)}, u32[]{:S(2)}) collective-permute-start(bf16[2,1024,128]{2,1,0:T(8,128)(2,1)} %slice.126), channel_id=1, source_target_pairs={{0,4},{4,8},{8,12},{12,0},{1,5},{5,9},{9,13},{13,1},{2,6},{6,10},{... | collective-permute-start | bytes 1572872 | tf_op jit(solution)/shard_map/ppermute | solution.py:10
  99.7 3.5 %reshape.104 = bf16[320,2048]{1,0:T(8,128)(2,1)} reshape(bf16[320,4,4,128]{3,2,1,0:T(4,128)(2,1)} %fusion.21) | data formatting | bytes 2621440 | tf_op jit(solution)/shard_map/reshape | solution.py:123
  103.3 3.8 %fusion.25 = (bf16[4,4,128,320]{2,3,1,0:T(8,128)(2,1)}, bf16[4,4,128,320]{2,3,1,0:T(8,128)(2,1)S(1)}) fusion(s32[]{:T(128)S(6)} %select_n.71, bf16[4,4,128,320]{2,3,1,0:T(8,128)(2,1)} %copy.61, bf16[4,4,128,320]{2,3,1,0:T(8,128)(2,1)} %copy.59), kind=kLoop, calls=%fused_computation.42 | loop fusion | flops 1310720 | bytes 5242884 | tf_op jit(solution)/shard_map/jit(_roll_dynamic)/concatenate | solution.py:88
  114.8 8.4 %convolution_convert_fusion = bf16[1024,2048]{1,0:T(8,128)(2,1)} fusion(bf16[320,2048]{1,0:T(8,128)(2,1)S(1)} %copy-done.7, bf16[4,4,1024,128]{3,2,1,0:T(8,128)(2,1)} %copy-done.1, f32[1024,320]{0,1:T(8,128)} %convolution_bitcast_fusion.1, s32[]{:T(128)S(6)} %select_n.73, bf16[4,4,128,320]{2,3,1,0:T(8,128)(2,1)S(1)} %copy-done.8), kind=kOutput, calls=%fused_computation.6 | convolution fusion | flops 2690383872 | bytes 12320772 | tf_op jit(solution)/shard_map/dot_general | solution.py:122
  123.2 4.8 %fusion.73 = (bf16[512,2048]{1,0:T(8,128)(2,1)}, bf16[512,2048]{1,0:T(8,128)(2,1)}) fusion(bf16[1024,2048]{1,0:T(8,128)(2,1)} %convolution_convert_fusion), kind=kLoop, calls=%fused_computation.128 | loop fusion | bytes 8388608 | tf_op jit(solution)/shard_map/slice | solution.py:38
  131.4 4.5 %slice.113 = bf16[512,4,512]{2,1,0:T(4,128)(2,1)} reshape(bf16[512,2048]{1,0:T(8,128)(2,1)} %get-tuple-element.7) | data formatting | bytes 4194304 | tf_op jit(solution)/shard_map/slice | solution.py:38
  135.9 8.8 %fusion.75 = (bf16[512,1,512]{2,1,0:T(2,128)(2,1)}, bf16[512,1,512]{2,1,0:T(2,128)(2,1)S(1)}, bf16[512,1,512]{2,1,0:T(2,128)(2,1)S(1)}, f32[512,1,512]{2,1,0:T(1,128)}) fusion(bf16[512,4,512]{2,1,0:T(4,128)(2,1)} %slice.113), kind=kLoop, calls=%fused_computation.130 | loop fusion | flops 262144 | bytes 4718592 | tf_op jit(solution)/shard_map/slice | solution.py:39
  146.7 4.2 %fusion.74 = (bf16[512,1,512]{2,1,0:T(2,128)(2,1)}, bf16[512,1,512]{2,1,0:T(2,128)(2,1)}, bf16[512,1,512]{2,1,0:T(2,128)(2,1)S(1)}, f32[512,1,512]{2,1,0:T(1,128)S(1)}) fusion(bf16[512,4,512]{2,1,0:T(4,128)(2,1)S(1)} %slice.101), kind=kLoop, calls=%fused_computation.129 | loop fusion | flops 262144 | bytes 4718592 | tf_op jit(solution)/shard_map/slice | solution.py:39
  151.9 5.1 %collective-permute-start.8 = (bf16[512,512]{1,0:T(8,128)(2,1)}, bf16[512,512]{1,0:T(8,128)(2,1)}, u32[]{:S(2)}, u32[]{:S(2)}) collective-permute-start(bf16[512,512]{1,0:T(8,128)(2,1)} %bitcast.116), channel_id=1, source_target_pairs={{0,4},{4,8},{8,12},{12,0},{1,5},{5,9},{9,13},{13,1},{2,6},{6,10},{... | collective-permute-start | bytes 1572872 | tf_op jit(solution)/shard_map/ppermute | solution.py:10
  168.7 5.6 %collective-permute-start.9 = (bf16[512,512]{1,0:T(8,128)(2,1)}, bf16[512,512]{1,0:T(8,128)(2,1)}, u32[]{:S(2)}, u32[]{:S(2)}) collective-permute-start(bf16[512,512]{1,0:T(8,128)(2,1)} %fusion.42), channel_id=1, source_target_pairs={{0,4},{4,8},{8,12},{12,0},{1,5},{5,9},{9,13},{13,1},{2,6},{6,10},{... | collective-permute-start | bytes 1572872 | tf_op jit(solution)/shard_map/ppermute | solution.py:10
  185.0 5.6 %collective-permute-start.10 = (bf16[512,512]{1,0:T(8,128)(2,1)}, bf16[512,512]{1,0:T(8,128)(2,1)}, u32[]{:S(2)}, u32[]{:S(2)}) collective-permute-start(bf16[512,512]{1,0:T(8,128)(2,1)} %fusion.41), channel_id=1, source_target_pairs={{0,4},{4,8},{8,12},{12,0},{1,5},{5,9},{9,13},{13,1},{2,6},{6,10},{... | collective-permute-start | bytes 1572872 | tf_op jit(solution)/shard_map/ppermute | solution.py:10
  200.5 4.6 %collective-permute-start.11 = (bf16[512,128]{1,0:T(8,128)(2,1)S(1)}, bf16[512,128]{1,0:T(8,128)(2,1)S(1)}, u32[]{:S(2)}, u32[]{:S(2)}) collective-permute-start(bf16[512,128]{1,0:T(8,128)(2,1)S(1)} %bitcast.134), channel_id=1, source_target_pairs={{0,1},{1,2},{2,3},{3,0},{4,5},{5,6},{6,7},{7,4},{8,9},{9,10},{10,1... | collective-permute-start | bytes 393224 | tf_op jit(solution)/shard_map/ppermute | solution.py:10
  213.3 5.8 %collective-permute-start.19 = (bf16[512,128]{1,0:T(8,128)(2,1)S(1)}, bf16[512,128]{1,0:T(8,128)(2,1)S(1)}, u32[]{:S(2)}, u32[]{:S(2)}) collective-permute-start(bf16[512,128]{1,0:T(8,128)(2,1)S(1)} %fusion.50), channel_id=1, source_target_pairs={{0,3},{1,0},{2,1},{3,2},{4,7},{5,4},{6,5},{7,6},{8,11},{9,8},{10,9... | collective-permute-start | bytes 393224 | tf_op jit(solution)/shard_map/ppermute | solution.py:10
  222.6 6.5 %collective-permute-done.13 = bf16[512,128]{1,0:T(8,128)(2,1)S(1)} collective-permute-done((bf16[512,128]{1,0:T(8,128)(2,1)S(1)}, bf16[512,128]{1,0:T(8,128)(2,1)S(1)}, u32[]{:S(2)}, u32[]{:S(2)}) %collective-permute-start.13) | collective-permute-done | bytes 131104 | tf_op jit(solution)/shard_map/ppermute | solution.py:10
  229.3 20.0 %all_to_all.11 = bf16[32,32,128]{2,1,0:T(8,128)(2,1)S(1)} all-to-all(bf16[32,32,128]{2,1,0:T(8,128)(2,1)S(1)} %fusion.49), channel_id=1, replica_groups=mesh['expert'=32,'mx'=4,'mz'=4] {'expert'}, dimensions={0} | all-to-all | bytes 524288 | tf_op jit(solution)/shard_map/all_to_all | solution.py:131
  (100 shorter events, 87.7 us)
Async XLA Ops:
  25.7 21.2 %collective-permute-start.1 = (bf16[1024,128]{1,0:T(8,128)(2,1)S(1)}, bf16[1024,128]{1,0:T(8,128)(2,1)S(1)}, u32[]{:S(2)}, u32[]{:S(2)}) collective-permute-start(bf16[1024,128]{1,0:T(8,128)(2,1)S(1)} %bitcast.123), channel_id=1, source_target_pairs={{0,1},{1,2},{2,3},{3,0},{4,5},{5,6},{6,7},{7,4},{8,9},{9,10},{10,1... | collective-permute-start | bytes 786440 | tf_op jit(solution)/shard_map/ppermute | solution.py:10
  31.8 17.1 %collective-permute-start = (bf16[1024,128]{1,0:T(8,128)(2,1)S(1)}, bf16[1024,128]{1,0:T(8,128)(2,1)S(1)}, u32[]{:S(2)}, u32[]{:S(2)}) collective-permute-start(bf16[1024,128]{1,0:T(8,128)(2,1)S(1)} %bitcast.124), channel_id=1, source_target_pairs={{0,3},{1,0},{2,1},{3,2},{4,7},{5,4},{6,5},{7,6},{8,11},{9,8},{10,9... | collective-permute-start | bytes 786440 | tf_op jit(solution)/shard_map/ppermute | solution.py:10
  47.0 9.0 %collective-permute-start.2 = (bf16[512,128]{1,0:T(8,128)(2,1)S(1)}, bf16[512,128]{1,0:T(8,128)(2,1)S(1)}, u32[]{:S(2)}, u32[]{:S(2)}) collective-permute-start(bf16[512,128]{1,0:T(8,128)(2,1)S(1)} %slice.124), channel_id=1, source_target_pairs={{0,1},{1,2},{2,3},{3,0},{4,5},{5,6},{6,7},{7,4},{8,9},{9,10},{10,1... | collective-permute-start | bytes 393224 | tf_op jit(solution)/shard_map/ppermute | solution.py:10
  48.9 9.5 %collective-permute-start.3 = (bf16[512,128]{1,0:T(8,128)(2,1)S(1)}, bf16[512,128]{1,0:T(8,128)(2,1)S(1)}, u32[]{:S(2)}, u32[]{:S(2)}) collective-permute-start(bf16[512,128]{1,0:T(8,128)(2,1)S(1)} %slice.125), channel_id=1, source_target_pairs={{0,3},{1,0},{2,1},{3,2},{4,7},{5,4},{6,5},{7,6},{8,11},{9,8},{10,9... | collective-permute-start | bytes 393224 | tf_op jit(solution)/shard_map/ppermute | solution.py:10
  59.6 27.8 %collective-permute-start.4 = (bf16[4,1024,128]{2,1,0:T(8,128)(2,1)}, bf16[4,1024,128]{2,1,0:T(8,128)(2,1)S(1)}, u32[]{:S(2)}, u32[]{:S(2)}) collective-permute-start(bf16[4,1024,128]{2,1,0:T(8,128)(2,1)} %get-tuple-element.17), channel_id=1, source_target_pairs={{0,12},{4,0},{8,4},{12,8},{1,13},{5,1},{9,5},{13,9},{2,14},{6,2},{... | collective-permute-start | bytes 3145736 | tf_op jit(solution)/shard_map/ppermute | solution.py:10
  62.3 27.8 %collective-permute-start.5 = (bf16[4,1024,128]{2,1,0:T(8,128)(2,1)}, bf16[4,1024,128]{2,1,0:T(8,128)(2,1)S(1)}, u32[]{:S(2)}, u32[]{:S(2)}) collective-permute-start(bf16[4,1024,128]{2,1,0:T(8,128)(2,1)} %get-tuple-element.17), channel_id=1, source_target_pairs={{0,4},{4,8},{8,12},{12,0},{1,5},{5,9},{9,13},{13,1},{2,6},{6,10},{... | collective-permute-start | bytes 3145736 | tf_op jit(solution)/shard_map/ppermute | solution.py:10
  88.2 18.9 %collective-permute-start.7 = (bf16[2,1024,128]{2,1,0:T(8,128)(2,1)}, bf16[2,1024,128]{2,1,0:T(8,128)(2,1)}, u32[]{:S(2)}, u32[]{:S(2)}) collective-permute-start(bf16[2,1024,128]{2,1,0:T(8,128)(2,1)} %slice.127), channel_id=1, source_target_pairs={{0,12},{4,0},{8,4},{12,8},{1,13},{5,1},{9,5},{13,9},{2,14},{6,2},{... | collective-permute-start | bytes 1572872 | tf_op jit(solution)/shard_map/ppermute | solution.py:10
  91.0 12.2 %copy-start.9 = (f32[2048]{0:T(1024)S(1)}, f32[2048]{0:T(1024)}, u32[]{:S(2)}) copy-start(f32[2048]{0:T(1024)} %param.12) | copy-start | bytes 24580
  91.0 16.0 %collective-permute-start.6 = (bf16[2,1024,128]{2,1,0:T(8,128)(2,1)}, bf16[2,1024,128]{2,1,0:T(8,128)(2,1)}, u32[]{:S(2)}, u32[]{:S(2)}) collective-permute-start(bf16[2,1024,128]{2,1,0:T(8,128)(2,1)} %slice.126), channel_id=1, source_target_pairs={{0,4},{4,8},{8,12},{12,0},{1,5},{5,9},{9,13},{13,1},{2,6},{6,10},{... | collective-permute-start | bytes 1572872 | tf_op jit(solution)/shard_map/ppermute | solution.py:10
  144.8 15.1 %collective-permute-start.14 = (bf16[512,512]{1,0:T(8,128)(2,1)S(1)}, bf16[512,512]{1,0:T(8,128)(2,1)S(1)}, u32[]{:S(2)}, u32[]{:S(2)}) collective-permute-start(bf16[512,512]{1,0:T(8,128)(2,1)S(1)} %bitcast.130), channel_id=1, source_target_pairs={{0,12},{4,0},{8,4},{12,8},{1,13},{5,1},{9,5},{13,9},{2,14},{6,2},{... | collective-permute-start | bytes 1572872 | tf_op jit(solution)/shard_map/ppermute | solution.py:10
  150.9 15.6 %copy-start.6 = (bf16[512,1,512]{2,1,0:T(2,128)(2,1)S(1)}, bf16[512,1,512]{2,1,0:T(2,128)(2,1)}, u32[]{:S(2)}) copy-start(bf16[512,1,512]{2,1,0:T(2,128)(2,1)} %get-tuple-element.9) | copy-start | bytes 1572868
  151.9 14.7 %collective-permute-start.8 = (bf16[512,512]{1,0:T(8,128)(2,1)}, bf16[512,512]{1,0:T(8,128)(2,1)}, u32[]{:S(2)}, u32[]{:S(2)}) collective-permute-start(bf16[512,512]{1,0:T(8,128)(2,1)} %bitcast.116), channel_id=1, source_target_pairs={{0,4},{4,8},{8,12},{12,0},{1,5},{5,9},{9,13},{13,1},{2,6},{6,10},{... | collective-permute-start | bytes 1572872 | tf_op jit(solution)/shard_map/ppermute | solution.py:10
  159.9 15.5 %copy-start.5 = (bf16[512,1,512]{2,1,0:T(2,128)(2,1)S(1)}, bf16[512,1,512]{2,1,0:T(2,128)(2,1)}, u32[]{:S(2)}) copy-start(bf16[512,1,512]{2,1,0:T(2,128)(2,1)} %get-tuple-element.12) | copy-start | bytes 1572868
  160.9 14.5 %collective-permute-start.15 = (bf16[512,512]{1,0:T(8,128)(2,1)}, bf16[512,512]{1,0:T(8,128)(2,1)}, u32[]{:S(2)}, u32[]{:S(2)}) collective-permute-start(bf16[512,512]{1,0:T(8,128)(2,1)} %fusion.40), channel_id=1, source_target_pairs={{0,12},{4,0},{8,4},{12,8},{1,13},{5,1},{9,5},{13,9},{2,14},{6,2},{... | collective-permute-start | bytes 1572872 | tf_op jit(solution)/shard_map/ppermute | solution.py:10
  166.6 13.0 %copy-start.2 = (bf16[4,4,1024,128]{3,2,1,0:T(8,128)(2,1)S(1)}, bf16[4,4,1024,128]{3,2,1,0:T(8,128)(2,1)}, u32[]{:S(2)}) copy-start(bf16[4,4,1024,128]{3,2,1,0:T(8,128)(2,1)} %copy-done.1) | copy-start | bytes 12582916
  168.7 14.2 %collective-permute-start.9 = (bf16[512,512]{1,0:T(8,128)(2,1)}, bf16[512,512]{1,0:T(8,128)(2,1)}, u32[]{:S(2)}, u32[]{:S(2)}) collective-permute-start(bf16[512,512]{1,0:T(8,128)(2,1)} %fusion.42), channel_id=1, source_target_pairs={{0,4},{4,8},{8,12},{12,0},{1,5},{5,9},{9,13},{13,1},{2,6},{6,10},{... | collective-permute-start | bytes 1572872 | tf_op jit(solution)/shard_map/ppermute | solution.py:10
  177.5 13.7 %collective-permute-start.16 = (bf16[512,512]{1,0:T(8,128)(2,1)}, bf16[512,512]{1,0:T(8,128)(2,1)}, u32[]{:S(2)}, u32[]{:S(2)}) collective-permute-start(bf16[512,512]{1,0:T(8,128)(2,1)} %fusion.39), channel_id=1, source_target_pairs={{0,12},{4,0},{8,4},{12,8},{1,13},{5,1},{9,5},{13,9},{2,14},{6,2},{... | collective-permute-start | bytes 1572872 | tf_op jit(solution)/shard_map/ppermute | solution.py:10
  185.0 13.3 %collective-permute-start.10 = (bf16[512,512]{1,0:T(8,128)(2,1)}, bf16[512,512]{1,0:T(8,128)(2,1)}, u32[]{:S(2)}, u32[]{:S(2)}) collective-permute-start(bf16[512,512]{1,0:T(8,128)(2,1)} %fusion.41), channel_id=1, source_target_pairs={{0,4},{4,8},{8,12},{12,0},{1,5},{5,9},{9,13},{13,1},{2,6},{6,10},{... | collective-permute-start | bytes 1572872 | tf_op jit(solution)/shard_map/ppermute | solution.py:10
  193.3 11.8 %collective-permute-start.17 = (bf16[512,128]{1,0:T(8,128)(2,1)S(1)}, bf16[512,128]{1,0:T(8,128)(2,1)S(1)}, u32[]{:S(2)}, u32[]{:S(2)}) collective-permute-start(bf16[512,128]{1,0:T(8,128)(2,1)S(1)} %bitcast.133), channel_id=1, source_target_pairs={{0,3},{1,0},{2,1},{3,2},{4,7},{5,4},{6,5},{7,6},{8,11},{9,8},{10,9... | collective-permute-start | bytes 393224 | tf_op jit(solution)/shard_map/ppermute | solution.py:10
  200.5 10.6 %collective-permute-start.11 = (bf16[512,128]{1,0:T(8,128)(2,1)S(1)}, bf16[512,128]{1,0:T(8,128)(2,1)S(1)}, u32[]{:S(2)}, u32[]{:S(2)}) collective-permute-start(bf16[512,128]{1,0:T(8,128)(2,1)S(1)} %bitcast.134), channel_id=1, source_target_pairs={{0,1},{1,2},{2,3},{3,0},{4,5},{5,6},{6,7},{7,4},{8,9},{9,10},{10,1... | collective-permute-start | bytes 393224 | tf_op jit(solution)/shard_map/ppermute | solution.py:10
  205.1 8.1 %collective-permute-start.18 = (bf16[512,128]{1,0:T(8,128)(2,1)S(1)}, bf16[512,128]{1,0:T(8,128)(2,1)S(1)}, u32[]{:S(2)}, u32[]{:S(2)}) collective-permute-start(bf16[512,128]{1,0:T(8,128)(2,1)S(1)} %fusion.51), channel_id=1, source_target_pairs={{0,3},{1,0},{2,1},{3,2},{4,7},{5,4},{6,5},{7,6},{8,11},{9,8},{10,9... | collective-permute-start | bytes 393224 | tf_op jit(solution)/shard_map/ppermute | solution.py:10
  211.1 9.0 %collective-permute-start.12 = (bf16[512,128]{1,0:T(8,128)(2,1)S(1)}, bf16[512,128]{1,0:T(8,128)(2,1)S(1)}, u32[]{:S(2)}, u32[]{:S(2)}) collective-permute-start(bf16[512,128]{1,0:T(8,128)(2,1)S(1)} %fusion.54), channel_id=1, source_target_pairs={{0,1},{1,2},{2,3},{3,0},{4,5},{5,6},{6,7},{7,4},{8,9},{9,10},{10,1... | collective-permute-start | bytes 393224 | tf_op jit(solution)/shard_map/ppermute | solution.py:10
  213.3 9.3 %collective-permute-start.19 = (bf16[512,128]{1,0:T(8,128)(2,1)S(1)}, bf16[512,128]{1,0:T(8,128)(2,1)S(1)}, u32[]{:S(2)}, u32[]{:S(2)}) collective-permute-start(bf16[512,128]{1,0:T(8,128)(2,1)S(1)} %fusion.50), channel_id=1, source_target_pairs={{0,3},{1,0},{2,1},{3,2},{4,7},{5,4},{6,5},{7,6},{8,11},{9,8},{10,9... | collective-permute-start | bytes 393224 | tf_op jit(solution)/shard_map/ppermute | solution.py:10
  220.1 9.0 %collective-permute-start.13 = (bf16[512,128]{1,0:T(8,128)(2,1)S(1)}, bf16[512,128]{1,0:T(8,128)(2,1)S(1)}, u32[]{:S(2)}, u32[]{:S(2)}) collective-permute-start(bf16[512,128]{1,0:T(8,128)(2,1)S(1)} %fusion.53), channel_id=1, source_target_pairs={{0,1},{1,2},{2,3},{3,0},{4,5},{5,6},{6,7},{7,4},{8,9},{9,10},{10,1... | collective-permute-start | bytes 393224 | tf_op jit(solution)/shard_map/ppermute | solution.py:10
  (6 other events, 27.2 us)

commit v5 on v4

--- a/solution.py
+++ b/solution.py
@@ -29,26 +29,19 @@
     return jnp.stack(pieces)
 
 
-def ring_reduce_scatter(parts, axis, n):
+def ring_reduce_scatter(term, axis, n):
     if n == 1:
-        return parts[:, 0].astype(jnp.float32)
-    half = parts.shape[0] // 2
-
-    def term(offset, lower):
-        rows = parts[:half] if lower else parts[half:]
-        return rows[:, offset % n]
-
+        return [term(0, True).astype(jnp.float32), term(0, False).astype(jnp.float32)]
     results = []
     for lower, direction in ((True, 1), (False, -1)):
-        carried = term(-direction, lower)
+        carried = term(-direction % n, lower)
         for step in range(1, n):
             arrived = shift(carried, axis, n, direction)
-            total = arrived.astype(jnp.float32) + term(-direction * (step + 1), lower).astype(
-                jnp.float32
-            )
-            carried = total.astype(parts.dtype) if step < n - 1 else total
+            own = term((-direction * (step + 1)) % n, lower)
+            total = arrived.astype(jnp.float32) + own.astype(jnp.float32)
+            carried = total.astype(own.dtype) if step < n - 1 else total
         results.append(carried)
-    return jnp.concatenate(results, axis=0)
+    return results
 
 
 def shards(
@@ -119,13 +112,21 @@
     pre_gate = lax.dot_general(normed, w_gate, dims, preferred_element_type=jnp.float32)
     pre_up = lax.dot_general(normed, w_up, dims, preferred_element_type=jnp.float32)
     hidden = (jax.nn.gelu(pre_gate, approximate=True) * pre_up).astype(jnp.bfloat16)
-    block_out = jnp.dot(
-        hidden, w_down.reshape(ff_local, model_width), preferred_element_type=jnp.float32
-    ).astype(jnp.bfloat16)
-    across_x = ring_reduce_scatter(block_out.reshape(cells, n_x, -1), "mx", n_x)
-    summed = ring_reduce_scatter(
-        across_x.astype(jnp.bfloat16).reshape(cells, n_z, shard_width), "mz", n_z
-    ).astype(jnp.bfloat16)
+    rows_half = cells // 2
+    hidden_halves = {True: hidden[:rows_half], False: hidden[rows_half:]}
+    w_down = w_down.reshape(ff_local, n_x, n_z * shard_width)
+
+    def x_term(k, lower):
+        return jnp.dot(
+            hidden_halves[lower], w_down[:, k], preferred_element_type=jnp.float32
+        ).astype(jnp.bfloat16)
+
+    across_x = [part.astype(jnp.bfloat16) for part in ring_reduce_scatter(x_term, "mx", n_x)]
+
+    def z_term(k, lower):
+        return across_x[0 if lower else 1][:, k * shard_width : (k + 1) * shard_width]
+
+    summed = jnp.concatenate(ring_reduce_scatter(z_term, "mz", n_z), axis=0).astype(jnp.bfloat16)
     gated = (gate_prob[:, None] * summed.astype(jnp.float32)).astype(jnp.bfloat16)
 
     returned = lax.all_to_all(

time: 256 us -> 229 us (0.89); the launches traced: 251 us -> 228 us
  other arithmetic: 41.6 us -> 19 us
  local copies, waits for them, and re-layouts: 39.8 us -> 22.1 us
  waiting for transfers between devices: 33.8 us -> 49.4 us
  starting transfers between devices: 77.7 us -> 80.6 us
    slice x5 -> x0, other arithmetic: 16.2 us -> none  [the longest x3 13.7 us: term(): return rows[:, offset % n]]
    ppermute x20, waiting for transfers between devices: 33.8 us -> 49.4 us  [shift(): return lax.ppermute(value, axis, [(i, (i + step) % n) for i in range(n)])]
    slice x6 -> x3, local copies, waits for them, and re-layouts: 13.7 us -> 2.97 us  [the longest x1 2.93 us: x_term(): w_down[:, k]]
    convert_element_type x8, other arithmetic: 7.38 us -> 0.8 us  [the longest x6 0.48 us: ring_reduce_scatter(): carried = total.astype(own.dtype) if step < n - 1 else total]
    dot_general x1 -> x9, matrix products: 8.44 us -> 5.43 us  [the longest x8 3.77 us: x_term(): jnp.dot(hidden_halves[lower], w_down[:, k], preferred_element_type=jnp.fl...]
    ppermute x20, starting transfers between devices: 77.7 us -> 80.6 us  [shift(): return lax.ppermute(value, axis, [(i, (i + step) % n) for i in range(n)])]
  transfers between devices with their start and end apart: 20 -> 20, of which waited for: 12 -> 14; matrix products, arithmetic and copies ran while one was open for 21% -> 15% of each run, Pallas kernels for 0% -> 0%
where the time goes in v5:
time: 229 us; the launch traced here: 228 us
  starting transfers between devices  80.6 us (35%)
  waiting for transfers between devices  49.4 us (22%)
  blocking collectives  43.2 us (19%)
  local copies, waits for them, and re-layouts  22.1 us (10%)
  other arithmetic  19 us (8%)
  matrix products  13.3 us (6%)
    ppermute x20, starting transfers between devices, shift(): return lax.ppermute(value, axis, [(i, (i + step) % n) for i in range(n)])  80.6 us
    ppermute x20, waiting for transfers between devices, shift(): return lax.ppermute(value, axis, [(i, (i + step) % n) for i in range(n)])  49.4 us
    all_to_all x1, blocking collectives, shards(): lax.all_to_all(masked.reshape(experts, slot_count, shard_width), 'expert'...  22.3 us
    all_to_all x1, blocking collectives, shards(): lax.all_to_all(gated.reshape(experts, slot_count, shard_width), 'expert',...  21 us
    concatenate x6, other arithmetic, relative(): return jnp.roll(blocks, (-at_x, -at_z), axis=axes)  9.34 us
    another operation x2, local copies, waits for them, and re-layouts, shards(): gate_proj[0].reshape(n_x, n_z, shard_width, ff_local)  4.63 us
    another operation x2, local copies, waits for them, and re-layouts, shards(): w_up = relative(up_proj[0].reshape(n_x, n_z, shard_width, ff_local), (0, 1))  4.62 us
  transfers between devices with their start and end apart: 20, of which 14 were waited for; matrix products, arithmetic and copies ran while one was open for 15% of the time, Pallas kernels for 0%

profile of v5, /device:TPU:6, one launch (start us, length us, event | category | flops | bytes accessed | tf_op | source)
XLA Modules:
  0.0 228.2 jit_solution(14056146082366592683)
XLA Ops:
  3.5 22.3 %all_to_all.10 = bf16[32,32,128]{2,1,0:T(8,128)(2,1)S(1)} all-to-all(bf16[32,32,128]{2,1,0:T(8,128)(2,1)S(1)} %bitcast.73), channel_id=1, replica_groups=mesh['expert'=32,'mx'=4,'mz'=4] {'expert'}, dimensions={0} | all-to-all | bytes 524288 | tf_op jit(solution)/shard_map/all_to_all | solution.py:69
  25.7 6.1 %collective-permute-start.1 = (bf16[1024,128]{1,0:T(8,128)(2,1)S(1)}, bf16[1024,128]{1,0:T(8,128)(2,1)S(1)}, u32[]{:S(2)}, u32[]{:S(2)}) collective-permute-start(bf16[1024,128]{1,0:T(8,128)(2,1)S(1)} %bitcast.66), channel_id=1, source_target_pairs={{0,1},{1,2},{2,3},{3,0},{4,5},{5,6},{6,7},{7,4},{8,9},{9,10},{10,1... | collective-permute-start | bytes 786440 | tf_op jit(solution)/shard_map/ppermute | solution.py:10
  31.8 5.9 %collective-permute-start = (bf16[1024,128]{1,0:T(8,128)(2,1)S(1)}, bf16[1024,128]{1,0:T(8,128)(2,1)S(1)}, u32[]{:S(2)}, u32[]{:S(2)}) collective-permute-start(bf16[1024,128]{1,0:T(8,128)(2,1)S(1)} %bitcast.67), channel_id=1, source_target_pairs={{0,3},{1,0},{2,1},{3,2},{4,7},{5,4},{6,5},{7,6},{8,11},{9,8},{10,9... | collective-permute-start | bytes 786440 | tf_op jit(solution)/shard_map/ppermute | solution.py:10
  37.7 9.2 %collective-permute-done.1 = bf16[1024,128]{1,0:T(8,128)(2,1)S(1)} collective-permute-done((bf16[1024,128]{1,0:T(8,128)(2,1)S(1)}, bf16[1024,128]{1,0:T(8,128)(2,1)S(1)}, u32[]{:S(2)}, u32[]{:S(2)}) %collective-permute-start.1) | collective-permute-done | bytes 262176 | tf_op jit(solution)/shard_map/ppermute | solution.py:10
  48.9 6.0 %collective-permute-start.3 = (bf16[512,128]{1,0:T(8,128)(2,1)S(1)}, bf16[512,128]{1,0:T(8,128)(2,1)S(1)}, u32[]{:S(2)}, u32[]{:S(2)}) collective-permute-start(bf16[512,128]{1,0:T(8,128)(2,1)S(1)} %slice.77), channel_id=1, source_target_pairs={{0,3},{1,0},{2,1},{3,2},{4,7},{5,4},{6,5},{7,6},{8,11},{9,8},{10,9... | collective-permute-start | bytes 393224 | tf_op jit(solution)/shard_map/ppermute | solution.py:10
  62.3 4.5 %collective-permute-start.5 = (bf16[4,1024,128]{2,1,0:T(8,128)(2,1)}, bf16[4,1024,128]{2,1,0:T(8,128)(2,1)}, u32[]{:S(2)}, u32[]{:S(2)}) collective-permute-start(bf16[4,1024,128]{2,1,0:T(8,128)(2,1)} %get-tuple-element.11), channel_id=1, source_target_pairs={{0,4},{4,8},{8,12},{12,0},{1,5},{5,9},{9,13},{13,1},{2,6},{6,10},{... | collective-permute-start | bytes 3145736 | tf_op jit(solution)/shard_map/ppermute | solution.py:10
  67.0 3.2 %reshape_squeeze.9 = bf16[4,4,128,320]{2,1,0,3:T(4,128)(2,1)S(1)} reshape(bf16[1,2048,320]{1,2,0:T(8,128)(2,1)} %param.14) | data formatting | bytes 2621440 | tf_op jit(solution)/shard_map/reshape;squeeze | solution.py:106
  71.6 3.2 %reshape_squeeze.10 = bf16[4,4,128,320]{2,1,0,3:T(4,128)(2,1)S(1)} reshape(bf16[1,2048,320]{1,2,0:T(8,128)(2,1)} %param.15) | data formatting | bytes 2621440 | tf_op jit(solution)/shard_map/reshape;squeeze | solution.py:107
  81.1 3.4 %fusion.21 = bf16[320,4,4,128]{3,2,1,0:T(4,128)(2,1)} fusion(s32[]{:T(128)S(6)} %select_n.73, bf16[320,4,4,128]{3,2,1,0:T(4,128)(2,1)S(1)} %fusion.22), kind=kLoop, calls=%fused_computation.38 | loop fusion | flops 2621440 | bytes 2621444 | tf_op jit(solution)/shard_map/jit(_roll_dynamic)/concatenate | solution.py:81
  87.5 4.2 %fusion.25 = (bf16[4,4,128,320]{2,3,1,0:T(8,128)(2,1)}, bf16[4,4,128,320]{2,3,1,0:T(8,128)(2,1)}) fusion(s32[]{:T(128)S(6)} %select_n.71, bf16[4,4,128,320]{2,3,1,0:T(8,128)(2,1)} %copy.22, bf16[4,4,128,320]{2,3,1,0:T(8,128)(2,1)} %copy.20), kind=kLoop, calls=%fused_computation.41 | loop fusion | flops 1310720 | bytes 5242884 | tf_op jit(solution)/shard_map/jit(_roll_dynamic)/concatenate | solution.py:81
  95.8 5.4 %collective-permute-start.6 = (bf16[2,1024,128]{2,1,0:T(8,128)(2,1)S(1)}, bf16[2,1024,128]{2,1,0:T(8,128)(2,1)S(1)}, u32[]{:S(2)}, u32[]{:S(2)}) collective-permute-start(bf16[2,1024,128]{2,1,0:T(8,128)(2,1)S(1)} %slice.78), channel_id=1, source_target_pairs={{0,4},{4,8},{8,12},{12,0},{1,5},{5,9},{9,13},{13,1},{2,6},{6,10},{... | collective-permute-start | bytes 1572872 | tf_op jit(solution)/shard_map/ppermute | solution.py:10
  104.1 4.4 %collective-permute-done.7 = bf16[2,1024,128]{2,1,0:T(8,128)(2,1)S(1)} collective-permute-done((bf16[2,1024,128]{2,1,0:T(8,128)(2,1)S(1)}, bf16[2,1024,128]{2,1,0:T(8,128)(2,1)S(1)}, u32[]{:S(2)}, u32[]{:S(2)}) %collective-permute-start.7) | collective-permute-done | bytes 524320 | tf_op jit(solution)/shard_map/ppermute | solution.py:10
  118.2 3.9 %convolution_bitcast_fusion.1 = f32[1024,320]{0,1:T(8,128)S(1)} fusion(bf16[4,4,1024,128]{3,2,1,0:T(8,128)(2,1)} %copy-done.1, s32[]{:T(128)S(6)} %select_n.73, bf16[4,4,128,320]{2,3,1,0:T(8,128)(2,1)S(1)} %copy-done.6), kind=kOutput, calls=%fused_computation.29 | convolution fusion | flops 1342832640 | bytes 6815748 | tf_op jit(solution)/shard_map/dot_general | solution.py:112
  125.4 5.7 %collective-permute-start.8 = (bf16[512,512]{1,0:T(8,128)(2,1)S(1)}, bf16[512,512]{1,0:T(8,128)(2,1)S(1)}, u32[]{:S(2)}, u32[]{:S(2)}) collective-permute-start(bf16[512,512]{1,0:T(8,128)(2,1)S(1)} %convolution_convert_fusion.7), channel_id=1, source_target_pairs={{0,4},{4,8},{8,12},{12,0},{1,5},{5,9},{9,13},{13,1},{2,6},{6,10},{... | collective-permute-start | bytes 1572872 | tf_op jit(solution)/shard_map/ppermute | solution.py:10
  134.0 11.3 %collective-permute-done.14 = bf16[512,512]{1,0:T(8,128)(2,1)S(1)} collective-permute-done((bf16[512,512]{1,0:T(8,128)(2,1)S(1)}, bf16[512,512]{1,0:T(8,128)(2,1)S(1)}, u32[]{:S(2)}, u32[]{:S(2)}) %collective-permute-start.14) | collective-permute-done | bytes 524320 | tf_op jit(solution)/shard_map/ppermute | solution.py:10
  148.2 5.1 %collective-permute-start.9 = (bf16[512,512]{1,0:T(8,128)(2,1)S(1)}, bf16[512,512]{1,0:T(8,128)(2,1)S(1)}, u32[]{:S(2)}, u32[]{:S(2)}) collective-permute-start(bf16[512,512]{1,0:T(8,128)(2,1)S(1)} %add_convert_fusion.5), channel_id=1, source_target_pairs={{0,4},{4,8},{8,12},{12,0},{1,5},{5,9},{9,13},{13,1},{2,6},{6,10},{... | collective-permute-start | bytes 1572872 | tf_op jit(solution)/shard_map/ppermute | solution.py:10
  153.9 5.3 %collective-permute-done.15 = bf16[512,512]{1,0:T(8,128)(2,1)S(1)} collective-permute-done((bf16[512,512]{1,0:T(8,128)(2,1)S(1)}, bf16[512,512]{1,0:T(8,128)(2,1)S(1)}, u32[]{:S(2)}, u32[]{:S(2)}) %collective-permute-start.15) | collective-permute-done | bytes 524320 | tf_op jit(solution)/shard_map/ppermute | solution.py:10
  161.4 5.2 %collective-permute-start.10 = (bf16[512,512]{1,0:T(8,128)(2,1)S(1)}, bf16[512,512]{1,0:T(8,128)(2,1)S(1)}, u32[]{:S(2)}, u32[]{:S(2)}) collective-permute-start(bf16[512,512]{1,0:T(8,128)(2,1)S(1)} %add_convert_fusion.4), channel_id=1, source_target_pairs={{0,4},{4,8},{8,12},{12,0},{1,5},{5,9},{9,13},{13,1},{2,6},{6,10},{... | collective-permute-start | bytes 1572872 | tf_op jit(solution)/shard_map/ppermute | solution.py:10
  167.0 4.6 %collective-permute-done.16 = bf16[512,512]{1,0:T(8,128)(2,1)S(1)} collective-permute-done((bf16[512,512]{1,0:T(8,128)(2,1)S(1)}, bf16[512,512]{1,0:T(8,128)(2,1)S(1)}, u32[]{:S(2)}, u32[]{:S(2)}) %collective-permute-start.16) | collective-permute-done | bytes 524320 | tf_op jit(solution)/shard_map/ppermute | solution.py:10
  174.7 4.1 %collective-permute-start.11 = (bf16[512,128]{1,0:T(8,128)(2,1)S(1)}, bf16[512,128]{1,0:T(8,128)(2,1)S(1)}, u32[]{:S(2)}, u32[]{:S(2)}) collective-permute-start(bf16[512,128]{1,0:T(8,128)(2,1)S(1)} %slice.85), channel_id=1, source_target_pairs={{0,1},{1,2},{2,3},{3,0},{4,5},{5,6},{6,7},{7,4},{8,9},{9,10},{10,1... | collective-permute-start | bytes 393224 | tf_op jit(solution)/shard_map/ppermute | solution.py:10
  182.0 3.8 %collective-permute-start.18 = (bf16[512,128]{1,0:T(8,128)(2,1)S(1)}, bf16[512,128]{1,0:T(8,128)(2,1)S(1)}, u32[]{:S(2)}, u32[]{:S(2)}) collective-permute-start(bf16[512,128]{1,0:T(8,128)(2,1)S(1)} %add_convert_fusion.8), channel_id=1, source_target_pairs={{0,3},{1,0},{2,1},{3,2},{4,7},{5,4},{6,5},{7,6},{8,11},{9,8},{10,9... | collective-permute-start | bytes 393224 | tf_op jit(solution)/shard_map/ppermute | solution.py:10
  190.3 5.5 %collective-permute-start.19 = (bf16[512,128]{1,0:T(8,128)(2,1)S(1)}, bf16[512,128]{1,0:T(8,128)(2,1)S(1)}, u32[]{:S(2)}, u32[]{:S(2)}) collective-permute-start(bf16[512,128]{1,0:T(8,128)(2,1)S(1)} %add_convert_fusion.7), channel_id=1, source_target_pairs={{0,3},{1,0},{2,1},{3,2},{4,7},{5,4},{6,5},{7,6},{8,11},{9,8},{10,9... | collective-permute-start | bytes 393224 | tf_op jit(solution)/shard_map/ppermute | solution.py:10
  196.5 5.2 %collective-permute-start.13 = (bf16[512,128]{1,0:T(8,128)(2,1)S(1)}, bf16[512,128]{1,0:T(8,128)(2,1)S(1)}, u32[]{:S(2)}, u32[]{:S(2)}) collective-permute-start(bf16[512,128]{1,0:T(8,128)(2,1)S(1)} %add_convert_fusion.10), channel_id=1, source_target_pairs={{0,1},{1,2},{2,3},{3,0},{4,5},{5,6},{6,7},{7,4},{8,9},{9,10},{10,1... | collective-permute-start | bytes 393224 | tf_op jit(solution)/shard_map/ppermute | solution.py:10
  205.8 21.0 %all_to_all.11 = bf16[32,32,128]{2,1,0:T(8,128)(2,1)S(1)} all-to-all(bf16[32,32,128]{2,1,0:T(8,128)(2,1)S(1)} %fusion.43), channel_id=1, replica_groups=mesh['expert'=32,'mx'=4,'mz'=4] {'expert'}, dimensions={0} | all-to-all | bytes 524288 | tf_op jit(solution)/shard_map/all_to_all | solution.py:132
  (96 shorter events, 69.2 us)
Async XLA Ops:
  25.7 21.2 %collective-permute-start.1 = (bf16[1024,128]{1,0:T(8,128)(2,1)S(1)}, bf16[1024,128]{1,0:T(8,128)(2,1)S(1)}, u32[]{:S(2)}, u32[]{:S(2)}) collective-permute-start(bf16[1024,128]{1,0:T(8,128)(2,1)S(1)} %bitcast.66), channel_id=1, source_target_pairs={{0,1},{1,2},{2,3},{3,0},{4,5},{5,6},{6,7},{7,4},{8,9},{9,10},{10,1... | collective-permute-start | bytes 786440 | tf_op jit(solution)/shard_map/ppermute | solution.py:10
  31.8 17.1 %collective-permute-start = (bf16[1024,128]{1,0:T(8,128)(2,1)S(1)}, bf16[1024,128]{1,0:T(8,128)(2,1)S(1)}, u32[]{:S(2)}, u32[]{:S(2)}) collective-permute-start(bf16[1024,128]{1,0:T(8,128)(2,1)S(1)} %bitcast.67), channel_id=1, source_target_pairs={{0,3},{1,0},{2,1},{3,2},{4,7},{5,4},{6,5},{7,6},{8,11},{9,8},{10,9... | collective-permute-start | bytes 786440 | tf_op jit(solution)/shard_map/ppermute | solution.py:10
  47.0 9.0 %collective-permute-start.2 = (bf16[512,128]{1,0:T(8,128)(2,1)S(1)}, bf16[512,128]{1,0:T(8,128)(2,1)S(1)}, u32[]{:S(2)}, u32[]{:S(2)}) collective-permute-start(bf16[512,128]{1,0:T(8,128)(2,1)S(1)} %slice.76), channel_id=1, source_target_pairs={{0,1},{1,2},{2,3},{3,0},{4,5},{5,6},{6,7},{7,4},{8,9},{9,10},{10,1... | collective-permute-start | bytes 393224 | tf_op jit(solution)/shard_map/ppermute | solution.py:10
  48.9 9.5 %collective-permute-start.3 = (bf16[512,128]{1,0:T(8,128)(2,1)S(1)}, bf16[512,128]{1,0:T(8,128)(2,1)S(1)}, u32[]{:S(2)}, u32[]{:S(2)}) collective-permute-start(bf16[512,128]{1,0:T(8,128)(2,1)S(1)} %slice.77), channel_id=1, source_target_pairs={{0,3},{1,0},{2,1},{3,2},{4,7},{5,4},{6,5},{7,6},{8,11},{9,8},{10,9... | collective-permute-start | bytes 393224 | tf_op jit(solution)/shard_map/ppermute | solution.py:10
  58.4 8.4 %copy-start.8 = (bf16[2048,32]{0,1:T(8,128)(2,1)S(1)}, bf16[2048,32]{0,1:T(8,128)(2,1)}, u32[]{:S(2)}) copy-start(bf16[2048,32]{0,1:T(8,128)(2,1)} %param.13) | copy-start | bytes 393220
  59.6 32.1 %collective-permute-start.4 = (bf16[4,1024,128]{2,1,0:T(8,128)(2,1)}, bf16[4,1024,128]{2,1,0:T(8,128)(2,1)}, u32[]{:S(2)}, u32[]{:S(2)}) collective-permute-start(bf16[4,1024,128]{2,1,0:T(8,128)(2,1)} %get-tuple-element.11), channel_id=1, source_target_pairs={{0,12},{4,0},{8,4},{12,8},{1,13},{5,1},{9,5},{13,9},{2,14},{6,2},{... | collective-permute-start | bytes 3145736 | tf_op jit(solution)/shard_map/ppermute | solution.py:10
  62.3 32.4 %collective-permute-start.5 = (bf16[4,1024,128]{2,1,0:T(8,128)(2,1)}, bf16[4,1024,128]{2,1,0:T(8,128)(2,1)}, u32[]{:S(2)}, u32[]{:S(2)}) collective-permute-start(bf16[4,1024,128]{2,1,0:T(8,128)(2,1)} %get-tuple-element.11), channel_id=1, source_target_pairs={{0,4},{4,8},{8,12},{12,0},{1,5},{5,9},{9,13},{13,1},{2,6},{6,10},{... | collective-permute-start | bytes 3145736 | tf_op jit(solution)/shard_map/ppermute | solution.py:10
  92.8 15.7 %collective-permute-start.7 = (bf16[2,1024,128]{2,1,0:T(8,128)(2,1)S(1)}, bf16[2,1024,128]{2,1,0:T(8,128)(2,1)S(1)}, u32[]{:S(2)}, u32[]{:S(2)}) collective-permute-start(bf16[2,1024,128]{2,1,0:T(8,128)(2,1)S(1)} %slice.79), channel_id=1, source_target_pairs={{0,12},{4,0},{8,4},{12,8},{1,13},{5,1},{9,5},{13,9},{2,14},{6,2},{... | collective-permute-start | bytes 1572872 | tf_op jit(solution)/shard_map/ppermute | solution.py:10
  95.8 14.9 %collective-permute-start.6 = (bf16[2,1024,128]{2,1,0:T(8,128)(2,1)S(1)}, bf16[2,1024,128]{2,1,0:T(8,128)(2,1)S(1)}, u32[]{:S(2)}, u32[]{:S(2)}) collective-permute-start(bf16[2,1024,128]{2,1,0:T(8,128)(2,1)S(1)} %slice.78), channel_id=1, source_target_pairs={{0,4},{4,8},{8,12},{12,0},{1,5},{5,9},{9,13},{13,1},{2,6},{6,10},{... | collective-permute-start | bytes 1572872 | tf_op jit(solution)/shard_map/ppermute | solution.py:10
  118.2 3.9 %copy-start.2 = (bf16[4,4,1024,128]{3,2,1,0:T(8,128)(2,1)S(1)}, bf16[4,4,1024,128]{3,2,1,0:T(8,128)(2,1)}, u32[]{:S(2)}) copy-start(bf16[4,4,1024,128]{3,2,1,0:T(8,128)(2,1)} %copy-done.1) | copy-start | bytes 12582916
  118.2 3.9 %copy-start.5 = (bf16[4,4,128,320]{2,3,1,0:T(8,128)(2,1)S(1)}, bf16[4,4,128,320]{2,3,1,0:T(8,128)(2,1)}, u32[]{:S(2)}) copy-start(bf16[4,4,128,320]{2,3,1,0:T(8,128)(2,1)} %get-tuple-element.12) | copy-start | bytes 3932164
  125.4 20.0 %copy-start.7 = (bf16[320,1,512]{2,1,0:T(2,128)(2,1)S(1)}, bf16[320,1,512]{2,1,0:T(2,128)(2,1)}, u32[]{:S(2)}) copy-start(bf16[320,1,512]{2,1,0:T(2,128)(2,1)} %get-tuple-element.6) | copy-start | bytes 983044
  125.4 22.4 %collective-permute-start.8 = (bf16[512,512]{1,0:T(8,128)(2,1)S(1)}, bf16[512,512]{1,0:T(8,128)(2,1)S(1)}, u32[]{:S(2)}, u32[]{:S(2)}) collective-permute-start(bf16[512,512]{1,0:T(8,128)(2,1)S(1)} %convolution_convert_fusion.7), channel_id=1, source_target_pairs={{0,4},{4,8},{8,12},{12,0},{1,5},{5,9},{9,13},{13,1},{2,6},{6,10},{... | collective-permute-start | bytes 1572872 | tf_op jit(solution)/shard_map/ppermute | solution.py:10
  131.1 14.2 %collective-permute-start.14 = (bf16[512,512]{1,0:T(8,128)(2,1)S(1)}, bf16[512,512]{1,0:T(8,128)(2,1)S(1)}, u32[]{:S(2)}, u32[]{:S(2)}) collective-permute-start(bf16[512,512]{1,0:T(8,128)(2,1)S(1)} %convolution_convert_fusion.3), channel_id=1, source_target_pairs={{0,12},{4,0},{8,4},{12,8},{1,13},{5,1},{9,5},{13,9},{2,14},{6,2},{... | collective-permute-start | bytes 1572872 | tf_op jit(solution)/shard_map/ppermute | solution.py:10
  145.8 13.3 %collective-permute-start.15 = (bf16[512,512]{1,0:T(8,128)(2,1)S(1)}, bf16[512,512]{1,0:T(8,128)(2,1)S(1)}, u32[]{:S(2)}, u32[]{:S(2)}) collective-permute-start(bf16[512,512]{1,0:T(8,128)(2,1)S(1)} %add_convert_fusion.2), channel_id=1, source_target_pairs={{0,12},{4,0},{8,4},{12,8},{1,13},{5,1},{9,5},{13,9},{2,14},{6,2},{... | collective-permute-start | bytes 1572872 | tf_op jit(solution)/shard_map/ppermute | solution.py:10
  148.2 13.0 %collective-permute-start.9 = (bf16[512,512]{1,0:T(8,128)(2,1)S(1)}, bf16[512,512]{1,0:T(8,128)(2,1)S(1)}, u32[]{:S(2)}, u32[]{:S(2)}) collective-permute-start(bf16[512,512]{1,0:T(8,128)(2,1)S(1)} %add_convert_fusion.5), channel_id=1, source_target_pairs={{0,4},{4,8},{8,12},{12,0},{1,5},{5,9},{9,13},{13,1},{2,6},{6,10},{... | collective-permute-start | bytes 1572872 | tf_op jit(solution)/shard_map/ppermute | solution.py:10
  159.3 12.4 %collective-permute-start.16 = (bf16[512,512]{1,0:T(8,128)(2,1)S(1)}, bf16[512,512]{1,0:T(8,128)(2,1)S(1)}, u32[]{:S(2)}, u32[]{:S(2)}) collective-permute-start(bf16[512,512]{1,0:T(8,128)(2,1)S(1)} %add_convert_fusion.1), channel_id=1, source_target_pairs={{0,12},{4,0},{8,4},{12,8},{1,13},{5,1},{9,5},{13,9},{2,14},{6,2},{... | collective-permute-start | bytes 1572872 | tf_op jit(solution)/shard_map/ppermute | solution.py:10
  161.4 13.1 %collective-permute-start.10 = (bf16[512,512]{1,0:T(8,128)(2,1)S(1)}, bf16[512,512]{1,0:T(8,128)(2,1)S(1)}, u32[]{:S(2)}, u32[]{:S(2)}) collective-permute-start(bf16[512,512]{1,0:T(8,128)(2,1)S(1)} %add_convert_fusion.4), channel_id=1, source_target_pairs={{0,4},{4,8},{8,12},{12,0},{1,5},{5,9},{9,13},{13,1},{2,6},{6,10},{... | collective-permute-start | bytes 1572872 | tf_op jit(solution)/shard_map/ppermute | solution.py:10
  171.8 10.1 %collective-permute-start.17 = (bf16[512,128]{1,0:T(8,128)(2,1)S(1)}, bf16[512,128]{1,0:T(8,128)(2,1)S(1)}, u32[]{:S(2)}, u32[]{:S(2)}) collective-permute-start(bf16[512,128]{1,0:T(8,128)(2,1)S(1)} %slice.90), channel_id=1, source_target_pairs={{0,3},{1,0},{2,1},{3,2},{4,7},{5,4},{6,5},{7,6},{8,11},{9,8},{10,9... | collective-permute-start | bytes 393224 | tf_op jit(solution)/shard_map/ppermute | solution.py:10
  174.7 11.4 %collective-permute-start.11 = (bf16[512,128]{1,0:T(8,128)(2,1)S(1)}, bf16[512,128]{1,0:T(8,128)(2,1)S(1)}, u32[]{:S(2)}, u32[]{:S(2)}) collective-permute-start(bf16[512,128]{1,0:T(8,128)(2,1)S(1)} %slice.85), channel_id=1, source_target_pairs={{0,1},{1,2},{2,3},{3,0},{4,5},{5,6},{6,7},{7,4},{8,9},{9,10},{10,1... | collective-permute-start | bytes 393224 | tf_op jit(solution)/shard_map/ppermute | solution.py:10
  182.0 8.2 %collective-permute-start.18 = (bf16[512,128]{1,0:T(8,128)(2,1)S(1)}, bf16[512,128]{1,0:T(8,128)(2,1)S(1)}, u32[]{:S(2)}, u32[]{:S(2)}) collective-permute-start(bf16[512,128]{1,0:T(8,128)(2,1)S(1)} %add_convert_fusion.8), channel_id=1, source_target_pairs={{0,3},{1,0},{2,1},{3,2},{4,7},{5,4},{6,5},{7,6},{8,11},{9,8},{10,9... | collective-permute-start | bytes 393224 | tf_op jit(solution)/shard_map/ppermute | solution.py:10
  186.1 10.4 %collective-permute-start.12 = (bf16[512,128]{1,0:T(8,128)(2,1)S(1)}, bf16[512,128]{1,0:T(8,128)(2,1)S(1)}, u32[]{:S(2)}, u32[]{:S(2)}) collective-permute-start(bf16[512,128]{1,0:T(8,128)(2,1)S(1)} %add_convert_fusion.11), channel_id=1, source_target_pairs={{0,1},{1,2},{2,3},{3,0},{4,5},{5,6},{6,7},{7,4},{8,9},{9,10},{10,1... | collective-permute-start | bytes 393224 | tf_op jit(solution)/shard_map/ppermute | solution.py:10
  190.3 12.5 %collective-permute-start.19 = (bf16[512,128]{1,0:T(8,128)(2,1)S(1)}, bf16[512,128]{1,0:T(8,128)(2,1)S(1)}, u32[]{:S(2)}, u32[]{:S(2)}) collective-permute-start(bf16[512,128]{1,0:T(8,128)(2,1)S(1)} %add_convert_fusion.7), channel_id=1, source_target_pairs={{0,3},{1,0},{2,1},{3,2},{4,7},{5,4},{6,5},{7,6},{8,11},{9,8},{10,9... | collective-permute-start | bytes 393224 | tf_op jit(solution)/shard_map/ppermute | solution.py:10
  196.5 9.0 %collective-permute-start.13 = (bf16[512,128]{1,0:T(8,128)(2,1)S(1)}, bf16[512,128]{1,0:T(8,128)(2,1)S(1)}, u32[]{:S(2)}, u32[]{:S(2)}) collective-permute-start(bf16[512,128]{1,0:T(8,128)(2,1)S(1)} %add_convert_fusion.10), channel_id=1, source_target_pairs={{0,1},{1,2},{2,3},{3,0},{4,5},{5,6},{6,7},{7,4},{8,9},{9,10},{10,1... | collective-permute-start | bytes 393224 | tf_op jit(solution)/shard_map/ppermute | solution.py:10
  (6 other events, 12.1 us)

commit v6 on v5

--- a/solution.py
+++ b/solution.py
@@ -77,54 +77,48 @@
     n_x = n_mp // n_z
     at_x, at_z = lax.axis_index("mx"), lax.axis_index("mz")
 
-    def relative(blocks, axes):
-        return jnp.roll(blocks, (-at_x, -at_z), axis=axes)
+    def rows_relative(w):
+        lead = w.shape[0]
+        w = jnp.roll(w, -at_x * (lead // n_x), axis=0)
+        w = jnp.roll(w.reshape(n_x, lead // n_x, *w.shape[1:]), -at_z * (lead // n_mp), axis=1)
+        return w.reshape(lead, *w.shape[2:])
 
     part = ring_gather(received, "mz", n_z)
     whole = ring_gather(part, "mx", n_x).reshape(n_mp, cells, shard_width)
 
-    features = whole.astype(jnp.float32)
-    mean_square = jnp.sum(features * features, axis=(0, 2)) / model_width
+    features = jnp.transpose(whole, (1, 0, 2)).reshape(cells, model_width).astype(jnp.float32)
+    mean_square = jnp.sum(features * features, axis=1) / model_width
     scale = lax.rsqrt(mean_square + norm_eps)
-    gain = relative(norm_gain.reshape(n_x, n_z, shard_width), (0, 1)).reshape(n_mp, 1, shard_width)
-    normed = (features * scale[None, :, None] * gain).astype(jnp.bfloat16)
+    normed = (features * scale[:, None] * rows_relative(norm_gain)).astype(jnp.bfloat16)
 
-    logits = lax.dot_general(
-        normed,
-        relative(router_weight.reshape(n_x, n_z, shard_width, experts), (0, 1)).reshape(
-            n_mp, shard_width, experts
-        ),
-        (((0, 2), (0, 1)), ((), ())),
-        preferred_element_type=jnp.float32,
-    )
+    logits = jnp.dot(normed, rows_relative(router_weight), preferred_element_type=jnp.float32)
     picked = jnp.sum(
         jnp.where(jnp.arange(experts, dtype=jnp.int32)[None, :] == me, logits, 0.0), axis=1
     )
     gate_prob = jax.nn.sigmoid(picked)
 
     ff_local = gate_proj.shape[2]
-    w_gate = relative(gate_proj[0].reshape(n_x, n_z, shard_width, ff_local), (0, 1))
-    w_up = relative(up_proj[0].reshape(n_x, n_z, shard_width, ff_local), (0, 1))
-    w_gate = w_gate.reshape(n_mp, shard_width, ff_local)
-    w_up = w_up.reshape(n_mp, shard_width, ff_local)
-    w_down = relative(down_proj[0].reshape(ff_local, n_x, n_z, shard_width), (1, 2))
-    dims = (((0, 2), (0, 1)), ((), ()))
-    pre_gate = lax.dot_general(normed, w_gate, dims, preferred_element_type=jnp.float32)
-    pre_up = lax.dot_general(normed, w_up, dims, preferred_element_type=jnp.float32)
+    pre_gate = jnp.dot(normed, rows_relative(gate_proj[0]), preferred_element_type=jnp.float32)
+    pre_up = jnp.dot(normed, rows_relative(up_proj[0]), preferred_element_type=jnp.float32)
     hidden = (jax.nn.gelu(pre_gate, approximate=True) * pre_up).astype(jnp.bfloat16)
     rows_half = cells // 2
     hidden_halves = {True: hidden[:rows_half], False: hidden[rows_half:]}
-    w_down = w_down.reshape(ff_local, n_x, n_z * shard_width)
+    x_width = model_width // n_x
 
     def x_term(k, lower):
-        return jnp.dot(
-            hidden_halves[lower], w_down[:, k], preferred_element_type=jnp.float32
-        ).astype(jnp.bfloat16)
+        columns = lax.dynamic_slice_in_dim(
+            down_proj[0], ((at_x + k) % n_x) * x_width, x_width, axis=1
+        )
+        return jnp.dot(hidden_halves[lower], columns, preferred_element_type=jnp.float32).astype(
+            jnp.bfloat16
+        )
 
     across_x = [part.astype(jnp.bfloat16) for part in ring_reduce_scatter(x_term, "mx", n_x)]
 
     def z_term(k, lower):
-        return across_x[0 if lower else 1][:, k * shard_width : (k + 1) * shard_width]
+        return lax.dynamic_slice_in_dim(
+            across_x[0 if lower else 1], ((at_z + k) % n_z) * shard_width, shard_width, axis=1
+        )
 
     summed = jnp.concatenate(ring_reduce_scatter(z_term, "mz", n_z), axis=0).astype(jnp.bfloat16)
     gated = (gate_prob[:, None] * summed.astype(jnp.float32)).astype(jnp.bfloat16)

time: 229 us -> 219 us (0.956)
  starting transfers between devices: 80.6 us -> 69.3 us
  local copies, waits for them, and re-layouts: 22.1 us -> 11.4 us
  waiting for transfers between devices: 49.4 us -> 57.8 us
    another operation x5 -> x1, local copies, waits for them, and re-layouts: 12.5 us -> 0.14 us  [ring_gather(): return jnp.stack(pieces)]
    ppermute x20, starting transfers between devices: 80.6 us -> 69.3 us  [shift(): return lax.ppermute(value, axis, [(i, (i + step) % n) for i in range(n)])]
    ppermute x20, waiting for transfers between devices: 49.4 us -> 57.8 us  [shift(): return lax.ppermute(value, axis, [(i, (i + step) % n) for i in range(n)])]
    another operation x3 -> x4, other arithmetic: 1.24 us -> 4.64 us  [ring_gather(): return jnp.stack(pieces)]
    slice x3 -> x0, local copies, waits for them, and re-layouts: 2.97 us -> none  [the longest x1 2.93 us: x_term(): w_down[:, k]]
    unnamed x20 -> x19, local copies, waits for them, and re-layouts: 1.48 us -> 4.25 us
    concatenate x6 -> x7, other arithmetic: 9.34 us -> 8.93 us  [the longest x3 5.03 us: rows_relative(): jnp.roll(w.reshape(n_x, lead // n_x, *w.shape[1:]), -at_z * (lead // n_mp...]
  transfers between devices with their start and end apart: 20 -> 20, of which waited for: 14 -> 15; matrix products, arithmetic and copies ran while one was open for 15% -> 13% of each run, Pallas kernels for 0% -> 0%
where the time goes in v6:
time: 219 us; the launch traced here: 216 us
  starting transfers between devices  69.3 us (32%)
  waiting for transfers between devices  57.8 us (26%)
  blocking collectives  42.3 us (19%)
  other arithmetic  20.6 us (9%)
  matrix products  14.3 us (7%)
  local copies, waits for them, and re-layouts  11.4 us (5%)
    ppermute x20, starting transfers between devices, shift(): return lax.ppermute(value, axis, [(i, (i + step) % n) for i in range(n)])  69.3 us
    ppermute x20, waiting for transfers between devices, shift(): return lax.ppermute(value, axis, [(i, (i + step) % n) for i in range(n)])  57.8 us
    all_to_all x1, blocking collectives, shards(): lax.all_to_all(masked.reshape(experts, slot_count, shard_width), 'expert'...  22.3 us
    all_to_all x1, blocking collectives, shards(): lax.all_to_all(gated.reshape(experts, slot_count, shard_width), 'expert',...  20.1 us
    dot_general x8, matrix products, x_term(): jnp.dot(hidden_halves[lower], columns, preferred_element_type=jnp.float32)  6.59 us
    concatenate x3, other arithmetic, rows_relative(): jnp.roll(w.reshape(n_x, lead // n_x, *w.shape[1:]), -at_z * (lead // n_mp...  5.03 us
    another operation x4, other arithmetic, ring_gather(): return jnp.stack(pieces)  4.64 us
  transfers between devices with their start and end apart: 20, of which 15 were waited for; matrix products, arithmetic and copies ran while one was open for 13% of the time, Pallas kernels for 0%

profile of v6, /device:TPU:6, one launch (start us, length us, event | category | flops | bytes accessed | tf_op | source)
XLA Modules:
  0.0 216.4 jit_solution(12585720411374658886)
XLA Ops:
  4.5 22.3 %all_to_all.10 = bf16[32,32,128]{2,1,0:T(8,128)(2,1)S(1)} all-to-all(bf16[32,32,128]{2,1,0:T(8,128)(2,1)S(1)} %bitcast.92), channel_id=1, replica_groups=mesh['expert'=32,'mx'=4,'mz'=4] {'expert'}, dimensions={0} | all-to-all | bytes 524288 | tf_op jit(solution)/shard_map/all_to_all | solution.py:69
  26.9 6.1 %collective-permute-start.1 = (bf16[1024,128]{0,1:T(8,128)(2,1)S(1)}, bf16[1024,128]{0,1:T(8,128)(2,1)S(1)}, u32[]{:S(2)}, u32[]{:S(2)}) collective-permute-start(bf16[1024,128]{0,1:T(8,128)(2,1)S(1)} %copy.13), channel_id=1, source_target_pairs={{0,1},{1,2},{2,3},{3,0},{4,5},{5,6},{6,7},{7,4},{8,9},{9,10},{10,1... | collective-permute-start | bytes 786440 | tf_op jit(solution)/shard_map/ppermute | solution.py:10
  33.0 5.9 %collective-permute-start = (bf16[1024,128]{0,1:T(8,128)(2,1)S(1)}, bf16[1024,128]{0,1:T(8,128)(2,1)S(1)}, u32[]{:S(2)}, u32[]{:S(2)}) collective-permute-start(bf16[1024,128]{0,1:T(8,128)(2,1)S(1)} %copy.13), channel_id=1, source_target_pairs={{0,3},{1,0},{2,1},{3,2},{4,7},{5,4},{6,5},{7,6},{8,11},{9,8},{10,9... | collective-permute-start | bytes 786440 | tf_op jit(solution)/shard_map/ppermute | solution.py:10
  38.9 9.2 %collective-permute-done.1 = bf16[1024,128]{0,1:T(8,128)(2,1)S(1)} collective-permute-done((bf16[1024,128]{0,1:T(8,128)(2,1)S(1)}, bf16[1024,128]{0,1:T(8,128)(2,1)S(1)}, u32[]{:S(2)}, u32[]{:S(2)}) %collective-permute-start.1) | collective-permute-done | bytes 262176 | tf_op jit(solution)/shard_map/ppermute | solution.py:10
  50.1 6.0 %collective-permute-start.3 = (bf16[512,128]{0,1:T(8,128)(2,1)S(1)}, bf16[512,128]{0,1:T(8,128)(2,1)S(1)}, u32[]{:S(2)}, u32[]{:S(2)}) collective-permute-start(bf16[512,128]{0,1:T(8,128)(2,1)S(1)} %slice.25), channel_id=1, source_target_pairs={{0,3},{1,0},{2,1},{3,2},{4,7},{5,4},{6,5},{7,6},{8,11},{9,8},{10,9... | collective-permute-start | bytes 393224 | tf_op jit(solution)/shard_map/ppermute | solution.py:10
  63.5 3.5 %collective-permute-start.4 = (bf16[4,1024,128]{1,2,0:T(8,128)(2,1)}, bf16[4,1024,128]{1,2,0:T(8,128)(2,1)}, u32[]{:S(2)}, u32[]{:S(2)}) collective-permute-start(bf16[4,1024,128]{1,2,0:T(8,128)(2,1)} %get-tuple-element.8), channel_id=1, source_target_pairs={{0,12},{4,0},{8,4},{12,8},{1,13},{5,1},{9,5},{13,9},{2,14},{6,2},{... | collective-permute-start | bytes 3145736 | tf_op jit(solution)/shard_map/ppermute | solution.py:10
  74.6 4.9 %fusion.20 = (bf16[4,512,320]{1,0,2:T(4,128)(2,1)S(1)}, bf16[4,512,320]{1,0,2:T(4,128)(2,1)}) fusion(s32[]{:T(128)S(6)} %select_n.143, bf16[4,512,320]{1,0,2:T(4,128)(2,1)} %reshape.116, bf16[4,512,320]{1,0,2:T(4,128)(2,1)} %reshape.114), kind=kLoop, calls=%fused_computation.32 | loop fusion | flops 5242880 | bytes 5242884 | tf_op jit(solution)/shard_map/jit(_roll_dynamic)/concatenate | solution.py:83
  79.5 8.2 %collective-permute-done.5 = bf16[4,1024,128]{1,2,0:T(8,128)(2,1)} collective-permute-done((bf16[4,1024,128]{1,2,0:T(8,128)(2,1)}, bf16[4,1024,128]{1,2,0:T(8,128)(2,1)}, u32[]{:S(2)}, u32[]{:S(2)}) %collective-permute-start.5) | collective-permute-done | bytes 1048608 | tf_op jit(solution)/shard_map/ppermute | solution.py:10
  88.8 3.6 %collective-permute-start.6 = (bf16[2,1024,128]{1,2,0:T(8,128)(2,1)S(1)}, bf16[2,1024,128]{1,2,0:T(8,128)(2,1)}, u32[]{:S(2)}, u32[]{:S(2)}) collective-permute-start(bf16[2,1024,128]{1,2,0:T(8,128)(2,1)S(1)} %slice.26), channel_id=1, source_target_pairs={{0,4},{4,8},{8,12},{12,0},{1,5},{5,9},{9,13},{13,1},{2,6},{6,10},{... | collective-permute-start | bytes 1572872 | tf_op jit(solution)/shard_map/ppermute | solution.py:10
  96.7 2.8 %copy.17 = bf16[40,8,4,512]{3,1,2,0:T(8,128)(2,1)} copy(bf16[40,8,4,512]{3,2,1,0:T(4,128)(2,1)} %bitcast.79) | data formatting | bytes 2621440
  103.0 6.6 %collective-permute-done.7 = bf16[2,1024,128]{1,2,0:T(8,128)(2,1)} collective-permute-done((bf16[2,1024,128]{1,2,0:T(8,128)(2,1)}, bf16[2,1024,128]{1,2,0:T(8,128)(2,1)}, u32[]{:S(2)}, u32[]{:S(2)}) %collective-permute-start.7) | collective-permute-done | bytes 524320 | tf_op jit(solution)/shard_map/ppermute | solution.py:10
  122.3 3.9 %collective-permute-start.14 = (bf16[512,512]{1,0:T(8,128)(2,1)}, bf16[512,512]{1,0:T(8,128)(2,1)}, u32[]{:S(2)}, u32[]{:S(2)}) collective-permute-start(bf16[512,512]{1,0:T(8,128)(2,1)} %convolution_convert_fusion.3), channel_id=1, source_target_pairs={{0,12},{4,0},{8,4},{12,8},{1,13},{5,1},{9,5},{13,9},{2,14},{6,2},{... | collective-permute-start | bytes 1572872 | tf_op jit(solution)/shard_map/ppermute | solution.py:10
  128.0 4.0 %collective-permute-done.8 = bf16[512,512]{1,0:T(8,128)(2,1)S(1)} collective-permute-done((bf16[512,512]{1,0:T(8,128)(2,1)S(1)}, bf16[512,512]{1,0:T(8,128)(2,1)S(1)}, u32[]{:S(2)}, u32[]{:S(2)}) %collective-permute-start.8) | collective-permute-done | bytes 524320 | tf_op jit(solution)/shard_map/ppermute | solution.py:10
  133.3 3.4 %collective-permute-start.9 = (bf16[512,512]{1,0:T(8,128)(2,1)}, bf16[512,512]{1,0:T(8,128)(2,1)}, u32[]{:S(2)}, u32[]{:S(2)}) collective-permute-start(bf16[512,512]{1,0:T(8,128)(2,1)} %add_convert_fusion.5), channel_id=1, source_target_pairs={{0,4},{4,8},{8,12},{12,0},{1,5},{5,9},{9,13},{13,1},{2,6},{6,10},{... | collective-permute-start | bytes 1572872 | tf_op jit(solution)/shard_map/ppermute | solution.py:10
  141.4 4.2 %collective-permute-done.9 = bf16[512,512]{1,0:T(8,128)(2,1)} collective-permute-done((bf16[512,512]{1,0:T(8,128)(2,1)}, bf16[512,512]{1,0:T(8,128)(2,1)}, u32[]{:S(2)}, u32[]{:S(2)}) %collective-permute-start.9) | collective-permute-done | bytes 524320 | tf_op jit(solution)/shard_map/ppermute | solution.py:10
  146.8 4.9 %collective-permute-start.10 = (bf16[512,512]{1,0:T(8,128)(2,1)S(1)}, bf16[512,512]{1,0:T(8,128)(2,1)S(1)}, u32[]{:S(2)}, u32[]{:S(2)}) collective-permute-start(bf16[512,512]{1,0:T(8,128)(2,1)S(1)} %add_convert_fusion.4), channel_id=1, source_target_pairs={{0,4},{4,8},{8,12},{12,0},{1,5},{5,9},{9,13},{13,1},{2,6},{6,10},{... | collective-permute-start | bytes 1572872 | tf_op jit(solution)/shard_map/ppermute | solution.py:10
  154.3 4.4 %collective-permute-done.10 = bf16[512,512]{1,0:T(8,128)(2,1)S(1)} collective-permute-done((bf16[512,512]{1,0:T(8,128)(2,1)S(1)}, bf16[512,512]{1,0:T(8,128)(2,1)S(1)}, u32[]{:S(2)}, u32[]{:S(2)}) %collective-permute-start.10) | collective-permute-done | bytes 524320 | tf_op jit(solution)/shard_map/ppermute | solution.py:10
  158.9 3.9 %collective-permute-start.11 = (bf16[512,128]{1,0:T(8,128)(2,1)S(1)}, bf16[512,128]{1,0:T(8,128)(2,1)S(1)}, u32[]{:S(2)}, u32[]{:S(2)}) collective-permute-start(bf16[512,128]{1,0:T(8,128)(2,1)S(1)} %constant_dynamic-slice_fusion.1), channel_id=1, source_target_pairs={{0,1},{1,2},{2,3},{3,0},{4,5},{5,6},{6,7},{7,4},{8,9},{9,10},{10,1... | collective-permute-start | bytes 393224 | tf_op jit(solution)/shard_map/ppermute | solution.py:10
  173.9 3.3 %collective-permute-start.18 = (bf16[512,128]{1,0:T(8,128)(2,1)S(1)}, bf16[512,128]{1,0:T(8,128)(2,1)S(1)}, u32[]{:S(2)}, u32[]{:S(2)}) collective-permute-start(bf16[512,128]{1,0:T(8,128)(2,1)S(1)} %add_convert_fusion.8), channel_id=1, source_target_pairs={{0,3},{1,0},{2,1},{3,2},{4,7},{5,4},{6,5},{7,6},{8,11},{9,8},{10,9... | collective-permute-start | bytes 393224 | tf_op jit(solution)/shard_map/ppermute | solution.py:10
  178.2 3.8 %collective-permute-start.13 = (bf16[512,128]{1,0:T(8,128)(2,1)S(1)}, bf16[512,128]{1,0:T(8,128)(2,1)S(1)}, u32[]{:S(2)}, u32[]{:S(2)}) collective-permute-start(bf16[512,128]{1,0:T(8,128)(2,1)S(1)} %add_convert_fusion.10), channel_id=1, source_target_pairs={{0,1},{1,2},{2,3},{3,0},{4,5},{5,6},{6,7},{7,4},{8,9},{9,10},{10,1... | collective-permute-start | bytes 393224 | tf_op jit(solution)/shard_map/ppermute | solution.py:10
  182.0 2.8 %collective-permute-done.18 = bf16[512,128]{1,0:T(8,128)(2,1)S(1)} collective-permute-done((bf16[512,128]{1,0:T(8,128)(2,1)S(1)}, bf16[512,128]{1,0:T(8,128)(2,1)S(1)}, u32[]{:S(2)}, u32[]{:S(2)}) %collective-permute-start.18) | collective-permute-done | bytes 131104 | tf_op jit(solution)/shard_map/ppermute | solution.py:10
  184.9 3.3 %collective-permute-start.19 = (bf16[512,128]{1,0:T(8,128)(2,1)S(1)}, bf16[512,128]{1,0:T(8,128)(2,1)S(1)}, u32[]{:S(2)}, u32[]{:S(2)}) collective-permute-start(bf16[512,128]{1,0:T(8,128)(2,1)S(1)} %add_convert_fusion.7), channel_id=1, source_target_pairs={{0,3},{1,0},{2,1},{3,2},{4,7},{5,4},{6,5},{7,6},{8,11},{9,8},{10,9... | collective-permute-start | bytes 393224 | tf_op jit(solution)/shard_map/ppermute | solution.py:10
  188.3 6.3 %collective-permute-done.19 = bf16[512,128]{1,0:T(8,128)(2,1)S(1)} collective-permute-done((bf16[512,128]{1,0:T(8,128)(2,1)S(1)}, bf16[512,128]{1,0:T(8,128)(2,1)S(1)}, u32[]{:S(2)}, u32[]{:S(2)}) %collective-permute-start.19) | collective-permute-done | bytes 131104 | tf_op jit(solution)/shard_map/ppermute | solution.py:10
  194.9 20.1 %all_to_all.11 = bf16[32,32,128]{2,1,0:T(8,128)(2,1)S(1)} all-to-all(bf16[32,32,128]{2,1,0:T(8,128)(2,1)S(1)} %fusion.37), channel_id=1, replica_groups=mesh['expert'=32,'mx'=4,'mz'=4] {'expert'}, dimensions={0} | all-to-all | bytes 524288 | tf_op jit(solution)/shard_map/all_to_all | solution.py:126
  (95 shorter events, 68.4 us)
Async XLA Ops:
  0.0 118.6 %copy-start = (bf16[1,320,2048]{2,1,0:T(8,128)(2,1)S(1)}, bf16[1,320,2048]{2,1,0:T(8,128)(2,1)}, u32[]{:S(2)}) copy-start(bf16[1,320,2048]{2,1,0:T(8,128)(2,1)} %param.18) | copy-start | bytes 3932164
  26.9 21.2 %collective-permute-start.1 = (bf16[1024,128]{0,1:T(8,128)(2,1)S(1)}, bf16[1024,128]{0,1:T(8,128)(2,1)S(1)}, u32[]{:S(2)}, u32[]{:S(2)}) collective-permute-start(bf16[1024,128]{0,1:T(8,128)(2,1)S(1)} %copy.13), channel_id=1, source_target_pairs={{0,1},{1,2},{2,3},{3,0},{4,5},{5,6},{6,7},{7,4},{8,9},{9,10},{10,1... | collective-permute-start | bytes 786440 | tf_op jit(solution)/shard_map/ppermute | solution.py:10
  33.0 17.1 %collective-permute-start = (bf16[1024,128]{0,1:T(8,128)(2,1)S(1)}, bf16[1024,128]{0,1:T(8,128)(2,1)S(1)}, u32[]{:S(2)}, u32[]{:S(2)}) collective-permute-start(bf16[1024,128]{0,1:T(8,128)(2,1)S(1)} %copy.13), channel_id=1, source_target_pairs={{0,3},{1,0},{2,1},{3,2},{4,7},{5,4},{6,5},{7,6},{8,11},{9,8},{10,9... | collective-permute-start | bytes 786440 | tf_op jit(solution)/shard_map/ppermute | solution.py:10
  48.1 9.0 %collective-permute-start.2 = (bf16[512,128]{0,1:T(8,128)(2,1)S(1)}, bf16[512,128]{0,1:T(8,128)(2,1)S(1)}, u32[]{:S(2)}, u32[]{:S(2)}) collective-permute-start(bf16[512,128]{0,1:T(8,128)(2,1)S(1)} %slice.24), channel_id=1, source_target_pairs={{0,1},{1,2},{2,3},{3,0},{4,5},{5,6},{6,7},{7,4},{8,9},{9,10},{10,1... | collective-permute-start | bytes 393224 | tf_op jit(solution)/shard_map/ppermute | solution.py:10
  50.1 9.5 %collective-permute-start.3 = (bf16[512,128]{0,1:T(8,128)(2,1)S(1)}, bf16[512,128]{0,1:T(8,128)(2,1)S(1)}, u32[]{:S(2)}, u32[]{:S(2)}) collective-permute-start(bf16[512,128]{0,1:T(8,128)(2,1)S(1)} %slice.25), channel_id=1, source_target_pairs={{0,3},{1,0},{2,1},{3,2},{4,7},{5,4},{6,5},{7,6},{8,11},{9,8},{10,9... | collective-permute-start | bytes 393224 | tf_op jit(solution)/shard_map/ppermute | solution.py:10
  59.6 7.5 %copy-start.7 = (f32[2048]{0:T(1024)S(1)}, f32[2048]{0:T(1024)}, u32[]{:S(2)}) copy-start(f32[2048]{0:T(1024)} %param.14) | copy-start | bytes 24580
  61.1 26.6 %collective-permute-start.5 = (bf16[4,1024,128]{1,2,0:T(8,128)(2,1)}, bf16[4,1024,128]{1,2,0:T(8,128)(2,1)}, u32[]{:S(2)}, u32[]{:S(2)}) collective-permute-start(bf16[4,1024,128]{1,2,0:T(8,128)(2,1)} %get-tuple-element.8), channel_id=1, source_target_pairs={{0,4},{4,8},{8,12},{12,0},{1,5},{5,9},{9,13},{13,1},{2,6},{6,10},{... | collective-permute-start | bytes 3145736 | tf_op jit(solution)/shard_map/ppermute | solution.py:10
  63.5 28.9 %collective-permute-start.4 = (bf16[4,1024,128]{1,2,0:T(8,128)(2,1)}, bf16[4,1024,128]{1,2,0:T(8,128)(2,1)}, u32[]{:S(2)}, u32[]{:S(2)}) collective-permute-start(bf16[4,1024,128]{1,2,0:T(8,128)(2,1)} %get-tuple-element.8), channel_id=1, source_target_pairs={{0,12},{4,0},{8,4},{12,8},{1,13},{5,1},{9,5},{13,9},{2,14},{6,2},{... | collective-permute-start | bytes 3145736 | tf_op jit(solution)/shard_map/ppermute | solution.py:10
  88.8 14.2 %collective-permute-start.6 = (bf16[2,1024,128]{1,2,0:T(8,128)(2,1)S(1)}, bf16[2,1024,128]{1,2,0:T(8,128)(2,1)}, u32[]{:S(2)}, u32[]{:S(2)}) collective-permute-start(bf16[2,1024,128]{1,2,0:T(8,128)(2,1)S(1)} %slice.26), channel_id=1, source_target_pairs={{0,4},{4,8},{8,12},{12,0},{1,5},{5,9},{9,13},{13,1},{2,6},{6,10},{... | collective-permute-start | bytes 1572872 | tf_op jit(solution)/shard_map/ppermute | solution.py:10
  94.2 15.4 %collective-permute-start.7 = (bf16[2,1024,128]{1,2,0:T(8,128)(2,1)}, bf16[2,1024,128]{1,2,0:T(8,128)(2,1)}, u32[]{:S(2)}, u32[]{:S(2)}) collective-permute-start(bf16[2,1024,128]{1,2,0:T(8,128)(2,1)} %slice.27), channel_id=1, source_target_pairs={{0,12},{4,0},{8,4},{12,8},{1,13},{5,1},{9,5},{13,9},{2,14},{6,2},{... | collective-permute-start | bytes 1572872 | tf_op jit(solution)/shard_map/ppermute | solution.py:10
  101.1 9.8 %copy-start.1 = (bf16[1,4,1024,128]{2,3,1,0:T(8,128)(2,1)S(1)}, bf16[1,4,1024,128]{2,3,1,0:T(8,128)(2,1)}, u32[]{:S(2)}) copy-start(bf16[1,4,1024,128]{2,3,1,0:T(8,128)(2,1)} %get-tuple-element.6) | copy-start | bytes 3145732
  118.6 13.4 %copy-start.2 = (bf16[1024,320]{0,1:T(8,128)(2,1)}, bf16[1024,320]{0,1:T(8,128)(2,1)S(1)}, u32[]{:S(2)}) copy-start(bf16[1024,320]{0,1:T(8,128)(2,1)S(1)} %fusion.12) | copy-start | bytes 1966084
  119.1 12.9 %collective-permute-start.8 = (bf16[512,512]{1,0:T(8,128)(2,1)S(1)}, bf16[512,512]{1,0:T(8,128)(2,1)S(1)}, u32[]{:S(2)}, u32[]{:S(2)}) collective-permute-start(bf16[512,512]{1,0:T(8,128)(2,1)S(1)} %convolution_convert_fusion.7), channel_id=1, source_target_pairs={{0,4},{4,8},{8,12},{12,0},{1,5},{5,9},{9,13},{13,1},{2,6},{6,10},{... | collective-permute-start | bytes 1572872 | tf_op jit(solution)/shard_map/ppermute | solution.py:10
  122.3 14.5 %collective-permute-start.14 = (bf16[512,512]{1,0:T(8,128)(2,1)}, bf16[512,512]{1,0:T(8,128)(2,1)}, u32[]{:S(2)}, u32[]{:S(2)}) collective-permute-start(bf16[512,512]{1,0:T(8,128)(2,1)} %convolution_convert_fusion.3), channel_id=1, source_target_pairs={{0,12},{4,0},{8,4},{12,8},{1,13},{5,1},{9,5},{13,9},{2,14},{6,2},{... | collective-permute-start | bytes 1572872 | tf_op jit(solution)/shard_map/ppermute | solution.py:10
  133.3 12.3 %collective-permute-start.9 = (bf16[512,512]{1,0:T(8,128)(2,1)}, bf16[512,512]{1,0:T(8,128)(2,1)}, u32[]{:S(2)}, u32[]{:S(2)}) collective-permute-start(bf16[512,512]{1,0:T(8,128)(2,1)} %add_convert_fusion.5), channel_id=1, source_target_pairs={{0,4},{4,8},{8,12},{12,0},{1,5},{5,9},{9,13},{13,1},{2,6},{6,10},{... | collective-permute-start | bytes 1572872 | tf_op jit(solution)/shard_map/ppermute | solution.py:10
  138.5 13.2 %collective-permute-start.15 = (bf16[512,512]{1,0:T(8,128)(2,1)S(1)}, bf16[512,512]{1,0:T(8,128)(2,1)S(1)}, u32[]{:S(2)}, u32[]{:S(2)}) collective-permute-start(bf16[512,512]{1,0:T(8,128)(2,1)S(1)} %add_convert_fusion.2), channel_id=1, source_target_pairs={{0,12},{4,0},{8,4},{12,8},{1,13},{5,1},{9,5},{13,9},{2,14},{6,2},{... | collective-permute-start | bytes 1572872 | tf_op jit(solution)/shard_map/ppermute | solution.py:10
  146.8 11.9 %collective-permute-start.10 = (bf16[512,512]{1,0:T(8,128)(2,1)S(1)}, bf16[512,512]{1,0:T(8,128)(2,1)S(1)}, u32[]{:S(2)}, u32[]{:S(2)}) collective-permute-start(bf16[512,512]{1,0:T(8,128)(2,1)S(1)} %add_convert_fusion.4), channel_id=1, source_target_pairs={{0,4},{4,8},{8,12},{12,0},{1,5},{5,9},{9,13},{13,1},{2,6},{6,10},{... | collective-permute-start | bytes 1572872 | tf_op jit(solution)/shard_map/ppermute | solution.py:10
  151.9 12.3 %collective-permute-start.16 = (bf16[512,512]{1,0:T(8,128)(2,1)S(1)}, bf16[512,512]{1,0:T(8,128)(2,1)S(1)}, u32[]{:S(2)}, u32[]{:S(2)}) collective-permute-start(bf16[512,512]{1,0:T(8,128)(2,1)S(1)} %add_convert_fusion.1), channel_id=1, source_target_pairs={{0,12},{4,0},{8,4},{12,8},{1,13},{5,1},{9,5},{13,9},{2,14},{6,2},{... | collective-permute-start | bytes 1572872 | tf_op jit(solution)/shard_map/ppermute | solution.py:10
  158.9 10.2 %collective-permute-start.11 = (bf16[512,128]{1,0:T(8,128)(2,1)S(1)}, bf16[512,128]{1,0:T(8,128)(2,1)S(1)}, u32[]{:S(2)}, u32[]{:S(2)}) collective-permute-start(bf16[512,128]{1,0:T(8,128)(2,1)S(1)} %constant_dynamic-slice_fusion.1), channel_id=1, source_target_pairs={{0,1},{1,2},{2,3},{3,0},{4,5},{5,6},{6,7},{7,4},{8,9},{9,10},{10,1... | collective-permute-start | bytes 393224 | tf_op jit(solution)/shard_map/ppermute | solution.py:10
  164.4 9.4 %collective-permute-start.17 = (bf16[512,128]{1,0:T(8,128)(2,1)S(1)}, bf16[512,128]{1,0:T(8,128)(2,1)S(1)}, u32[]{:S(2)}, u32[]{:S(2)}) collective-permute-start(bf16[512,128]{1,0:T(8,128)(2,1)S(1)} %constant_dynamic-slice_fusion), channel_id=1, source_target_pairs={{0,3},{1,0},{2,1},{3,2},{4,7},{5,4},{6,5},{7,6},{8,11},{9,8},{10,9... | collective-permute-start | bytes 393224 | tf_op jit(solution)/shard_map/ppermute | solution.py:10
  169.2 9.0 %collective-permute-start.12 = (bf16[512,128]{1,0:T(8,128)(2,1)S(1)}, bf16[512,128]{1,0:T(8,128)(2,1)S(1)}, u32[]{:S(2)}, u32[]{:S(2)}) collective-permute-start(bf16[512,128]{1,0:T(8,128)(2,1)S(1)} %add_convert_fusion.11), channel_id=1, source_target_pairs={{0,1},{1,2},{2,3},{3,0},{4,5},{5,6},{6,7},{7,4},{8,9},{9,10},{10,1... | collective-permute-start | bytes 393224 | tf_op jit(solution)/shard_map/ppermute | solution.py:10
  173.9 11.0 %collective-permute-start.18 = (bf16[512,128]{1,0:T(8,128)(2,1)S(1)}, bf16[512,128]{1,0:T(8,128)(2,1)S(1)}, u32[]{:S(2)}, u32[]{:S(2)}) collective-permute-start(bf16[512,128]{1,0:T(8,128)(2,1)S(1)} %add_convert_fusion.8), channel_id=1, source_target_pairs={{0,3},{1,0},{2,1},{3,2},{4,7},{5,4},{6,5},{7,6},{8,11},{9,8},{10,9... | collective-permute-start | bytes 393224 | tf_op jit(solution)/shard_map/ppermute | solution.py:10
  178.2 10.1 %collective-permute-start.13 = (bf16[512,128]{1,0:T(8,128)(2,1)S(1)}, bf16[512,128]{1,0:T(8,128)(2,1)S(1)}, u32[]{:S(2)}, u32[]{:S(2)}) collective-permute-start(bf16[512,128]{1,0:T(8,128)(2,1)S(1)} %add_convert_fusion.10), channel_id=1, source_target_pairs={{0,1},{1,2},{2,3},{3,0},{4,5},{5,6},{6,7},{7,4},{8,9},{9,10},{10,1... | collective-permute-start | bytes 393224 | tf_op jit(solution)/shard_map/ppermute | solution.py:10
  184.9 9.7 %collective-permute-start.19 = (bf16[512,128]{1,0:T(8,128)(2,1)S(1)}, bf16[512,128]{1,0:T(8,128)(2,1)S(1)}, u32[]{:S(2)}, u32[]{:S(2)}) collective-permute-start(bf16[512,128]{1,0:T(8,128)(2,1)S(1)} %add_convert_fusion.7), channel_id=1, source_target_pairs={{0,3},{1,0},{2,1},{3,2},{4,7},{5,4},{6,5},{7,6},{8,11},{9,8},{10,9... | collective-permute-start | bytes 393224 | tf_op jit(solution)/shard_map/ppermute | solution.py:10
  (4 other events, 8.5 us)

commit v7 on v6

--- a/solution.py
+++ b/solution.py
@@ -66,27 +66,28 @@
     masked = lax.dot_general(
         route, tokens, (((0,), (0,)), ((), ())), preferred_element_type=jnp.float32
     ).astype(jnp.bfloat16)
+    n_z = lax.psum(1, "mz")
+    n_x = n_mp // n_z
+    groups = lax.psum(1, "expert")
+    spread = jnp.broadcast_to(
+        masked.reshape(experts, 1, slot_count, shard_width), (experts, n_z, slot_count, shard_width)
+    )
     received = lax.all_to_all(
-        masked.reshape(experts, slot_count, shard_width),
-        "expert",
+        spread.reshape(experts * n_z, slot_count, shard_width),
+        ("expert", "mz"),
         split_axis=0,
         concat_axis=0,
         tiled=True,
-    ).reshape(cells, shard_width)
-    n_z = lax.psum(1, "mz")
-    n_x = n_mp // n_z
-    at_x, at_z = lax.axis_index("mx"), lax.axis_index("mz")
+    ).reshape(groups, n_z, slot_count, shard_width)
+    at_x = lax.axis_index("mx")
+    x_width = model_width // n_x
 
     def rows_relative(w):
-        lead = w.shape[0]
-        w = jnp.roll(w, -at_x * (lead // n_x), axis=0)
-        w = jnp.roll(w.reshape(n_x, lead // n_x, *w.shape[1:]), -at_z * (lead // n_mp), axis=1)
-        return w.reshape(lead, *w.shape[2:])
+        return jnp.roll(w, -at_x * x_width, axis=0)
 
-    part = ring_gather(received, "mz", n_z)
-    whole = ring_gather(part, "mx", n_x).reshape(n_mp, cells, shard_width)
-
-    features = jnp.transpose(whole, (1, 0, 2)).reshape(cells, model_width).astype(jnp.float32)
+    whole = ring_gather(received, "mx", n_x)
+    features = jnp.transpose(whole, (1, 3, 0, 2, 4)).reshape(cells, model_width)
+    features = features.astype(jnp.float32)
     mean_square = jnp.sum(features * features, axis=1) / model_width
     scale = lax.rsqrt(mean_square + norm_eps)
     normed = (features * scale[:, None] * rows_relative(norm_gain)).astype(jnp.bfloat16)
@@ -97,13 +98,11 @@
     )
     gate_prob = jax.nn.sigmoid(picked)
 
-    ff_local = gate_proj.shape[2]
     pre_gate = jnp.dot(normed, rows_relative(gate_proj[0]), preferred_element_type=jnp.float32)
     pre_up = jnp.dot(normed, rows_relative(up_proj[0]), preferred_element_type=jnp.float32)
     hidden = (jax.nn.gelu(pre_gate, approximate=True) * pre_up).astype(jnp.bfloat16)
     rows_half = cells // 2
     hidden_halves = {True: hidden[:rows_half], False: hidden[rows_half:]}
-    x_width = model_width // n_x
 
     def x_term(k, lower):
         columns = lax.dynamic_slice_in_dim(
@@ -113,24 +112,18 @@
             jnp.bfloat16
         )
 
-    across_x = [part.astype(jnp.bfloat16) for part in ring_reduce_scatter(x_term, "mx", n_x)]
-
-    def z_term(k, lower):
-        return lax.dynamic_slice_in_dim(
-            across_x[0 if lower else 1], ((at_z + k) % n_z) * shard_width, shard_width, axis=1
-        )
-
-    summed = jnp.concatenate(ring_reduce_scatter(z_term, "mz", n_z), axis=0).astype(jnp.bfloat16)
-    gated = (gate_prob[:, None] * summed.astype(jnp.float32)).astype(jnp.bfloat16)
-
+    across_x = jnp.concatenate(ring_reduce_scatter(x_term, "mx", n_x), axis=0)
+    gated = (gate_prob[:, None] * across_x).astype(jnp.bfloat16)
+    gated = jnp.transpose(gated.reshape(groups, slot_count, n_z, shard_width), (0, 2, 1, 3))
     returned = lax.all_to_all(
-        gated.reshape(experts, slot_count, shard_width),
-        "expert",
+        gated.reshape(groups * n_z, slot_count, shard_width),
+        ("expert", "mz"),
         split_axis=0,
         concat_axis=0,
         tiled=True,
-    ).reshape(cells, shard_width)
-    update = jnp.dot(route, returned, preferred_element_type=jnp.float32)
+    ).reshape(experts, n_z, slot_count, shard_width)
+    returned = jnp.sum(returned.astype(jnp.float32), axis=1).astype(jnp.bfloat16)
+    update = jnp.dot(route, returned.reshape(cells, shard_width), preferred_element_type=jnp.float32)
     return update.astype(jnp.bfloat16)
 
 

time: 219 us -> 237 us (1.082)
  blocking collectives: 42.3 us -> 96 us
  starting transfers between devices: 69.3 us -> 30.3 us
  local copies, waits for them, and re-layouts: 11.4 us -> 28.7 us
  waiting for transfers between devices: 57.8 us -> 48 us
  other arithmetic: 20.6 us -> 16.3 us
    all_to_all x2, blocking collectives: 42.3 us -> 96 us  [the longest x1 48 us: shards(): lax.all_to_all(spread.reshape(experts * n_z, slot_count, shard_width), ('...]
    ppermute x20 -> x10, starting transfers between devices: 69.3 us -> 30.3 us  [shift(): return lax.ppermute(value, axis, [(i, (i + step) % n) for i in range(n)])]
    convert_element_type x0 -> x2, local copies, waits for them, and re-layouts: none -> 24 us  [shards(): features = features.astype(jnp.float32)]
    ppermute x20 -> x10, waiting for transfers between devices: 57.8 us -> 48 us  [shift(): return lax.ppermute(value, axis, [(i, (i + step) % n) for i in range(n)])]
    concatenate x8 -> x2, other arithmetic: 8.95 us -> 0.26 us  [the longest x1 0.17 us: shards(): across_x = jnp.concatenate(ring_reduce_scatter(x_term, 'mx', n_x), axis=0)]
    convert_element_type x3 -> x2, other arithmetic: 0.52 us -> 5.43 us  [the longest x1 3.59 us: shards(): features = features.astype(jnp.float32)]
    reshape x5 -> x0, local copies, waits for them, and re-layouts: 3.94 us -> none  [the longest x4 3.8 us: rows_relative(): w.reshape(n_x, lead // n_x, *w.shape[1:])]
    another operation x4 -> x1, other arithmetic: 4.64 us -> 1.29 us  [ring_gather(): return jnp.stack(pieces)]
  transfers between devices with their start and end apart: 20 -> 10, of which waited for: 15 -> 7; matrix products, arithmetic and copies ran while one was open for 13% -> 4% of each run, Pallas kernels for 0% -> 0%
where the time goes in v7:
time: 237 us; the launch traced here: 236 us
  blocking collectives  96 us (41%)
  waiting for transfers between devices  48 us (20%)
  starting transfers between devices  30.3 us (13%)
  local copies, waits for them, and re-layouts  28.7 us (12%)
  other arithmetic  16.3 us (7%)
  matrix products  15.9 us (7%)
    all_to_all x1, blocking collectives, shards(): lax.all_to_all(spread.reshape(experts * n_z, slot_count, shard_width), ('...  48 us
    ppermute x10, waiting for transfers between devices, shift(): return lax.ppermute(value, axis, [(i, (i + step) % n) for i in range(n)])  48 us
    all_to_all x1, blocking collectives, shards(): lax.all_to_all(gated.reshape(groups * n_z, slot_count, shard_width), ('ex...  48 us
    ppermute x10, starting transfers between devices, shift(): return lax.ppermute(value, axis, [(i, (i + step) % n) for i in range(n)])  30.3 us
    convert_element_type x2, local copies, waits for them, and re-layouts, shards(): features = features.astype(jnp.float32)  24 us
    dot_general x8, matrix products, x_term(): jnp.dot(hidden_halves[lower], columns, preferred_element_type=jnp.float32)  7.53 us
  transfers between devices with their start and end apart: 10, of which 7 were waited for; matrix products, arithmetic and copies ran while one was open for 4% of the time, Pallas kernels for 0%

profile of v7, /device:TPU:6, one launch (start us, length us, event | category | flops | bytes accessed | tf_op | source)
XLA Modules:
  0.0 235.7 jit_solution(7523692338222241712)
XLA Ops:
  2.3 2.1 fusion.30
  4.6 48.0 %all_to_all.10 = bf16[128,32,128]{2,1,0:T(8,128)(2,1)S(1)} all-to-all(bf16[128,32,128]{2,1,0:T(8,128)(2,1)S(1)} %bitcast.56), channel_id=1, replica_groups=mesh['expert'=32,'mx'=4,'mz'=4] {'expert','mz'}, dimensions={0} | all-to-all | bytes 2097152 | tf_op jit(solution)/shard_map/all_to_all | solution.py:75
  52.6 2.4 %collective-permute-start.1 = (bf16[32,4,32,128]{3,2,1,0:T(8,128)(2,1)S(1)}, bf16[32,4,32,128]{3,2,1,0:T(8,128)(2,1)S(1)}, u32[]{:S(2)}, u32[]{:S(2)}) collective-permute-start(bf16[32,4,32,128]{3,2,1,0:T(8,128)(2,1)S(1)} %bitcast.47), channel_id=1, source_target_pairs={{0,4},{4,8},{8,12},{12,0},{1,5},{5,9},{9,13},{13,1},{2,6},{6,10},{... | collective-permute-start | bytes 3145736 | tf_op jit(solution)/shard_map/ppermute | solution.py:10
  55.0 3.5 %collective-permute-start = (bf16[32,4,32,128]{3,2,1,0:T(8,128)(2,1)S(1)}, bf16[32,4,32,128]{3,2,1,0:T(8,128)(2,1)S(1)}, u32[]{:S(2)}, u32[]{:S(2)}) collective-permute-start(bf16[32,4,32,128]{3,2,1,0:T(8,128)(2,1)S(1)} %bitcast.48), channel_id=1, source_target_pairs={{0,12},{4,0},{8,4},{12,8},{1,13},{5,1},{9,5},{13,9},{2,14},{6,2},{... | collective-permute-start | bytes 3145736 | tf_op jit(solution)/shard_map/ppermute | solution.py:10
  58.5 19.7 %collective-permute-done.1 = bf16[32,4,32,128]{3,2,1,0:T(8,128)(2,1)S(1)} collective-permute-done((bf16[32,4,32,128]{3,2,1,0:T(8,128)(2,1)S(1)}, bf16[32,4,32,128]{3,2,1,0:T(8,128)(2,1)S(1)}, u32[]{:S(2)}, u32[]{:S(2)}) %collective-permute-start.1) | collective-permute-done | bytes 1048608 | tf_op jit(solution)/shard_map/ppermute | solution.py:10
  79.0 3.6 %collective-permute-start.2 = (bf16[16,4,32,128]{3,2,1,0:T(8,128)(2,1)}, bf16[16,4,32,128]{3,2,1,0:T(8,128)(2,1)}, u32[]{:S(2)}, u32[]{:S(2)}) collective-permute-start(bf16[16,4,32,128]{3,2,1,0:T(8,128)(2,1)} %slice.16), channel_id=1, source_target_pairs={{0,4},{4,8},{8,12},{12,0},{1,5},{5,9},{9,13},{13,1},{2,6},{6,10},{... | collective-permute-start | bytes 1572872 | tf_op jit(solution)/shard_map/ppermute | solution.py:10
  84.4 2.4 %collective-permute-start.3 = (bf16[16,4,32,128]{3,2,1,0:T(8,128)(2,1)}, bf16[16,4,32,128]{3,2,1,0:T(8,128)(2,1)}, u32[]{:S(2)}, u32[]{:S(2)}) collective-permute-start(bf16[16,4,32,128]{3,2,1,0:T(8,128)(2,1)} %slice.17), channel_id=1, source_target_pairs={{0,12},{4,0},{8,4},{12,8},{1,13},{5,1},{9,5},{13,9},{2,14},{6,2},{... | collective-permute-start | bytes 1572872 | tf_op jit(solution)/shard_map/ppermute | solution.py:10
  87.1 5.7 %collective-permute-done.2 = bf16[16,4,32,128]{3,2,1,0:T(8,128)(2,1)} collective-permute-done((bf16[16,4,32,128]{3,2,1,0:T(8,128)(2,1)}, bf16[16,4,32,128]{3,2,1,0:T(8,128)(2,1)}, u32[]{:S(2)}, u32[]{:S(2)}) %collective-permute-start.2) | collective-permute-done | bytes 524320 | tf_op jit(solution)/shard_map/ppermute | solution.py:10
  92.7 6.3 %collective-permute-done.3 = bf16[16,4,32,128]{3,2,1,0:T(8,128)(2,1)} collective-permute-done((bf16[16,4,32,128]{3,2,1,0:T(8,128)(2,1)}, bf16[16,4,32,128]{3,2,1,0:T(8,128)(2,1)}, u32[]{:S(2)}, u32[]{:S(2)}) %collective-permute-start.3) | collective-permute-done | bytes 524320 | tf_op jit(solution)/shard_map/ppermute | solution.py:10
  101.4 3.6 %convert_bitcast_fusion = f32[32,32,4,4,128]{4,1,3,0,2:T(8,128)} fusion(bf16[1,32,4,32,128]{4,3,2,1,0:T(8,128)(2,1)S(1)} %bitcast.52, bf16[1,32,4,32,128]{4,3,2,1,0:T(8,128)(2,1)S(1)} %maximum_bitcast_fusion, bf16[1,32,4,32,128]{4,3,2,1,0:T(8,128)(2,1)S(1)} %bitcast.54, bf16[1,32,4,32,128]{4,3,2,1,0:T(8,128)(2,1)S(1)} %bitcast.50), kind=kLoop, calls=%fused_computation.1 | loop fusion | flops 8388608 | bytes 12582912 | tf_op jit(solution)/shard_map/convert_element_type | solution.py:90
  105.0 13.7 %copy.15 = f32[32,32,4,4,128]{4,3,2,1,0:T(4,128)} copy(f32[32,32,4,4,128]{4,1,3,0,2:T(8,128)} %convert_bitcast_fusion) | data formatting | bytes 16777216 | tf_op jit(solution)/shard_map/convert_element_type | solution.py:90
  118.8 10.3 %reshape.73 = f32[1024,2048]{1,0:T(8,128)} reshape(f32[32,32,4,4,128]{4,3,2,1,0:T(4,128)} %copy.15) | data formatting | bytes 16777216 | tf_op jit(solution)/shard_map/convert_element_type | solution.py:90
  129.0 4.2 %multiply_convert_fusion = bf16[1024,2048]{1,0:T(8,128)(2,1)S(1)} fusion(f32[1024,2048]{1,0:T(8,128)} %reshape.73, f32[2048]{0:T(1024)S(1)} %fusion.67, f32[1024]{0:T(1024)S(1)} %rsqrt.11), kind=kLoop, calls=%fused_computation.3 | loop fusion | flops 6291456 | bytes 12595200 | tf_op jit(solution)/shard_map/convert_element_type | solution.py:93
  138.5 1.9 collective-permute-start.4
  140.5 3.9 %collective-permute-start.7 = (bf16[512,512]{1,0:T(8,128)(2,1)}, bf16[512,512]{1,0:T(8,128)(2,1)}, u32[]{:S(2)}, u32[]{:S(2)}) collective-permute-start(bf16[512,512]{1,0:T(8,128)(2,1)} %convolution_convert_fusion.3), channel_id=1, source_target_pairs={{0,12},{4,0},{8,4},{12,8},{1,13},{5,1},{9,5},{13,9},{2,14},{6,2},{... | collective-permute-start | bytes 1572872 | tf_op jit(solution)/shard_map/ppermute | solution.py:10
  146.7 4.0 %collective-permute-done.4 = bf16[512,512]{1,0:T(8,128)(2,1)S(1)} collective-permute-done((bf16[512,512]{1,0:T(8,128)(2,1)S(1)}, bf16[512,512]{1,0:T(8,128)(2,1)S(1)}, u32[]{:S(2)}, u32[]{:S(2)}) %collective-permute-start.4) | collective-permute-done | bytes 524320 | tf_op jit(solution)/shard_map/ppermute | solution.py:10
  152.0 3.4 %collective-permute-start.5 = (bf16[512,512]{1,0:T(8,128)(2,1)}, bf16[512,512]{1,0:T(8,128)(2,1)}, u32[]{:S(2)}, u32[]{:S(2)}) collective-permute-start(bf16[512,512]{1,0:T(8,128)(2,1)} %add_convert_fusion.3), channel_id=1, source_target_pairs={{0,4},{4,8},{8,12},{12,0},{1,5},{5,9},{9,13},{13,1},{2,6},{6,10},{... | collective-permute-start | bytes 1572872 | tf_op jit(solution)/shard_map/ppermute | solution.py:10
  157.1 2.4 %collective-permute-start.8 = (bf16[512,512]{1,0:T(8,128)(2,1)S(1)}, bf16[512,512]{1,0:T(8,128)(2,1)S(1)}, u32[]{:S(2)}, u32[]{:S(2)}) collective-permute-start(bf16[512,512]{1,0:T(8,128)(2,1)S(1)} %add_convert_fusion.1), channel_id=1, source_target_pairs={{0,12},{4,0},{8,4},{12,8},{1,13},{5,1},{9,5},{13,9},{2,14},{6,2},{... | collective-permute-start | bytes 1572872 | tf_op jit(solution)/shard_map/ppermute | solution.py:10
  161.0 2.6 %collective-permute-done.5 = bf16[512,512]{1,0:T(8,128)(2,1)} collective-permute-done((bf16[512,512]{1,0:T(8,128)(2,1)}, bf16[512,512]{1,0:T(8,128)(2,1)}, u32[]{:S(2)}, u32[]{:S(2)}) %collective-permute-start.5) | collective-permute-done | bytes 524320 | tf_op jit(solution)/shard_map/ppermute | solution.py:10
  164.8 4.9 %collective-permute-start.6 = (bf16[512,512]{1,0:T(8,128)(2,1)S(1)}, bf16[512,512]{1,0:T(8,128)(2,1)S(1)}, u32[]{:S(2)}, u32[]{:S(2)}) collective-permute-start(bf16[512,512]{1,0:T(8,128)(2,1)S(1)} %add_convert_fusion.2), channel_id=1, source_target_pairs={{0,4},{4,8},{8,12},{12,0},{1,5},{5,9},{9,13},{13,1},{2,6},{6,10},{... | collective-permute-start | bytes 1572872 | tf_op jit(solution)/shard_map/ppermute | solution.py:10
  169.9 1.9 collective-permute-start.9
  172.3 4.1 %collective-permute-done.6 = bf16[512,512]{1,0:T(8,128)(2,1)S(1)} collective-permute-done((bf16[512,512]{1,0:T(8,128)(2,1)S(1)}, bf16[512,512]{1,0:T(8,128)(2,1)S(1)}, u32[]{:S(2)}, u32[]{:S(2)}) %collective-permute-start.6) | collective-permute-done | bytes 524320 | tf_op jit(solution)/shard_map/ppermute | solution.py:10
  176.5 5.6 %collective-permute-done.9 = bf16[512,512]{1,0:T(8,128)(2,1)S(1)} collective-permute-done((bf16[512,512]{1,0:T(8,128)(2,1)S(1)}, bf16[512,512]{1,0:T(8,128)(2,1)S(1)}, u32[]{:S(2)}, u32[]{:S(2)}) %collective-permute-start.9) | collective-permute-done | bytes 524320 | tf_op jit(solution)/shard_map/ppermute | solution.py:10
  186.1 48.0 %all_to_all.11 = bf16[128,32,128]{2,1,0:T(8,128)(2,1)S(1)} all-to-all(bf16[128,32,128]{2,1,0:T(8,128)(2,1)S(1)} %bitcast.55), channel_id=1, replica_groups=mesh['expert'=32,'mx'=4,'mz'=4] {'expert','mz'}, dimensions={0} | all-to-all | bytes 2097152 | tf_op jit(solution)/shard_map/all_to_all | solution.py:118
  (55 shorter events, 27.1 us)
Async XLA Ops:
  0.0 136.8 %copy-start = (bf16[1,320,2048]{2,1,0:T(8,128)(2,1)S(1)}, bf16[1,320,2048]{2,1,0:T(8,128)(2,1)}, u32[]{:S(2)}) copy-start(bf16[1,320,2048]{2,1,0:T(8,128)(2,1)} %param.16) | copy-start | bytes 3932164
  4.6 82.3 %copy-start.6 = (f32[2048]{0:T(1024)S(1)}, f32[2048]{0:T(1024)}, u32[]{:S(2)}) copy-start(f32[2048]{0:T(1024)} %param.12) | copy-start | bytes 24580
  52.6 25.5 %collective-permute-start.1 = (bf16[32,4,32,128]{3,2,1,0:T(8,128)(2,1)S(1)}, bf16[32,4,32,128]{3,2,1,0:T(8,128)(2,1)S(1)}, u32[]{:S(2)}, u32[]{:S(2)}) collective-permute-start(bf16[32,4,32,128]{3,2,1,0:T(8,128)(2,1)S(1)} %bitcast.47), channel_id=1, source_target_pairs={{0,4},{4,8},{8,12},{12,0},{1,5},{5,9},{9,13},{13,1},{2,6},{6,10},{... | collective-permute-start | bytes 3145736 | tf_op jit(solution)/shard_map/ppermute | solution.py:10
  55.0 27.6 %collective-permute-start = (bf16[32,4,32,128]{3,2,1,0:T(8,128)(2,1)S(1)}, bf16[32,4,32,128]{3,2,1,0:T(8,128)(2,1)S(1)}, u32[]{:S(2)}, u32[]{:S(2)}) collective-permute-start(bf16[32,4,32,128]{3,2,1,0:T(8,128)(2,1)S(1)} %bitcast.48), channel_id=1, source_target_pairs={{0,12},{4,0},{8,4},{12,8},{1,13},{5,1},{9,5},{13,9},{2,14},{6,2},{... | collective-permute-start | bytes 3145736 | tf_op jit(solution)/shard_map/ppermute | solution.py:10
  79.0 13.7 %collective-permute-start.2 = (bf16[16,4,32,128]{3,2,1,0:T(8,128)(2,1)}, bf16[16,4,32,128]{3,2,1,0:T(8,128)(2,1)}, u32[]{:S(2)}, u32[]{:S(2)}) collective-permute-start(bf16[16,4,32,128]{3,2,1,0:T(8,128)(2,1)} %slice.16), channel_id=1, source_target_pairs={{0,4},{4,8},{8,12},{12,0},{1,5},{5,9},{9,13},{13,1},{2,6},{6,10},{... | collective-permute-start | bytes 1572872 | tf_op jit(solution)/shard_map/ppermute | solution.py:10
  82.6 1.0 copy-start.1
  84.4 14.6 %collective-permute-start.3 = (bf16[16,4,32,128]{3,2,1,0:T(8,128)(2,1)}, bf16[16,4,32,128]{3,2,1,0:T(8,128)(2,1)}, u32[]{:S(2)}, u32[]{:S(2)}) collective-permute-start(bf16[16,4,32,128]{3,2,1,0:T(8,128)(2,1)} %slice.17), channel_id=1, source_target_pairs={{0,12},{4,0},{8,4},{12,8},{1,13},{5,1},{9,5},{13,9},{2,14},{6,2},{... | collective-permute-start | bytes 1572872 | tf_op jit(solution)/shard_map/ppermute | solution.py:10
  86.9 13.4 %copy-start.2 = (bf16[32,4,32,128]{3,2,1,0:T(8,128)(2,1)S(1)}, bf16[32,4,32,128]{3,2,1,0:T(8,128)(2,1)}, u32[]{:S(2)}) copy-start(bf16[32,4,32,128]{3,2,1,0:T(8,128)(2,1)} %copy-done.1) | copy-start | bytes 3145732
  129.0 4.2 %copy-start.7 = (bf16[1,2048,320]{1,2,0:T(8,128)(2,1)S(1)}, bf16[1,2048,320]{1,2,0:T(8,128)(2,1)}, u32[]{:S(2)}) copy-start(bf16[1,2048,320]{1,2,0:T(8,128)(2,1)} %param.14) | copy-start | bytes 3932164
  133.3 1.6 copy-start.8
  136.8 14.0 %copy-start.3 = (bf16[1024,320]{0,1:T(8,128)(2,1)}, bf16[1024,320]{0,1:T(8,128)(2,1)S(1)}, u32[]{:S(2)}) copy-start(bf16[1024,320]{0,1:T(8,128)(2,1)S(1)} %fusion.11) | copy-start | bytes 1966084
  136.8 7.6 %copy-start.5 = (bf16[2048,32]{0,1:T(8,128)(2,1)S(1)}, bf16[2048,32]{0,1:T(8,128)(2,1)}, u32[]{:S(2)}) copy-start(bf16[2048,32]{0,1:T(8,128)(2,1)} %param.13) | copy-start | bytes 393220
  138.5 12.2 %collective-permute-start.4 = (bf16[512,512]{1,0:T(8,128)(2,1)S(1)}, bf16[512,512]{1,0:T(8,128)(2,1)S(1)}, u32[]{:S(2)}, u32[]{:S(2)}) collective-permute-start(bf16[512,512]{1,0:T(8,128)(2,1)S(1)} %convolution_convert_fusion.7), channel_id=1, source_target_pairs={{0,4},{4,8},{8,12},{12,0},{1,5},{5,9},{9,13},{13,1},{2,6},{6,10},{... | collective-permute-start | bytes 1572872 | tf_op jit(solution)/shard_map/ppermute | solution.py:10
  140.5 15.0 %collective-permute-start.7 = (bf16[512,512]{1,0:T(8,128)(2,1)}, bf16[512,512]{1,0:T(8,128)(2,1)}, u32[]{:S(2)}, u32[]{:S(2)}) collective-permute-start(bf16[512,512]{1,0:T(8,128)(2,1)} %convolution_convert_fusion.3), channel_id=1, source_target_pairs={{0,12},{4,0},{8,4},{12,8},{1,13},{5,1},{9,5},{13,9},{2,14},{6,2},{... | collective-permute-start | bytes 1572872 | tf_op jit(solution)/shard_map/ppermute | solution.py:10
  152.0 11.6 %collective-permute-start.5 = (bf16[512,512]{1,0:T(8,128)(2,1)}, bf16[512,512]{1,0:T(8,128)(2,1)}, u32[]{:S(2)}, u32[]{:S(2)}) collective-permute-start(bf16[512,512]{1,0:T(8,128)(2,1)} %add_convert_fusion.3), channel_id=1, source_target_pairs={{0,4},{4,8},{8,12},{12,0},{1,5},{5,9},{9,13},{13,1},{2,6},{6,10},{... | collective-permute-start | bytes 1572872 | tf_op jit(solution)/shard_map/ppermute | solution.py:10
  157.1 12.6 %collective-permute-start.8 = (bf16[512,512]{1,0:T(8,128)(2,1)S(1)}, bf16[512,512]{1,0:T(8,128)(2,1)S(1)}, u32[]{:S(2)}, u32[]{:S(2)}) collective-permute-start(bf16[512,512]{1,0:T(8,128)(2,1)S(1)} %add_convert_fusion.1), channel_id=1, source_target_pairs={{0,12},{4,0},{8,4},{12,8},{1,13},{5,1},{9,5},{13,9},{2,14},{6,2},{... | collective-permute-start | bytes 1572872 | tf_op jit(solution)/shard_map/ppermute | solution.py:10
  161.0 10.8 %copy-start.4 = (bf16[1024,320]{0,1:T(8,128)(2,1)S(1)}, bf16[1024,320]{0,1:T(8,128)(2,1)}, u32[]{:S(2)}) copy-start(bf16[1024,320]{0,1:T(8,128)(2,1)} %copy-done.3) | copy-start | bytes 1966084
  164.8 11.6 %collective-permute-start.6 = (bf16[512,512]{1,0:T(8,128)(2,1)S(1)}, bf16[512,512]{1,0:T(8,128)(2,1)S(1)}, u32[]{:S(2)}, u32[]{:S(2)}) collective-permute-start(bf16[512,512]{1,0:T(8,128)(2,1)S(1)} %add_convert_fusion.2), channel_id=1, source_target_pairs={{0,4},{4,8},{8,12},{12,0},{1,5},{5,9},{9,13},{13,1},{2,6},{6,10},{... | collective-permute-start | bytes 1572872 | tf_op jit(solution)/shard_map/ppermute | solution.py:10
  169.9 12.3 %collective-permute-start.9 = (bf16[512,512]{1,0:T(8,128)(2,1)S(1)}, bf16[512,512]{1,0:T(8,128)(2,1)S(1)}, u32[]{:S(2)}, u32[]{:S(2)}) collective-permute-start(bf16[512,512]{1,0:T(8,128)(2,1)S(1)} %add_convert_fusion), channel_id=1, source_target_pairs={{0,12},{4,0},{8,4},{12,8},{1,13},{5,1},{9,5},{13,9},{2,14},{6,2},{... | collective-permute-start | bytes 1572872 | tf_op jit(solution)/shard_map/ppermute | solution.py:10

commit v8 on v6

--- a/solution.py
+++ b/solution.py
@@ -75,15 +75,14 @@
     ).reshape(cells, shard_width)
     n_z = lax.psum(1, "mz")
     n_x = n_mp // n_z
-    at_x, at_z = lax.axis_index("mx"), lax.axis_index("mz")
+    at_x = lax.axis_index("mx")
+    x_width = model_width // n_x
 
     def rows_relative(w):
-        lead = w.shape[0]
-        w = jnp.roll(w, -at_x * (lead // n_x), axis=0)
-        w = jnp.roll(w.reshape(n_x, lead // n_x, *w.shape[1:]), -at_z * (lead // n_mp), axis=1)
-        return w.reshape(lead, *w.shape[2:])
+        return jnp.roll(w, -at_x * x_width, axis=0)
 
-    part = ring_gather(received, "mz", n_z)
+    copies = jnp.broadcast_to(received[None], (n_z, cells, shard_width))
+    part = lax.all_to_all(copies, "mz", split_axis=0, concat_axis=0, tiled=True)
     whole = ring_gather(part, "mx", n_x).reshape(n_mp, cells, shard_width)
 
     features = jnp.transpose(whole, (1, 0, 2)).reshape(cells, model_width).astype(jnp.float32)
@@ -103,7 +102,6 @@
     hidden = (jax.nn.gelu(pre_gate, approximate=True) * pre_up).astype(jnp.bfloat16)
     rows_half = cells // 2
     hidden_halves = {True: hidden[:rows_half], False: hidden[rows_half:]}
-    x_width = model_width // n_x
 
     def x_term(k, lower):
         columns = lax.dynamic_slice_in_dim(
@@ -115,12 +113,11 @@
 
     across_x = [part.astype(jnp.bfloat16) for part in ring_reduce_scatter(x_term, "mx", n_x)]
 
-    def z_term(k, lower):
-        return lax.dynamic_slice_in_dim(
-            across_x[0 if lower else 1], ((at_z + k) % n_z) * shard_width, shard_width, axis=1
-        )
-
-    summed = jnp.concatenate(ring_reduce_scatter(z_term, "mz", n_z), axis=0).astype(jnp.bfloat16)
+    across_x = jnp.concatenate(across_x, axis=0).reshape(cells, n_z, shard_width)
+    z_terms = lax.all_to_all(
+        jnp.transpose(across_x, (1, 0, 2)), "mz", split_axis=0, concat_axis=0, tiled=True
+    )
+    summed = jnp.sum(z_terms.astype(jnp.float32), axis=0).astype(jnp.bfloat16)
     gated = (gate_prob[:, None] * summed.astype(jnp.float32)).astype(jnp.bfloat16)
 
     returned = lax.all_to_all(

time: 219 us -> 210 us (0.959); the launches traced: 216 us -> 210 us
  blocking collectives: 42.3 us -> 78.2 us
  starting transfers between devices: 69.3 us -> 39.5 us
  other arithmetic: 20.6 us -> 9.13 us
  local copies, waits for them, and re-layouts: 11.4 us -> 3.64 us
  waiting for transfers between devices: 57.8 us -> 64.7 us
    ppermute x20 -> x10, starting transfers between devices: 69.3 us -> 29 us  [shift(): return lax.ppermute(value, axis, [(i, (i + step) % n) for i in range(n)])]
    all_to_all x0 -> x1, blocking collectives: none -> 35.6 us  [shards(): part = lax.all_to_all(copies, 'mz', split_axis=0, concat_axis=0, tiled=True)]
    all_to_all x0 -> x1, waiting for transfers between devices: none -> 13 us  [shards(): lax.all_to_all(jnp.transpose(across_x, (1, 0, 2)), 'mz', split_axis=0, co...]
    all_to_all x0 -> x1, starting transfers between devices: none -> 10.6 us  [shards(): lax.all_to_all(jnp.transpose(across_x, (1, 0, 2)), 'mz', split_axis=0, co...]
    concatenate x8 -> x1, other arithmetic: 8.95 us -> 0.08 us  [rows_relative(): return jnp.roll(w, -at_x * x_width, axis=0)]
    ppermute x20 -> x10, waiting for transfers between devices: 57.8 us -> 51.7 us  [shift(): return lax.ppermute(value, axis, [(i, (i + step) % n) for i in range(n)])]
    reshape x5 -> x0, local copies, waits for them, and re-layouts: 3.94 us -> none  [the longest x4 3.8 us: rows_relative(): w.reshape(n_x, lead // n_x, *w.shape[1:])]
    another operation x4 -> x1, other arithmetic: 4.64 us -> 1.29 us  [ring_gather(): return jnp.stack(pieces)]
  transfers between devices with their start and end apart: 20 -> 11, of which waited for: 15 -> 9; matrix products, arithmetic and copies ran while one was open for 13% -> 4% of each run, Pallas kernels for 0% -> 0%
where the time goes in v8:
time: 210 us
  blocking collectives  78.2 us (37%)
  waiting for transfers between devices  64.7 us (31%)
  starting transfers between devices  39.5 us (19%)
  matrix products  13.9 us (7%)
  other arithmetic  9.13 us (4%)
  local copies, waits for them, and re-layouts  3.64 us (2%)
    ppermute x10, waiting for transfers between devices, shift(): return lax.ppermute(value, axis, [(i, (i + step) % n) for i in range(n)])  51.7 us
    all_to_all x1, blocking collectives, shards(): part = lax.all_to_all(copies, 'mz', split_axis=0, concat_axis=0, tiled=True)  35.6 us
    ppermute x10, starting transfers between devices, shift(): return lax.ppermute(value, axis, [(i, (i + step) % n) for i in range(n)])  29 us
    all_to_all x1, blocking collectives, shards(): lax.all_to_all(masked.reshape(experts, slot_count, shard_width), 'expert'...  22.3 us
    all_to_all x1, blocking collectives, shards(): lax.all_to_all(gated.reshape(experts, slot_count, shard_width), 'expert',...  20.3 us
    all_to_all x1, waiting for transfers between devices, shards(): lax.all_to_all(jnp.transpose(across_x, (1, 0, 2)), 'mz', split_axis=0, co...  13 us
    all_to_all x1, starting transfers between devices, shards(): lax.all_to_all(jnp.transpose(across_x, (1, 0, 2)), 'mz', split_axis=0, co...  10.6 us
  transfers between devices with their start and end apart: 11, of which 9 were waited for; matrix products, arithmetic and copies ran while one was open for 4% of the time, Pallas kernels for 0%

profile of v8, /device:TPU:6, one launch (start us, length us, event | category | flops | bytes accessed | tf_op | source)
XLA Modules:
  0.0 209.6 jit_solution(7862361308710135420)
XLA Ops:
  2.3 2.1 %fusion.32 = bf16[1024,128]{1,0:T(8,128)(2,1)S(1)} fusion(bf16[768,128]{1,0:T(8,128)(2,1)} %param.11, s32[768]{0:T(1024)S(1)} %multiply_add_fusion, pred[768]{0:T(1024)(128)(4,1)S(1)} %lt.70), kind=kOutput, calls=%fused_computation.45 | convolution fusion | flops 203030528 | bytes 462592 | tf_op jit(solution)/shard_map/dot_general | solution.py:66
  4.5 22.3 %all_to_all.20 = bf16[32,32,128]{2,1,0:T(8,128)(2,1)S(1)} all-to-all(bf16[32,32,128]{2,1,0:T(8,128)(2,1)S(1)} %bitcast.67), channel_id=1, replica_groups=mesh['expert'=32,'mx'=4,'mz'=4] {'expert'}, dimensions={0} | all-to-all | bytes 524288 | tf_op jit(solution)/shard_map/all_to_all | solution.py:69
  27.0 35.6 %all_to_all.21 = bf16[4,1024,128]{1,2,0:T(8,128)(2,1)S(1)} all-to-all(bf16[4,1024,128]{1,2,0:T(8,128)(2,1)S(1)} %broadcast_in_dim.45), channel_id=1, replica_groups=mesh['expert'=32,'mx'=4,'mz'=4] {'mz'}, dimensions={0} | all-to-all | bytes 2097152 | tf_op jit(solution)/shard_map/all_to_all | solution.py:85
  62.7 2.4 %collective-permute-start.1 = (bf16[4,1024,128]{1,2,0:T(8,128)(2,1)S(1)}, bf16[4,1024,128]{1,2,0:T(8,128)(2,1)S(1)}, u32[]{:S(2)}, u32[]{:S(2)}) collective-permute-start(bf16[4,1024,128]{1,2,0:T(8,128)(2,1)S(1)} %all_to_all.21), channel_id=1, source_target_pairs={{0,4},{4,8},{8,12},{12,0},{1,5},{5,9},{9,13},{13,1},{2,6},{6,10},{... | collective-permute-start | bytes 3145736 | tf_op jit(solution)/shard_map/ppermute | solution.py:10
  65.0 3.5 %collective-permute-start = (bf16[4,1024,128]{1,2,0:T(8,128)(2,1)S(1)}, bf16[4,1024,128]{1,2,0:T(8,128)(2,1)S(1)}, u32[]{:S(2)}, u32[]{:S(2)}) collective-permute-start(bf16[4,1024,128]{1,2,0:T(8,128)(2,1)S(1)} %all_to_all.21), channel_id=1, source_target_pairs={{0,12},{4,0},{8,4},{12,8},{1,13},{5,1},{9,5},{13,9},{2,14},{6,2},{... | collective-permute-start | bytes 3145736 | tf_op jit(solution)/shard_map/ppermute | solution.py:10
  68.5 19.4 %collective-permute-done.1 = bf16[4,1024,128]{1,2,0:T(8,128)(2,1)S(1)} collective-permute-done((bf16[4,1024,128]{1,2,0:T(8,128)(2,1)S(1)}, bf16[4,1024,128]{1,2,0:T(8,128)(2,1)S(1)}, u32[]{:S(2)}, u32[]{:S(2)}) %collective-permute-start.1) | collective-permute-done | bytes 1048608 | tf_op jit(solution)/shard_map/ppermute | solution.py:10
  88.7 3.6 %collective-permute-start.2 = (bf16[2,1024,128]{1,2,0:T(8,128)(2,1)}, bf16[2,1024,128]{1,2,0:T(8,128)(2,1)}, u32[]{:S(2)}, u32[]{:S(2)}) collective-permute-start(bf16[2,1024,128]{1,2,0:T(8,128)(2,1)} %slice.16), channel_id=1, source_target_pairs={{0,4},{4,8},{8,12},{12,0},{1,5},{5,9},{9,13},{13,1},{2,6},{6,10},{... | collective-permute-start | bytes 1572872 | tf_op jit(solution)/shard_map/ppermute | solution.py:10
  94.1 2.2 %collective-permute-start.3 = (bf16[2,1024,128]{1,2,0:T(8,128)(2,1)}, bf16[2,1024,128]{1,2,0:T(8,128)(2,1)}, u32[]{:S(2)}, u32[]{:S(2)}) collective-permute-start(bf16[2,1024,128]{1,2,0:T(8,128)(2,1)} %slice.17), channel_id=1, source_target_pairs={{0,12},{4,0},{8,4},{12,8},{1,13},{5,1},{9,5},{13,9},{2,14},{6,2},{... | collective-permute-start | bytes 1572872 | tf_op jit(solution)/shard_map/ppermute | solution.py:10
  96.5 5.6 %collective-permute-done.2 = bf16[2,1024,128]{1,2,0:T(8,128)(2,1)} collective-permute-done((bf16[2,1024,128]{1,2,0:T(8,128)(2,1)}, bf16[2,1024,128]{1,2,0:T(8,128)(2,1)}, u32[]{:S(2)}, u32[]{:S(2)}) %collective-permute-start.2) | collective-permute-done | bytes 524320 | tf_op jit(solution)/shard_map/ppermute | solution.py:10
  102.2 6.3 %collective-permute-done.3 = bf16[2,1024,128]{1,2,0:T(8,128)(2,1)} collective-permute-done((bf16[2,1024,128]{1,2,0:T(8,128)(2,1)}, bf16[2,1024,128]{1,2,0:T(8,128)(2,1)}, u32[]{:S(2)}, u32[]{:S(2)}) %collective-permute-start.3) | collective-permute-done | bytes 524320 | tf_op jit(solution)/shard_map/ppermute | solution.py:10
  117.8 1.9 collective-permute-start.4
  120.2 3.9 %collective-permute-start.7 = (bf16[512,512]{1,0:T(8,128)(2,1)S(1)}, bf16[512,512]{1,0:T(8,128)(2,1)S(1)}, u32[]{:S(2)}, u32[]{:S(2)}) collective-permute-start(bf16[512,512]{1,0:T(8,128)(2,1)S(1)} %convolution_convert_fusion.3), channel_id=1, source_target_pairs={{0,12},{4,0},{8,4},{12,8},{1,13},{5,1},{9,5},{13,9},{2,14},{6,2},{... | collective-permute-start | bytes 1572872 | tf_op jit(solution)/shard_map/ppermute | solution.py:10
  124.6 5.1 %collective-permute-done.4 = bf16[512,512]{1,0:T(8,128)(2,1)S(1)} collective-permute-done((bf16[512,512]{1,0:T(8,128)(2,1)S(1)}, bf16[512,512]{1,0:T(8,128)(2,1)S(1)}, u32[]{:S(2)}, u32[]{:S(2)}) %collective-permute-start.4) | collective-permute-done | bytes 524320 | tf_op jit(solution)/shard_map/ppermute | solution.py:10
  130.2 3.4 %collective-permute-start.5 = (bf16[512,512]{1,0:T(8,128)(2,1)S(1)}, bf16[512,512]{1,0:T(8,128)(2,1)S(1)}, u32[]{:S(2)}, u32[]{:S(2)}) collective-permute-start(bf16[512,512]{1,0:T(8,128)(2,1)S(1)} %add_convert_fusion.5), channel_id=1, source_target_pairs={{0,4},{4,8},{8,12},{12,0},{1,5},{5,9},{9,13},{13,1},{2,6},{6,10},{... | collective-permute-start | bytes 1572872 | tf_op jit(solution)/shard_map/ppermute | solution.py:10
  134.5 2.4 %collective-permute-start.8 = (bf16[512,512]{1,0:T(8,128)(2,1)S(1)}, bf16[512,512]{1,0:T(8,128)(2,1)S(1)}, u32[]{:S(2)}, u32[]{:S(2)}) collective-permute-start(bf16[512,512]{1,0:T(8,128)(2,1)S(1)} %add_convert_fusion.2), channel_id=1, source_target_pairs={{0,12},{4,0},{8,4},{12,8},{1,13},{5,1},{9,5},{13,9},{2,14},{6,2},{... | collective-permute-start | bytes 1572872 | tf_op jit(solution)/shard_map/ppermute | solution.py:10
  137.4 4.9 %collective-permute-done.5 = bf16[512,512]{1,0:T(8,128)(2,1)S(1)} collective-permute-done((bf16[512,512]{1,0:T(8,128)(2,1)S(1)}, bf16[512,512]{1,0:T(8,128)(2,1)S(1)}, u32[]{:S(2)}, u32[]{:S(2)}) %collective-permute-start.5) | collective-permute-done | bytes 524320 | tf_op jit(solution)/shard_map/ppermute | solution.py:10
  142.5 3.7 %collective-permute-start.6 = (bf16[512,512]{1,0:T(8,128)(2,1)S(1)}, bf16[512,512]{1,0:T(8,128)(2,1)S(1)}, u32[]{:S(2)}, u32[]{:S(2)}) collective-permute-start(bf16[512,512]{1,0:T(8,128)(2,1)S(1)} %add_convert_fusion.4), channel_id=1, source_target_pairs={{0,4},{4,8},{8,12},{12,0},{1,5},{5,9},{9,13},{13,1},{2,6},{6,10},{... | collective-permute-start | bytes 1572872 | tf_op jit(solution)/shard_map/ppermute | solution.py:10
  147.0 1.9 collective-permute-start.9
  149.4 4.2 %collective-permute-done.6 = bf16[512,512]{1,0:T(8,128)(2,1)S(1)} collective-permute-done((bf16[512,512]{1,0:T(8,128)(2,1)S(1)}, bf16[512,512]{1,0:T(8,128)(2,1)S(1)}, u32[]{:S(2)}, u32[]{:S(2)}) %collective-permute-start.6) | collective-permute-done | bytes 524320 | tf_op jit(solution)/shard_map/ppermute | solution.py:10
  153.8 5.5 %collective-permute-done.9 = bf16[512,512]{1,0:T(8,128)(2,1)S(1)} collective-permute-done((bf16[512,512]{1,0:T(8,128)(2,1)S(1)}, bf16[512,512]{1,0:T(8,128)(2,1)S(1)}, u32[]{:S(2)}, u32[]{:S(2)}) %collective-permute-start.9) | collective-permute-done | bytes 524320 | tf_op jit(solution)/shard_map/ppermute | solution.py:10
  160.6 10.6 %all-to-all-start.2 = ((bf16[4,1024,128]{2,1,0:T(8,128)(2,1)}), bf16[4,1024,128]{2,1,0:T(8,128)(2,1)S(1)}, u32[]{:S(2)}, u32[]{:S(2)}) async-start(bf16[4,1024,128]{2,1,0:T(8,128)(2,1)} %bitcast_bitcast_fusion), calls=%async_computation.2 | async-start | bytes 2097152 | tf_op jit(solution)/shard_map/all_to_all | solution.py:117
  171.2 3.0 %fusion.40 = f32[1024]{0:T(1024)S(1)} fusion(bf16[1024,2048]{0,1:T(8,128)(2,1)} %copy-done.1, s32[]{:T(128)S(6)} %select_n.78, bf16[2048,32]{0,1:T(8,128)(2,1)S(1)} %copy-done.4, pred[32]{0:T(512)(128)(4,1)S(1)} %iota_compare_fusion.2), kind=kOutput, calls=%fused_computation.48 | convolution fusion | flops 134544384 | bytes 4329508 | tf_op jit(solution)/shard_map/dot_general | solution.py:93
  174.3 13.0 %all-to-all-done.2 = bf16[4,1024,128]{2,1,0:T(8,128)(2,1)S(1)} async-done(((bf16[4,1024,128]{2,1,0:T(8,128)(2,1)}), bf16[4,1024,128]{2,1,0:T(8,128)(2,1)S(1)}, u32[]{:S(2)}, u32[]{:S(2)}) %all-to-all-start.2) | async-done | bytes 1048608 | tf_op jit(solution)/shard_map/all_to_all | solution.py:117
  187.8 20.3 %all_to_all.22 = bf16[32,32,128]{2,1,0:T(8,128)(2,1)S(1)} all-to-all(bf16[32,32,128]{2,1,0:T(8,128)(2,1)S(1)} %fusion.41), channel_id=1, replica_groups=mesh['expert'=32,'mx'=4,'mz'=4] {'expert'}, dimensions={0} | all-to-all | bytes 524288 | tf_op jit(solution)/shard_map/all_to_all | solution.py:123
  (53 shorter events, 22.1 us)
Async XLA Ops:
  0.0 117.3 %copy-start = (bf16[1,320,2048]{2,1,0:T(8,128)(2,1)S(1)}, bf16[1,320,2048]{2,1,0:T(8,128)(2,1)}, u32[]{:S(2)}) copy-start(bf16[1,320,2048]{2,1,0:T(8,128)(2,1)} %param.16) | copy-start | bytes 3932164
  27.0 69.4 %copy-start.5 = (f32[2048]{0:T(1024)S(1)}, f32[2048]{0:T(1024)}, u32[]{:S(2)}) copy-start(f32[2048]{0:T(1024)} %param.12) | copy-start | bytes 24580
  62.7 25.3 %collective-permute-start.1 = (bf16[4,1024,128]{1,2,0:T(8,128)(2,1)S(1)}, bf16[4,1024,128]{1,2,0:T(8,128)(2,1)S(1)}, u32[]{:S(2)}, u32[]{:S(2)}) collective-permute-start(bf16[4,1024,128]{1,2,0:T(8,128)(2,1)S(1)} %all_to_all.21), channel_id=1, source_target_pairs={{0,4},{4,8},{8,12},{12,0},{1,5},{5,9},{9,13},{13,1},{2,6},{6,10},{... | collective-permute-start | bytes 3145736 | tf_op jit(solution)/shard_map/ppermute | solution.py:10
  65.0 27.3 %collective-permute-start = (bf16[4,1024,128]{1,2,0:T(8,128)(2,1)S(1)}, bf16[4,1024,128]{1,2,0:T(8,128)(2,1)S(1)}, u32[]{:S(2)}, u32[]{:S(2)}) collective-permute-start(bf16[4,1024,128]{1,2,0:T(8,128)(2,1)S(1)} %all_to_all.21), channel_id=1, source_target_pairs={{0,12},{4,0},{8,4},{12,8},{1,13},{5,1},{9,5},{13,9},{2,14},{6,2},{... | collective-permute-start | bytes 3145736 | tf_op jit(solution)/shard_map/ppermute | solution.py:10
  88.7 13.4 %collective-permute-start.2 = (bf16[2,1024,128]{1,2,0:T(8,128)(2,1)}, bf16[2,1024,128]{1,2,0:T(8,128)(2,1)}, u32[]{:S(2)}, u32[]{:S(2)}) collective-permute-start(bf16[2,1024,128]{1,2,0:T(8,128)(2,1)} %slice.16), channel_id=1, source_target_pairs={{0,4},{4,8},{8,12},{12,0},{1,5},{5,9},{9,13},{13,1},{2,6},{6,10},{... | collective-permute-start | bytes 1572872 | tf_op jit(solution)/shard_map/ppermute | solution.py:10
  92.3 1.0 copy-start.2
  94.1 14.3 %collective-permute-start.3 = (bf16[2,1024,128]{1,2,0:T(8,128)(2,1)}, bf16[2,1024,128]{1,2,0:T(8,128)(2,1)}, u32[]{:S(2)}, u32[]{:S(2)}) collective-permute-start(bf16[2,1024,128]{1,2,0:T(8,128)(2,1)} %slice.17), channel_id=1, source_target_pairs={{0,12},{4,0},{8,4},{12,8},{1,13},{5,1},{9,5},{13,9},{2,14},{6,2},{... | collective-permute-start | bytes 1572872 | tf_op jit(solution)/shard_map/ppermute | solution.py:10
  96.4 13.4 %copy-start.3 = (bf16[4,1024,128]{1,2,0:T(8,128)(2,1)S(1)}, bf16[4,1024,128]{1,2,0:T(8,128)(2,1)}, u32[]{:S(2)}) copy-start(bf16[4,1024,128]{1,2,0:T(8,128)(2,1)} %copy-done.2) | copy-start | bytes 3145732
  111.6 1.4 copy-start.6
  113.0 1.9 copy-start.1
  113.1 2.3 %copy-start.7 = (bf16[1,2048,320]{1,2,0:T(8,128)(2,1)S(1)}, bf16[1,2048,320]{1,2,0:T(8,128)(2,1)}, u32[]{:S(2)}) copy-start(bf16[1,2048,320]{1,2,0:T(8,128)(2,1)} %param.15) | copy-start | bytes 3932164
  117.8 11.9 %collective-permute-start.4 = (bf16[512,512]{1,0:T(8,128)(2,1)S(1)}, bf16[512,512]{1,0:T(8,128)(2,1)S(1)}, u32[]{:S(2)}, u32[]{:S(2)}) collective-permute-start(bf16[512,512]{1,0:T(8,128)(2,1)S(1)} %convolution_convert_fusion.7), channel_id=1, source_target_pairs={{0,4},{4,8},{8,12},{12,0},{1,5},{5,9},{9,13},{13,1},{2,6},{6,10},{... | collective-permute-start | bytes 1572872 | tf_op jit(solution)/shard_map/ppermute | solution.py:10
  120.2 13.8 %collective-permute-start.7 = (bf16[512,512]{1,0:T(8,128)(2,1)S(1)}, bf16[512,512]{1,0:T(8,128)(2,1)S(1)}, u32[]{:S(2)}, u32[]{:S(2)}) collective-permute-start(bf16[512,512]{1,0:T(8,128)(2,1)S(1)} %convolution_convert_fusion.3), channel_id=1, source_target_pairs={{0,12},{4,0},{8,4},{12,8},{1,13},{5,1},{9,5},{13,9},{2,14},{6,2},{... | collective-permute-start | bytes 1572872 | tf_op jit(solution)/shard_map/ppermute | solution.py:10
  130.2 12.2 %collective-permute-start.5 = (bf16[512,512]{1,0:T(8,128)(2,1)S(1)}, bf16[512,512]{1,0:T(8,128)(2,1)S(1)}, u32[]{:S(2)}, u32[]{:S(2)}) collective-permute-start(bf16[512,512]{1,0:T(8,128)(2,1)S(1)} %add_convert_fusion.5), channel_id=1, source_target_pairs={{0,4},{4,8},{8,12},{12,0},{1,5},{5,9},{9,13},{13,1},{2,6},{6,10},{... | collective-permute-start | bytes 1572872 | tf_op jit(solution)/shard_map/ppermute | solution.py:10
  134.5 12.3 %collective-permute-start.8 = (bf16[512,512]{1,0:T(8,128)(2,1)S(1)}, bf16[512,512]{1,0:T(8,128)(2,1)S(1)}, u32[]{:S(2)}, u32[]{:S(2)}) collective-permute-start(bf16[512,512]{1,0:T(8,128)(2,1)S(1)} %add_convert_fusion.2), channel_id=1, source_target_pairs={{0,12},{4,0},{8,4},{12,8},{1,13},{5,1},{9,5},{13,9},{2,14},{6,2},{... | collective-permute-start | bytes 1572872 | tf_op jit(solution)/shard_map/ppermute | solution.py:10
  142.5 11.1 %collective-permute-start.6 = (bf16[512,512]{1,0:T(8,128)(2,1)S(1)}, bf16[512,512]{1,0:T(8,128)(2,1)S(1)}, u32[]{:S(2)}, u32[]{:S(2)}) collective-permute-start(bf16[512,512]{1,0:T(8,128)(2,1)S(1)} %add_convert_fusion.4), channel_id=1, source_target_pairs={{0,4},{4,8},{8,12},{12,0},{1,5},{5,9},{9,13},{13,1},{2,6},{6,10},{... | collective-permute-start | bytes 1572872 | tf_op jit(solution)/shard_map/ppermute | solution.py:10
  147.0 12.3 %collective-permute-start.9 = (bf16[512,512]{1,0:T(8,128)(2,1)S(1)}, bf16[512,512]{1,0:T(8,128)(2,1)S(1)}, u32[]{:S(2)}, u32[]{:S(2)}) collective-permute-start(bf16[512,512]{1,0:T(8,128)(2,1)S(1)} %add_convert_fusion.1), channel_id=1, source_target_pairs={{0,12},{4,0},{8,4},{12,8},{1,13},{5,1},{9,5},{13,9},{2,14},{6,2},{... | collective-permute-start | bytes 1572872 | tf_op jit(solution)/shard_map/ppermute | solution.py:10
  159.4 11.7 %copy-start.4 = (bf16[2048,32]{0,1:T(8,128)(2,1)S(1)}, bf16[2048,32]{0,1:T(8,128)(2,1)}, u32[]{:S(2)}) copy-start(bf16[2048,32]{0,1:T(8,128)(2,1)} %param.13) | copy-start | bytes 393220
  160.6 26.8 %all-to-all-start.2 = ((bf16[4,1024,128]{2,1,0:T(8,128)(2,1)}), bf16[4,1024,128]{2,1,0:T(8,128)(2,1)S(1)}, u32[]{:S(2)}, u32[]{:S(2)}) async-start(bf16[4,1024,128]{2,1,0:T(8,128)(2,1)} %bitcast_bitcast_fusion), calls=%async_computation.2 | async-start | bytes 2097152 | tf_op jit(solution)/shard_map/all_to_all | solution.py:117

commit v9 on v8

--- a/solution.py
+++ b/solution.py
@@ -66,13 +66,6 @@
     masked = lax.dot_general(
         route, tokens, (((0,), (0,)), ((), ())), preferred_element_type=jnp.float32
     ).astype(jnp.bfloat16)
-    received = lax.all_to_all(
-        masked.reshape(experts, slot_count, shard_width),
-        "expert",
-        split_axis=0,
-        concat_axis=0,
-        tiled=True,
-    ).reshape(cells, shard_width)
     n_z = lax.psum(1, "mz")
     n_x = n_mp // n_z
     at_x = lax.axis_index("mx")
@@ -81,8 +74,14 @@
     def rows_relative(w):
         return jnp.roll(w, -at_x * x_width, axis=0)
 
-    copies = jnp.broadcast_to(received[None], (n_z, cells, shard_width))
-    part = lax.all_to_all(copies, "mz", split_axis=0, concat_axis=0, tiled=True)
+    copies = jnp.broadcast_to(masked[None], (n_z, cells, shard_width))
+    part = lax.all_to_all(
+        copies.reshape(n_z * experts, slot_count, shard_width),
+        ("mz", "expert"),
+        split_axis=0,
+        concat_axis=0,
+        tiled=True,
+    ).reshape(n_z, cells, shard_width)
     whole = ring_gather(part, "mx", n_x).reshape(n_mp, cells, shard_width)
 
     features = jnp.transpose(whole, (1, 0, 2)).reshape(cells, model_width).astype(jnp.float32)

time: 210 us -> 224 us (1.067)
  waiting for transfers between devices: 64.7 us -> 78.5 us
  blocking collectives: 78.2 us -> 66.3 us
  local copies, waits for them, and re-layouts: 3.64 us -> 12.8 us
  other arithmetic: 9.13 us -> 14.5 us
    all_to_all x2 -> x1, blocking collectives: 57.9 us -> 47.9 us  [shards(): lax.all_to_all(copies.reshape(n_z * experts, slot_count, shard_width), ('...]
    convert_element_type x0 -> x1, local copies, waits for them, and re-layouts: none -> 9.24 us  [shards(): jnp.transpose(whole, (1, 0, 2)).reshape(cells, model_width)]
    ppermute x10, waiting for transfers between devices: 51.7 us -> 59.2 us  [shift(): return lax.ppermute(value, axis, [(i, (i + step) % n) for i in range(n)])]
    all_to_all x1, waiting for transfers between devices: 13 us -> 19.3 us  [shards(): lax.all_to_all(jnp.transpose(across_x, (1, 0, 2)), 'mz', split_axis=0, co...]
    all_to_all x1, starting transfers between devices: 10.6 us -> 6.91 us  [shards(): lax.all_to_all(jnp.transpose(across_x, (1, 0, 2)), 'mz', split_axis=0, co...]
    convert_element_type x1, other arithmetic: 0.74 us -> 3.63 us  [shards(): jnp.transpose(whole, (1, 0, 2)).reshape(cells, model_width)]
    convert_element_type x1, other arithmetic: 1.4 us -> 3.98 us  [shards(): (features * scale[:, None] * rows_relative(norm_gain)).astype(jnp.bfloat16)]
where the time goes in v9:
time: 224 us
  waiting for transfers between devices  78.5 us (35%)
  blocking collectives  66.3 us (30%)
  starting transfers between devices  37.3 us (17%)
  other arithmetic  14.5 us (6%)
  matrix products  13.9 us (6%)
  local copies, waits for them, and re-layouts  12.8 us (6%)
    ppermute x10, waiting for transfers between devices, shift(): return lax.ppermute(value, axis, [(i, (i + step) % n) for i in range(n)])  59.2 us
    all_to_all x1, blocking collectives, shards(): lax.all_to_all(copies.reshape(n_z * experts, slot_count, shard_width), ('...  47.9 us
    ppermute x10, starting transfers between devices, shift(): return lax.ppermute(value, axis, [(i, (i + step) % n) for i in range(n)])  30.3 us
    all_to_all x1, waiting for transfers between devices, shards(): lax.all_to_all(jnp.transpose(across_x, (1, 0, 2)), 'mz', split_axis=0, co...  19.3 us
    all_to_all x1, blocking collectives, shards(): lax.all_to_all(gated.reshape(experts, slot_count, shard_width), 'expert',...  18.4 us
    convert_element_type x1, local copies, waits for them, and re-layouts, shards(): jnp.transpose(whole, (1, 0, 2)).reshape(cells, model_width)  9.24 us
    all_to_all x1, starting transfers between devices, shards(): lax.all_to_all(jnp.transpose(across_x, (1, 0, 2)), 'mz', split_axis=0, co...  6.91 us
  transfers between devices with their start and end apart: 11, of which 9 were waited for; matrix products, arithmetic and copies ran while one was open for 4% of the time, Pallas kernels for 0%

profile of v9, /device:TPU:6, one launch (start us, length us, event | category | flops | bytes accessed | tf_op | source)
XLA Modules:
  0.0 223.7 jit_solution(13242152361094835246)
XLA Ops:
  2.3 2.1 fusion.30
  4.6 47.9 %all_to_all.15 = bf16[128,32,128]{2,1,0:T(8,128)(2,1)S(1)} all-to-all(bf16[128,32,128]{2,1,0:T(8,128)(2,1)S(1)} %bitcast.66), channel_id=1, replica_groups=mesh['expert'=32,'mx'=4,'mz'=4] {'mz','expert'}, dimensions={0} | all-to-all | bytes 2097152 | tf_op jit(solution)/shard_map/all_to_all | solution.py:78
  52.5 2.4 %collective-permute-start.1 = (bf16[4,1024,128]{2,1,0:T(8,128)(2,1)S(1)}, bf16[4,1024,128]{2,1,0:T(8,128)(2,1)S(1)}, u32[]{:S(2)}, u32[]{:S(2)}) collective-permute-start(bf16[4,1024,128]{2,1,0:T(8,128)(2,1)S(1)} %bitcast.58), channel_id=1, source_target_pairs={{0,4},{4,8},{8,12},{12,0},{1,5},{5,9},{9,13},{13,1},{2,6},{6,10},{... | collective-permute-start | bytes 3145736 | tf_op jit(solution)/shard_map/ppermute | solution.py:10
  54.9 3.5 %collective-permute-start = (bf16[4,1024,128]{2,1,0:T(8,128)(2,1)S(1)}, bf16[4,1024,128]{2,1,0:T(8,128)(2,1)S(1)}, u32[]{:S(2)}, u32[]{:S(2)}) collective-permute-start(bf16[4,1024,128]{2,1,0:T(8,128)(2,1)S(1)} %bitcast.59), channel_id=1, source_target_pairs={{0,12},{4,0},{8,4},{12,8},{1,13},{5,1},{9,5},{13,9},{2,14},{6,2},{... | collective-permute-start | bytes 3145736 | tf_op jit(solution)/shard_map/ppermute | solution.py:10
  58.4 21.3 %collective-permute-done.1 = bf16[4,1024,128]{2,1,0:T(8,128)(2,1)S(1)} collective-permute-done((bf16[4,1024,128]{2,1,0:T(8,128)(2,1)S(1)}, bf16[4,1024,128]{2,1,0:T(8,128)(2,1)S(1)}, u32[]{:S(2)}, u32[]{:S(2)}) %collective-permute-start.1) | collective-permute-done | bytes 1048608 | tf_op jit(solution)/shard_map/ppermute | solution.py:10
  80.5 3.6 %collective-permute-start.2 = (bf16[2,1024,128]{2,1,0:T(8,128)(2,1)}, bf16[2,1024,128]{2,1,0:T(8,128)(2,1)}, u32[]{:S(2)}, u32[]{:S(2)}) collective-permute-start(bf16[2,1024,128]{2,1,0:T(8,128)(2,1)} %slice.16), channel_id=1, source_target_pairs={{0,4},{4,8},{8,12},{12,0},{1,5},{5,9},{9,13},{13,1},{2,6},{6,10},{... | collective-permute-start | bytes 1572872 | tf_op jit(solution)/shard_map/ppermute | solution.py:10
  85.9 2.2 collective-permute-start.3
  88.3 7.6 %collective-permute-done.2 = bf16[2,1024,128]{2,1,0:T(8,128)(2,1)} collective-permute-done((bf16[2,1024,128]{2,1,0:T(8,128)(2,1)}, bf16[2,1024,128]{2,1,0:T(8,128)(2,1)}, u32[]{:S(2)}, u32[]{:S(2)}) %collective-permute-start.2) | collective-permute-done | bytes 524320 | tf_op jit(solution)/shard_map/ppermute | solution.py:10
  96.0 6.3 %collective-permute-done.3 = bf16[2,1024,128]{2,1,0:T(8,128)(2,1)} collective-permute-done((bf16[2,1024,128]{2,1,0:T(8,128)(2,1)}, bf16[2,1024,128]{2,1,0:T(8,128)(2,1)}, u32[]{:S(2)}, u32[]{:S(2)}) %collective-permute-start.3) | collective-permute-done | bytes 524320 | tf_op jit(solution)/shard_map/ppermute | solution.py:10
  104.6 3.6 %maximum_convert_fusion = f32[4,4,1024,128]{3,2,1,0:T(8,128)} fusion(bf16[1,4,1024,128]{3,2,1,0:T(8,128)(2,1)S(1)} %bitcast.63, bf16[1,4,1024,128]{3,2,1,0:T(8,128)(2,1)S(1)} %maximum_bitcast_fusion, bf16[1,4,1024,128]{3,2,1,0:T(8,128)(2,1)S(1)} %bitcast.65, bf16[1,4,1024,128]{3,2,1,0:T(8,128)(2,1)S(1)} %bitcast.61), kind=kLoop, calls=%fused_computation.4 | loop fusion | flops 8388608 | bytes 12582912 | tf_op jit(solution)/shard_map/convert_element_type | solution.py:87
  108.2 9.2 %copy.13 = f32[16,1024,128]{1,2,0:T(8,128)} copy(f32[16,1024,128]{2,1,0:T(8,128)} %bitcast.57) | data formatting | bytes 16777216 | tf_op jit(solution)/shard_map/convert_element_type | solution.py:87
  117.5 4.0 %fusion.1 = bf16[1024,2048]{0,1:T(8,128)(2,1)S(1)} fusion(f32[16,1024,128]{1,2,0:T(8,128)} %copy.13, f32[2048]{0:T(1024)S(1)} %fusion.68, f32[1024]{0:T(1024)S(1)} %add_rsqrt_fusion), kind=kLoop, calls=%fused_computation.2 | loop fusion | flops 6291456 | bytes 12595200 | tf_op jit(solution)/shard_map/convert_element_type | solution.py:90
  128.6 3.9 %collective-permute-start.7 = (bf16[512,512]{1,0:T(8,128)(2,1)S(1)}, bf16[512,512]{1,0:T(8,128)(2,1)S(1)}, u32[]{:S(2)}, u32[]{:S(2)}) collective-permute-start(bf16[512,512]{1,0:T(8,128)(2,1)S(1)} %convolution_convert_fusion.3), channel_id=1, source_target_pairs={{0,12},{4,0},{8,4},{12,8},{1,13},{5,1},{9,5},{13,9},{2,14},{6,2},{... | collective-permute-start | bytes 1572872 | tf_op jit(solution)/shard_map/ppermute | solution.py:10
  133.0 7.1 %collective-permute-done.4 = bf16[512,512]{1,0:T(8,128)(2,1)S(1)} collective-permute-done((bf16[512,512]{1,0:T(8,128)(2,1)S(1)}, bf16[512,512]{1,0:T(8,128)(2,1)S(1)}, u32[]{:S(2)}, u32[]{:S(2)}) %collective-permute-start.4) | collective-permute-done | bytes 524320 | tf_op jit(solution)/shard_map/ppermute | solution.py:10
  140.6 3.4 %collective-permute-start.5 = (bf16[512,512]{1,0:T(8,128)(2,1)S(1)}, bf16[512,512]{1,0:T(8,128)(2,1)S(1)}, u32[]{:S(2)}, u32[]{:S(2)}) collective-permute-start(bf16[512,512]{1,0:T(8,128)(2,1)S(1)} %add_convert_fusion.5), channel_id=1, source_target_pairs={{0,4},{4,8},{8,12},{12,0},{1,5},{5,9},{9,13},{13,1},{2,6},{6,10},{... | collective-permute-start | bytes 1572872 | tf_op jit(solution)/shard_map/ppermute | solution.py:10
  144.9 2.4 %collective-permute-start.8 = (bf16[512,512]{1,0:T(8,128)(2,1)S(1)}, bf16[512,512]{1,0:T(8,128)(2,1)S(1)}, u32[]{:S(2)}, u32[]{:S(2)}) collective-permute-start(bf16[512,512]{1,0:T(8,128)(2,1)S(1)} %add_convert_fusion.2), channel_id=1, source_target_pairs={{0,12},{4,0},{8,4},{12,8},{1,13},{5,1},{9,5},{13,9},{2,14},{6,2},{... | collective-permute-start | bytes 1572872 | tf_op jit(solution)/shard_map/ppermute | solution.py:10
  147.8 5.7 %collective-permute-done.5 = bf16[512,512]{1,0:T(8,128)(2,1)S(1)} collective-permute-done((bf16[512,512]{1,0:T(8,128)(2,1)S(1)}, bf16[512,512]{1,0:T(8,128)(2,1)S(1)}, u32[]{:S(2)}, u32[]{:S(2)}) %collective-permute-start.5) | collective-permute-done | bytes 524320 | tf_op jit(solution)/shard_map/ppermute | solution.py:10
  153.7 5.1 %collective-permute-start.6 = (bf16[512,512]{1,0:T(8,128)(2,1)S(1)}, bf16[512,512]{1,0:T(8,128)(2,1)S(1)}, u32[]{:S(2)}, u32[]{:S(2)}) collective-permute-start(bf16[512,512]{1,0:T(8,128)(2,1)S(1)} %add_convert_fusion.4), channel_id=1, source_target_pairs={{0,4},{4,8},{8,12},{12,0},{1,5},{5,9},{9,13},{13,1},{2,6},{6,10},{... | collective-permute-start | bytes 1572872 | tf_op jit(solution)/shard_map/ppermute | solution.py:10
  161.8 4.9 %collective-permute-done.6 = bf16[512,512]{1,0:T(8,128)(2,1)S(1)} collective-permute-done((bf16[512,512]{1,0:T(8,128)(2,1)S(1)}, bf16[512,512]{1,0:T(8,128)(2,1)S(1)}, u32[]{:S(2)}, u32[]{:S(2)}) %collective-permute-start.6) | collective-permute-done | bytes 524320 | tf_op jit(solution)/shard_map/ppermute | solution.py:10
  166.8 5.9 %collective-permute-done.9 = bf16[512,512]{1,0:T(8,128)(2,1)S(1)} collective-permute-done((bf16[512,512]{1,0:T(8,128)(2,1)S(1)}, bf16[512,512]{1,0:T(8,128)(2,1)S(1)}, u32[]{:S(2)}, u32[]{:S(2)}) %collective-permute-start.9) | collective-permute-done | bytes 524320 | tf_op jit(solution)/shard_map/ppermute | solution.py:10
  174.0 6.9 %all-to-all-start.1 = ((bf16[4,1024,128]{2,1,0:T(8,128)(2,1)}), bf16[4,1024,128]{2,1,0:T(8,128)(2,1)S(1)}, u32[]{:S(2)}, u32[]{:S(2)}) async-start(bf16[4,1024,128]{2,1,0:T(8,128)(2,1)} %bitcast_bitcast_fusion), calls=%async_computation.1 | async-start | bytes 2097152 | tf_op jit(solution)/shard_map/all_to_all | solution.py:116
  180.9 3.0 %fusion.36 = f32[1024]{0:T(1024)S(1)} fusion(bf16[1024,2048]{0,1:T(8,128)(2,1)} %copy-done.1, s32[]{:T(128)S(6)} %select_n.78, bf16[2048,32]{0,1:T(8,128)(2,1)S(1)} %copy-done.4, pred[32]{0:T(512)(128)(4,1)S(1)} %iota_compare_fusion.2), kind=kOutput, calls=%fused_computation.47 | convolution fusion | flops 134544384 | bytes 4329508 | tf_op jit(solution)/shard_map/dot_general | solution.py:92
  184.0 19.3 %all-to-all-done.1 = bf16[4,1024,128]{2,1,0:T(8,128)(2,1)S(1)} async-done(((bf16[4,1024,128]{2,1,0:T(8,128)(2,1)}), bf16[4,1024,128]{2,1,0:T(8,128)(2,1)S(1)}, u32[]{:S(2)}, u32[]{:S(2)}) %all-to-all-start.1) | async-done | bytes 1048608 | tf_op jit(solution)/shard_map/all_to_all | solution.py:116
  203.8 18.4 %all_to_all.16 = bf16[32,32,128]{2,1,0:T(8,128)(2,1)S(1)} all-to-all(bf16[32,32,128]{2,1,0:T(8,128)(2,1)S(1)} %fusion.37), channel_id=1, replica_groups=mesh['expert'=32,'mx'=4,'mz'=4] {'expert'}, dimensions={0} | all-to-all | bytes 524288 | tf_op jit(solution)/shard_map/all_to_all | solution.py:122
  (52 shorter events, 23.3 us)
Async XLA Ops:
  0.0 125.7 %copy-start = (bf16[1,320,2048]{2,1,0:T(8,128)(2,1)S(1)}, bf16[1,320,2048]{2,1,0:T(8,128)(2,1)}, u32[]{:S(2)}) copy-start(bf16[1,320,2048]{2,1,0:T(8,128)(2,1)} %param.16) | copy-start | bytes 3932164
  4.6 83.6 %copy-start.5 = (f32[2048]{0:T(1024)S(1)}, f32[2048]{0:T(1024)}, u32[]{:S(2)}) copy-start(f32[2048]{0:T(1024)} %param.12) | copy-start | bytes 24580
  52.5 27.2 %collective-permute-start.1 = (bf16[4,1024,128]{2,1,0:T(8,128)(2,1)S(1)}, bf16[4,1024,128]{2,1,0:T(8,128)(2,1)S(1)}, u32[]{:S(2)}, u32[]{:S(2)}) collective-permute-start(bf16[4,1024,128]{2,1,0:T(8,128)(2,1)S(1)} %bitcast.58), channel_id=1, source_target_pairs={{0,4},{4,8},{8,12},{12,0},{1,5},{5,9},{9,13},{13,1},{2,6},{6,10},{... | collective-permute-start | bytes 3145736 | tf_op jit(solution)/shard_map/ppermute | solution.py:10
  54.9 29.2 %collective-permute-start = (bf16[4,1024,128]{2,1,0:T(8,128)(2,1)S(1)}, bf16[4,1024,128]{2,1,0:T(8,128)(2,1)S(1)}, u32[]{:S(2)}, u32[]{:S(2)}) collective-permute-start(bf16[4,1024,128]{2,1,0:T(8,128)(2,1)S(1)} %bitcast.59), channel_id=1, source_target_pairs={{0,12},{4,0},{8,4},{12,8},{1,13},{5,1},{9,5},{13,9},{2,14},{6,2},{... | collective-permute-start | bytes 3145736 | tf_op jit(solution)/shard_map/ppermute | solution.py:10
  80.5 15.4 %collective-permute-start.2 = (bf16[2,1024,128]{2,1,0:T(8,128)(2,1)}, bf16[2,1024,128]{2,1,0:T(8,128)(2,1)}, u32[]{:S(2)}, u32[]{:S(2)}) collective-permute-start(bf16[2,1024,128]{2,1,0:T(8,128)(2,1)} %slice.16), channel_id=1, source_target_pairs={{0,4},{4,8},{8,12},{12,0},{1,5},{5,9},{9,13},{13,1},{2,6},{6,10},{... | collective-permute-start | bytes 1572872 | tf_op jit(solution)/shard_map/ppermute | solution.py:10
  84.1 1.0 copy-start.2
  85.9 16.4 %collective-permute-start.3 = (bf16[2,1024,128]{2,1,0:T(8,128)(2,1)}, bf16[2,1024,128]{2,1,0:T(8,128)(2,1)}, u32[]{:S(2)}, u32[]{:S(2)}) collective-permute-start(bf16[2,1024,128]{2,1,0:T(8,128)(2,1)} %slice.17), channel_id=1, source_target_pairs={{0,12},{4,0},{8,4},{12,8},{1,13},{5,1},{9,5},{13,9},{2,14},{6,2},{... | collective-permute-start | bytes 1572872 | tf_op jit(solution)/shard_map/ppermute | solution.py:10
  88.2 15.4 %copy-start.3 = (bf16[4,1024,128]{2,1,0:T(8,128)(2,1)S(1)}, bf16[4,1024,128]{2,1,0:T(8,128)(2,1)}, u32[]{:S(2)}) copy-start(bf16[4,1024,128]{2,1,0:T(8,128)(2,1)} %copy-done.2) | copy-start | bytes 3145732
  117.5 4.0 %copy-start.6 = (bf16[1,2048,320]{1,2,0:T(8,128)(2,1)S(1)}, bf16[1,2048,320]{1,2,0:T(8,128)(2,1)}, u32[]{:S(2)}) copy-start(bf16[1,2048,320]{1,2,0:T(8,128)(2,1)} %param.14) | copy-start | bytes 3932164
  121.5 1.9 copy-start.1
  121.5 2.3 %copy-start.7 = (bf16[1,2048,320]{1,2,0:T(8,128)(2,1)S(1)}, bf16[1,2048,320]{1,2,0:T(8,128)(2,1)}, u32[]{:S(2)}) copy-start(bf16[1,2048,320]{1,2,0:T(8,128)(2,1)} %param.15) | copy-start | bytes 3932164
  126.2 13.9 %collective-permute-start.4 = (bf16[512,512]{1,0:T(8,128)(2,1)S(1)}, bf16[512,512]{1,0:T(8,128)(2,1)S(1)}, u32[]{:S(2)}, u32[]{:S(2)}) collective-permute-start(bf16[512,512]{1,0:T(8,128)(2,1)S(1)} %convolution_convert_fusion.7), channel_id=1, source_target_pairs={{0,4},{4,8},{8,12},{12,0},{1,5},{5,9},{9,13},{13,1},{2,6},{6,10},{... | collective-permute-start | bytes 1572872 | tf_op jit(solution)/shard_map/ppermute | solution.py:10
  128.6 15.8 %collective-permute-start.7 = (bf16[512,512]{1,0:T(8,128)(2,1)S(1)}, bf16[512,512]{1,0:T(8,128)(2,1)S(1)}, u32[]{:S(2)}, u32[]{:S(2)}) collective-permute-start(bf16[512,512]{1,0:T(8,128)(2,1)S(1)} %convolution_convert_fusion.3), channel_id=1, source_target_pairs={{0,12},{4,0},{8,4},{12,8},{1,13},{5,1},{9,5},{13,9},{2,14},{6,2},{... | collective-permute-start | bytes 1572872 | tf_op jit(solution)/shard_map/ppermute | solution.py:10
  140.6 13.0 %collective-permute-start.5 = (bf16[512,512]{1,0:T(8,128)(2,1)S(1)}, bf16[512,512]{1,0:T(8,128)(2,1)S(1)}, u32[]{:S(2)}, u32[]{:S(2)}) collective-permute-start(bf16[512,512]{1,0:T(8,128)(2,1)S(1)} %add_convert_fusion.5), channel_id=1, source_target_pairs={{0,4},{4,8},{8,12},{12,0},{1,5},{5,9},{9,13},{13,1},{2,6},{6,10},{... | collective-permute-start | bytes 1572872 | tf_op jit(solution)/shard_map/ppermute | solution.py:10
  144.9 14.2 %collective-permute-start.8 = (bf16[512,512]{1,0:T(8,128)(2,1)S(1)}, bf16[512,512]{1,0:T(8,128)(2,1)S(1)}, u32[]{:S(2)}, u32[]{:S(2)}) collective-permute-start(bf16[512,512]{1,0:T(8,128)(2,1)S(1)} %add_convert_fusion.2), channel_id=1, source_target_pairs={{0,12},{4,0},{8,4},{12,8},{1,13},{5,1},{9,5},{13,9},{2,14},{6,2},{... | collective-permute-start | bytes 1572872 | tf_op jit(solution)/shard_map/ppermute | solution.py:10
  153.7 12.9 %collective-permute-start.6 = (bf16[512,512]{1,0:T(8,128)(2,1)S(1)}, bf16[512,512]{1,0:T(8,128)(2,1)S(1)}, u32[]{:S(2)}, u32[]{:S(2)}) collective-permute-start(bf16[512,512]{1,0:T(8,128)(2,1)S(1)} %add_convert_fusion.4), channel_id=1, source_target_pairs={{0,4},{4,8},{8,12},{12,0},{1,5},{5,9},{9,13},{13,1},{2,6},{6,10},{... | collective-permute-start | bytes 1572872 | tf_op jit(solution)/shard_map/ppermute | solution.py:10
  159.3 13.3 %collective-permute-start.9 = (bf16[512,512]{1,0:T(8,128)(2,1)S(1)}, bf16[512,512]{1,0:T(8,128)(2,1)S(1)}, u32[]{:S(2)}, u32[]{:S(2)}) collective-permute-start(bf16[512,512]{1,0:T(8,128)(2,1)S(1)} %add_convert_fusion.1), channel_id=1, source_target_pairs={{0,12},{4,0},{8,4},{12,8},{1,13},{5,1},{9,5},{13,9},{2,14},{6,2},{... | collective-permute-start | bytes 1572872 | tf_op jit(solution)/shard_map/ppermute | solution.py:10
  172.8 8.1 %copy-start.4 = (bf16[2048,32]{0,1:T(8,128)(2,1)S(1)}, bf16[2048,32]{0,1:T(8,128)(2,1)}, u32[]{:S(2)}) copy-start(bf16[2048,32]{0,1:T(8,128)(2,1)} %param.13) | copy-start | bytes 393220
  174.0 29.4 %all-to-all-start.1 = ((bf16[4,1024,128]{2,1,0:T(8,128)(2,1)}), bf16[4,1024,128]{2,1,0:T(8,128)(2,1)S(1)}, u32[]{:S(2)}, u32[]{:S(2)}) async-start(bf16[4,1024,128]{2,1,0:T(8,128)(2,1)} %bitcast_bitcast_fusion), calls=%async_computation.1 | async-start | bytes 2097152 | tf_op jit(solution)/shard_map/all_to_all | solution.py:116

commit v10 on v9

--- a/solution.py
+++ b/solution.py
@@ -12,7 +12,7 @@
 
 def ring_gather(block, axis, n):
     if n == 1:
-        return block[None]
+        return [block]
     half = block.shape[0] // 2
     pieces = [None] * n
     pieces[0] = block
@@ -26,7 +26,7 @@
         first = shift(rightward[:half], axis, n, 1)
         second = shift(leftward[half:], axis, n, -1)
         pieces[n // 2] = jnp.concatenate([first, second], axis=0)
-    return jnp.stack(pieces)
+    return pieces
 
 
 def ring_reduce_scatter(term, axis, n):
@@ -82,22 +82,41 @@
         concat_axis=0,
         tiled=True,
     ).reshape(n_z, cells, shard_width)
-    whole = ring_gather(part, "mx", n_x).reshape(n_mp, cells, shard_width)
+    part = jnp.swapaxes(part, 1, 2)
+    blocks = [block.reshape(x_width, cells) for block in ring_gather(part, "mx", n_x)]
+    mean_square = sum(
+        jnp.sum(jnp.square(block.astype(jnp.float32)), axis=0) for block in blocks
+    ) / model_width
+    scale = lax.rsqrt(mean_square + norm_eps)
+    gain = rows_relative(norm_gain)
+    normed = [
+        (block.astype(jnp.float32) * scale[None, :] * gain[k * x_width : (k + 1) * x_width, None])
+        .astype(jnp.bfloat16)
+        for k, block in enumerate(blocks)
+    ]
+    by_feature = (((0,), (0,)), ((), ()))
 
-    features = jnp.transpose(whole, (1, 0, 2)).reshape(cells, model_width).astype(jnp.float32)
-    mean_square = jnp.sum(features * features, axis=1) / model_width
-    scale = lax.rsqrt(mean_square + norm_eps)
-    normed = (features * scale[:, None] * rows_relative(norm_gain)).astype(jnp.bfloat16)
+    def project(w):
+        w = rows_relative(w)
+        return sum(
+            lax.dot_general(
+                block,
+                w[k * x_width : (k + 1) * x_width],
+                by_feature,
+                preferred_element_type=jnp.float32,
+            )
+            for k, block in enumerate(normed)
+        )
 
-    logits = jnp.dot(normed, rows_relative(router_weight), preferred_element_type=jnp.float32)
+    logits = project(router_weight)
     picked = jnp.sum(
         jnp.where(jnp.arange(experts, dtype=jnp.int32)[None, :] == me, logits, 0.0), axis=1
     )
     gate_prob = jax.nn.sigmoid(picked)
 
     ff_local = gate_proj.shape[2]
-    pre_gate = jnp.dot(normed, rows_relative(gate_proj[0]), preferred_element_type=jnp.float32)
-    pre_up = jnp.dot(normed, rows_relative(up_proj[0]), preferred_element_type=jnp.float32)
+    pre_gate = project(gate_proj[0])
+    pre_up = project(up_proj[0])
     hidden = (jax.nn.gelu(pre_gate, approximate=True) * pre_up).astype(jnp.bfloat16)
     rows_half = cells // 2
     hidden_halves = {True: hidden[:rows_half], False: hidden[rows_half:]}

time: 224 us -> 221 us (0.987)
  waiting for transfers between devices: 78.5 us -> 65.3 us
  other arithmetic: 14.5 us -> 19.8 us
  matrix products: 13.9 us -> 17 us
    ppermute x10, waiting for transfers between devices: 59.2 us -> 45.8 us  [shift(): return lax.ppermute(value, axis, [(i, (i + step) % n) for i in range(n)])]
    concatenate x1 -> x4, other arithmetic: 0.08 us -> 5.16 us  [rows_relative(): return jnp.roll(w, -at_x * x_width, axis=0)]
    dot_general x8, matrix products: 3.73 us -> 6.64 us  [x_term(): jnp.dot(hidden_halves[lower], columns, preferred_element_type=jnp.float32)]
    reduce_sum x1 -> x4, other arithmetic: 0.99 us -> 3.53 us  [shards(): jnp.sum(jnp.square(block.astype(jnp.float32)), axis=0)]
    convert_element_type x2, other arithmetic: 7.6 us -> 5.31 us  [the longest x1 3.97 us: shards(): normed = [(block.astype(jnp.float32) * scale[None, :] * gain[k * x_width:...]
    convert_element_type x1 -> x4, local copies, waits for them, and re-layouts: 9.24 us -> 7.63 us  [the longest x3 6.02 us: shards(): block.astype(jnp.float32)]
    dot_general x3 -> x12, matrix products: 6.57 us -> 6.74 us  [project(): lax.dot_general(block, w[k * x_width:(k + 1) * x_width], by_feature, pref...]
  transfers between devices with their start and end apart: 11 -> 11, of which waited for: 9 -> 9; matrix products, arithmetic and copies ran while one was open for 4% -> 11% of each run, Pallas kernels for 0% -> 0%
where the time goes in v10:
time: 221 us; the launch traced here: 220 us
  blocking collectives  66.8 us (30%)
  waiting for transfers between devices  65.3 us (30%)
  starting transfers between devices  37.4 us (17%)
  other arithmetic  19.8 us (9%)
  matrix products  17 us (8%)
  local copies, waits for them, and re-layouts  13.6 us (6%)
    all_to_all x1, blocking collectives, shards(): lax.all_to_all(copies.reshape(n_z * experts, slot_count, shard_width), ('...  47.9 us
    ppermute x10, waiting for transfers between devices, shift(): return lax.ppermute(value, axis, [(i, (i + step) % n) for i in range(n)])  45.8 us
    ppermute x10, starting transfers between devices, shift(): return lax.ppermute(value, axis, [(i, (i + step) % n) for i in range(n)])  30.3 us
    all_to_all x1, waiting for transfers between devices, shards(): lax.all_to_all(jnp.transpose(across_x, (1, 0, 2)), 'mz', split_axis=0, co...  19.5 us
    all_to_all x1, blocking collectives, shards(): lax.all_to_all(gated.reshape(experts, slot_count, shard_width), 'expert',...  18.9 us
    all_to_all x1, starting transfers between devices, shards(): lax.all_to_all(jnp.transpose(across_x, (1, 0, 2)), 'mz', split_axis=0, co...  7.1 us
    dot_general x12, matrix products, project(): lax.dot_general(block, w[k * x_width:(k + 1) * x_width], by_feature, pref...  6.74 us
    dot_general x8, matrix products, x_term(): jnp.dot(hidden_halves[lower], columns, preferred_element_type=jnp.float32)  6.64 us
  transfers between devices with their start and end apart: 11, of which 9 were waited for; matrix products, arithmetic and copies ran while one was open for 11% of the time, Pallas kernels for 0%

profile of v10, /device:TPU:6, one launch (start us, length us, event | category | flops | bytes accessed | tf_op | source)
XLA Modules:
  0.0 220.4 jit_solution(11567481340248890514)
XLA Ops:
  2.3 2.1 fusion.34
  4.6 47.9 %all_to_all.15 = bf16[128,32,128]{2,1,0:T(8,128)(2,1)S(1)} all-to-all(bf16[128,32,128]{2,1,0:T(8,128)(2,1)S(1)} %bitcast.82), channel_id=1, replica_groups=mesh['expert'=32,'mx'=4,'mz'=4] {'mz','expert'}, dimensions={0} | all-to-all | bytes 2097152 | tf_op jit(solution)/shard_map/all_to_all | solution.py:78
  52.5 2.4 %collective-permute-start.1 = (bf16[4,128,1024]{1,2,0:T(8,128)(2,1)S(1)}, bf16[4,128,1024]{1,2,0:T(8,128)(2,1)S(1)}, u32[]{:S(2)}, u32[]{:S(2)}) collective-permute-start(bf16[4,128,1024]{1,2,0:T(8,128)(2,1)S(1)} %bitcast.78), channel_id=1, source_target_pairs={{0,4},{4,8},{8,12},{12,0},{1,5},{5,9},{9,13},{13,1},{2,6},{6,10},{... | collective-permute-start | bytes 3145736 | tf_op jit(solution)/shard_map/ppermute | solution.py:10
  54.9 3.5 %collective-permute-start = (bf16[4,128,1024]{1,2,0:T(8,128)(2,1)S(1)}, bf16[4,128,1024]{1,2,0:T(8,128)(2,1)}, u32[]{:S(2)}, u32[]{:S(2)}) collective-permute-start(bf16[4,128,1024]{1,2,0:T(8,128)(2,1)S(1)} %bitcast.79), channel_id=1, source_target_pairs={{0,12},{4,0},{8,4},{12,8},{1,13},{5,1},{9,5},{13,9},{2,14},{6,2},{... | collective-permute-start | bytes 3145736 | tf_op jit(solution)/shard_map/ppermute | solution.py:10
  58.5 3.1 %fusion.26 = bf16[2048,320]{0,1:T(8,128)(2,1)} fusion(s32[]{:T(128)S(6)} %select_n.78, bf16[2048,320]{0,1:T(8,128)(2,1)} %bitcast.83), kind=kLoop, calls=%fused_computation.44 | loop fusion | flops 2621440 | bytes 2621444 | tf_op jit(solution)/shard_map/jit(_roll_dynamic)/concatenate | solution.py:75
  65.1 14.6 %collective-permute-done.1 = bf16[4,128,1024]{1,2,0:T(8,128)(2,1)S(1)} collective-permute-done((bf16[4,128,1024]{1,2,0:T(8,128)(2,1)S(1)}, bf16[4,128,1024]{1,2,0:T(8,128)(2,1)S(1)}, u32[]{:S(2)}, u32[]{:S(2)}) %collective-permute-start.1) | collective-permute-done | bytes 1048608 | tf_op jit(solution)/shard_map/ppermute | solution.py:10
  80.5 3.6 %collective-permute-start.2 = (bf16[2,128,1024]{1,2,0:T(8,128)(2,1)}, bf16[2,128,1024]{1,2,0:T(8,128)(2,1)}, u32[]{:S(2)}, u32[]{:S(2)}) collective-permute-start(bf16[2,128,1024]{1,2,0:T(8,128)(2,1)} %slice.81), channel_id=1, source_target_pairs={{0,4},{4,8},{8,12},{12,0},{1,5},{5,9},{9,13},{13,1},{2,6},{6,10},{... | collective-permute-start | bytes 1572872 | tf_op jit(solution)/shard_map/ppermute | solution.py:10
  86.0 2.2 %collective-permute-start.3 = (bf16[2,128,1024]{1,2,0:T(8,128)(2,1)}, bf16[2,128,1024]{1,2,0:T(8,128)(2,1)}, u32[]{:S(2)}, u32[]{:S(2)}) collective-permute-start(bf16[2,128,1024]{1,2,0:T(8,128)(2,1)} %slice.82), channel_id=1, source_target_pairs={{0,12},{4,0},{8,4},{12,8},{1,13},{5,1},{9,5},{13,9},{2,14},{6,2},{... | collective-permute-start | bytes 1572872 | tf_op jit(solution)/shard_map/ppermute | solution.py:10
  88.5 2.6 %copy.20 = f32[4,128,1024]{2,1,0:T(8,128)} copy(bf16[4,128,1024]{1,2,0:T(8,128)(2,1)} %collective-permute-done) | data formatting | bytes 3145728 | tf_op jit(solution)/shard_map/convert_element_type | solution.py:88
  96.0 6.3 %collective-permute-done.3 = bf16[2,128,1024]{1,2,0:T(8,128)(2,1)} collective-permute-done((bf16[2,128,1024]{1,2,0:T(8,128)(2,1)}, bf16[2,128,1024]{1,2,0:T(8,128)(2,1)}, u32[]{:S(2)}, u32[]{:S(2)}) %collective-permute-start.3) | collective-permute-done | bytes 524320 | tf_op jit(solution)/shard_map/ppermute | solution.py:10
  107.1 4.0 %fusion.6 = (bf16[512,1024]{1,0:T(8,128)(2,1)S(1)}, bf16[512,1024]{1,0:T(8,128)(2,1)S(1)}, bf16[512,1024]{1,0:T(8,128)(2,1)S(1)}, bf16[512,1024]{1,0:T(8,128)(2,1)S(1)}) fusion(f32[4,128,1024]{2,1,0:T(8,128)} %copy.22, f32[512]{0:T(512)S(1)} %get-tuple-element.6, f32[1024]{0:T(1024)S(1)} %add_rsqrt_fusion, f32[512]{0:T(512)S(1)} %get-tuple-element.8, ...), kind=kLoop, calls=%fused_computation.10 | loop fusion | flops 6291456 | bytes 12595200 | tf_op jit(solution)/shard_map/convert_element_type | solution.py:94
  119.2 2.1 collective-permute-start.4
  122.9 3.7 %collective-permute-start.7 = (bf16[512,512]{1,0:T(8,128)(2,1)S(1)}, bf16[512,512]{1,0:T(8,128)(2,1)S(1)}, u32[]{:S(2)}, u32[]{:S(2)}) collective-permute-start(bf16[512,512]{1,0:T(8,128)(2,1)S(1)} %convolution_convert_fusion.3), channel_id=1, source_target_pairs={{0,12},{4,0},{8,4},{12,8},{1,13},{5,1},{9,5},{13,9},{2,14},{6,2},{... | collective-permute-start | bytes 1572872 | tf_op jit(solution)/shard_map/ppermute | solution.py:10
  127.1 6.4 %collective-permute-done.4 = bf16[512,512]{1,0:T(8,128)(2,1)} collective-permute-done((bf16[512,512]{1,0:T(8,128)(2,1)}, bf16[512,512]{1,0:T(8,128)(2,1)}, u32[]{:S(2)}, u32[]{:S(2)}) %collective-permute-start.4) | collective-permute-done | bytes 524320 | tf_op jit(solution)/shard_map/ppermute | solution.py:10
  135.0 3.6 %collective-permute-start.5 = (bf16[512,512]{1,0:T(8,128)(2,1)S(1)}, bf16[512,512]{1,0:T(8,128)(2,1)S(1)}, u32[]{:S(2)}, u32[]{:S(2)}) collective-permute-start(bf16[512,512]{1,0:T(8,128)(2,1)S(1)} %add_convert_fusion.5), channel_id=1, source_target_pairs={{0,4},{4,8},{8,12},{12,0},{1,5},{5,9},{9,13},{13,1},{2,6},{6,10},{... | collective-permute-start | bytes 1572872 | tf_op jit(solution)/shard_map/ppermute | solution.py:10
  139.5 2.3 %collective-permute-start.8 = (bf16[512,512]{1,0:T(8,128)(2,1)S(1)}, bf16[512,512]{1,0:T(8,128)(2,1)S(1)}, u32[]{:S(2)}, u32[]{:S(2)}) collective-permute-start(bf16[512,512]{1,0:T(8,128)(2,1)S(1)} %add_convert_fusion.2), channel_id=1, source_target_pairs={{0,12},{4,0},{8,4},{12,8},{1,13},{5,1},{9,5},{13,9},{2,14},{6,2},{... | collective-permute-start | bytes 1572872 | tf_op jit(solution)/shard_map/ppermute | solution.py:10
  142.2 5.7 %collective-permute-done.5 = bf16[512,512]{1,0:T(8,128)(2,1)S(1)} collective-permute-done((bf16[512,512]{1,0:T(8,128)(2,1)S(1)}, bf16[512,512]{1,0:T(8,128)(2,1)S(1)}, u32[]{:S(2)}, u32[]{:S(2)}) %collective-permute-start.5) | collective-permute-done | bytes 524320 | tf_op jit(solution)/shard_map/ppermute | solution.py:10
  148.1 5.1 %collective-permute-start.6 = (bf16[512,512]{1,0:T(8,128)(2,1)S(1)}, bf16[512,512]{1,0:T(8,128)(2,1)S(1)}, u32[]{:S(2)}, u32[]{:S(2)}) collective-permute-start(bf16[512,512]{1,0:T(8,128)(2,1)S(1)} %add_convert_fusion.4), channel_id=1, source_target_pairs={{0,4},{4,8},{8,12},{12,0},{1,5},{5,9},{9,13},{13,1},{2,6},{6,10},{... | collective-permute-start | bytes 1572872 | tf_op jit(solution)/shard_map/ppermute | solution.py:10
  153.9 1.9 collective-permute-start.9
  156.3 4.9 %collective-permute-done.6 = bf16[512,512]{1,0:T(8,128)(2,1)S(1)} collective-permute-done((bf16[512,512]{1,0:T(8,128)(2,1)S(1)}, bf16[512,512]{1,0:T(8,128)(2,1)S(1)}, u32[]{:S(2)}, u32[]{:S(2)}) %collective-permute-start.6) | collective-permute-done | bytes 524320 | tf_op jit(solution)/shard_map/ppermute | solution.py:10
  161.3 5.9 %collective-permute-done.9 = bf16[512,512]{1,0:T(8,128)(2,1)S(1)} collective-permute-done((bf16[512,512]{1,0:T(8,128)(2,1)S(1)}, bf16[512,512]{1,0:T(8,128)(2,1)S(1)}, u32[]{:S(2)}, u32[]{:S(2)}) %collective-permute-start.9) | collective-permute-done | bytes 524320 | tf_op jit(solution)/shard_map/ppermute | solution.py:10
  168.6 7.1 %all-to-all-start.1 = ((bf16[4,1024,128]{2,1,0:T(8,128)(2,1)}), bf16[4,1024,128]{2,1,0:T(8,128)(2,1)}, u32[]{:S(2)}, u32[]{:S(2)}) async-start(bf16[4,1024,128]{2,1,0:T(8,128)(2,1)} %bitcast_bitcast_fusion), calls=%async_computation.1 | async-start | bytes 2097152 | tf_op jit(solution)/shard_map/all_to_all | solution.py:135
  178.9 19.5 %all-to-all-done.1 = bf16[4,1024,128]{2,1,0:T(8,128)(2,1)} async-done(((bf16[4,1024,128]{2,1,0:T(8,128)(2,1)}), bf16[4,1024,128]{2,1,0:T(8,128)(2,1)}, u32[]{:S(2)}, u32[]{:S(2)}) %all-to-all-start.1) | async-done | bytes 1048608 | tf_op jit(solution)/shard_map/all_to_all | solution.py:135
  200.1 18.9 %all_to_all.16 = bf16[32,32,128]{2,1,0:T(8,128)(2,1)S(1)} all-to-all(bf16[32,32,128]{2,1,0:T(8,128)(2,1)S(1)} %fusion.42), channel_id=1, replica_groups=mesh['expert'=32,'mx'=4,'mz'=4] {'expert'}, dimensions={0} | all-to-all | bytes 524288 | tf_op jit(solution)/shard_map/all_to_all | solution.py:141
  (76 shorter events, 40.7 us)
Async XLA Ops:
  0.0 117.9 %copy-start = (bf16[1,320,2048]{2,1,0:T(8,128)(2,1)S(1)}, bf16[1,320,2048]{2,1,0:T(8,128)(2,1)}, u32[]{:S(2)}) copy-start(bf16[1,320,2048]{2,1,0:T(8,128)(2,1)} %param.16) | copy-start | bytes 3932164
  4.6 53.8 %copy-start.10 = (f32[2048]{0:T(1024)S(1)}, f32[2048]{0:T(1024)}, u32[]{:S(2)}) copy-start(f32[2048]{0:T(1024)} %param.12) | copy-start | bytes 24580
  52.5 27.2 %collective-permute-start.1 = (bf16[4,128,1024]{1,2,0:T(8,128)(2,1)S(1)}, bf16[4,128,1024]{1,2,0:T(8,128)(2,1)S(1)}, u32[]{:S(2)}, u32[]{:S(2)}) collective-permute-start(bf16[4,128,1024]{1,2,0:T(8,128)(2,1)S(1)} %bitcast.78), channel_id=1, source_target_pairs={{0,4},{4,8},{8,12},{12,0},{1,5},{5,9},{9,13},{13,1},{2,6},{6,10},{... | collective-permute-start | bytes 3145736 | tf_op jit(solution)/shard_map/ppermute | solution.py:10
  54.9 29.2 %collective-permute-start = (bf16[4,128,1024]{1,2,0:T(8,128)(2,1)S(1)}, bf16[4,128,1024]{1,2,0:T(8,128)(2,1)}, u32[]{:S(2)}, u32[]{:S(2)}) collective-permute-start(bf16[4,128,1024]{1,2,0:T(8,128)(2,1)S(1)} %bitcast.79), channel_id=1, source_target_pairs={{0,12},{4,0},{8,4},{12,8},{1,13},{5,1},{9,5},{13,9},{2,14},{6,2},{... | collective-permute-start | bytes 3145736 | tf_op jit(solution)/shard_map/ppermute | solution.py:10
  58.5 3.1 %copy-start.8 = (bf16[1,2048,320]{1,2,0:T(8,128)(2,1)S(1)}, bf16[1,2048,320]{1,2,0:T(8,128)(2,1)}, u32[]{:S(2)}) copy-start(bf16[1,2048,320]{1,2,0:T(8,128)(2,1)} %param.14) | copy-start | bytes 3932164
  80.5 15.5 %collective-permute-start.2 = (bf16[2,128,1024]{1,2,0:T(8,128)(2,1)}, bf16[2,128,1024]{1,2,0:T(8,128)(2,1)}, u32[]{:S(2)}, u32[]{:S(2)}) collective-permute-start(bf16[2,128,1024]{1,2,0:T(8,128)(2,1)} %slice.81), channel_id=1, source_target_pairs={{0,4},{4,8},{8,12},{12,0},{1,5},{5,9},{9,13},{13,1},{2,6},{6,10},{... | collective-permute-start | bytes 1572872 | tf_op jit(solution)/shard_map/ppermute | solution.py:10
  86.0 16.4 %collective-permute-start.3 = (bf16[2,128,1024]{1,2,0:T(8,128)(2,1)}, bf16[2,128,1024]{1,2,0:T(8,128)(2,1)}, u32[]{:S(2)}, u32[]{:S(2)}) collective-permute-start(bf16[2,128,1024]{1,2,0:T(8,128)(2,1)} %slice.82), channel_id=1, source_target_pairs={{0,12},{4,0},{8,4},{12,8},{1,13},{5,1},{9,5},{13,9},{2,14},{6,2},{... | collective-permute-start | bytes 1572872 | tf_op jit(solution)/shard_map/ppermute | solution.py:10
  107.1 4.0 %copy-start.6 = (bf16[2048,320]{0,1:T(8,128)(2,1)S(1)}, bf16[2048,320]{0,1:T(8,128)(2,1)}, u32[]{:S(2)}) copy-start(bf16[2048,320]{0,1:T(8,128)(2,1)} %fusion.26) | copy-start | bytes 3932164
  111.1 1.0 copy-start.1
  111.1 5.5 %copy-start.2 = (bf16[512,1024]{1,0:T(8,128)(2,1)}, bf16[512,1024]{1,0:T(8,128)(2,1)S(1)}, u32[]{:S(2)}) copy-start(bf16[512,1024]{1,0:T(8,128)(2,1)S(1)} %get-tuple-element.10) | copy-start | bytes 3145732
  111.1 2.1 copy-start.7
  117.1 0.9 copy-start.4
  119.2 14.2 %collective-permute-start.4 = (bf16[512,512]{1,0:T(8,128)(2,1)}, bf16[512,512]{1,0:T(8,128)(2,1)}, u32[]{:S(2)}, u32[]{:S(2)}) collective-permute-start(bf16[512,512]{1,0:T(8,128)(2,1)} %convolution_convert_fusion.7), channel_id=1, source_target_pairs={{0,4},{4,8},{8,12},{12,0},{1,5},{5,9},{9,13},{13,1},{2,6},{6,10},{... | collective-permute-start | bytes 1572872 | tf_op jit(solution)/shard_map/ppermute | solution.py:10
  121.3 5.3 %copy-start.5 = (bf16[1024,320]{0,1:T(8,128)(2,1)S(1)}, bf16[1024,320]{0,1:T(8,128)(2,1)}, u32[]{:S(2)}) copy-start(bf16[1024,320]{0,1:T(8,128)(2,1)} %copy-done.4) | copy-start | bytes 1966084
  122.9 16.2 %collective-permute-start.7 = (bf16[512,512]{1,0:T(8,128)(2,1)S(1)}, bf16[512,512]{1,0:T(8,128)(2,1)S(1)}, u32[]{:S(2)}, u32[]{:S(2)}) collective-permute-start(bf16[512,512]{1,0:T(8,128)(2,1)S(1)} %convolution_convert_fusion.3), channel_id=1, source_target_pairs={{0,12},{4,0},{8,4},{12,8},{1,13},{5,1},{9,5},{13,9},{2,14},{6,2},{... | collective-permute-start | bytes 1572872 | tf_op jit(solution)/shard_map/ppermute | solution.py:10
  135.0 13.0 %collective-permute-start.5 = (bf16[512,512]{1,0:T(8,128)(2,1)S(1)}, bf16[512,512]{1,0:T(8,128)(2,1)S(1)}, u32[]{:S(2)}, u32[]{:S(2)}) collective-permute-start(bf16[512,512]{1,0:T(8,128)(2,1)S(1)} %add_convert_fusion.5), channel_id=1, source_target_pairs={{0,4},{4,8},{8,12},{12,0},{1,5},{5,9},{9,13},{13,1},{2,6},{6,10},{... | collective-permute-start | bytes 1572872 | tf_op jit(solution)/shard_map/ppermute | solution.py:10
  139.5 14.2 %collective-permute-start.8 = (bf16[512,512]{1,0:T(8,128)(2,1)S(1)}, bf16[512,512]{1,0:T(8,128)(2,1)S(1)}, u32[]{:S(2)}, u32[]{:S(2)}) collective-permute-start(bf16[512,512]{1,0:T(8,128)(2,1)S(1)} %add_convert_fusion.2), channel_id=1, source_target_pairs={{0,12},{4,0},{8,4},{12,8},{1,13},{5,1},{9,5},{13,9},{2,14},{6,2},{... | collective-permute-start | bytes 1572872 | tf_op jit(solution)/shard_map/ppermute | solution.py:10
  148.1 13.1 %collective-permute-start.6 = (bf16[512,512]{1,0:T(8,128)(2,1)S(1)}, bf16[512,512]{1,0:T(8,128)(2,1)S(1)}, u32[]{:S(2)}, u32[]{:S(2)}) collective-permute-start(bf16[512,512]{1,0:T(8,128)(2,1)S(1)} %add_convert_fusion.4), channel_id=1, source_target_pairs={{0,4},{4,8},{8,12},{12,0},{1,5},{5,9},{9,13},{13,1},{2,6},{6,10},{... | collective-permute-start | bytes 1572872 | tf_op jit(solution)/shard_map/ppermute | solution.py:10
  153.9 13.3 %collective-permute-start.9 = (bf16[512,512]{1,0:T(8,128)(2,1)S(1)}, bf16[512,512]{1,0:T(8,128)(2,1)S(1)}, u32[]{:S(2)}, u32[]{:S(2)}) collective-permute-start(bf16[512,512]{1,0:T(8,128)(2,1)S(1)} %add_convert_fusion.1), channel_id=1, source_target_pairs={{0,12},{4,0},{8,4},{12,8},{1,13},{5,1},{9,5},{13,9},{2,14},{6,2},{... | collective-permute-start | bytes 1572872 | tf_op jit(solution)/shard_map/ppermute | solution.py:10
  168.6 7.1 %copy-start.9 = (bf16[2048,32]{0,1:T(8,128)(2,1)S(1)}, bf16[2048,32]{0,1:T(8,128)(2,1)}, u32[]{:S(2)}) copy-start(bf16[2048,32]{0,1:T(8,128)(2,1)} %param.13) | copy-start | bytes 393220
  168.6 29.8 %all-to-all-start.1 = ((bf16[4,1024,128]{2,1,0:T(8,128)(2,1)}), bf16[4,1024,128]{2,1,0:T(8,128)(2,1)}, u32[]{:S(2)}, u32[]{:S(2)}) async-start(bf16[4,1024,128]{2,1,0:T(8,128)(2,1)} %bitcast_bitcast_fusion), calls=%async_computation.1 | async-start | bytes 2097152 | tf_op jit(solution)/shard_map/all_to_all | solution.py:135
  177.3 1.2 copy-start.3

commit v11 on v8

--- a/solution.py
+++ b/solution.py
@@ -81,9 +81,12 @@
     def rows_relative(w):
         return jnp.roll(w, -at_x * x_width, axis=0)
 
-    copies = jnp.broadcast_to(received[None], (n_z, cells, shard_width))
-    part = lax.all_to_all(copies, "mz", split_axis=0, concat_axis=0, tiled=True)
-    whole = ring_gather(part, "mx", n_x).reshape(n_mp, cells, shard_width)
+    halves = []
+    for rows in (received[: cells // 2], received[cells // 2 :]):
+        copies = jnp.broadcast_to(rows[None], (n_z,) + rows.shape)
+        part = lax.all_to_all(copies, "mz", split_axis=0, concat_axis=0, tiled=True)
+        halves.append(ring_gather(part, "mx", n_x).reshape(n_mp, cells // 2, shard_width))
+    whole = jnp.concatenate(halves, axis=1)
 
     features = jnp.transpose(whole, (1, 0, 2)).reshape(cells, model_width).astype(jnp.float32)
     mean_square = jnp.sum(features * features, axis=1) / model_width

time: 210 us -> 202 us (0.962)
  blocking collectives: 78.2 us -> 45.7 us
  starting transfers between devices: 39.5 us -> 58.7 us
  other arithmetic: 9.13 us -> 11.9 us
  local copies, waits for them, and re-layouts: 3.64 us -> 6.08 us
    all_to_all x1 -> x0, blocking collectives: 35.6 us -> none  [shards(): part = lax.all_to_all(copies, 'mz', split_axis=0, concat_axis=0, tiled=True)]
    ppermute x10 -> x14, waiting for transfers between devices: 51.7 us -> 27.3 us  [shift(): return lax.ppermute(value, axis, [(i, (i + step) % n) for i in range(n)])]
    all_to_all x0 -> x2, waiting for transfers between devices: none -> 22.6 us  [shards(): part = lax.all_to_all(copies, 'mz', split_axis=0, concat_axis=0, tiled=True)]
    all_to_all x0 -> x2, starting transfers between devices: none -> 13.8 us  [shards(): part = lax.all_to_all(copies, 'mz', split_axis=0, concat_axis=0, tiled=True)]
    ppermute x10 -> x14, starting transfers between devices: 29 us -> 40.8 us  [shift(): return lax.ppermute(value, axis, [(i, (i + step) % n) for i in range(n)])]
    all_to_all x1, starting transfers between devices: 10.6 us -> 4.07 us  [shards(): lax.all_to_all(jnp.transpose(across_x, (1, 0, 2)), 'mz', split_axis=0, co...]
    all_to_all x1, blocking collectives: 20.3 us -> 23.4 us  [shards(): lax.all_to_all(gated.reshape(experts, slot_count, shard_width), 'expert',...]
    another operation x1 -> x4, other arithmetic: 1.29 us -> 3.73 us  [ring_gather(): return jnp.stack(pieces)]
  transfers between devices with their start and end apart: 11 -> 17, of which waited for: 9 -> 10; matrix products, arithmetic and copies ran while one was open for 4% -> 6% of each run, Pallas kernels for 0% -> 0%
where the time goes in v11:
time: 202 us; the launch traced here: 201 us
  waiting for transfers between devices  63.8 us (32%)
  starting transfers between devices  58.7 us (29%)
  blocking collectives  45.7 us (23%)
  matrix products  13.9 us (7%)
  other arithmetic  11.9 us (6%)
  local copies, waits for them, and re-layouts  6.08 us (3%)
    ppermute x14, starting transfers between devices, shift(): return lax.ppermute(value, axis, [(i, (i + step) % n) for i in range(n)])  40.8 us
    ppermute x14, waiting for transfers between devices, shift(): return lax.ppermute(value, axis, [(i, (i + step) % n) for i in range(n)])  27.3 us
    all_to_all x1, blocking collectives, shards(): lax.all_to_all(gated.reshape(experts, slot_count, shard_width), 'expert',...  23.4 us
    all_to_all x2, waiting for transfers between devices, shards(): part = lax.all_to_all(copies, 'mz', split_axis=0, concat_axis=0, tiled=True)  22.6 us
    all_to_all x1, blocking collectives, shards(): lax.all_to_all(masked.reshape(experts, slot_count, shard_width), 'expert'...  22.3 us
    all_to_all x1, waiting for transfers between devices, shards(): lax.all_to_all(jnp.transpose(across_x, (1, 0, 2)), 'mz', split_axis=0, co...  13.8 us
    all_to_all x2, starting transfers between devices, shards(): part = lax.all_to_all(copies, 'mz', split_axis=0, concat_axis=0, tiled=True)  13.8 us
    all_to_all x1, starting transfers between devices, shards(): lax.all_to_all(jnp.transpose(across_x, (1, 0, 2)), 'mz', split_axis=0, co...  4.07 us
  transfers between devices with their start and end apart: 17, of which 10 were waited for; matrix products, arithmetic and copies ran while one was open for 6% of the time, Pallas kernels for 0%

profile of v11, /device:TPU:6, one launch (start us, length us, event | category | flops | bytes accessed | tf_op | source)
XLA Modules:
  0.0 200.5 jit_solution(9422662262314154796)
XLA Ops:
  4.5 22.3 %all_to_all.25 = bf16[32,32,128]{2,1,0:T(8,128)(2,1)S(1)} all-to-all(bf16[32,32,128]{2,1,0:T(8,128)(2,1)S(1)} %bitcast.76), channel_id=1, replica_groups=mesh['expert'=32,'mx'=4,'mz'=4] {'expert'}, dimensions={0} | all-to-all | bytes 524288 | tf_op jit(solution)/shard_map/all_to_all | solution.py:69
  27.7 9.5 %all-to-all-start.1 = ((bf16[4,512,128]{1,2,0:T(8,128)(2,1)}), bf16[4,512,128]{1,2,0:T(8,128)(2,1)S(1)}, u32[]{:S(2)}, u32[]{:S(2)}) async-start(bf16[4,512,128]{1,2,0:T(8,128)(2,1)} %broadcast_in_dim.54), calls=%async_computation.1 | async-start | bytes 1048576 | tf_op jit(solution)/shard_map/all_to_all | solution.py:87
  37.4 14.0 %all-to-all-done.1 = bf16[4,512,128]{1,2,0:T(8,128)(2,1)S(1)} async-done(((bf16[4,512,128]{1,2,0:T(8,128)(2,1)}), bf16[4,512,128]{1,2,0:T(8,128)(2,1)S(1)}, u32[]{:S(2)}, u32[]{:S(2)}) %all-to-all-start.1) | async-done | bytes 524320 | tf_op jit(solution)/shard_map/all_to_all | solution.py:87
  52.2 4.2 %all-to-all-start.2 = ((bf16[4,512,128]{1,2,0:T(8,128)(2,1)}), bf16[4,512,128]{1,2,0:T(8,128)(2,1)S(1)}, u32[]{:S(2)}, u32[]{:S(2)}) async-start(bf16[4,512,128]{1,2,0:T(8,128)(2,1)} %broadcast_in_dim.56), calls=%async_computation.2 | async-start | bytes 1048576 | tf_op jit(solution)/shard_map/all_to_all | solution.py:87
  56.4 2.4 %collective-permute-start.1 = (bf16[4,512,128]{1,2,0:T(8,128)(2,1)S(1)}, bf16[4,512,128]{1,2,0:T(8,128)(2,1)S(1)}, u32[]{:S(2)}, u32[]{:S(2)}) collective-permute-start(bf16[4,512,128]{1,2,0:T(8,128)(2,1)S(1)} %all-to-all-done.1), channel_id=1, source_target_pairs={{0,4},{4,8},{8,12},{12,0},{1,5},{5,9},{9,13},{13,1},{2,6},{6,10},{... | collective-permute-start | bytes 1572872 | tf_op jit(solution)/shard_map/ppermute | solution.py:10
  58.8 3.5 %collective-permute-start = (bf16[4,512,128]{1,2,0:T(8,128)(2,1)S(1)}, bf16[4,512,128]{1,2,0:T(8,128)(2,1)}, u32[]{:S(2)}, u32[]{:S(2)}) collective-permute-start(bf16[4,512,128]{1,2,0:T(8,128)(2,1)S(1)} %all-to-all-done.1), channel_id=1, source_target_pairs={{0,12},{4,0},{8,4},{12,8},{1,13},{5,1},{9,5},{13,9},{2,14},{6,2},{... | collective-permute-start | bytes 1572872 | tf_op jit(solution)/shard_map/ppermute | solution.py:10
  62.3 8.6 %all-to-all-done.2 = bf16[4,512,128]{1,2,0:T(8,128)(2,1)S(1)} async-done(((bf16[4,512,128]{1,2,0:T(8,128)(2,1)}), bf16[4,512,128]{1,2,0:T(8,128)(2,1)S(1)}, u32[]{:S(2)}, u32[]{:S(2)}) %all-to-all-start.2) | async-done | bytes 524320 | tf_op jit(solution)/shard_map/all_to_all | solution.py:87
  70.9 2.4 %collective-permute-start.5 = (bf16[4,512,128]{1,2,0:T(8,128)(2,1)S(1)}, bf16[4,512,128]{1,2,0:T(8,128)(2,1)S(1)}, u32[]{:S(2)}, u32[]{:S(2)}) collective-permute-start(bf16[4,512,128]{1,2,0:T(8,128)(2,1)S(1)} %all-to-all-done.2), channel_id=1, source_target_pairs={{0,4},{4,8},{8,12},{12,0},{1,5},{5,9},{9,13},{13,1},{2,6},{6,10},{... | collective-permute-start | bytes 1572872 | tf_op jit(solution)/shard_map/ppermute | solution.py:10
  73.3 3.5 %collective-permute-start.4 = (bf16[4,512,128]{1,2,0:T(8,128)(2,1)S(1)}, bf16[4,512,128]{1,2,0:T(8,128)(2,1)}, u32[]{:S(2)}, u32[]{:S(2)}) collective-permute-start(bf16[4,512,128]{1,2,0:T(8,128)(2,1)S(1)} %all-to-all-done.2), channel_id=1, source_target_pairs={{0,12},{4,0},{8,4},{12,8},{1,13},{5,1},{9,5},{13,9},{2,14},{6,2},{... | collective-permute-start | bytes 1572872 | tf_op jit(solution)/shard_map/ppermute | solution.py:10
  77.5 3.6 %collective-permute-start.2 = (bf16[2,512,128]{1,2,0:T(8,128)(2,1)}, bf16[2,512,128]{1,2,0:T(8,128)(2,1)}, u32[]{:S(2)}, u32[]{:S(2)}) collective-permute-start(bf16[2,512,128]{1,2,0:T(8,128)(2,1)} %slice.35), channel_id=1, source_target_pairs={{0,4},{4,8},{8,12},{12,0},{1,5},{5,9},{9,13},{13,1},{2,6},{6,10},{... | collective-permute-start | bytes 786440 | tf_op jit(solution)/shard_map/ppermute | solution.py:10
  86.6 3.4 %collective-permute-start.6 = (bf16[2,512,128]{1,2,0:T(8,128)(2,1)S(1)}, bf16[2,512,128]{1,2,0:T(8,128)(2,1)S(1)}, u32[]{:S(2)}, u32[]{:S(2)}) collective-permute-start(bf16[2,512,128]{1,2,0:T(8,128)(2,1)S(1)} %slice.38), channel_id=1, source_target_pairs={{0,4},{4,8},{8,12},{12,0},{1,5},{5,9},{9,13},{13,1},{2,6},{6,10},{... | collective-permute-start | bytes 786440 | tf_op jit(solution)/shard_map/ppermute | solution.py:10
  91.0 2.5 %collective-permute-start.7 = (bf16[2,512,128]{1,2,0:T(8,128)(2,1)S(1)}, bf16[2,512,128]{1,2,0:T(8,128)(2,1)S(1)}, u32[]{:S(2)}, u32[]{:S(2)}) collective-permute-start(bf16[2,512,128]{1,2,0:T(8,128)(2,1)S(1)} %slice.39), channel_id=1, source_target_pairs={{0,12},{4,0},{8,4},{12,8},{1,13},{5,1},{9,5},{13,9},{2,14},{6,2},{... | collective-permute-start | bytes 786440 | tf_op jit(solution)/shard_map/ppermute | solution.py:10
  95.9 4.6 %collective-permute-done.7 = bf16[2,512,128]{1,2,0:T(8,128)(2,1)S(1)} collective-permute-done((bf16[2,512,128]{1,2,0:T(8,128)(2,1)S(1)}, bf16[2,512,128]{1,2,0:T(8,128)(2,1)S(1)}, u32[]{:S(2)}, u32[]{:S(2)}) %collective-permute-start.7) | collective-permute-done | bytes 262176 | tf_op jit(solution)/shard_map/ppermute | solution.py:10
  112.6 3.9 %collective-permute-start.11 = (bf16[512,512]{1,0:T(8,128)(2,1)S(1)}, bf16[512,512]{1,0:T(8,128)(2,1)S(1)}, u32[]{:S(2)}, u32[]{:S(2)}) collective-permute-start(bf16[512,512]{1,0:T(8,128)(2,1)S(1)} %convolution_convert_fusion.3), channel_id=1, source_target_pairs={{0,12},{4,0},{8,4},{12,8},{1,13},{5,1},{9,5},{13,9},{2,14},{6,2},{... | collective-permute-start | bytes 1572872 | tf_op jit(solution)/shard_map/ppermute | solution.py:10
  117.0 5.7 %collective-permute-done.8 = bf16[512,512]{1,0:T(8,128)(2,1)S(1)} collective-permute-done((bf16[512,512]{1,0:T(8,128)(2,1)S(1)}, bf16[512,512]{1,0:T(8,128)(2,1)S(1)}, u32[]{:S(2)}, u32[]{:S(2)}) %collective-permute-start.8) | collective-permute-done | bytes 524320 | tf_op jit(solution)/shard_map/ppermute | solution.py:10
  126.1 3.9 %collective-permute-start.12 = (bf16[512,512]{1,0:T(8,128)(2,1)S(1)}, bf16[512,512]{1,0:T(8,128)(2,1)S(1)}, u32[]{:S(2)}, u32[]{:S(2)}) collective-permute-start(bf16[512,512]{1,0:T(8,128)(2,1)S(1)} %add_convert_fusion.2), channel_id=1, source_target_pairs={{0,12},{4,0},{8,4},{12,8},{1,13},{5,1},{9,5},{13,9},{2,14},{6,2},{... | collective-permute-start | bytes 1572872 | tf_op jit(solution)/shard_map/ppermute | solution.py:10
  130.5 6.7 %collective-permute-done.9 = bf16[512,512]{1,0:T(8,128)(2,1)S(1)} collective-permute-done((bf16[512,512]{1,0:T(8,128)(2,1)S(1)}, bf16[512,512]{1,0:T(8,128)(2,1)S(1)}, u32[]{:S(2)}, u32[]{:S(2)}) %collective-permute-start.9) | collective-permute-done | bytes 524320 | tf_op jit(solution)/shard_map/ppermute | solution.py:10
  140.5 3.9 %collective-permute-start.13 = (bf16[512,512]{1,0:T(8,128)(2,1)S(1)}, bf16[512,512]{1,0:T(8,128)(2,1)S(1)}, u32[]{:S(2)}, u32[]{:S(2)}) collective-permute-start(bf16[512,512]{1,0:T(8,128)(2,1)S(1)} %add_convert_fusion.1), channel_id=1, source_target_pairs={{0,12},{4,0},{8,4},{12,8},{1,13},{5,1},{9,5},{13,9},{2,14},{6,2},{... | collective-permute-start | bytes 1572872 | tf_op jit(solution)/shard_map/ppermute | solution.py:10
  144.9 3.4 %collective-permute-done.10 = bf16[512,512]{1,0:T(8,128)(2,1)S(1)} collective-permute-done((bf16[512,512]{1,0:T(8,128)(2,1)S(1)}, bf16[512,512]{1,0:T(8,128)(2,1)S(1)}, u32[]{:S(2)}, u32[]{:S(2)}) %collective-permute-start.10) | collective-permute-done | bytes 524320 | tf_op jit(solution)/shard_map/ppermute | solution.py:10
  148.5 4.3 %collective-permute-done.13 = bf16[512,512]{1,0:T(8,128)(2,1)S(1)} collective-permute-done((bf16[512,512]{1,0:T(8,128)(2,1)S(1)}, bf16[512,512]{1,0:T(8,128)(2,1)S(1)}, u32[]{:S(2)}, u32[]{:S(2)}) %collective-permute-start.13) | collective-permute-done | bytes 524320 | tf_op jit(solution)/shard_map/ppermute | solution.py:10
  154.2 4.1 %all-to-all-start.3 = ((bf16[4,1024,128]{2,1,0:T(8,128)(2,1)}), bf16[4,1024,128]{2,1,0:T(8,128)(2,1)S(1)}, u32[]{:S(2)}, u32[]{:S(2)}) async-start(bf16[4,1024,128]{2,1,0:T(8,128)(2,1)} %bitcast_bitcast_fusion), calls=%async_computation.3 | async-start | bytes 2097152 | tf_op jit(solution)/shard_map/all_to_all | solution.py:120
  158.2 3.0 %fusion.36 = f32[1024]{0:T(1024)S(1)} fusion(bf16[1024,2048]{0,1:T(8,128)(2,1)} %copy-done.1, s32[]{:T(128)S(6)} %select_n.78, bf16[2048,32]{0,1:T(8,128)(2,1)S(1)} %copy-done.2, pred[32]{0:T(512)(128)(4,1)S(1)} %iota_compare_fusion.2), kind=kOutput, calls=%fused_computation.49 | convolution fusion | flops 134544384 | bytes 4329508 | tf_op jit(solution)/shard_map/dot_general | solution.py:96
  161.4 13.8 %all-to-all-done.3 = bf16[4,1024,128]{2,1,0:T(8,128)(2,1)S(1)} async-done(((bf16[4,1024,128]{2,1,0:T(8,128)(2,1)}), bf16[4,1024,128]{2,1,0:T(8,128)(2,1)S(1)}, u32[]{:S(2)}, u32[]{:S(2)}) %all-to-all-start.3) | async-done | bytes 1048608 | tf_op jit(solution)/shard_map/all_to_all | solution.py:120
  175.7 23.4 %all_to_all.26 = bf16[32,32,128]{2,1,0:T(8,128)(2,1)S(1)} all-to-all(bf16[32,32,128]{2,1,0:T(8,128)(2,1)S(1)} %fusion.37), channel_id=1, replica_groups=mesh['expert'=32,'mx'=4,'mz'=4] {'expert'}, dimensions={0} | all-to-all | bytes 524288 | tf_op jit(solution)/shard_map/all_to_all | solution.py:126
  (68 shorter events, 39.5 us)
Async XLA Ops:
  0.0 109.7 %copy-start = (bf16[1,320,2048]{2,1,0:T(8,128)(2,1)S(1)}, bf16[1,320,2048]{2,1,0:T(8,128)(2,1)}, u32[]{:S(2)}) copy-start(bf16[1,320,2048]{2,1,0:T(8,128)(2,1)} %param.16) | copy-start | bytes 3932164
  27.7 57.4 %copy-start.3 = (f32[2048]{0:T(1024)S(1)}, f32[2048]{0:T(1024)}, u32[]{:S(2)}) copy-start(f32[2048]{0:T(1024)} %param.12) | copy-start | bytes 24580
  27.7 23.7 %all-to-all-start.1 = ((bf16[4,512,128]{1,2,0:T(8,128)(2,1)}), bf16[4,512,128]{1,2,0:T(8,128)(2,1)S(1)}, u32[]{:S(2)}, u32[]{:S(2)}) async-start(bf16[4,512,128]{1,2,0:T(8,128)(2,1)} %broadcast_in_dim.54), calls=%async_computation.1 | async-start | bytes 1048576 | tf_op jit(solution)/shard_map/all_to_all | solution.py:87
  52.2 18.7 %all-to-all-start.2 = ((bf16[4,512,128]{1,2,0:T(8,128)(2,1)}), bf16[4,512,128]{1,2,0:T(8,128)(2,1)S(1)}, u32[]{:S(2)}, u32[]{:S(2)}) async-start(bf16[4,512,128]{1,2,0:T(8,128)(2,1)} %broadcast_in_dim.56), calls=%async_computation.2 | async-start | bytes 1048576 | tf_op jit(solution)/shard_map/all_to_all | solution.py:87
  56.4 20.3 %collective-permute-start.1 = (bf16[4,512,128]{1,2,0:T(8,128)(2,1)S(1)}, bf16[4,512,128]{1,2,0:T(8,128)(2,1)S(1)}, u32[]{:S(2)}, u32[]{:S(2)}) collective-permute-start(bf16[4,512,128]{1,2,0:T(8,128)(2,1)S(1)} %all-to-all-done.1), channel_id=1, source_target_pairs={{0,4},{4,8},{8,12},{12,0},{1,5},{5,9},{9,13},{13,1},{2,6},{6,10},{... | collective-permute-start | bytes 1572872 | tf_op jit(solution)/shard_map/ppermute | solution.py:10
  58.8 22.3 %collective-permute-start = (bf16[4,512,128]{1,2,0:T(8,128)(2,1)S(1)}, bf16[4,512,128]{1,2,0:T(8,128)(2,1)}, u32[]{:S(2)}, u32[]{:S(2)}) collective-permute-start(bf16[4,512,128]{1,2,0:T(8,128)(2,1)S(1)} %all-to-all-done.1), channel_id=1, source_target_pairs={{0,12},{4,0},{8,4},{12,8},{1,13},{5,1},{9,5},{13,9},{2,14},{6,2},{... | collective-permute-start | bytes 1572872 | tf_op jit(solution)/shard_map/ppermute | solution.py:10
  70.9 15.7 %collective-permute-start.5 = (bf16[4,512,128]{1,2,0:T(8,128)(2,1)S(1)}, bf16[4,512,128]{1,2,0:T(8,128)(2,1)S(1)}, u32[]{:S(2)}, u32[]{:S(2)}) collective-permute-start(bf16[4,512,128]{1,2,0:T(8,128)(2,1)S(1)} %all-to-all-done.2), channel_id=1, source_target_pairs={{0,4},{4,8},{8,12},{12,0},{1,5},{5,9},{9,13},{13,1},{2,6},{6,10},{... | collective-permute-start | bytes 1572872 | tf_op jit(solution)/shard_map/ppermute | solution.py:10
  73.3 16.7 %collective-permute-start.4 = (bf16[4,512,128]{1,2,0:T(8,128)(2,1)S(1)}, bf16[4,512,128]{1,2,0:T(8,128)(2,1)}, u32[]{:S(2)}, u32[]{:S(2)}) collective-permute-start(bf16[4,512,128]{1,2,0:T(8,128)(2,1)S(1)} %all-to-all-done.2), channel_id=1, source_target_pairs={{0,12},{4,0},{8,4},{12,8},{1,13},{5,1},{9,5},{13,9},{2,14},{6,2},{... | collective-permute-start | bytes 1572872 | tf_op jit(solution)/shard_map/ppermute | solution.py:10
  77.5 16.0 %collective-permute-start.2 = (bf16[2,512,128]{1,2,0:T(8,128)(2,1)}, bf16[2,512,128]{1,2,0:T(8,128)(2,1)}, u32[]{:S(2)}, u32[]{:S(2)}) collective-permute-start(bf16[2,512,128]{1,2,0:T(8,128)(2,1)} %slice.35), channel_id=1, source_target_pairs={{0,4},{4,8},{8,12},{12,0},{1,5},{5,9},{9,13},{13,1},{2,6},{6,10},{... | collective-permute-start | bytes 786440 | tf_op jit(solution)/shard_map/ppermute | solution.py:10
  82.8 10.7 %collective-permute-start.3 = (bf16[2,512,128]{1,2,0:T(8,128)(2,1)}, bf16[2,512,128]{1,2,0:T(8,128)(2,1)}, u32[]{:S(2)}, u32[]{:S(2)}) collective-permute-start(bf16[2,512,128]{1,2,0:T(8,128)(2,1)} %slice.36), channel_id=1, source_target_pairs={{0,12},{4,0},{8,4},{12,8},{1,13},{5,1},{9,5},{13,9},{2,14},{6,2},{... | collective-permute-start | bytes 786440 | tf_op jit(solution)/shard_map/ppermute | solution.py:10
  86.6 9.3 %collective-permute-start.6 = (bf16[2,512,128]{1,2,0:T(8,128)(2,1)S(1)}, bf16[2,512,128]{1,2,0:T(8,128)(2,1)S(1)}, u32[]{:S(2)}, u32[]{:S(2)}) collective-permute-start(bf16[2,512,128]{1,2,0:T(8,128)(2,1)S(1)} %slice.38), channel_id=1, source_target_pairs={{0,4},{4,8},{8,12},{12,0},{1,5},{5,9},{9,13},{13,1},{2,6},{6,10},{... | collective-permute-start | bytes 786440 | tf_op jit(solution)/shard_map/ppermute | solution.py:10
  91.0 9.5 %collective-permute-start.7 = (bf16[2,512,128]{1,2,0:T(8,128)(2,1)S(1)}, bf16[2,512,128]{1,2,0:T(8,128)(2,1)S(1)}, u32[]{:S(2)}, u32[]{:S(2)}) collective-permute-start(bf16[2,512,128]{1,2,0:T(8,128)(2,1)S(1)} %slice.39), channel_id=1, source_target_pairs={{0,12},{4,0},{8,4},{12,8},{1,13},{5,1},{9,5},{13,9},{2,14},{6,2},{... | collective-permute-start | bytes 786440 | tf_op jit(solution)/shard_map/ppermute | solution.py:10
  104.0 1.4 copy-start.4
  105.4 2.0 copy-start.1
  105.4 2.3 %copy-start.5 = (bf16[1,2048,320]{1,2,0:T(8,128)(2,1)S(1)}, bf16[1,2048,320]{1,2,0:T(8,128)(2,1)}, u32[]{:S(2)}) copy-start(bf16[1,2048,320]{1,2,0:T(8,128)(2,1)} %param.15) | copy-start | bytes 3932164
  110.1 12.6 %collective-permute-start.8 = (bf16[512,512]{1,0:T(8,128)(2,1)S(1)}, bf16[512,512]{1,0:T(8,128)(2,1)S(1)}, u32[]{:S(2)}, u32[]{:S(2)}) collective-permute-start(bf16[512,512]{1,0:T(8,128)(2,1)S(1)} %convolution_convert_fusion.7), channel_id=1, source_target_pairs={{0,4},{4,8},{8,12},{12,0},{1,5},{5,9},{9,13},{13,1},{2,6},{6,10},{... | collective-permute-start | bytes 1572872 | tf_op jit(solution)/shard_map/ppermute | solution.py:10
  112.6 13.0 %collective-permute-start.11 = (bf16[512,512]{1,0:T(8,128)(2,1)S(1)}, bf16[512,512]{1,0:T(8,128)(2,1)S(1)}, u32[]{:S(2)}, u32[]{:S(2)}) collective-permute-start(bf16[512,512]{1,0:T(8,128)(2,1)S(1)} %convolution_convert_fusion.3), channel_id=1, source_target_pairs={{0,12},{4,0},{8,4},{12,8},{1,13},{5,1},{9,5},{13,9},{2,14},{6,2},{... | collective-permute-start | bytes 1572872 | tf_op jit(solution)/shard_map/ppermute | solution.py:10
  123.2 14.0 %collective-permute-start.9 = (bf16[512,512]{1,0:T(8,128)(2,1)S(1)}, bf16[512,512]{1,0:T(8,128)(2,1)S(1)}, u32[]{:S(2)}, u32[]{:S(2)}) collective-permute-start(bf16[512,512]{1,0:T(8,128)(2,1)S(1)} %add_convert_fusion.5), channel_id=1, source_target_pairs={{0,4},{4,8},{8,12},{12,0},{1,5},{5,9},{9,13},{13,1},{2,6},{6,10},{... | collective-permute-start | bytes 1572872 | tf_op jit(solution)/shard_map/ppermute | solution.py:10
  126.1 14.3 %collective-permute-start.12 = (bf16[512,512]{1,0:T(8,128)(2,1)S(1)}, bf16[512,512]{1,0:T(8,128)(2,1)S(1)}, u32[]{:S(2)}, u32[]{:S(2)}) collective-permute-start(bf16[512,512]{1,0:T(8,128)(2,1)S(1)} %add_convert_fusion.2), channel_id=1, source_target_pairs={{0,12},{4,0},{8,4},{12,8},{1,13},{5,1},{9,5},{13,9},{2,14},{6,2},{... | collective-permute-start | bytes 1572872 | tf_op jit(solution)/shard_map/ppermute | solution.py:10
  137.3 11.1 %collective-permute-start.10 = (bf16[512,512]{1,0:T(8,128)(2,1)S(1)}, bf16[512,512]{1,0:T(8,128)(2,1)S(1)}, u32[]{:S(2)}, u32[]{:S(2)}) collective-permute-start(bf16[512,512]{1,0:T(8,128)(2,1)S(1)} %add_convert_fusion.4), channel_id=1, source_target_pairs={{0,4},{4,8},{8,12},{12,0},{1,5},{5,9},{9,13},{13,1},{2,6},{6,10},{... | collective-permute-start | bytes 1572872 | tf_op jit(solution)/shard_map/ppermute | solution.py:10
  140.5 12.3 %collective-permute-start.13 = (bf16[512,512]{1,0:T(8,128)(2,1)S(1)}, bf16[512,512]{1,0:T(8,128)(2,1)S(1)}, u32[]{:S(2)}, u32[]{:S(2)}) collective-permute-start(bf16[512,512]{1,0:T(8,128)(2,1)S(1)} %add_convert_fusion.1), channel_id=1, source_target_pairs={{0,12},{4,0},{8,4},{12,8},{1,13},{5,1},{9,5},{13,9},{2,14},{6,2},{... | collective-permute-start | bytes 1572872 | tf_op jit(solution)/shard_map/ppermute | solution.py:10
  153.0 5.2 %copy-start.2 = (bf16[2048,32]{0,1:T(8,128)(2,1)S(1)}, bf16[2048,32]{0,1:T(8,128)(2,1)}, u32[]{:S(2)}) copy-start(bf16[2048,32]{0,1:T(8,128)(2,1)} %param.13) | copy-start | bytes 393220
  154.2 21.0 %all-to-all-start.3 = ((bf16[4,1024,128]{2,1,0:T(8,128)(2,1)}), bf16[4,1024,128]{2,1,0:T(8,128)(2,1)S(1)}, u32[]{:S(2)}, u32[]{:S(2)}) async-start(bf16[4,1024,128]{2,1,0:T(8,128)(2,1)} %bitcast_bitcast_fusion), calls=%async_computation.3 | async-start | bytes 2097152 | tf_op jit(solution)/shard_map/all_to_all | solution.py:120

commit v12 on v11

--- a/solution.py
+++ b/solution.py
@@ -66,13 +66,13 @@
     masked = lax.dot_general(
         route, tokens, (((0,), (0,)), ((), ())), preferred_element_type=jnp.float32
     ).astype(jnp.bfloat16)
-    received = lax.all_to_all(
-        masked.reshape(experts, slot_count, shard_width),
-        "expert",
-        split_axis=0,
-        concat_axis=0,
-        tiled=True,
-    ).reshape(cells, shard_width)
+    by_half = masked.reshape(experts, 2, slot_count // 2, shard_width)
+    received = [
+        lax.all_to_all(by_half[:, h], "expert", split_axis=0, concat_axis=0, tiled=True).reshape(
+            cells // 2, shard_width
+        )
+        for h in range(2)
+    ]
     n_z = lax.psum(1, "mz")
     n_x = n_mp // n_z
     at_x = lax.axis_index("mx")
@@ -82,7 +82,7 @@
         return jnp.roll(w, -at_x * x_width, axis=0)
 
     halves = []
-    for rows in (received[: cells // 2], received[cells // 2 :]):
+    for rows in received:
         copies = jnp.broadcast_to(rows[None], (n_z,) + rows.shape)
         part = lax.all_to_all(copies, "mz", split_axis=0, concat_axis=0, tiled=True)
         halves.append(ring_gather(part, "mx", n_x).reshape(n_mp, cells // 2, shard_width))
@@ -123,6 +123,7 @@
     summed = jnp.sum(z_terms.astype(jnp.float32), axis=0).astype(jnp.bfloat16)
     gated = (gate_prob[:, None] * summed.astype(jnp.float32)).astype(jnp.bfloat16)
 
+    gated = jnp.swapaxes(gated.reshape(2, experts, slot_count // 2, shard_width), 0, 1)
     returned = lax.all_to_all(
         gated.reshape(experts, slot_count, shard_width),
         "expert",

time: 202 us -> 215 us (1.064)
  waiting for transfers between devices: 63.8 us -> 73.9 us
  starting transfers between devices: 58.7 us -> 62.5 us
    all_to_all x0 -> x1, waiting for transfers between devices: none -> 10.3 us  [shards(): lax.all_to_all(by_half[:, h], 'expert', split_axis=0, concat_axis=0, tile...]
    all_to_all x0 -> x1, starting transfers between devices: none -> 3.86 us  [shards(): lax.all_to_all(by_half[:, h], 'expert', split_axis=0, concat_axis=0, tile...]
    all_to_all x1, blocking collectives: 22.3 us -> 19.5 us  [shards(): lax.all_to_all(by_half[:, h], 'expert', split_axis=0, concat_axis=0, tile...]
  transfers between devices with their start and end apart: 17 -> 18, of which waited for: 10 -> 11; matrix products, arithmetic and copies ran while one was open for 6% -> 6% of each run, Pallas kernels for 0% -> 0%
where the time goes in v12:
time: 215 us; the launch traced here: 213 us
  waiting for transfers between devices  73.9 us (34%)
  starting transfers between devices  62.5 us (29%)
  blocking collectives  43.8 us (20%)
  matrix products  13.9 us (6%)
  other arithmetic  11.9 us (6%)
  local copies, waits for them, and re-layouts  6.76 us (3%)
    ppermute x14, starting transfers between devices, shift(): return lax.ppermute(value, axis, [(i, (i + step) % n) for i in range(n)])  40.9 us
    ppermute x14, waiting for transfers between devices, shift(): return lax.ppermute(value, axis, [(i, (i + step) % n) for i in range(n)])  27.3 us
    all_to_all x1, blocking collectives, shards(): lax.all_to_all(gated.reshape(experts, slot_count, shard_width), 'expert',...  24.2 us
    all_to_all x2, waiting for transfers between devices, shards(): part = lax.all_to_all(copies, 'mz', split_axis=0, concat_axis=0, tiled=True)  22.6 us
    all_to_all x1, blocking collectives, shards(): lax.all_to_all(by_half[:, h], 'expert', split_axis=0, concat_axis=0, tile...  19.5 us
    all_to_all x2, starting transfers between devices, shards(): part = lax.all_to_all(copies, 'mz', split_axis=0, concat_axis=0, tiled=True)  13.7 us
    all_to_all x1, waiting for transfers between devices, shards(): lax.all_to_all(jnp.transpose(across_x, (1, 0, 2)), 'mz', split_axis=0, co...  13.7 us
    all_to_all x1, waiting for transfers between devices, shards(): lax.all_to_all(by_half[:, h], 'expert', split_axis=0, concat_axis=0, tile...  10.3 us
  transfers between devices with their start and end apart: 18, of which 11 were waited for; matrix products, arithmetic and copies ran while one was open for 6% of the time, Pallas kernels for 0%

profile of v12, /device:TPU:6, one launch (start us, length us, event | category | flops | bytes accessed | tf_op | source)
XLA Modules:
  0.0 213.3 jit_solution(1982117290878323569)
XLA Ops:
  5.1 19.5 %all_to_all.30 = bf16[32,16,128]{2,1,0:T(8,128)(2,1)S(1)} all-to-all(bf16[32,16,128]{2,1,0:T(8,128)(2,1)S(1)} %get-tuple-element.6), channel_id=1, replica_groups=mesh['expert'=32,'mx'=4,'mz'=4] {'expert'}, dimensions={0} | all-to-all | bytes 262144 | tf_op jit(solution)/shard_map/all_to_all | solution.py:71
  24.7 3.9 %all-to-all-start.2 = ((bf16[32,16,128]{2,1,0:T(8,128)(2,1)}), bf16[32,16,128]{2,1,0:T(8,128)(2,1)S(1)}, u32[]{:S(2)}, u32[]{:S(2)}) async-start(bf16[32,16,128]{2,1,0:T(8,128)(2,1)} %get-tuple-element.7), calls=%async_computation.2 | async-start | bytes 262144 | tf_op jit(solution)/shard_map/all_to_all | solution.py:71
  28.7 10.3 %all-to-all-done.2 = bf16[32,16,128]{2,1,0:T(8,128)(2,1)S(1)} async-done(((bf16[32,16,128]{2,1,0:T(8,128)(2,1)}), bf16[32,16,128]{2,1,0:T(8,128)(2,1)S(1)}, u32[]{:S(2)}, u32[]{:S(2)}) %all-to-all-start.2) | async-done | bytes 131104 | tf_op jit(solution)/shard_map/all_to_all | solution.py:71
  39.8 9.5 %all-to-all-start.1 = ((bf16[4,512,128]{1,2,0:T(8,128)(2,1)}), bf16[4,512,128]{1,2,0:T(8,128)(2,1)S(1)}, u32[]{:S(2)}, u32[]{:S(2)}) async-start(bf16[4,512,128]{1,2,0:T(8,128)(2,1)} %broadcast_in_dim.52), calls=%async_computation.1 | async-start | bytes 1048576 | tf_op jit(solution)/shard_map/all_to_all | solution.py:87
  49.5 14.1 %all-to-all-done.1 = bf16[4,512,128]{1,2,0:T(8,128)(2,1)S(1)} async-done(((bf16[4,512,128]{1,2,0:T(8,128)(2,1)}), bf16[4,512,128]{1,2,0:T(8,128)(2,1)S(1)}, u32[]{:S(2)}, u32[]{:S(2)}) %all-to-all-start.1) | async-done | bytes 524320 | tf_op jit(solution)/shard_map/all_to_all | solution.py:87
  64.4 4.2 %all-to-all-start.3 = ((bf16[4,512,128]{1,2,0:T(8,128)(2,1)}), bf16[4,512,128]{1,2,0:T(8,128)(2,1)S(1)}, u32[]{:S(2)}, u32[]{:S(2)}) async-start(bf16[4,512,128]{1,2,0:T(8,128)(2,1)} %broadcast_in_dim.54), calls=%async_computation.3 | async-start | bytes 1048576 | tf_op jit(solution)/shard_map/all_to_all | solution.py:87
  70.9 3.5 %collective-permute-start = (bf16[4,512,128]{1,2,0:T(8,128)(2,1)S(1)}, bf16[4,512,128]{1,2,0:T(8,128)(2,1)}, u32[]{:S(2)}, u32[]{:S(2)}) collective-permute-start(bf16[4,512,128]{1,2,0:T(8,128)(2,1)S(1)} %all-to-all-done.1), channel_id=1, source_target_pairs={{0,12},{4,0},{8,4},{12,8},{1,13},{5,1},{9,5},{13,9},{2,14},{6,2},{... | collective-permute-start | bytes 1572872 | tf_op jit(solution)/shard_map/ppermute | solution.py:10
  74.4 8.6 %all-to-all-done.3 = bf16[4,512,128]{1,2,0:T(8,128)(2,1)S(1)} async-done(((bf16[4,512,128]{1,2,0:T(8,128)(2,1)}), bf16[4,512,128]{1,2,0:T(8,128)(2,1)S(1)}, u32[]{:S(2)}, u32[]{:S(2)}) %all-to-all-start.3) | async-done | bytes 524320 | tf_op jit(solution)/shard_map/all_to_all | solution.py:87
  85.4 3.5 %collective-permute-start.4 = (bf16[4,512,128]{1,2,0:T(8,128)(2,1)S(1)}, bf16[4,512,128]{1,2,0:T(8,128)(2,1)}, u32[]{:S(2)}, u32[]{:S(2)}) collective-permute-start(bf16[4,512,128]{1,2,0:T(8,128)(2,1)S(1)} %all-to-all-done.3), channel_id=1, source_target_pairs={{0,12},{4,0},{8,4},{12,8},{1,13},{5,1},{9,5},{13,9},{2,14},{6,2},{... | collective-permute-start | bytes 1572872 | tf_op jit(solution)/shard_map/ppermute | solution.py:10
  89.6 3.6 %collective-permute-start.2 = (bf16[2,512,128]{1,2,0:T(8,128)(2,1)}, bf16[2,512,128]{1,2,0:T(8,128)(2,1)}, u32[]{:S(2)}, u32[]{:S(2)}) collective-permute-start(bf16[2,512,128]{1,2,0:T(8,128)(2,1)} %slice.33), channel_id=1, source_target_pairs={{0,4},{4,8},{8,12},{12,0},{1,5},{5,9},{9,13},{13,1},{2,6},{6,10},{... | collective-permute-start | bytes 786440 | tf_op jit(solution)/shard_map/ppermute | solution.py:10
  98.7 3.4 %collective-permute-start.6 = (bf16[2,512,128]{1,2,0:T(8,128)(2,1)S(1)}, bf16[2,512,128]{1,2,0:T(8,128)(2,1)S(1)}, u32[]{:S(2)}, u32[]{:S(2)}) collective-permute-start(bf16[2,512,128]{1,2,0:T(8,128)(2,1)S(1)} %slice.36), channel_id=1, source_target_pairs={{0,4},{4,8},{8,12},{12,0},{1,5},{5,9},{9,13},{13,1},{2,6},{6,10},{... | collective-permute-start | bytes 786440 | tf_op jit(solution)/shard_map/ppermute | solution.py:10
  103.1 2.4 %collective-permute-start.7 = (bf16[2,512,128]{1,2,0:T(8,128)(2,1)S(1)}, bf16[2,512,128]{1,2,0:T(8,128)(2,1)S(1)}, u32[]{:S(2)}, u32[]{:S(2)}) collective-permute-start(bf16[2,512,128]{1,2,0:T(8,128)(2,1)S(1)} %slice.37), channel_id=1, source_target_pairs={{0,12},{4,0},{8,4},{12,8},{1,13},{5,1},{9,5},{13,9},{2,14},{6,2},{... | collective-permute-start | bytes 786440 | tf_op jit(solution)/shard_map/ppermute | solution.py:10
  108.0 4.6 %collective-permute-done.7 = bf16[2,512,128]{1,2,0:T(8,128)(2,1)S(1)} collective-permute-done((bf16[2,512,128]{1,2,0:T(8,128)(2,1)S(1)}, bf16[2,512,128]{1,2,0:T(8,128)(2,1)S(1)}, u32[]{:S(2)}, u32[]{:S(2)}) %collective-permute-start.7) | collective-permute-done | bytes 262176 | tf_op jit(solution)/shard_map/ppermute | solution.py:10
  124.7 3.9 %collective-permute-start.11 = (bf16[512,512]{1,0:T(8,128)(2,1)S(1)}, bf16[512,512]{1,0:T(8,128)(2,1)S(1)}, u32[]{:S(2)}, u32[]{:S(2)}) collective-permute-start(bf16[512,512]{1,0:T(8,128)(2,1)S(1)} %convolution_convert_fusion.3), channel_id=1, source_target_pairs={{0,12},{4,0},{8,4},{12,8},{1,13},{5,1},{9,5},{13,9},{2,14},{6,2},{... | collective-permute-start | bytes 1572872 | tf_op jit(solution)/shard_map/ppermute | solution.py:10
  129.1 5.7 %collective-permute-done.8 = bf16[512,512]{1,0:T(8,128)(2,1)S(1)} collective-permute-done((bf16[512,512]{1,0:T(8,128)(2,1)S(1)}, bf16[512,512]{1,0:T(8,128)(2,1)S(1)}, u32[]{:S(2)}, u32[]{:S(2)}) %collective-permute-start.8) | collective-permute-done | bytes 524320 | tf_op jit(solution)/shard_map/ppermute | solution.py:10
  138.2 3.9 %collective-permute-start.12 = (bf16[512,512]{1,0:T(8,128)(2,1)S(1)}, bf16[512,512]{1,0:T(8,128)(2,1)S(1)}, u32[]{:S(2)}, u32[]{:S(2)}) collective-permute-start(bf16[512,512]{1,0:T(8,128)(2,1)S(1)} %add_convert_fusion.2), channel_id=1, source_target_pairs={{0,12},{4,0},{8,4},{12,8},{1,13},{5,1},{9,5},{13,9},{2,14},{6,2},{... | collective-permute-start | bytes 1572872 | tf_op jit(solution)/shard_map/ppermute | solution.py:10
  142.6 6.7 %collective-permute-done.9 = bf16[512,512]{1,0:T(8,128)(2,1)S(1)} collective-permute-done((bf16[512,512]{1,0:T(8,128)(2,1)S(1)}, bf16[512,512]{1,0:T(8,128)(2,1)S(1)}, u32[]{:S(2)}, u32[]{:S(2)}) %collective-permute-start.9) | collective-permute-done | bytes 524320 | tf_op jit(solution)/shard_map/ppermute | solution.py:10
  152.6 3.7 %collective-permute-start.13 = (bf16[512,512]{1,0:T(8,128)(2,1)S(1)}, bf16[512,512]{1,0:T(8,128)(2,1)S(1)}, u32[]{:S(2)}, u32[]{:S(2)}) collective-permute-start(bf16[512,512]{1,0:T(8,128)(2,1)S(1)} %add_convert_fusion.1), channel_id=1, source_target_pairs={{0,12},{4,0},{8,4},{12,8},{1,13},{5,1},{9,5},{13,9},{2,14},{6,2},{... | collective-permute-start | bytes 1572872 | tf_op jit(solution)/shard_map/ppermute | solution.py:10
  156.8 3.6 %collective-permute-done.10 = bf16[512,512]{1,0:T(8,128)(2,1)S(1)} collective-permute-done((bf16[512,512]{1,0:T(8,128)(2,1)S(1)}, bf16[512,512]{1,0:T(8,128)(2,1)S(1)}, u32[]{:S(2)}, u32[]{:S(2)}) %collective-permute-start.10) | collective-permute-done | bytes 524320 | tf_op jit(solution)/shard_map/ppermute | solution.py:10
  160.6 4.3 %collective-permute-done.13 = bf16[512,512]{1,0:T(8,128)(2,1)S(1)} collective-permute-done((bf16[512,512]{1,0:T(8,128)(2,1)S(1)}, bf16[512,512]{1,0:T(8,128)(2,1)S(1)}, u32[]{:S(2)}, u32[]{:S(2)}) %collective-permute-start.13) | collective-permute-done | bytes 524320 | tf_op jit(solution)/shard_map/ppermute | solution.py:10
  166.3 4.1 %all-to-all-start.4 = ((bf16[4,1024,128]{2,1,0:T(8,128)(2,1)}), bf16[4,1024,128]{2,1,0:T(8,128)(2,1)S(1)}, u32[]{:S(2)}, u32[]{:S(2)}) async-start(bf16[4,1024,128]{2,1,0:T(8,128)(2,1)} %bitcast_bitcast_fusion), calls=%async_computation.4 | async-start | bytes 2097152 | tf_op jit(solution)/shard_map/all_to_all | solution.py:120
  170.4 3.0 %fusion.36 = f32[1024]{0:T(1024)S(1)} fusion(bf16[1024,2048]{0,1:T(8,128)(2,1)} %copy-done.1, s32[]{:T(128)S(6)} %select_n.78, bf16[2048,32]{0,1:T(8,128)(2,1)S(1)} %copy-done.2, pred[32]{0:T(512)(128)(4,1)S(1)} %iota_compare_fusion.2), kind=kOutput, calls=%fused_computation.49 | convolution fusion | flops 134544384 | bytes 4329508 | tf_op jit(solution)/shard_map/dot_general | solution.py:96
  173.5 13.7 %all-to-all-done.4 = bf16[4,1024,128]{2,1,0:T(8,128)(2,1)S(1)} async-done(((bf16[4,1024,128]{2,1,0:T(8,128)(2,1)}), bf16[4,1024,128]{2,1,0:T(8,128)(2,1)S(1)}, u32[]{:S(2)}, u32[]{:S(2)}) %all-to-all-start.4) | async-done | bytes 1048608 | tf_op jit(solution)/shard_map/all_to_all | solution.py:120
  187.6 24.2 %all_to_all.31 = bf16[32,32,128]{2,1,0:T(8,128)(2,1)S(1)} all-to-all(bf16[32,32,128]{2,1,0:T(8,128)(2,1)S(1)} %bitcast.80), channel_id=1, replica_groups=mesh['expert'=32,'mx'=4,'mz'=4] {'expert'}, dimensions={0} | all-to-all | bytes 524288 | tf_op jit(solution)/shard_map/all_to_all | solution.py:127
  (71 shorter events, 44.9 us)
Async XLA Ops:
  0.0 121.7 %copy-start = (bf16[1,320,2048]{2,1,0:T(8,128)(2,1)S(1)}, bf16[1,320,2048]{2,1,0:T(8,128)(2,1)}, u32[]{:S(2)}) copy-start(bf16[1,320,2048]{2,1,0:T(8,128)(2,1)} %param.16) | copy-start | bytes 3932164
  24.7 14.3 %all-to-all-start.2 = ((bf16[32,16,128]{2,1,0:T(8,128)(2,1)}), bf16[32,16,128]{2,1,0:T(8,128)(2,1)S(1)}, u32[]{:S(2)}, u32[]{:S(2)}) async-start(bf16[32,16,128]{2,1,0:T(8,128)(2,1)} %get-tuple-element.7), calls=%async_computation.2 | async-start | bytes 262144 | tf_op jit(solution)/shard_map/all_to_all | solution.py:71
  39.8 57.3 %copy-start.3 = (f32[2048]{0:T(1024)S(1)}, f32[2048]{0:T(1024)}, u32[]{:S(2)}) copy-start(f32[2048]{0:T(1024)} %param.12) | copy-start | bytes 24580
  39.8 23.7 %all-to-all-start.1 = ((bf16[4,512,128]{1,2,0:T(8,128)(2,1)}), bf16[4,512,128]{1,2,0:T(8,128)(2,1)S(1)}, u32[]{:S(2)}, u32[]{:S(2)}) async-start(bf16[4,512,128]{1,2,0:T(8,128)(2,1)} %broadcast_in_dim.52), calls=%async_computation.1 | async-start | bytes 1048576 | tf_op jit(solution)/shard_map/all_to_all | solution.py:87
  64.4 18.6 %all-to-all-start.3 = ((bf16[4,512,128]{1,2,0:T(8,128)(2,1)}), bf16[4,512,128]{1,2,0:T(8,128)(2,1)S(1)}, u32[]{:S(2)}, u32[]{:S(2)}) async-start(bf16[4,512,128]{1,2,0:T(8,128)(2,1)} %broadcast_in_dim.54), calls=%async_computation.3 | async-start | bytes 1048576 | tf_op jit(solution)/shard_map/all_to_all | solution.py:87
  68.6 20.3 %collective-permute-start.1 = (bf16[4,512,128]{1,2,0:T(8,128)(2,1)S(1)}, bf16[4,512,128]{1,2,0:T(8,128)(2,1)S(1)}, u32[]{:S(2)}, u32[]{:S(2)}) collective-permute-start(bf16[4,512,128]{1,2,0:T(8,128)(2,1)S(1)} %all-to-all-done.1), channel_id=1, source_target_pairs={{0,4},{4,8},{8,12},{12,0},{1,5},{5,9},{9,13},{13,1},{2,6},{6,10},{... | collective-permute-start | bytes 1572872 | tf_op jit(solution)/shard_map/ppermute | solution.py:10
  70.9 22.2 %collective-permute-start = (bf16[4,512,128]{1,2,0:T(8,128)(2,1)S(1)}, bf16[4,512,128]{1,2,0:T(8,128)(2,1)}, u32[]{:S(2)}, u32[]{:S(2)}) collective-permute-start(bf16[4,512,128]{1,2,0:T(8,128)(2,1)S(1)} %all-to-all-done.1), channel_id=1, source_target_pairs={{0,12},{4,0},{8,4},{12,8},{1,13},{5,1},{9,5},{13,9},{2,14},{6,2},{... | collective-permute-start | bytes 1572872 | tf_op jit(solution)/shard_map/ppermute | solution.py:10
  83.0 15.7 %collective-permute-start.5 = (bf16[4,512,128]{1,2,0:T(8,128)(2,1)S(1)}, bf16[4,512,128]{1,2,0:T(8,128)(2,1)S(1)}, u32[]{:S(2)}, u32[]{:S(2)}) collective-permute-start(bf16[4,512,128]{1,2,0:T(8,128)(2,1)S(1)} %all-to-all-done.3), channel_id=1, source_target_pairs={{0,4},{4,8},{8,12},{12,0},{1,5},{5,9},{9,13},{13,1},{2,6},{6,10},{... | collective-permute-start | bytes 1572872 | tf_op jit(solution)/shard_map/ppermute | solution.py:10
  85.4 16.7 %collective-permute-start.4 = (bf16[4,512,128]{1,2,0:T(8,128)(2,1)S(1)}, bf16[4,512,128]{1,2,0:T(8,128)(2,1)}, u32[]{:S(2)}, u32[]{:S(2)}) collective-permute-start(bf16[4,512,128]{1,2,0:T(8,128)(2,1)S(1)} %all-to-all-done.3), channel_id=1, source_target_pairs={{0,12},{4,0},{8,4},{12,8},{1,13},{5,1},{9,5},{13,9},{2,14},{6,2},{... | collective-permute-start | bytes 1572872 | tf_op jit(solution)/shard_map/ppermute | solution.py:10
  89.6 16.0 %collective-permute-start.2 = (bf16[2,512,128]{1,2,0:T(8,128)(2,1)}, bf16[2,512,128]{1,2,0:T(8,128)(2,1)}, u32[]{:S(2)}, u32[]{:S(2)}) collective-permute-start(bf16[2,512,128]{1,2,0:T(8,128)(2,1)} %slice.33), channel_id=1, source_target_pairs={{0,4},{4,8},{8,12},{12,0},{1,5},{5,9},{9,13},{13,1},{2,6},{6,10},{... | collective-permute-start | bytes 786440 | tf_op jit(solution)/shard_map/ppermute | solution.py:10
  94.9 10.7 %collective-permute-start.3 = (bf16[2,512,128]{1,2,0:T(8,128)(2,1)}, bf16[2,512,128]{1,2,0:T(8,128)(2,1)}, u32[]{:S(2)}, u32[]{:S(2)}) collective-permute-start(bf16[2,512,128]{1,2,0:T(8,128)(2,1)} %slice.34), channel_id=1, source_target_pairs={{0,12},{4,0},{8,4},{12,8},{1,13},{5,1},{9,5},{13,9},{2,14},{6,2},{... | collective-permute-start | bytes 786440 | tf_op jit(solution)/shard_map/ppermute | solution.py:10
  98.7 9.3 %collective-permute-start.6 = (bf16[2,512,128]{1,2,0:T(8,128)(2,1)S(1)}, bf16[2,512,128]{1,2,0:T(8,128)(2,1)S(1)}, u32[]{:S(2)}, u32[]{:S(2)}) collective-permute-start(bf16[2,512,128]{1,2,0:T(8,128)(2,1)S(1)} %slice.36), channel_id=1, source_target_pairs={{0,4},{4,8},{8,12},{12,0},{1,5},{5,9},{9,13},{13,1},{2,6},{6,10},{... | collective-permute-start | bytes 786440 | tf_op jit(solution)/shard_map/ppermute | solution.py:10
  103.1 9.5 %collective-permute-start.7 = (bf16[2,512,128]{1,2,0:T(8,128)(2,1)S(1)}, bf16[2,512,128]{1,2,0:T(8,128)(2,1)S(1)}, u32[]{:S(2)}, u32[]{:S(2)}) collective-permute-start(bf16[2,512,128]{1,2,0:T(8,128)(2,1)S(1)} %slice.37), channel_id=1, source_target_pairs={{0,12},{4,0},{8,4},{12,8},{1,13},{5,1},{9,5},{13,9},{2,14},{6,2},{... | collective-permute-start | bytes 786440 | tf_op jit(solution)/shard_map/ppermute | solution.py:10
  116.1 1.4 copy-start.4
  117.5 2.0 copy-start.1
  117.5 2.3 %copy-start.5 = (bf16[1,2048,320]{1,2,0:T(8,128)(2,1)S(1)}, bf16[1,2048,320]{1,2,0:T(8,128)(2,1)}, u32[]{:S(2)}) copy-start(bf16[1,2048,320]{1,2,0:T(8,128)(2,1)} %param.15) | copy-start | bytes 3932164
  122.2 12.6 %collective-permute-start.8 = (bf16[512,512]{1,0:T(8,128)(2,1)S(1)}, bf16[512,512]{1,0:T(8,128)(2,1)S(1)}, u32[]{:S(2)}, u32[]{:S(2)}) collective-permute-start(bf16[512,512]{1,0:T(8,128)(2,1)S(1)} %convolution_convert_fusion.7), channel_id=1, source_target_pairs={{0,4},{4,8},{8,12},{12,0},{1,5},{5,9},{9,13},{13,1},{2,6},{6,10},{... | collective-permute-start | bytes 1572872 | tf_op jit(solution)/shard_map/ppermute | solution.py:10
  124.7 13.0 %collective-permute-start.11 = (bf16[512,512]{1,0:T(8,128)(2,1)S(1)}, bf16[512,512]{1,0:T(8,128)(2,1)S(1)}, u32[]{:S(2)}, u32[]{:S(2)}) collective-permute-start(bf16[512,512]{1,0:T(8,128)(2,1)S(1)} %convolution_convert_fusion.3), channel_id=1, source_target_pairs={{0,12},{4,0},{8,4},{12,8},{1,13},{5,1},{9,5},{13,9},{2,14},{6,2},{... | collective-permute-start | bytes 1572872 | tf_op jit(solution)/shard_map/ppermute | solution.py:10
  135.3 14.0 %collective-permute-start.9 = (bf16[512,512]{1,0:T(8,128)(2,1)S(1)}, bf16[512,512]{1,0:T(8,128)(2,1)S(1)}, u32[]{:S(2)}, u32[]{:S(2)}) collective-permute-start(bf16[512,512]{1,0:T(8,128)(2,1)S(1)} %add_convert_fusion.5), channel_id=1, source_target_pairs={{0,4},{4,8},{8,12},{12,0},{1,5},{5,9},{9,13},{13,1},{2,6},{6,10},{... | collective-permute-start | bytes 1572872 | tf_op jit(solution)/shard_map/ppermute | solution.py:10
  138.2 14.3 %collective-permute-start.12 = (bf16[512,512]{1,0:T(8,128)(2,1)S(1)}, bf16[512,512]{1,0:T(8,128)(2,1)S(1)}, u32[]{:S(2)}, u32[]{:S(2)}) collective-permute-start(bf16[512,512]{1,0:T(8,128)(2,1)S(1)} %add_convert_fusion.2), channel_id=1, source_target_pairs={{0,12},{4,0},{8,4},{12,8},{1,13},{5,1},{9,5},{13,9},{2,14},{6,2},{... | collective-permute-start | bytes 1572872 | tf_op jit(solution)/shard_map/ppermute | solution.py:10
  149.4 11.1 %collective-permute-start.10 = (bf16[512,512]{1,0:T(8,128)(2,1)S(1)}, bf16[512,512]{1,0:T(8,128)(2,1)S(1)}, u32[]{:S(2)}, u32[]{:S(2)}) collective-permute-start(bf16[512,512]{1,0:T(8,128)(2,1)S(1)} %add_convert_fusion.4), channel_id=1, source_target_pairs={{0,4},{4,8},{8,12},{12,0},{1,5},{5,9},{9,13},{13,1},{2,6},{6,10},{... | collective-permute-start | bytes 1572872 | tf_op jit(solution)/shard_map/ppermute | solution.py:10
  152.6 12.3 %collective-permute-start.13 = (bf16[512,512]{1,0:T(8,128)(2,1)S(1)}, bf16[512,512]{1,0:T(8,128)(2,1)S(1)}, u32[]{:S(2)}, u32[]{:S(2)}) collective-permute-start(bf16[512,512]{1,0:T(8,128)(2,1)S(1)} %add_convert_fusion.1), channel_id=1, source_target_pairs={{0,12},{4,0},{8,4},{12,8},{1,13},{5,1},{9,5},{13,9},{2,14},{6,2},{... | collective-permute-start | bytes 1572872 | tf_op jit(solution)/shard_map/ppermute | solution.py:10
  165.1 5.3 %copy-start.2 = (bf16[2048,32]{0,1:T(8,128)(2,1)S(1)}, bf16[2048,32]{0,1:T(8,128)(2,1)}, u32[]{:S(2)}) copy-start(bf16[2048,32]{0,1:T(8,128)(2,1)} %param.13) | copy-start | bytes 393220
  166.3 20.9 %all-to-all-start.4 = ((bf16[4,1024,128]{2,1,0:T(8,128)(2,1)}), bf16[4,1024,128]{2,1,0:T(8,128)(2,1)S(1)}, u32[]{:S(2)}, u32[]{:S(2)}) async-start(bf16[4,1024,128]{2,1,0:T(8,128)(2,1)} %bitcast_bitcast_fusion), calls=%async_computation.4 | async-start | bytes 2097152 | tf_op jit(solution)/shard_map/all_to_all | solution.py:120

commit v13 on v11

--- a/solution.py
+++ b/solution.py
@@ -81,11 +81,13 @@
     def rows_relative(w):
         return jnp.roll(w, -at_x * x_width, axis=0)
 
+    chunk = cells // 4
     halves = []
-    for rows in (received[: cells // 2], received[cells // 2 :]):
+    for at in range(0, cells, chunk):
+        rows = received[at : at + chunk]
         copies = jnp.broadcast_to(rows[None], (n_z,) + rows.shape)
         part = lax.all_to_all(copies, "mz", split_axis=0, concat_axis=0, tiled=True)
-        halves.append(ring_gather(part, "mx", n_x).reshape(n_mp, cells // 2, shard_width))
+        halves.append(ring_gather(part, "mx", n_x).reshape(n_mp, chunk, shard_width))
     whole = jnp.concatenate(halves, axis=1)
 
     features = jnp.transpose(whole, (1, 0, 2)).reshape(cells, model_width).astype(jnp.float32)

time: 202 us -> 250 us (1.24)
  starting transfers between devices: 58.7 us -> 98.3 us
  waiting for transfers between devices: 63.8 us -> 72.6 us
  blocking collectives: 45.7 us -> 41.8 us
    ppermute x14 -> x22, starting transfers between devices: 40.8 us -> 71.5 us  [shift(): return lax.ppermute(value, axis, [(i, (i + step) % n) for i in range(n)])]
    all_to_all x2 -> x4, starting transfers between devices: 13.8 us -> 19.6 us  [shards(): part = lax.all_to_all(copies, 'mz', split_axis=0, concat_axis=0, tiled=True)]
    ppermute x14 -> x22, waiting for transfers between devices: 27.3 us -> 32.8 us  [shift(): return lax.ppermute(value, axis, [(i, (i + step) % n) for i in range(n)])]
    all_to_all x2 -> x4, waiting for transfers between devices: 22.6 us -> 28 us  [shards(): part = lax.all_to_all(copies, 'mz', split_axis=0, concat_axis=0, tiled=True)]
    all_to_all x1, blocking collectives: 23.4 us -> 19.5 us  [shards(): lax.all_to_all(gated.reshape(experts, slot_count, shard_width), 'expert',...]
    all_to_all x1, starting transfers between devices: 4.07 us -> 7.14 us  [shards(): lax.all_to_all(jnp.transpose(across_x, (1, 0, 2)), 'mz', split_axis=0, co...]
  transfers between devices with their start and end apart: 17 -> 27, of which waited for: 10 -> 10; matrix products, arithmetic and copies ran while one was open for 6% -> 6% of each run, Pallas kernels for 0% -> 0%
where the time goes in v13:
time: 250 us; the launch traced here: 249 us
  starting transfers between devices  98.3 us (39%)
  waiting for transfers between devices  72.6 us (29%)
  blocking collectives  41.8 us (17%)
  matrix products  13.9 us (6%)
  other arithmetic  12.8 us (5%)
  local copies, waits for them, and re-layouts  8.48 us (3%)
    ppermute x22, starting transfers between devices, shift(): return lax.ppermute(value, axis, [(i, (i + step) % n) for i in range(n)])  71.5 us
    ppermute x22, waiting for transfers between devices, shift(): return lax.ppermute(value, axis, [(i, (i + step) % n) for i in range(n)])  32.8 us
    all_to_all x4, waiting for transfers between devices, shards(): part = lax.all_to_all(copies, 'mz', split_axis=0, concat_axis=0, tiled=True)  28 us
    all_to_all x1, blocking collectives, shards(): lax.all_to_all(masked.reshape(experts, slot_count, shard_width), 'expert'...  22.3 us
    all_to_all x4, starting transfers between devices, shards(): part = lax.all_to_all(copies, 'mz', split_axis=0, concat_axis=0, tiled=True)  19.6 us
    all_to_all x1, blocking collectives, shards(): lax.all_to_all(gated.reshape(experts, slot_count, shard_width), 'expert',...  19.5 us
    all_to_all x1, waiting for transfers between devices, shards(): lax.all_to_all(jnp.transpose(across_x, (1, 0, 2)), 'mz', split_axis=0, co...  11.9 us
    all_to_all x1, starting transfers between devices, shards(): lax.all_to_all(jnp.transpose(across_x, (1, 0, 2)), 'mz', split_axis=0, co...  7.14 us
  transfers between devices with their start and end apart: 27, of which 10 were waited for; matrix products, arithmetic and copies ran while one was open for 6% of the time, Pallas kernels for 0%

profile of v13, /device:TPU:6, one launch (start us, length us, event | category | flops | bytes accessed | tf_op | source)
XLA Modules:
  0.0 248.6 jit_solution(10447876699917590507)
XLA Ops:
  4.5 22.3 %all_to_all.35 = bf16[32,32,128]{2,1,0:T(8,128)(2,1)S(1)} all-to-all(bf16[32,32,128]{2,1,0:T(8,128)(2,1)S(1)} %bitcast.97), channel_id=1, replica_groups=mesh['expert'=32,'mx'=4,'mz'=4] {'expert'}, dimensions={0} | all-to-all | bytes 524288 | tf_op jit(solution)/shard_map/all_to_all | solution.py:69
  27.6 9.4 %all-to-all-start.2 = ((bf16[4,256,128]{1,2,0:T(8,128)(2,1)}), bf16[4,256,128]{1,2,0:T(8,128)(2,1)S(1)}, u32[]{:S(2)}, u32[]{:S(2)}) async-start(bf16[4,256,128]{1,2,0:T(8,128)(2,1)} %broadcast_in_dim.72), calls=%async_computation.2 | async-start | bytes 524288 | tf_op jit(solution)/shard_map/all_to_all | solution.py:89
  37.1 9.5 %all-to-all-done.2 = bf16[4,256,128]{1,2,0:T(8,128)(2,1)S(1)} async-done(((bf16[4,256,128]{1,2,0:T(8,128)(2,1)}), bf16[4,256,128]{1,2,0:T(8,128)(2,1)S(1)}, u32[]{:S(2)}, u32[]{:S(2)}) %all-to-all-start.2) | async-done | bytes 262176 | tf_op jit(solution)/shard_map/all_to_all | solution.py:89
  50.9 9.2 %all-to-all-done.1 = bf16[4,256,128]{1,2,0:T(8,128)(2,1)S(1)} async-done(((bf16[4,256,128]{1,2,0:T(8,128)(2,1)}), bf16[4,256,128]{1,2,0:T(8,128)(2,1)S(1)}, u32[]{:S(2)}, u32[]{:S(2)}) %all-to-all-start.1) | async-done | bytes 262176 | tf_op jit(solution)/shard_map/all_to_all | solution.py:89
  64.4 9.2 %all-to-all-done.3 = bf16[4,256,128]{1,2,0:T(8,128)(2,1)S(1)} async-done(((bf16[4,256,128]{1,2,0:T(8,128)(2,1)}), bf16[4,256,128]{1,2,0:T(8,128)(2,1)S(1)}, u32[]{:S(2)}, u32[]{:S(2)}) %all-to-all-start.3) | async-done | bytes 262176 | tf_op jit(solution)/shard_map/all_to_all | solution.py:89
  80.1 3.5 %collective-permute-start.4 = (bf16[4,256,128]{1,2,0:T(8,128)(2,1)S(1)}, bf16[4,256,128]{1,2,0:T(8,128)(2,1)}, u32[]{:S(2)}, u32[]{:S(2)}) collective-permute-start(bf16[4,256,128]{1,2,0:T(8,128)(2,1)S(1)} %all-to-all-done.2), channel_id=1, source_target_pairs={{0,12},{4,0},{8,4},{12,8},{1,13},{5,1},{9,5},{13,9},{2,14},{6,2},{... | collective-permute-start | bytes 786440 | tf_op jit(solution)/shard_map/ppermute | solution.py:10
  83.6 3.6 %collective-permute-start.1 = (bf16[4,256,128]{1,2,0:T(8,128)(2,1)S(1)}, bf16[4,256,128]{1,2,0:T(8,128)(2,1)S(1)}, u32[]{:S(2)}, u32[]{:S(2)}) collective-permute-start(bf16[4,256,128]{1,2,0:T(8,128)(2,1)S(1)} %all-to-all-done.1), channel_id=1, source_target_pairs={{0,4},{4,8},{8,12},{12,0},{1,5},{5,9},{9,13},{13,1},{2,6},{6,10},{... | collective-permute-start | bytes 786440 | tf_op jit(solution)/shard_map/ppermute | solution.py:10
  89.5 4.8 %collective-permute-start.9 = (bf16[4,256,128]{1,2,0:T(8,128)(2,1)S(1)}, bf16[4,256,128]{1,2,0:T(8,128)(2,1)S(1)}, u32[]{:S(2)}, u32[]{:S(2)}) collective-permute-start(bf16[4,256,128]{1,2,0:T(8,128)(2,1)S(1)} %all-to-all-done.3), channel_id=1, source_target_pairs={{0,4},{4,8},{8,12},{12,0},{1,5},{5,9},{9,13},{13,1},{2,6},{6,10},{... | collective-permute-start | bytes 786440 | tf_op jit(solution)/shard_map/ppermute | solution.py:10
  96.3 5.1 %collective-permute-start.13 = (bf16[4,256,128]{1,2,0:T(8,128)(2,1)S(1)}, bf16[4,256,128]{1,2,0:T(8,128)(2,1)S(1)}, u32[]{:S(2)}, u32[]{:S(2)}) collective-permute-start(bf16[4,256,128]{1,2,0:T(8,128)(2,1)S(1)} %all-to-all-done.4), channel_id=1, source_target_pairs={{0,4},{4,8},{8,12},{12,0},{1,5},{5,9},{9,13},{13,1},{2,6},{6,10},{... | collective-permute-start | bytes 786440 | tf_op jit(solution)/shard_map/ppermute | solution.py:10
  105.8 5.1 %collective-permute-start.6 = (bf16[2,256,128]{1,2,0:T(8,128)(2,1)}, bf16[2,256,128]{1,2,0:T(8,128)(2,1)}, u32[]{:S(2)}, u32[]{:S(2)}) collective-permute-start(bf16[2,256,128]{1,2,0:T(8,128)(2,1)} %slice.64), channel_id=1, source_target_pairs={{0,4},{4,8},{8,12},{12,0},{1,5},{5,9},{9,13},{13,1},{2,6},{6,10},{... | collective-permute-start | bytes 393224 | tf_op jit(solution)/shard_map/ppermute | solution.py:10
  114.0 5.1 %collective-permute-start.2 = (bf16[2,256,128]{1,2,0:T(8,128)(2,1)S(1)}, bf16[2,256,128]{1,2,0:T(8,128)(2,1)S(1)}, u32[]{:S(2)}, u32[]{:S(2)}) collective-permute-start(bf16[2,256,128]{1,2,0:T(8,128)(2,1)S(1)} %slice.61), channel_id=1, source_target_pairs={{0,4},{4,8},{8,12},{12,0},{1,5},{5,9},{9,13},{13,1},{2,6},{6,10},{... | collective-permute-start | bytes 393224 | tf_op jit(solution)/shard_map/ppermute | solution.py:10
  121.1 5.1 %collective-permute-start.10 = (bf16[2,256,128]{1,2,0:T(8,128)(2,1)S(1)}, bf16[2,256,128]{1,2,0:T(8,128)(2,1)S(1)}, u32[]{:S(2)}, u32[]{:S(2)}) collective-permute-start(bf16[2,256,128]{1,2,0:T(8,128)(2,1)S(1)} %slice.67), channel_id=1, source_target_pairs={{0,4},{4,8},{8,12},{12,0},{1,5},{5,9},{9,13},{13,1},{2,6},{6,10},{... | collective-permute-start | bytes 393224 | tf_op jit(solution)/shard_map/ppermute | solution.py:10
  129.1 5.1 %collective-permute-start.14 = (bf16[2,256,128]{1,2,0:T(8,128)(2,1)S(1)}, bf16[2,256,128]{1,2,0:T(8,128)(2,1)S(1)}, u32[]{:S(2)}, u32[]{:S(2)}) collective-permute-start(bf16[2,256,128]{1,2,0:T(8,128)(2,1)S(1)} %slice.70), channel_id=1, source_target_pairs={{0,4},{4,8},{8,12},{12,0},{1,5},{5,9},{9,13},{13,1},{2,6},{6,10},{... | collective-permute-start | bytes 393224 | tf_op jit(solution)/shard_map/ppermute | solution.py:10
  139.7 4.8 %collective-permute-done.15 = bf16[2,256,128]{1,2,0:T(8,128)(2,1)S(1)} collective-permute-done((bf16[2,256,128]{1,2,0:T(8,128)(2,1)S(1)}, bf16[2,256,128]{1,2,0:T(8,128)(2,1)S(1)}, u32[]{:S(2)}, u32[]{:S(2)}) %collective-permute-start.15) | collective-permute-done | bytes 131104 | tf_op jit(solution)/shard_map/ppermute | solution.py:10
  156.4 3.9 %collective-permute-start.19 = (bf16[512,512]{1,0:T(8,128)(2,1)S(1)}, bf16[512,512]{1,0:T(8,128)(2,1)S(1)}, u32[]{:S(2)}, u32[]{:S(2)}) collective-permute-start(bf16[512,512]{1,0:T(8,128)(2,1)S(1)} %convolution_convert_fusion.3), channel_id=1, source_target_pairs={{0,12},{4,0},{8,4},{12,8},{1,13},{5,1},{9,5},{13,9},{2,14},{6,2},{... | collective-permute-start | bytes 1572872 | tf_op jit(solution)/shard_map/ppermute | solution.py:10
  160.8 9.7 %collective-permute-done.16 = bf16[512,512]{1,0:T(8,128)(2,1)S(1)} collective-permute-done((bf16[512,512]{1,0:T(8,128)(2,1)S(1)}, bf16[512,512]{1,0:T(8,128)(2,1)S(1)}, u32[]{:S(2)}, u32[]{:S(2)}) %collective-permute-start.16) | collective-permute-done | bytes 524320 | tf_op jit(solution)/shard_map/ppermute | solution.py:10
  173.9 4.1 %collective-permute-start.20 = (bf16[512,512]{1,0:T(8,128)(2,1)S(1)}, bf16[512,512]{1,0:T(8,128)(2,1)S(1)}, u32[]{:S(2)}, u32[]{:S(2)}) collective-permute-start(bf16[512,512]{1,0:T(8,128)(2,1)S(1)} %add_convert_fusion.2), channel_id=1, source_target_pairs={{0,12},{4,0},{8,4},{12,8},{1,13},{5,1},{9,5},{13,9},{2,14},{6,2},{... | collective-permute-start | bytes 1572872 | tf_op jit(solution)/shard_map/ppermute | solution.py:10
  178.5 8.2 %collective-permute-done.17 = bf16[512,512]{1,0:T(8,128)(2,1)S(1)} collective-permute-done((bf16[512,512]{1,0:T(8,128)(2,1)S(1)}, bf16[512,512]{1,0:T(8,128)(2,1)S(1)}, u32[]{:S(2)}, u32[]{:S(2)}) %collective-permute-start.17) | collective-permute-done | bytes 524320 | tf_op jit(solution)/shard_map/ppermute | solution.py:10
  186.8 4.0 %collective-permute-start.18 = (bf16[512,512]{1,0:T(8,128)(2,1)S(1)}, bf16[512,512]{1,0:T(8,128)(2,1)S(1)}, u32[]{:S(2)}, u32[]{:S(2)}) collective-permute-start(bf16[512,512]{1,0:T(8,128)(2,1)S(1)} %add_convert_fusion.4), channel_id=1, source_target_pairs={{0,4},{4,8},{8,12},{12,0},{1,5},{5,9},{9,13},{13,1},{2,6},{6,10},{... | collective-permute-start | bytes 1572872 | tf_op jit(solution)/shard_map/ppermute | solution.py:10
  193.8 4.1 %collective-permute-done.18 = bf16[512,512]{1,0:T(8,128)(2,1)S(1)} collective-permute-done((bf16[512,512]{1,0:T(8,128)(2,1)S(1)}, bf16[512,512]{1,0:T(8,128)(2,1)S(1)}, u32[]{:S(2)}, u32[]{:S(2)}) %collective-permute-start.18) | collective-permute-done | bytes 524320 | tf_op jit(solution)/shard_map/ppermute | solution.py:10
  198.1 5.6 %collective-permute-done.21 = bf16[512,512]{1,0:T(8,128)(2,1)S(1)} collective-permute-done((bf16[512,512]{1,0:T(8,128)(2,1)S(1)}, bf16[512,512]{1,0:T(8,128)(2,1)S(1)}, u32[]{:S(2)}, u32[]{:S(2)}) %collective-permute-start.21) | collective-permute-done | bytes 524320 | tf_op jit(solution)/shard_map/ppermute | solution.py:10
  205.0 7.1 %all-to-all-start.5 = ((bf16[4,1024,128]{2,1,0:T(8,128)(2,1)}), bf16[4,1024,128]{2,1,0:T(8,128)(2,1)S(1)}, u32[]{:S(2)}, u32[]{:S(2)}) async-start(bf16[4,1024,128]{2,1,0:T(8,128)(2,1)} %bitcast_bitcast_fusion), calls=%async_computation.5 | async-start | bytes 2097152 | tf_op jit(solution)/shard_map/all_to_all | solution.py:122
  215.3 11.9 %all-to-all-done.5 = bf16[4,1024,128]{2,1,0:T(8,128)(2,1)S(1)} async-done(((bf16[4,1024,128]{2,1,0:T(8,128)(2,1)}), bf16[4,1024,128]{2,1,0:T(8,128)(2,1)S(1)}, u32[]{:S(2)}, u32[]{:S(2)}) %all-to-all-start.5) | async-done | bytes 1048608 | tf_op jit(solution)/shard_map/all_to_all | solution.py:122
  227.7 19.5 %all_to_all.36 = bf16[32,32,128]{2,1,0:T(8,128)(2,1)S(1)} all-to-all(bf16[32,32,128]{2,1,0:T(8,128)(2,1)S(1)} %fusion.37), channel_id=1, replica_groups=mesh['expert'=32,'mx'=4,'mz'=4] {'expert'}, dimensions={0} | all-to-all | bytes 524288 | tf_op jit(solution)/shard_map/all_to_all | solution.py:128
  (102 shorter events, 67.7 us)
Async XLA Ops:
  27.6 19.1 %all-to-all-start.2 = ((bf16[4,256,128]{1,2,0:T(8,128)(2,1)}), bf16[4,256,128]{1,2,0:T(8,128)(2,1)S(1)}, u32[]{:S(2)}, u32[]{:S(2)}) async-start(bf16[4,256,128]{1,2,0:T(8,128)(2,1)} %broadcast_in_dim.72), calls=%async_computation.2 | async-start | bytes 524288 | tf_op jit(solution)/shard_map/all_to_all | solution.py:89
  47.4 12.7 %all-to-all-start.1 = ((bf16[4,256,128]{1,2,0:T(8,128)(2,1)}), bf16[4,256,128]{1,2,0:T(8,128)(2,1)S(1)}, u32[]{:S(2)}, u32[]{:S(2)}) async-start(bf16[4,256,128]{1,2,0:T(8,128)(2,1)} %broadcast_in_dim.70), calls=%async_computation.1 | async-start | bytes 524288 | tf_op jit(solution)/shard_map/all_to_all | solution.py:89
  60.9 12.7 %all-to-all-start.3 = ((bf16[4,256,128]{1,2,0:T(8,128)(2,1)}), bf16[4,256,128]{1,2,0:T(8,128)(2,1)S(1)}, u32[]{:S(2)}, u32[]{:S(2)}) async-start(bf16[4,256,128]{1,2,0:T(8,128)(2,1)} %broadcast_in_dim.74), calls=%async_computation.3 | async-start | bytes 524288 | tf_op jit(solution)/shard_map/all_to_all | solution.py:89
  74.3 21.9 %all-to-all-start.4 = ((bf16[4,256,128]{1,2,0:T(8,128)(2,1)}), bf16[4,256,128]{1,2,0:T(8,128)(2,1)S(1)}, u32[]{:S(2)}, u32[]{:S(2)}) async-start(bf16[4,256,128]{1,2,0:T(8,128)(2,1)} %broadcast_in_dim.76), calls=%async_computation.4 | async-start | bytes 524288 | tf_op jit(solution)/shard_map/all_to_all | solution.py:89
  77.7 16.5 %collective-permute-start.5 = (bf16[4,256,128]{1,2,0:T(8,128)(2,1)S(1)}, bf16[4,256,128]{1,2,0:T(8,128)(2,1)S(1)}, u32[]{:S(2)}, u32[]{:S(2)}) collective-permute-start(bf16[4,256,128]{1,2,0:T(8,128)(2,1)S(1)} %all-to-all-done.2), channel_id=1, source_target_pairs={{0,4},{4,8},{8,12},{12,0},{1,5},{5,9},{9,13},{13,1},{2,6},{6,10},{... | collective-permute-start | bytes 786440 | tf_op jit(solution)/shard_map/ppermute | solution.py:10
  80.1 16.1 %collective-permute-start.4 = (bf16[4,256,128]{1,2,0:T(8,128)(2,1)S(1)}, bf16[4,256,128]{1,2,0:T(8,128)(2,1)}, u32[]{:S(2)}, u32[]{:S(2)}) collective-permute-start(bf16[4,256,128]{1,2,0:T(8,128)(2,1)S(1)} %all-to-all-done.2), channel_id=1, source_target_pairs={{0,12},{4,0},{8,4},{12,8},{1,13},{5,1},{9,5},{13,9},{2,14},{6,2},{... | collective-permute-start | bytes 786440 | tf_op jit(solution)/shard_map/ppermute | solution.py:10
  83.6 17.8 %collective-permute-start.1 = (bf16[4,256,128]{1,2,0:T(8,128)(2,1)S(1)}, bf16[4,256,128]{1,2,0:T(8,128)(2,1)S(1)}, u32[]{:S(2)}, u32[]{:S(2)}) collective-permute-start(bf16[4,256,128]{1,2,0:T(8,128)(2,1)S(1)} %all-to-all-done.1), channel_id=1, source_target_pairs={{0,4},{4,8},{8,12},{12,0},{1,5},{5,9},{9,13},{13,1},{2,6},{6,10},{... | collective-permute-start | bytes 786440 | tf_op jit(solution)/shard_map/ppermute | solution.py:10
  87.2 18.6 %collective-permute-start = (bf16[4,256,128]{1,2,0:T(8,128)(2,1)S(1)}, bf16[4,256,128]{1,2,0:T(8,128)(2,1)}, u32[]{:S(2)}, u32[]{:S(2)}) collective-permute-start(bf16[4,256,128]{1,2,0:T(8,128)(2,1)S(1)} %all-to-all-done.1), channel_id=1, source_target_pairs={{0,12},{4,0},{8,4},{12,8},{1,13},{5,1},{9,5},{13,9},{2,14},{6,2},{... | collective-permute-start | bytes 786440 | tf_op jit(solution)/shard_map/ppermute | solution.py:10
  89.5 21.5 %collective-permute-start.9 = (bf16[4,256,128]{1,2,0:T(8,128)(2,1)S(1)}, bf16[4,256,128]{1,2,0:T(8,128)(2,1)S(1)}, u32[]{:S(2)}, u32[]{:S(2)}) collective-permute-start(bf16[4,256,128]{1,2,0:T(8,128)(2,1)S(1)} %all-to-all-done.3), channel_id=1, source_target_pairs={{0,4},{4,8},{8,12},{12,0},{1,5},{5,9},{9,13},{13,1},{2,6},{6,10},{... | collective-permute-start | bytes 786440 | tf_op jit(solution)/shard_map/ppermute | solution.py:10
  94.3 19.7 %collective-permute-start.8 = (bf16[4,256,128]{1,2,0:T(8,128)(2,1)S(1)}, bf16[4,256,128]{1,2,0:T(8,128)(2,1)S(1)}, u32[]{:S(2)}, u32[]{:S(2)}) collective-permute-start(bf16[4,256,128]{1,2,0:T(8,128)(2,1)S(1)} %all-to-all-done.3), channel_id=1, source_target_pairs={{0,12},{4,0},{8,4},{12,8},{1,13},{5,1},{9,5},{13,9},{2,14},{6,2},{... | collective-permute-start | bytes 786440 | tf_op jit(solution)/shard_map/ppermute | solution.py:10
  96.3 22.9 %collective-permute-start.13 = (bf16[4,256,128]{1,2,0:T(8,128)(2,1)S(1)}, bf16[4,256,128]{1,2,0:T(8,128)(2,1)S(1)}, u32[]{:S(2)}, u32[]{:S(2)}) collective-permute-start(bf16[4,256,128]{1,2,0:T(8,128)(2,1)S(1)} %all-to-all-done.4), channel_id=1, source_target_pairs={{0,4},{4,8},{8,12},{12,0},{1,5},{5,9},{9,13},{13,1},{2,6},{6,10},{... | collective-permute-start | bytes 786440 | tf_op jit(solution)/shard_map/ppermute | solution.py:10
  101.4 19.7 %collective-permute-start.12 = (bf16[4,256,128]{1,2,0:T(8,128)(2,1)S(1)}, bf16[4,256,128]{1,2,0:T(8,128)(2,1)}, u32[]{:S(2)}, u32[]{:S(2)}) collective-permute-start(bf16[4,256,128]{1,2,0:T(8,128)(2,1)S(1)} %all-to-all-done.4), channel_id=1, source_target_pairs={{0,12},{4,0},{8,4},{12,8},{1,13},{5,1},{9,5},{13,9},{2,14},{6,2},{... | collective-permute-start | bytes 786440 | tf_op jit(solution)/shard_map/ppermute | solution.py:10
  105.8 21.4 %collective-permute-start.6 = (bf16[2,256,128]{1,2,0:T(8,128)(2,1)}, bf16[2,256,128]{1,2,0:T(8,128)(2,1)}, u32[]{:S(2)}, u32[]{:S(2)}) collective-permute-start(bf16[2,256,128]{1,2,0:T(8,128)(2,1)} %slice.64), channel_id=1, source_target_pairs={{0,4},{4,8},{8,12},{12,0},{1,5},{5,9},{9,13},{13,1},{2,6},{6,10},{... | collective-permute-start | bytes 393224 | tf_op jit(solution)/shard_map/ppermute | solution.py:10
  111.0 18.2 %collective-permute-start.7 = (bf16[2,256,128]{1,2,0:T(8,128)(2,1)S(1)}, bf16[2,256,128]{1,2,0:T(8,128)(2,1)}, u32[]{:S(2)}, u32[]{:S(2)}) collective-permute-start(bf16[2,256,128]{1,2,0:T(8,128)(2,1)S(1)} %slice.65), channel_id=1, source_target_pairs={{0,12},{4,0},{8,4},{12,8},{1,13},{5,1},{9,5},{13,9},{2,14},{6,2},{... | collective-permute-start | bytes 393224 | tf_op jit(solution)/shard_map/ppermute | solution.py:10
  114.0 22.4 %collective-permute-start.2 = (bf16[2,256,128]{1,2,0:T(8,128)(2,1)S(1)}, bf16[2,256,128]{1,2,0:T(8,128)(2,1)S(1)}, u32[]{:S(2)}, u32[]{:S(2)}) collective-permute-start(bf16[2,256,128]{1,2,0:T(8,128)(2,1)S(1)} %slice.61), channel_id=1, source_target_pairs={{0,4},{4,8},{8,12},{12,0},{1,5},{5,9},{9,13},{13,1},{2,6},{6,10},{... | collective-permute-start | bytes 393224 | tf_op jit(solution)/shard_map/ppermute | solution.py:10
  119.2 19.2 %collective-permute-start.3 = (bf16[2,256,128]{1,2,0:T(8,128)(2,1)S(1)}, bf16[2,256,128]{1,2,0:T(8,128)(2,1)S(1)}, u32[]{:S(2)}, u32[]{:S(2)}) collective-permute-start(bf16[2,256,128]{1,2,0:T(8,128)(2,1)S(1)} %slice.62), channel_id=1, source_target_pairs={{0,12},{4,0},{8,4},{12,8},{1,13},{5,1},{9,5},{13,9},{2,14},{6,2},{... | collective-permute-start | bytes 393224 | tf_op jit(solution)/shard_map/ppermute | solution.py:10
  121.1 18.4 %collective-permute-start.10 = (bf16[2,256,128]{1,2,0:T(8,128)(2,1)S(1)}, bf16[2,256,128]{1,2,0:T(8,128)(2,1)S(1)}, u32[]{:S(2)}, u32[]{:S(2)}) collective-permute-start(bf16[2,256,128]{1,2,0:T(8,128)(2,1)S(1)} %slice.67), channel_id=1, source_target_pairs={{0,4},{4,8},{8,12},{12,0},{1,5},{5,9},{9,13},{13,1},{2,6},{6,10},{... | collective-permute-start | bytes 393224 | tf_op jit(solution)/shard_map/ppermute | solution.py:10
  127.2 12.3 %collective-permute-start.11 = (bf16[2,256,128]{1,2,0:T(8,128)(2,1)S(1)}, bf16[2,256,128]{1,2,0:T(8,128)(2,1)S(1)}, u32[]{:S(2)}, u32[]{:S(2)}) collective-permute-start(bf16[2,256,128]{1,2,0:T(8,128)(2,1)S(1)} %slice.68), channel_id=1, source_target_pairs={{0,12},{4,0},{8,4},{12,8},{1,13},{5,1},{9,5},{13,9},{2,14},{6,2},{... | collective-permute-start | bytes 393224 | tf_op jit(solution)/shard_map/ppermute | solution.py:10
  154.0 16.6 %collective-permute-start.16 = (bf16[512,512]{1,0:T(8,128)(2,1)S(1)}, bf16[512,512]{1,0:T(8,128)(2,1)S(1)}, u32[]{:S(2)}, u32[]{:S(2)}) collective-permute-start(bf16[512,512]{1,0:T(8,128)(2,1)S(1)} %convolution_convert_fusion.7), channel_id=1, source_target_pairs={{0,4},{4,8},{8,12},{12,0},{1,5},{5,9},{9,13},{13,1},{2,6},{6,10},{... | collective-permute-start | bytes 1572872 | tf_op jit(solution)/shard_map/ppermute | solution.py:10
  156.4 17.0 %collective-permute-start.19 = (bf16[512,512]{1,0:T(8,128)(2,1)S(1)}, bf16[512,512]{1,0:T(8,128)(2,1)S(1)}, u32[]{:S(2)}, u32[]{:S(2)}) collective-permute-start(bf16[512,512]{1,0:T(8,128)(2,1)S(1)} %convolution_convert_fusion.3), channel_id=1, source_target_pairs={{0,12},{4,0},{8,4},{12,8},{1,13},{5,1},{9,5},{13,9},{2,14},{6,2},{... | collective-permute-start | bytes 1572872 | tf_op jit(solution)/shard_map/ppermute | solution.py:10
  171.0 15.6 %collective-permute-start.17 = (bf16[512,512]{1,0:T(8,128)(2,1)S(1)}, bf16[512,512]{1,0:T(8,128)(2,1)S(1)}, u32[]{:S(2)}, u32[]{:S(2)}) collective-permute-start(bf16[512,512]{1,0:T(8,128)(2,1)S(1)} %add_convert_fusion.5), channel_id=1, source_target_pairs={{0,4},{4,8},{8,12},{12,0},{1,5},{5,9},{9,13},{13,1},{2,6},{6,10},{... | collective-permute-start | bytes 1572872 | tf_op jit(solution)/shard_map/ppermute | solution.py:10
  173.9 17.3 %collective-permute-start.20 = (bf16[512,512]{1,0:T(8,128)(2,1)S(1)}, bf16[512,512]{1,0:T(8,128)(2,1)S(1)}, u32[]{:S(2)}, u32[]{:S(2)}) collective-permute-start(bf16[512,512]{1,0:T(8,128)(2,1)S(1)} %add_convert_fusion.2), channel_id=1, source_target_pairs={{0,12},{4,0},{8,4},{12,8},{1,13},{5,1},{9,5},{13,9},{2,14},{6,2},{... | collective-permute-start | bytes 1572872 | tf_op jit(solution)/shard_map/ppermute | solution.py:10
  191.4 12.3 %collective-permute-start.21 = (bf16[512,512]{1,0:T(8,128)(2,1)S(1)}, bf16[512,512]{1,0:T(8,128)(2,1)S(1)}, u32[]{:S(2)}, u32[]{:S(2)}) collective-permute-start(bf16[512,512]{1,0:T(8,128)(2,1)S(1)} %add_convert_fusion.1), channel_id=1, source_target_pairs={{0,12},{4,0},{8,4},{12,8},{1,13},{5,1},{9,5},{13,9},{2,14},{6,2},{... | collective-permute-start | bytes 1572872 | tf_op jit(solution)/shard_map/ppermute | solution.py:10
  205.0 22.2 %all-to-all-start.5 = ((bf16[4,1024,128]{2,1,0:T(8,128)(2,1)}), bf16[4,1024,128]{2,1,0:T(8,128)(2,1)S(1)}, u32[]{:S(2)}, u32[]{:S(2)}) async-start(bf16[4,1024,128]{2,1,0:T(8,128)(2,1)} %bitcast_bitcast_fusion), calls=%async_computation.5 | async-start | bytes 2097152 | tf_op jit(solution)/shard_map/all_to_all | solution.py:122
  (10 other events, 285.4 us)

commit v14 on v11

--- a/solution.py
+++ b/solution.py
@@ -114,13 +114,14 @@
             jnp.bfloat16
         )
 
-    across_x = [part.astype(jnp.bfloat16) for part in ring_reduce_scatter(x_term, "mx", n_x)]
-
-    across_x = jnp.concatenate(across_x, axis=0).reshape(cells, n_z, shard_width)
-    z_terms = lax.all_to_all(
-        jnp.transpose(across_x, (1, 0, 2)), "mz", split_axis=0, concat_axis=0, tiled=True
-    )
-    summed = jnp.sum(z_terms.astype(jnp.float32), axis=0).astype(jnp.bfloat16)
+    summed = []
+    for part in ring_reduce_scatter(x_term, "mx", n_x):
+        part = part.astype(jnp.bfloat16).reshape(rows_half, n_z, shard_width)
+        z_terms = lax.all_to_all(
+            jnp.transpose(part, (1, 0, 2)), "mz", split_axis=0, concat_axis=0, tiled=True
+        )
+        summed.append(jnp.sum(z_terms.astype(jnp.float32), axis=0).astype(jnp.bfloat16))
+    summed = jnp.concatenate(summed, axis=0)
     gated = (gate_prob[:, None] * summed.astype(jnp.float32)).astype(jnp.bfloat16)
 
     returned = lax.all_to_all(

time: 202 us -> 212 us (1.050)
  blocking collectives: 45.7 us -> 50.9 us
  starting transfers between devices: 58.7 us -> 62.5 us
    all_to_all x1, blocking collectives: 23.4 us -> 28.6 us  [shards(): lax.all_to_all(gated.reshape(experts, slot_count, shard_width), 'expert',...]
    ppermute x14, waiting for transfers between devices: 27.3 us -> 23.1 us  [shift(): return lax.ppermute(value, axis, [(i, (i + step) % n) for i in range(n)])]
    all_to_all x1 -> x2, starting transfers between devices: 4.07 us -> 7.43 us  [shards(): lax.all_to_all(jnp.transpose(part, (1, 0, 2)), 'mz', split_axis=0, concat...]
    all_to_all x1 -> x2, waiting for transfers between devices: 13.8 us -> 17.1 us  [shards(): lax.all_to_all(jnp.transpose(part, (1, 0, 2)), 'mz', split_axis=0, concat...]
  transfers between devices with their start and end apart: 17 -> 18, of which waited for: 10 -> 10; matrix products, arithmetic and copies ran while one was open for 6% -> 7% of each run, Pallas kernels for 0% -> 0%
where the time goes in v14:
time: 212 us; the launch traced here: 209 us
  waiting for transfers between devices  62.8 us (30%)
  starting transfers between devices  62.5 us (29%)
  blocking collectives  50.9 us (24%)
  matrix products  13.9 us (7%)
  other arithmetic  12.2 us (6%)
  local copies, waits for them, and re-layouts  6.09 us (3%)
    ppermute x14, starting transfers between devices, shift(): return lax.ppermute(value, axis, [(i, (i + step) % n) for i in range(n)])  41.3 us
    all_to_all x1, blocking collectives, shards(): lax.all_to_all(gated.reshape(experts, slot_count, shard_width), 'expert',...  28.6 us
    ppermute x14, waiting for transfers between devices, shift(): return lax.ppermute(value, axis, [(i, (i + step) % n) for i in range(n)])  23.1 us
    all_to_all x2, waiting for transfers between devices, shards(): part = lax.all_to_all(copies, 'mz', split_axis=0, concat_axis=0, tiled=True)  22.6 us
    all_to_all x1, blocking collectives, shards(): lax.all_to_all(masked.reshape(experts, slot_count, shard_width), 'expert'...  22.3 us
    all_to_all x2, waiting for transfers between devices, shards(): lax.all_to_all(jnp.transpose(part, (1, 0, 2)), 'mz', split_axis=0, concat...  17.1 us
    all_to_all x2, starting transfers between devices, shards(): part = lax.all_to_all(copies, 'mz', split_axis=0, concat_axis=0, tiled=True)  13.8 us
    all_to_all x2, starting transfers between devices, shards(): lax.all_to_all(jnp.transpose(part, (1, 0, 2)), 'mz', split_axis=0, concat...  7.43 us
  transfers between devices with their start and end apart: 18, of which 10 were waited for; matrix products, arithmetic and copies ran while one was open for 7% of the time, Pallas kernels for 0%

profile of v14, /device:TPU:6, one launch (start us, length us, event | category | flops | bytes accessed | tf_op | source)
XLA Modules:
  0.0 208.9 jit_solution(11592052523128256099)
XLA Ops:
  4.5 22.3 %all_to_all.30 = bf16[32,32,128]{2,1,0:T(8,128)(2,1)S(1)} all-to-all(bf16[32,32,128]{2,1,0:T(8,128)(2,1)S(1)} %bitcast.83), channel_id=1, replica_groups=mesh['expert'=32,'mx'=4,'mz'=4] {'expert'}, dimensions={0} | all-to-all | bytes 524288 | tf_op jit(solution)/shard_map/all_to_all | solution.py:69
  27.7 9.5 %all-to-all-start.1 = ((bf16[4,512,128]{1,2,0:T(8,128)(2,1)}), bf16[4,512,128]{1,2,0:T(8,128)(2,1)S(1)}, u32[]{:S(2)}, u32[]{:S(2)}) async-start(bf16[4,512,128]{1,2,0:T(8,128)(2,1)} %broadcast_in_dim.54), calls=%async_computation.1 | async-start | bytes 1048576 | tf_op jit(solution)/shard_map/all_to_all | solution.py:87
  37.4 14.0 %all-to-all-done.1 = bf16[4,512,128]{1,2,0:T(8,128)(2,1)S(1)} async-done(((bf16[4,512,128]{1,2,0:T(8,128)(2,1)}), bf16[4,512,128]{1,2,0:T(8,128)(2,1)S(1)}, u32[]{:S(2)}, u32[]{:S(2)}) %all-to-all-start.1) | async-done | bytes 524320 | tf_op jit(solution)/shard_map/all_to_all | solution.py:87
  52.2 4.2 %all-to-all-start.2 = ((bf16[4,512,128]{1,2,0:T(8,128)(2,1)}), bf16[4,512,128]{1,2,0:T(8,128)(2,1)S(1)}, u32[]{:S(2)}, u32[]{:S(2)}) async-start(bf16[4,512,128]{1,2,0:T(8,128)(2,1)} %broadcast_in_dim.56), calls=%async_computation.2 | async-start | bytes 1048576 | tf_op jit(solution)/shard_map/all_to_all | solution.py:87
  58.8 3.5 %collective-permute-start = (bf16[4,512,128]{1,2,0:T(8,128)(2,1)S(1)}, bf16[4,512,128]{1,2,0:T(8,128)(2,1)}, u32[]{:S(2)}, u32[]{:S(2)}) collective-permute-start(bf16[4,512,128]{1,2,0:T(8,128)(2,1)S(1)} %all-to-all-done.1), channel_id=1, source_target_pairs={{0,12},{4,0},{8,4},{12,8},{1,13},{5,1},{9,5},{13,9},{2,14},{6,2},{... | collective-permute-start | bytes 1572872 | tf_op jit(solution)/shard_map/ppermute | solution.py:10
  62.3 8.6 %all-to-all-done.2 = bf16[4,512,128]{1,2,0:T(8,128)(2,1)S(1)} async-done(((bf16[4,512,128]{1,2,0:T(8,128)(2,1)}), bf16[4,512,128]{1,2,0:T(8,128)(2,1)S(1)}, u32[]{:S(2)}, u32[]{:S(2)}) %all-to-all-start.2) | async-done | bytes 524320 | tf_op jit(solution)/shard_map/all_to_all | solution.py:87
  70.9 2.4 %collective-permute-start.5 = (bf16[4,512,128]{1,2,0:T(8,128)(2,1)S(1)}, bf16[4,512,128]{1,2,0:T(8,128)(2,1)S(1)}, u32[]{:S(2)}, u32[]{:S(2)}) collective-permute-start(bf16[4,512,128]{1,2,0:T(8,128)(2,1)S(1)} %all-to-all-done.2), channel_id=1, source_target_pairs={{0,4},{4,8},{8,12},{12,0},{1,5},{5,9},{9,13},{13,1},{2,6},{6,10},{... | collective-permute-start | bytes 1572872 | tf_op jit(solution)/shard_map/ppermute | solution.py:10
  73.3 3.5 %collective-permute-start.4 = (bf16[4,512,128]{1,2,0:T(8,128)(2,1)S(1)}, bf16[4,512,128]{1,2,0:T(8,128)(2,1)}, u32[]{:S(2)}, u32[]{:S(2)}) collective-permute-start(bf16[4,512,128]{1,2,0:T(8,128)(2,1)S(1)} %all-to-all-done.2), channel_id=1, source_target_pairs={{0,12},{4,0},{8,4},{12,8},{1,13},{5,1},{9,5},{13,9},{2,14},{6,2},{... | collective-permute-start | bytes 1572872 | tf_op jit(solution)/shard_map/ppermute | solution.py:10
  77.5 3.6 %collective-permute-start.2 = (bf16[2,512,128]{1,2,0:T(8,128)(2,1)}, bf16[2,512,128]{1,2,0:T(8,128)(2,1)}, u32[]{:S(2)}, u32[]{:S(2)}) collective-permute-start(bf16[2,512,128]{1,2,0:T(8,128)(2,1)} %slice.35), channel_id=1, source_target_pairs={{0,4},{4,8},{8,12},{12,0},{1,5},{5,9},{9,13},{13,1},{2,6},{6,10},{... | collective-permute-start | bytes 786440 | tf_op jit(solution)/shard_map/ppermute | solution.py:10
  86.6 3.4 %collective-permute-start.6 = (bf16[2,512,128]{1,2,0:T(8,128)(2,1)S(1)}, bf16[2,512,128]{1,2,0:T(8,128)(2,1)S(1)}, u32[]{:S(2)}, u32[]{:S(2)}) collective-permute-start(bf16[2,512,128]{1,2,0:T(8,128)(2,1)S(1)} %slice.38), channel_id=1, source_target_pairs={{0,4},{4,8},{8,12},{12,0},{1,5},{5,9},{9,13},{13,1},{2,6},{6,10},{... | collective-permute-start | bytes 786440 | tf_op jit(solution)/shard_map/ppermute | solution.py:10
  91.0 2.5 %collective-permute-start.7 = (bf16[2,512,128]{1,2,0:T(8,128)(2,1)S(1)}, bf16[2,512,128]{1,2,0:T(8,128)(2,1)S(1)}, u32[]{:S(2)}, u32[]{:S(2)}) collective-permute-start(bf16[2,512,128]{1,2,0:T(8,128)(2,1)S(1)} %slice.39), channel_id=1, source_target_pairs={{0,12},{4,0},{8,4},{12,8},{1,13},{5,1},{9,5},{13,9},{2,14},{6,2},{... | collective-permute-start | bytes 786440 | tf_op jit(solution)/shard_map/ppermute | solution.py:10
  95.9 4.6 %collective-permute-done.7 = bf16[2,512,128]{1,2,0:T(8,128)(2,1)S(1)} collective-permute-done((bf16[2,512,128]{1,2,0:T(8,128)(2,1)S(1)}, bf16[2,512,128]{1,2,0:T(8,128)(2,1)S(1)}, u32[]{:S(2)}, u32[]{:S(2)}) %collective-permute-start.7) | collective-permute-done | bytes 262176 | tf_op jit(solution)/shard_map/ppermute | solution.py:10
  112.6 3.9 %collective-permute-start.11 = (bf16[512,512]{1,0:T(8,128)(2,1)S(1)}, bf16[512,512]{1,0:T(8,128)(2,1)S(1)}, u32[]{:S(2)}, u32[]{:S(2)}) collective-permute-start(bf16[512,512]{1,0:T(8,128)(2,1)S(1)} %convolution_convert_fusion.3), channel_id=1, source_target_pairs={{0,12},{4,0},{8,4},{12,8},{1,13},{5,1},{9,5},{13,9},{2,14},{6,2},{... | collective-permute-start | bytes 1572872 | tf_op jit(solution)/shard_map/ppermute | solution.py:10
  116.5 6.2 %collective-permute-done.8 = bf16[512,512]{1,0:T(8,128)(2,1)S(1)} collective-permute-done((bf16[512,512]{1,0:T(8,128)(2,1)S(1)}, bf16[512,512]{1,0:T(8,128)(2,1)S(1)}, u32[]{:S(2)}, u32[]{:S(2)}) %collective-permute-start.8) | collective-permute-done | bytes 524320 | tf_op jit(solution)/shard_map/ppermute | solution.py:10
  126.6 3.9 %collective-permute-start.12 = (bf16[512,512]{1,0:T(8,128)(2,1)S(1)}, bf16[512,512]{1,0:T(8,128)(2,1)S(1)}, u32[]{:S(2)}, u32[]{:S(2)}) collective-permute-start(bf16[512,512]{1,0:T(8,128)(2,1)S(1)} %add_convert_fusion.2), channel_id=1, source_target_pairs={{0,12},{4,0},{8,4},{12,8},{1,13},{5,1},{9,5},{13,9},{2,14},{6,2},{... | collective-permute-start | bytes 1572872 | tf_op jit(solution)/shard_map/ppermute | solution.py:10
  130.5 6.7 %collective-permute-done.9 = bf16[512,512]{1,0:T(8,128)(2,1)S(1)} collective-permute-done((bf16[512,512]{1,0:T(8,128)(2,1)S(1)}, bf16[512,512]{1,0:T(8,128)(2,1)S(1)}, u32[]{:S(2)}, u32[]{:S(2)}) %collective-permute-start.9) | collective-permute-done | bytes 524320 | tf_op jit(solution)/shard_map/ppermute | solution.py:10
  141.1 4.3 %collective-permute-start.13 = (bf16[512,512]{1,0:T(8,128)(2,1)S(1)}, bf16[512,512]{1,0:T(8,128)(2,1)S(1)}, u32[]{:S(2)}, u32[]{:S(2)}) collective-permute-start(bf16[512,512]{1,0:T(8,128)(2,1)S(1)} %add_convert_fusion.1), channel_id=1, source_target_pairs={{0,12},{4,0},{8,4},{12,8},{1,13},{5,1},{9,5},{13,9},{2,14},{6,2},{... | collective-permute-start | bytes 1572872 | tf_op jit(solution)/shard_map/ppermute | solution.py:10
  145.4 3.0 %collective-permute-done.10 = bf16[512,512]{1,0:T(8,128)(2,1)S(1)} collective-permute-done((bf16[512,512]{1,0:T(8,128)(2,1)S(1)}, bf16[512,512]{1,0:T(8,128)(2,1)S(1)}, u32[]{:S(2)}, u32[]{:S(2)}) %collective-permute-start.10) | collective-permute-done | bytes 524320 | tf_op jit(solution)/shard_map/ppermute | solution.py:10
  149.3 4.0 %all-to-all-start.3 = ((bf16[4,512,128]{2,1,0:T(8,128)(2,1)}), bf16[4,512,128]{2,1,0:T(8,128)(2,1)S(1)}, u32[]{:S(2)}, u32[]{:S(2)}) async-start(bf16[4,512,128]{2,1,0:T(8,128)(2,1)} %bitcast_bitcast_fusion.1), calls=%async_computation.3 | async-start | bytes 1048576 | tf_op jit(solution)/shard_map/all_to_all | solution.py:120
  154.7 9.1 %all-to-all-done.3 = bf16[4,512,128]{2,1,0:T(8,128)(2,1)S(1)} async-done(((bf16[4,512,128]{2,1,0:T(8,128)(2,1)}), bf16[4,512,128]{2,1,0:T(8,128)(2,1)S(1)}, u32[]{:S(2)}, u32[]{:S(2)}) %all-to-all-start.3) | async-done | bytes 524320 | tf_op jit(solution)/shard_map/all_to_all | solution.py:120
  163.8 3.5 %all-to-all-start.4 = ((bf16[4,512,128]{2,1,0:T(8,128)(2,1)}), bf16[4,512,128]{2,1,0:T(8,128)(2,1)S(1)}, u32[]{:S(2)}, u32[]{:S(2)}) async-start(bf16[4,512,128]{2,1,0:T(8,128)(2,1)} %bitcast_bitcast_fusion), calls=%async_computation.4 | async-start | bytes 1048576 | tf_op jit(solution)/shard_map/all_to_all | solution.py:120
  167.3 3.0 %fusion.36 = f32[1024]{0:T(1024)S(1)} fusion(bf16[1024,2048]{0,1:T(8,128)(2,1)} %copy-done.1, s32[]{:T(128)S(6)} %select_n.78, bf16[2048,32]{0,1:T(8,128)(2,1)S(1)} %copy-done.2, pred[32]{0:T(512)(128)(4,1)S(1)} %iota_compare_fusion.2), kind=kOutput, calls=%fused_computation.49 | convolution fusion | flops 134544384 | bytes 4329508 | tf_op jit(solution)/shard_map/dot_general | solution.py:96
  170.5 8.0 %all-to-all-done.4 = bf16[4,512,128]{2,1,0:T(8,128)(2,1)S(1)} async-done(((bf16[4,512,128]{2,1,0:T(8,128)(2,1)}), bf16[4,512,128]{2,1,0:T(8,128)(2,1)S(1)}, u32[]{:S(2)}, u32[]{:S(2)}) %all-to-all-start.4) | async-done | bytes 524320 | tf_op jit(solution)/shard_map/all_to_all | solution.py:120
  178.8 28.6 %all_to_all.31 = bf16[32,32,128]{2,1,0:T(8,128)(2,1)S(1)} all-to-all(bf16[32,32,128]{2,1,0:T(8,128)(2,1)S(1)} %fusion.39), channel_id=1, replica_groups=mesh['expert'=32,'mx'=4,'mz'=4] {'expert'}, dimensions={0} | all-to-all | bytes 524288 | tf_op jit(solution)/shard_map/all_to_all | solution.py:127
  (71 shorter events, 42.1 us)
Async XLA Ops:
  0.0 109.7 %copy-start = (bf16[1,320,2048]{2,1,0:T(8,128)(2,1)S(1)}, bf16[1,320,2048]{2,1,0:T(8,128)(2,1)}, u32[]{:S(2)}) copy-start(bf16[1,320,2048]{2,1,0:T(8,128)(2,1)} %param.16) | copy-start | bytes 3932164
  27.7 57.4 %copy-start.3 = (f32[2048]{0:T(1024)S(1)}, f32[2048]{0:T(1024)}, u32[]{:S(2)}) copy-start(f32[2048]{0:T(1024)} %param.12) | copy-start | bytes 24580
  27.7 23.7 %all-to-all-start.1 = ((bf16[4,512,128]{1,2,0:T(8,128)(2,1)}), bf16[4,512,128]{1,2,0:T(8,128)(2,1)S(1)}, u32[]{:S(2)}, u32[]{:S(2)}) async-start(bf16[4,512,128]{1,2,0:T(8,128)(2,1)} %broadcast_in_dim.54), calls=%async_computation.1 | async-start | bytes 1048576 | tf_op jit(solution)/shard_map/all_to_all | solution.py:87
  52.2 18.7 %all-to-all-start.2 = ((bf16[4,512,128]{1,2,0:T(8,128)(2,1)}), bf16[4,512,128]{1,2,0:T(8,128)(2,1)S(1)}, u32[]{:S(2)}, u32[]{:S(2)}) async-start(bf16[4,512,128]{1,2,0:T(8,128)(2,1)} %broadcast_in_dim.56), calls=%async_computation.2 | async-start | bytes 1048576 | tf_op jit(solution)/shard_map/all_to_all | solution.py:87
  56.5 20.3 %collective-permute-start.1 = (bf16[4,512,128]{1,2,0:T(8,128)(2,1)S(1)}, bf16[4,512,128]{1,2,0:T(8,128)(2,1)S(1)}, u32[]{:S(2)}, u32[]{:S(2)}) collective-permute-start(bf16[4,512,128]{1,2,0:T(8,128)(2,1)S(1)} %all-to-all-done.1), channel_id=1, source_target_pairs={{0,4},{4,8},{8,12},{12,0},{1,5},{5,9},{9,13},{13,1},{2,6},{6,10},{... | collective-permute-start | bytes 1572872 | tf_op jit(solution)/shard_map/ppermute | solution.py:10
  58.8 22.3 %collective-permute-start = (bf16[4,512,128]{1,2,0:T(8,128)(2,1)S(1)}, bf16[4,512,128]{1,2,0:T(8,128)(2,1)}, u32[]{:S(2)}, u32[]{:S(2)}) collective-permute-start(bf16[4,512,128]{1,2,0:T(8,128)(2,1)S(1)} %all-to-all-done.1), channel_id=1, source_target_pairs={{0,12},{4,0},{8,4},{12,8},{1,13},{5,1},{9,5},{13,9},{2,14},{6,2},{... | collective-permute-start | bytes 1572872 | tf_op jit(solution)/shard_map/ppermute | solution.py:10
  70.9 15.7 %collective-permute-start.5 = (bf16[4,512,128]{1,2,0:T(8,128)(2,1)S(1)}, bf16[4,512,128]{1,2,0:T(8,128)(2,1)S(1)}, u32[]{:S(2)}, u32[]{:S(2)}) collective-permute-start(bf16[4,512,128]{1,2,0:T(8,128)(2,1)S(1)} %all-to-all-done.2), channel_id=1, source_target_pairs={{0,4},{4,8},{8,12},{12,0},{1,5},{5,9},{9,13},{13,1},{2,6},{6,10},{... | collective-permute-start | bytes 1572872 | tf_op jit(solution)/shard_map/ppermute | solution.py:10
  73.3 16.7 %collective-permute-start.4 = (bf16[4,512,128]{1,2,0:T(8,128)(2,1)S(1)}, bf16[4,512,128]{1,2,0:T(8,128)(2,1)}, u32[]{:S(2)}, u32[]{:S(2)}) collective-permute-start(bf16[4,512,128]{1,2,0:T(8,128)(2,1)S(1)} %all-to-all-done.2), channel_id=1, source_target_pairs={{0,12},{4,0},{8,4},{12,8},{1,13},{5,1},{9,5},{13,9},{2,14},{6,2},{... | collective-permute-start | bytes 1572872 | tf_op jit(solution)/shard_map/ppermute | solution.py:10
  77.5 16.0 %collective-permute-start.2 = (bf16[2,512,128]{1,2,0:T(8,128)(2,1)}, bf16[2,512,128]{1,2,0:T(8,128)(2,1)}, u32[]{:S(2)}, u32[]{:S(2)}) collective-permute-start(bf16[2,512,128]{1,2,0:T(8,128)(2,1)} %slice.35), channel_id=1, source_target_pairs={{0,4},{4,8},{8,12},{12,0},{1,5},{5,9},{9,13},{13,1},{2,6},{6,10},{... | collective-permute-start | bytes 786440 | tf_op jit(solution)/shard_map/ppermute | solution.py:10
  82.8 10.7 %collective-permute-start.3 = (bf16[2,512,128]{1,2,0:T(8,128)(2,1)}, bf16[2,512,128]{1,2,0:T(8,128)(2,1)}, u32[]{:S(2)}, u32[]{:S(2)}) collective-permute-start(bf16[2,512,128]{1,2,0:T(8,128)(2,1)} %slice.36), channel_id=1, source_target_pairs={{0,12},{4,0},{8,4},{12,8},{1,13},{5,1},{9,5},{13,9},{2,14},{6,2},{... | collective-permute-start | bytes 786440 | tf_op jit(solution)/shard_map/ppermute | solution.py:10
  86.6 9.3 %collective-permute-start.6 = (bf16[2,512,128]{1,2,0:T(8,128)(2,1)S(1)}, bf16[2,512,128]{1,2,0:T(8,128)(2,1)S(1)}, u32[]{:S(2)}, u32[]{:S(2)}) collective-permute-start(bf16[2,512,128]{1,2,0:T(8,128)(2,1)S(1)} %slice.38), channel_id=1, source_target_pairs={{0,4},{4,8},{8,12},{12,0},{1,5},{5,9},{9,13},{13,1},{2,6},{6,10},{... | collective-permute-start | bytes 786440 | tf_op jit(solution)/shard_map/ppermute | solution.py:10
  91.0 9.5 %collective-permute-start.7 = (bf16[2,512,128]{1,2,0:T(8,128)(2,1)S(1)}, bf16[2,512,128]{1,2,0:T(8,128)(2,1)S(1)}, u32[]{:S(2)}, u32[]{:S(2)}) collective-permute-start(bf16[2,512,128]{1,2,0:T(8,128)(2,1)S(1)} %slice.39), channel_id=1, source_target_pairs={{0,12},{4,0},{8,4},{12,8},{1,13},{5,1},{9,5},{13,9},{2,14},{6,2},{... | collective-permute-start | bytes 786440 | tf_op jit(solution)/shard_map/ppermute | solution.py:10
  104.0 1.4 copy-start.4
  105.4 1.9 copy-start.1
  105.4 2.3 %copy-start.5 = (bf16[1,2048,320]{1,2,0:T(8,128)(2,1)S(1)}, bf16[1,2048,320]{1,2,0:T(8,128)(2,1)}, u32[]{:S(2)}) copy-start(bf16[1,2048,320]{1,2,0:T(8,128)(2,1)} %param.15) | copy-start | bytes 3932164
  110.1 12.6 %collective-permute-start.8 = (bf16[512,512]{1,0:T(8,128)(2,1)S(1)}, bf16[512,512]{1,0:T(8,128)(2,1)S(1)}, u32[]{:S(2)}, u32[]{:S(2)}) collective-permute-start(bf16[512,512]{1,0:T(8,128)(2,1)S(1)} %convolution_convert_fusion.7), channel_id=1, source_target_pairs={{0,4},{4,8},{8,12},{12,0},{1,5},{5,9},{9,13},{13,1},{2,6},{6,10},{... | collective-permute-start | bytes 1572872 | tf_op jit(solution)/shard_map/ppermute | solution.py:10
  112.6 13.5 %collective-permute-start.11 = (bf16[512,512]{1,0:T(8,128)(2,1)S(1)}, bf16[512,512]{1,0:T(8,128)(2,1)S(1)}, u32[]{:S(2)}, u32[]{:S(2)}) collective-permute-start(bf16[512,512]{1,0:T(8,128)(2,1)S(1)} %convolution_convert_fusion.3), channel_id=1, source_target_pairs={{0,12},{4,0},{8,4},{12,8},{1,13},{5,1},{9,5},{13,9},{2,14},{6,2},{... | collective-permute-start | bytes 1572872 | tf_op jit(solution)/shard_map/ppermute | solution.py:10
  123.2 14.0 %collective-permute-start.9 = (bf16[512,512]{1,0:T(8,128)(2,1)S(1)}, bf16[512,512]{1,0:T(8,128)(2,1)S(1)}, u32[]{:S(2)}, u32[]{:S(2)}) collective-permute-start(bf16[512,512]{1,0:T(8,128)(2,1)S(1)} %add_convert_fusion.5), channel_id=1, source_target_pairs={{0,4},{4,8},{8,12},{12,0},{1,5},{5,9},{9,13},{13,1},{2,6},{6,10},{... | collective-permute-start | bytes 1572872 | tf_op jit(solution)/shard_map/ppermute | solution.py:10
  126.6 14.3 %collective-permute-start.12 = (bf16[512,512]{1,0:T(8,128)(2,1)S(1)}, bf16[512,512]{1,0:T(8,128)(2,1)S(1)}, u32[]{:S(2)}, u32[]{:S(2)}) collective-permute-start(bf16[512,512]{1,0:T(8,128)(2,1)S(1)} %add_convert_fusion.2), channel_id=1, source_target_pairs={{0,12},{4,0},{8,4},{12,8},{1,13},{5,1},{9,5},{13,9},{2,14},{6,2},{... | collective-permute-start | bytes 1572872 | tf_op jit(solution)/shard_map/ppermute | solution.py:10
  137.3 11.1 %collective-permute-start.10 = (bf16[512,512]{1,0:T(8,128)(2,1)S(1)}, bf16[512,512]{1,0:T(8,128)(2,1)S(1)}, u32[]{:S(2)}, u32[]{:S(2)}) collective-permute-start(bf16[512,512]{1,0:T(8,128)(2,1)S(1)} %add_convert_fusion.4), channel_id=1, source_target_pairs={{0,4},{4,8},{8,12},{12,0},{1,5},{5,9},{9,13},{13,1},{2,6},{6,10},{... | collective-permute-start | bytes 1572872 | tf_op jit(solution)/shard_map/ppermute | solution.py:10
  141.1 12.7 %collective-permute-start.13 = (bf16[512,512]{1,0:T(8,128)(2,1)S(1)}, bf16[512,512]{1,0:T(8,128)(2,1)S(1)}, u32[]{:S(2)}, u32[]{:S(2)}) collective-permute-start(bf16[512,512]{1,0:T(8,128)(2,1)S(1)} %add_convert_fusion.1), channel_id=1, source_target_pairs={{0,12},{4,0},{8,4},{12,8},{1,13},{5,1},{9,5},{13,9},{2,14},{6,2},{... | collective-permute-start | bytes 1572872 | tf_op jit(solution)/shard_map/ppermute | solution.py:10
  149.3 14.4 %all-to-all-start.3 = ((bf16[4,512,128]{2,1,0:T(8,128)(2,1)}), bf16[4,512,128]{2,1,0:T(8,128)(2,1)S(1)}, u32[]{:S(2)}, u32[]{:S(2)}) async-start(bf16[4,512,128]{2,1,0:T(8,128)(2,1)} %bitcast_bitcast_fusion.1), calls=%async_computation.3 | async-start | bytes 1048576 | tf_op jit(solution)/shard_map/all_to_all | solution.py:120
  153.7 13.5 %copy-start.2 = (bf16[2048,32]{0,1:T(8,128)(2,1)S(1)}, bf16[2048,32]{0,1:T(8,128)(2,1)}, u32[]{:S(2)}) copy-start(bf16[2048,32]{0,1:T(8,128)(2,1)} %param.13) | copy-start | bytes 393220
  163.8 14.7 %all-to-all-start.4 = ((bf16[4,512,128]{2,1,0:T(8,128)(2,1)}), bf16[4,512,128]{2,1,0:T(8,128)(2,1)S(1)}, u32[]{:S(2)}, u32[]{:S(2)}) async-start(bf16[4,512,128]{2,1,0:T(8,128)(2,1)} %bitcast_bitcast_fusion), calls=%async_computation.4 | async-start | bytes 1048576 | tf_op jit(solution)/shard_map/all_to_all | solution.py:120

commit v15 on v11

--- a/solution.py
+++ b/solution.py
@@ -86,25 +86,28 @@
         copies = jnp.broadcast_to(rows[None], (n_z,) + rows.shape)
         part = lax.all_to_all(copies, "mz", split_axis=0, concat_axis=0, tiled=True)
         halves.append(ring_gather(part, "mx", n_x).reshape(n_mp, cells // 2, shard_width))
-    whole = jnp.concatenate(halves, axis=1)
+    hidden_halves = {}
+    gate_parts = []
+    for lower, whole in zip((True, False), halves):
+        rows_half = whole.shape[1]
+        features = jnp.transpose(whole, (1, 0, 2)).reshape(rows_half, model_width)
+        features = features.astype(jnp.float32)
+        mean_square = jnp.sum(features * features, axis=1) / model_width
+        scale = lax.rsqrt(mean_square + norm_eps)
+        normed = (features * scale[:, None] * rows_relative(norm_gain)).astype(jnp.bfloat16)
 
-    features = jnp.transpose(whole, (1, 0, 2)).reshape(cells, model_width).astype(jnp.float32)
-    mean_square = jnp.sum(features * features, axis=1) / model_width
-    scale = lax.rsqrt(mean_square + norm_eps)
-    normed = (features * scale[:, None] * rows_relative(norm_gain)).astype(jnp.bfloat16)
+        logits = jnp.dot(normed, rows_relative(router_weight), preferred_element_type=jnp.float32)
+        picked = jnp.sum(
+            jnp.where(jnp.arange(experts, dtype=jnp.int32)[None, :] == me, logits, 0.0), axis=1
+        )
+        gate_parts.append(jax.nn.sigmoid(picked))
 
-    logits = jnp.dot(normed, rows_relative(router_weight), preferred_element_type=jnp.float32)
-    picked = jnp.sum(
-        jnp.where(jnp.arange(experts, dtype=jnp.int32)[None, :] == me, logits, 0.0), axis=1
-    )
-    gate_prob = jax.nn.sigmoid(picked)
-
-    ff_local = gate_proj.shape[2]
-    pre_gate = jnp.dot(normed, rows_relative(gate_proj[0]), preferred_element_type=jnp.float32)
-    pre_up = jnp.dot(normed, rows_relative(up_proj[0]), preferred_element_type=jnp.float32)
-    hidden = (jax.nn.gelu(pre_gate, approximate=True) * pre_up).astype(jnp.bfloat16)
-    rows_half = cells // 2
-    hidden_halves = {True: hidden[:rows_half], False: hidden[rows_half:]}
+        pre_gate = jnp.dot(normed, rows_relative(gate_proj[0]), preferred_element_type=jnp.float32)
+        pre_up = jnp.dot(normed, rows_relative(up_proj[0]), preferred_element_type=jnp.float32)
+        hidden_halves[lower] = (jax.nn.gelu(pre_gate, approximate=True) * pre_up).astype(
+            jnp.bfloat16
+        )
+    gate_prob = jnp.concatenate(gate_parts)
 
     def x_term(k, lower):
         columns = lax.dynamic_slice_in_dim(

time: 202 us -> 201 us (level)
  waiting for transfers between devices: 63.8 us -> 55.8 us
  starting transfers between devices: 58.7 us -> 62.7 us
    ppermute x14, waiting for transfers between devices: 27.3 us -> 21.3 us  [shift(): return lax.ppermute(value, axis, [(i, (i + step) % n) for i in range(n)])]
    another operation x4 -> x2, other arithmetic: 3.73 us -> 1.12 us  [ring_gather(): return jnp.stack(pieces)]
    ppermute x14, starting transfers between devices: 40.8 us -> 43 us  [shift(): return lax.ppermute(value, axis, [(i, (i + step) % n) for i in range(n)])]
  transfers between devices with their start and end apart: 17 -> 17, of which waited for: 10 -> 11; matrix products, arithmetic and copies ran while one was open for 6% -> 9% of each run, Pallas kernels for 0% -> 0%
where the time goes in v15:
time: 201 us; the launch traced here: 200 us
  starting transfers between devices  62.7 us (31%)
  waiting for transfers between devices  55.8 us (28%)
  blocking collectives  47.4 us (24%)
  matrix products  14.4 us (7%)
  other arithmetic  12.8 us (6%)
  local copies, waits for them, and re-layouts  6.74 us (3%)
    ppermute x14, starting transfers between devices, shift(): return lax.ppermute(value, axis, [(i, (i + step) % n) for i in range(n)])  43 us
    all_to_all x1, blocking collectives, shards(): lax.all_to_all(gated.reshape(experts, slot_count, shard_width), 'expert',...  25.1 us
    all_to_all x2, waiting for transfers between devices, shards(): part = lax.all_to_all(copies, 'mz', split_axis=0, concat_axis=0, tiled=True)  22.6 us
    all_to_all x1, blocking collectives, shards(): lax.all_to_all(masked.reshape(experts, slot_count, shard_width), 'expert'...  22.3 us
    ppermute x14, waiting for transfers between devices, shift(): return lax.ppermute(value, axis, [(i, (i + step) % n) for i in range(n)])  21.3 us
    all_to_all x2, starting transfers between devices, shards(): part = lax.all_to_all(copies, 'mz', split_axis=0, concat_axis=0, tiled=True)  13.8 us
    all_to_all x1, waiting for transfers between devices, shards(): lax.all_to_all(jnp.transpose(across_x, (1, 0, 2)), 'mz', split_axis=0, co...  11.9 us
    all_to_all x1, starting transfers between devices, shards(): lax.all_to_all(jnp.transpose(across_x, (1, 0, 2)), 'mz', split_axis=0, co...  5.98 us
  transfers between devices with their start and end apart: 17, of which 11 were waited for; matrix products, arithmetic and copies ran while one was open for 9% of the time, Pallas kernels for 0%

profile of v15, /device:TPU:6, one launch (start us, length us, event | category | flops | bytes accessed | tf_op | source)
XLA Modules:
  0.0 200.2 jit_solution(4526732453669231659)
XLA Ops:
  4.5 22.3 %all_to_all.25 = bf16[32,32,128]{2,1,0:T(8,128)(2,1)S(1)} all-to-all(bf16[32,32,128]{2,1,0:T(8,128)(2,1)S(1)} %bitcast.97), channel_id=1, replica_groups=mesh['expert'=32,'mx'=4,'mz'=4] {'expert'}, dimensions={0} | all-to-all | bytes 524288 | tf_op jit(solution)/shard_map/all_to_all | solution.py:69
  27.7 9.5 %all-to-all-start.2 = ((bf16[4,512,128]{1,2,0:T(8,128)(2,1)}), bf16[4,512,128]{1,2,0:T(8,128)(2,1)S(1)}, u32[]{:S(2)}, u32[]{:S(2)}) async-start(bf16[4,512,128]{1,2,0:T(8,128)(2,1)} %broadcast_in_dim.64), calls=%async_computation.2 | async-start | bytes 1048576 | tf_op jit(solution)/shard_map/all_to_all | solution.py:87
  37.4 14.0 %all-to-all-done.2 = bf16[4,512,128]{1,2,0:T(8,128)(2,1)S(1)} async-done(((bf16[4,512,128]{1,2,0:T(8,128)(2,1)}), bf16[4,512,128]{1,2,0:T(8,128)(2,1)S(1)}, u32[]{:S(2)}, u32[]{:S(2)}) %all-to-all-start.2) | async-done | bytes 524320 | tf_op jit(solution)/shard_map/all_to_all | solution.py:87
  52.3 4.2 %all-to-all-start.1 = ((bf16[4,512,128]{1,2,0:T(8,128)(2,1)}), bf16[4,512,128]{1,2,0:T(8,128)(2,1)S(1)}, u32[]{:S(2)}, u32[]{:S(2)}) async-start(bf16[4,512,128]{1,2,0:T(8,128)(2,1)} %broadcast_in_dim.61), calls=%async_computation.1 | async-start | bytes 1048576 | tf_op jit(solution)/shard_map/all_to_all | solution.py:87
  56.5 2.4 %collective-permute-start.5 = (bf16[4,512,128]{1,2,0:T(8,128)(2,1)S(1)}, bf16[4,512,128]{1,2,0:T(8,128)(2,1)}, u32[]{:S(2)}, u32[]{:S(2)}) collective-permute-start(bf16[4,512,128]{1,2,0:T(8,128)(2,1)S(1)} %all-to-all-done.2), channel_id=1, source_target_pairs={{0,4},{4,8},{8,12},{12,0},{1,5},{5,9},{9,13},{13,1},{2,6},{6,10},{... | collective-permute-start | bytes 1572872 | tf_op jit(solution)/shard_map/ppermute | solution.py:10
  58.9 3.5 %collective-permute-start.4 = (bf16[4,512,128]{1,2,0:T(8,128)(2,1)S(1)}, bf16[4,512,128]{1,2,0:T(8,128)(2,1)}, u32[]{:S(2)}, u32[]{:S(2)}) collective-permute-start(bf16[4,512,128]{1,2,0:T(8,128)(2,1)S(1)} %all-to-all-done.2), channel_id=1, source_target_pairs={{0,12},{4,0},{8,4},{12,8},{1,13},{5,1},{9,5},{13,9},{2,14},{6,2},{... | collective-permute-start | bytes 1572872 | tf_op jit(solution)/shard_map/ppermute | solution.py:10
  62.3 8.6 %all-to-all-done.1 = bf16[4,512,128]{1,2,0:T(8,128)(2,1)S(1)} async-done(((bf16[4,512,128]{1,2,0:T(8,128)(2,1)}), bf16[4,512,128]{1,2,0:T(8,128)(2,1)S(1)}, u32[]{:S(2)}, u32[]{:S(2)}) %all-to-all-start.1) | async-done | bytes 524320 | tf_op jit(solution)/shard_map/all_to_all | solution.py:87
  71.0 2.4 %collective-permute-start.1 = (bf16[4,512,128]{1,2,0:T(8,128)(2,1)S(1)}, bf16[4,512,128]{1,2,0:T(8,128)(2,1)S(1)}, u32[]{:S(2)}, u32[]{:S(2)}) collective-permute-start(bf16[4,512,128]{1,2,0:T(8,128)(2,1)S(1)} %all-to-all-done.1), channel_id=1, source_target_pairs={{0,4},{4,8},{8,12},{12,0},{1,5},{5,9},{9,13},{13,1},{2,6},{6,10},{... | collective-permute-start | bytes 1572872 | tf_op jit(solution)/shard_map/ppermute | solution.py:10
  73.3 3.5 %collective-permute-start = (bf16[4,512,128]{1,2,0:T(8,128)(2,1)S(1)}, bf16[4,512,128]{1,2,0:T(8,128)(2,1)S(1)}, u32[]{:S(2)}, u32[]{:S(2)}) collective-permute-start(bf16[4,512,128]{1,2,0:T(8,128)(2,1)S(1)} %all-to-all-done.1), channel_id=1, source_target_pairs={{0,12},{4,0},{8,4},{12,8},{1,13},{5,1},{9,5},{13,9},{2,14},{6,2},{... | collective-permute-start | bytes 1572872 | tf_op jit(solution)/shard_map/ppermute | solution.py:10
  78.5 3.6 %collective-permute-start.6 = (bf16[2,512,128]{1,2,0:T(8,128)(2,1)}, bf16[2,512,128]{1,2,0:T(8,128)(2,1)}, u32[]{:S(2)}, u32[]{:S(2)}) collective-permute-start(bf16[2,512,128]{1,2,0:T(8,128)(2,1)} %slice.30), channel_id=1, source_target_pairs={{0,4},{4,8},{8,12},{12,0},{1,5},{5,9},{9,13},{13,1},{2,6},{6,10},{... | collective-permute-start | bytes 786440 | tf_op jit(solution)/shard_map/ppermute | solution.py:10
  83.8 2.2 %collective-permute-start.7 = (bf16[2,512,128]{1,2,0:T(8,128)(2,1)}, bf16[2,512,128]{1,2,0:T(8,128)(2,1)}, u32[]{:S(2)}, u32[]{:S(2)}) collective-permute-start(bf16[2,512,128]{1,2,0:T(8,128)(2,1)} %slice.31), channel_id=1, source_target_pairs={{0,12},{4,0},{8,4},{12,8},{1,13},{5,1},{9,5},{13,9},{2,14},{6,2},{... | collective-permute-start | bytes 786440 | tf_op jit(solution)/shard_map/ppermute | solution.py:10
  86.2 4.8 %collective-permute-start.2 = (bf16[2,512,128]{1,2,0:T(8,128)(2,1)S(1)}, bf16[2,512,128]{1,2,0:T(8,128)(2,1)S(1)}, u32[]{:S(2)}, u32[]{:S(2)}) collective-permute-start(bf16[2,512,128]{1,2,0:T(8,128)(2,1)S(1)} %slice.27), channel_id=1, source_target_pairs={{0,4},{4,8},{8,12},{12,0},{1,5},{5,9},{9,13},{13,1},{2,6},{6,10},{... | collective-permute-start | bytes 786440 | tf_op jit(solution)/shard_map/ppermute | solution.py:10
  111.0 3.9 %collective-permute-start.11 = (bf16[512,512]{1,0:T(8,128)(2,1)S(1)}, bf16[512,512]{1,0:T(8,128)(2,1)S(1)}, u32[]{:S(2)}, u32[]{:S(2)}) collective-permute-start(bf16[512,512]{1,0:T(8,128)(2,1)S(1)} %convolution_convert_fusion.3), channel_id=1, source_target_pairs={{0,12},{4,0},{8,4},{12,8},{1,13},{5,1},{9,5},{13,9},{2,14},{6,2},{... | collective-permute-start | bytes 1572872 | tf_op jit(solution)/shard_map/ppermute | solution.py:10
  115.4 2.9 %collective-permute-done.8 = bf16[512,512]{1,0:T(8,128)(2,1)S(1)} collective-permute-done((bf16[512,512]{1,0:T(8,128)(2,1)S(1)}, bf16[512,512]{1,0:T(8,128)(2,1)S(1)}, u32[]{:S(2)}, u32[]{:S(2)}) %collective-permute-start.8) | collective-permute-done | bytes 524320 | tf_op jit(solution)/shard_map/ppermute | solution.py:10
  118.7 3.0 %collective-permute-start.9 = (bf16[512,512]{1,0:T(8,128)(2,1)S(1)}, bf16[512,512]{1,0:T(8,128)(2,1)S(1)}, u32[]{:S(2)}, u32[]{:S(2)}) collective-permute-start(bf16[512,512]{1,0:T(8,128)(2,1)S(1)} %add_convert_fusion.5), channel_id=1, source_target_pairs={{0,4},{4,8},{8,12},{12,0},{1,5},{5,9},{9,13},{13,1},{2,6},{6,10},{... | collective-permute-start | bytes 1572872 | tf_op jit(solution)/shard_map/ppermute | solution.py:10
  123.9 3.5 %collective-permute-start.12 = (bf16[512,512]{1,0:T(8,128)(2,1)S(1)}, bf16[512,512]{1,0:T(8,128)(2,1)S(1)}, u32[]{:S(2)}, u32[]{:S(2)}) collective-permute-start(bf16[512,512]{1,0:T(8,128)(2,1)S(1)} %add_convert_fusion.2), channel_id=1, source_target_pairs={{0,12},{4,0},{8,4},{12,8},{1,13},{5,1},{9,5},{13,9},{2,14},{6,2},{... | collective-permute-start | bytes 1572872 | tf_op jit(solution)/shard_map/ppermute | solution.py:10
  127.9 3.4 %collective-permute-done.9 = bf16[512,512]{1,0:T(8,128)(2,1)S(1)} collective-permute-done((bf16[512,512]{1,0:T(8,128)(2,1)S(1)}, bf16[512,512]{1,0:T(8,128)(2,1)S(1)}, u32[]{:S(2)}, u32[]{:S(2)}) %collective-permute-start.9) | collective-permute-done | bytes 524320 | tf_op jit(solution)/shard_map/ppermute | solution.py:10
  131.5 3.1 %collective-permute-start.10 = (bf16[512,512]{1,0:T(8,128)(2,1)S(1)}, bf16[512,512]{1,0:T(8,128)(2,1)S(1)}, u32[]{:S(2)}, u32[]{:S(2)}) collective-permute-start(bf16[512,512]{1,0:T(8,128)(2,1)S(1)} %add_convert_fusion.4), channel_id=1, source_target_pairs={{0,4},{4,8},{8,12},{12,0},{1,5},{5,9},{9,13},{13,1},{2,6},{6,10},{... | collective-permute-start | bytes 1572872 | tf_op jit(solution)/shard_map/ppermute | solution.py:10
  134.6 2.2 %collective-permute-done.12 = bf16[512,512]{1,0:T(8,128)(2,1)S(1)} collective-permute-done((bf16[512,512]{1,0:T(8,128)(2,1)S(1)}, bf16[512,512]{1,0:T(8,128)(2,1)S(1)}, u32[]{:S(2)}, u32[]{:S(2)}) %collective-permute-start.12) | collective-permute-done | bytes 524320 | tf_op jit(solution)/shard_map/ppermute | solution.py:10
  137.0 3.2 %collective-permute-start.13 = (bf16[512,512]{1,0:T(8,128)(2,1)S(1)}, bf16[512,512]{1,0:T(8,128)(2,1)S(1)}, u32[]{:S(2)}, u32[]{:S(2)}) collective-permute-start(bf16[512,512]{1,0:T(8,128)(2,1)S(1)} %add_convert_fusion.1), channel_id=1, source_target_pairs={{0,12},{4,0},{8,4},{12,8},{1,13},{5,1},{9,5},{13,9},{2,14},{6,2},{... | collective-permute-start | bytes 1572872 | tf_op jit(solution)/shard_map/ppermute | solution.py:10
  142.7 6.6 %collective-permute-done.13 = bf16[512,512]{1,0:T(8,128)(2,1)S(1)} collective-permute-done((bf16[512,512]{1,0:T(8,128)(2,1)S(1)}, bf16[512,512]{1,0:T(8,128)(2,1)S(1)}, u32[]{:S(2)}, u32[]{:S(2)}) %collective-permute-start.13) | collective-permute-done | bytes 524320 | tf_op jit(solution)/shard_map/ppermute | solution.py:10
  150.7 6.0 %all-to-all-start.3 = ((bf16[4,1024,128]{2,1,0:T(8,128)(2,1)}), bf16[4,1024,128]{2,1,0:T(8,128)(2,1)}, u32[]{:S(2)}, u32[]{:S(2)}) async-start(bf16[4,1024,128]{2,1,0:T(8,128)(2,1)} %bitcast_bitcast_fusion), calls=%async_computation.3 | async-start | bytes 2097152 | tf_op jit(solution)/shard_map/all_to_all | solution.py:123
  160.1 11.9 %all-to-all-done.3 = bf16[4,1024,128]{2,1,0:T(8,128)(2,1)} async-done(((bf16[4,1024,128]{2,1,0:T(8,128)(2,1)}), bf16[4,1024,128]{2,1,0:T(8,128)(2,1)}, u32[]{:S(2)}, u32[]{:S(2)}) %all-to-all-start.3) | async-done | bytes 1048608 | tf_op jit(solution)/shard_map/all_to_all | solution.py:123
  173.7 25.1 %all_to_all.26 = bf16[32,32,128]{2,1,0:T(8,128)(2,1)S(1)} all-to-all(bf16[32,32,128]{2,1,0:T(8,128)(2,1)S(1)} %fusion.47), channel_id=1, replica_groups=mesh['expert'=32,'mx'=4,'mz'=4] {'expert'}, dimensions={0} | all-to-all | bytes 524288 | tf_op jit(solution)/shard_map/all_to_all | solution.py:129
  (81 shorter events, 44.0 us)
Async XLA Ops:
  0.0 106.1 %copy-start = (bf16[1,320,2048]{2,1,0:T(8,128)(2,1)S(1)}, bf16[1,320,2048]{2,1,0:T(8,128)(2,1)}, u32[]{:S(2)}) copy-start(bf16[1,320,2048]{2,1,0:T(8,128)(2,1)} %param.20) | copy-start | bytes 3932164
  2.3 2.2 %copy-start.5 = (pred[768]{0:T(1024)(128)(4,1)}, pred[768]{0:T(1024)(128)(4,1)S(1)}, u32[]{:S(2)}) copy-start(pred[768]{0:T(1024)(128)(4,1)S(1)} %lt.68) | copy-start | bytes 2308
  27.7 58.4 %copy-start.3 = (f32[2048]{0:T(1024)S(1)}, f32[2048]{0:T(1024)}, u32[]{:S(2)}) copy-start(f32[2048]{0:T(1024)} %param.16) | copy-start | bytes 24580
  27.7 23.7 %all-to-all-start.2 = ((bf16[4,512,128]{1,2,0:T(8,128)(2,1)}), bf16[4,512,128]{1,2,0:T(8,128)(2,1)S(1)}, u32[]{:S(2)}, u32[]{:S(2)}) async-start(bf16[4,512,128]{1,2,0:T(8,128)(2,1)} %broadcast_in_dim.64), calls=%async_computation.2 | async-start | bytes 1048576 | tf_op jit(solution)/shard_map/all_to_all | solution.py:87
  52.3 18.7 %all-to-all-start.1 = ((bf16[4,512,128]{1,2,0:T(8,128)(2,1)}), bf16[4,512,128]{1,2,0:T(8,128)(2,1)S(1)}, u32[]{:S(2)}, u32[]{:S(2)}) async-start(bf16[4,512,128]{1,2,0:T(8,128)(2,1)} %broadcast_in_dim.61), calls=%async_computation.1 | async-start | bytes 1048576 | tf_op jit(solution)/shard_map/all_to_all | solution.py:87
  56.5 20.3 %collective-permute-start.5 = (bf16[4,512,128]{1,2,0:T(8,128)(2,1)S(1)}, bf16[4,512,128]{1,2,0:T(8,128)(2,1)}, u32[]{:S(2)}, u32[]{:S(2)}) collective-permute-start(bf16[4,512,128]{1,2,0:T(8,128)(2,1)S(1)} %all-to-all-done.2), channel_id=1, source_target_pairs={{0,4},{4,8},{8,12},{12,0},{1,5},{5,9},{9,13},{13,1},{2,6},{6,10},{... | collective-permute-start | bytes 1572872 | tf_op jit(solution)/shard_map/ppermute | solution.py:10
  58.9 23.2 %collective-permute-start.4 = (bf16[4,512,128]{1,2,0:T(8,128)(2,1)S(1)}, bf16[4,512,128]{1,2,0:T(8,128)(2,1)}, u32[]{:S(2)}, u32[]{:S(2)}) collective-permute-start(bf16[4,512,128]{1,2,0:T(8,128)(2,1)S(1)} %all-to-all-done.2), channel_id=1, source_target_pairs={{0,12},{4,0},{8,4},{12,8},{1,13},{5,1},{9,5},{13,9},{2,14},{6,2},{... | collective-permute-start | bytes 1572872 | tf_op jit(solution)/shard_map/ppermute | solution.py:10
  71.0 15.2 %collective-permute-start.1 = (bf16[4,512,128]{1,2,0:T(8,128)(2,1)S(1)}, bf16[4,512,128]{1,2,0:T(8,128)(2,1)S(1)}, u32[]{:S(2)}, u32[]{:S(2)}) collective-permute-start(bf16[4,512,128]{1,2,0:T(8,128)(2,1)S(1)} %all-to-all-done.1), channel_id=1, source_target_pairs={{0,4},{4,8},{8,12},{12,0},{1,5},{5,9},{9,13},{13,1},{2,6},{6,10},{... | collective-permute-start | bytes 1572872 | tf_op jit(solution)/shard_map/ppermute | solution.py:10
  73.3 17.7 %collective-permute-start = (bf16[4,512,128]{1,2,0:T(8,128)(2,1)S(1)}, bf16[4,512,128]{1,2,0:T(8,128)(2,1)S(1)}, u32[]{:S(2)}, u32[]{:S(2)}) collective-permute-start(bf16[4,512,128]{1,2,0:T(8,128)(2,1)S(1)} %all-to-all-done.1), channel_id=1, source_target_pairs={{0,12},{4,0},{8,4},{12,8},{1,13},{5,1},{9,5},{13,9},{2,14},{6,2},{... | collective-permute-start | bytes 1572872 | tf_op jit(solution)/shard_map/ppermute | solution.py:10
  78.5 14.5 %collective-permute-start.6 = (bf16[2,512,128]{1,2,0:T(8,128)(2,1)}, bf16[2,512,128]{1,2,0:T(8,128)(2,1)}, u32[]{:S(2)}, u32[]{:S(2)}) collective-permute-start(bf16[2,512,128]{1,2,0:T(8,128)(2,1)} %slice.30), channel_id=1, source_target_pairs={{0,4},{4,8},{8,12},{12,0},{1,5},{5,9},{9,13},{13,1},{2,6},{6,10},{... | collective-permute-start | bytes 786440 | tf_op jit(solution)/shard_map/ppermute | solution.py:10
  83.8 11.4 %collective-permute-start.7 = (bf16[2,512,128]{1,2,0:T(8,128)(2,1)}, bf16[2,512,128]{1,2,0:T(8,128)(2,1)}, u32[]{:S(2)}, u32[]{:S(2)}) collective-permute-start(bf16[2,512,128]{1,2,0:T(8,128)(2,1)} %slice.31), channel_id=1, source_target_pairs={{0,12},{4,0},{8,4},{12,8},{1,13},{5,1},{9,5},{13,9},{2,14},{6,2},{... | collective-permute-start | bytes 786440 | tf_op jit(solution)/shard_map/ppermute | solution.py:10
  86.2 13.3 %collective-permute-start.2 = (bf16[2,512,128]{1,2,0:T(8,128)(2,1)S(1)}, bf16[2,512,128]{1,2,0:T(8,128)(2,1)S(1)}, u32[]{:S(2)}, u32[]{:S(2)}) collective-permute-start(bf16[2,512,128]{1,2,0:T(8,128)(2,1)S(1)} %slice.27), channel_id=1, source_target_pairs={{0,4},{4,8},{8,12},{12,0},{1,5},{5,9},{9,13},{13,1},{2,6},{6,10},{... | collective-permute-start | bytes 786440 | tf_op jit(solution)/shard_map/ppermute | solution.py:10
  91.1 9.5 %collective-permute-start.3 = (bf16[2,512,128]{1,2,0:T(8,128)(2,1)S(1)}, bf16[2,512,128]{1,2,0:T(8,128)(2,1)S(1)}, u32[]{:S(2)}, u32[]{:S(2)}) collective-permute-start(bf16[2,512,128]{1,2,0:T(8,128)(2,1)S(1)} %slice.28), channel_id=1, source_target_pairs={{0,12},{4,0},{8,4},{12,8},{1,13},{5,1},{9,5},{13,9},{2,14},{6,2},{... | collective-permute-start | bytes 786440 | tf_op jit(solution)/shard_map/ppermute | solution.py:10
  103.0 2.1 %copy-start.8 = (bf16[1,2048,320]{1,2,0:T(8,128)(2,1)S(1)}, bf16[1,2048,320]{1,2,0:T(8,128)(2,1)}, u32[]{:S(2)}) copy-start(bf16[1,2048,320]{1,2,0:T(8,128)(2,1)} %param.19) | copy-start | bytes 3932164
  106.6 11.6 %collective-permute-start.8 = (bf16[512,512]{1,0:T(8,128)(2,1)S(1)}, bf16[512,512]{1,0:T(8,128)(2,1)S(1)}, u32[]{:S(2)}, u32[]{:S(2)}) collective-permute-start(bf16[512,512]{1,0:T(8,128)(2,1)S(1)} %convolution_convert_fusion.7), channel_id=1, source_target_pairs={{0,4},{4,8},{8,12},{12,0},{1,5},{5,9},{9,13},{13,1},{2,6},{6,10},{... | collective-permute-start | bytes 1572872 | tf_op jit(solution)/shard_map/ppermute | solution.py:10
  111.0 12.4 %collective-permute-start.11 = (bf16[512,512]{1,0:T(8,128)(2,1)S(1)}, bf16[512,512]{1,0:T(8,128)(2,1)S(1)}, u32[]{:S(2)}, u32[]{:S(2)}) collective-permute-start(bf16[512,512]{1,0:T(8,128)(2,1)S(1)} %convolution_convert_fusion.3), channel_id=1, source_target_pairs={{0,12},{4,0},{8,4},{12,8},{1,13},{5,1},{9,5},{13,9},{2,14},{6,2},{... | collective-permute-start | bytes 1572872 | tf_op jit(solution)/shard_map/ppermute | solution.py:10
  118.7 12.5 %collective-permute-start.9 = (bf16[512,512]{1,0:T(8,128)(2,1)S(1)}, bf16[512,512]{1,0:T(8,128)(2,1)S(1)}, u32[]{:S(2)}, u32[]{:S(2)}) collective-permute-start(bf16[512,512]{1,0:T(8,128)(2,1)S(1)} %add_convert_fusion.5), channel_id=1, source_target_pairs={{0,4},{4,8},{8,12},{12,0},{1,5},{5,9},{9,13},{13,1},{2,6},{6,10},{... | collective-permute-start | bytes 1572872 | tf_op jit(solution)/shard_map/ppermute | solution.py:10
  123.9 12.9 %collective-permute-start.12 = (bf16[512,512]{1,0:T(8,128)(2,1)S(1)}, bf16[512,512]{1,0:T(8,128)(2,1)S(1)}, u32[]{:S(2)}, u32[]{:S(2)}) collective-permute-start(bf16[512,512]{1,0:T(8,128)(2,1)S(1)} %add_convert_fusion.2), channel_id=1, source_target_pairs={{0,12},{4,0},{8,4},{12,8},{1,13},{5,1},{9,5},{13,9},{2,14},{6,2},{... | collective-permute-start | bytes 1572872 | tf_op jit(solution)/shard_map/ppermute | solution.py:10
  131.5 11.1 %collective-permute-start.10 = (bf16[512,512]{1,0:T(8,128)(2,1)S(1)}, bf16[512,512]{1,0:T(8,128)(2,1)S(1)}, u32[]{:S(2)}, u32[]{:S(2)}) collective-permute-start(bf16[512,512]{1,0:T(8,128)(2,1)S(1)} %add_convert_fusion.4), channel_id=1, source_target_pairs={{0,4},{4,8},{8,12},{12,0},{1,5},{5,9},{9,13},{13,1},{2,6},{6,10},{... | collective-permute-start | bytes 1572872 | tf_op jit(solution)/shard_map/ppermute | solution.py:10
  137.0 12.3 %collective-permute-start.13 = (bf16[512,512]{1,0:T(8,128)(2,1)S(1)}, bf16[512,512]{1,0:T(8,128)(2,1)S(1)}, u32[]{:S(2)}, u32[]{:S(2)}) collective-permute-start(bf16[512,512]{1,0:T(8,128)(2,1)S(1)} %add_convert_fusion.1), channel_id=1, source_target_pairs={{0,12},{4,0},{8,4},{12,8},{1,13},{5,1},{9,5},{13,9},{2,14},{6,2},{... | collective-permute-start | bytes 1572872 | tf_op jit(solution)/shard_map/ppermute | solution.py:10
  149.5 7.2 %copy-start.2 = (bf16[2048,32]{0,1:T(8,128)(2,1)S(1)}, bf16[2048,32]{0,1:T(8,128)(2,1)}, u32[]{:S(2)}) copy-start(bf16[2048,32]{0,1:T(8,128)(2,1)} %param.17) | copy-start | bytes 393220
  150.7 21.3 %all-to-all-start.3 = ((bf16[4,1024,128]{2,1,0:T(8,128)(2,1)}), bf16[4,1024,128]{2,1,0:T(8,128)(2,1)}, u32[]{:S(2)}, u32[]{:S(2)}) async-start(bf16[4,1024,128]{2,1,0:T(8,128)(2,1)} %bitcast_bitcast_fusion), calls=%async_computation.3 | async-start | bytes 2097152 | tf_op jit(solution)/shard_map/all_to_all | solution.py:123
  156.7 2.1 %copy-start.4 = (pred[32]{0:T(512)(128)(4,1)}, pred[32]{0:T(512)(128)(4,1)S(1)}, u32[]{:S(2)}) copy-start(pred[32]{0:T(512)(128)(4,1)S(1)} %iota_compare_fusion.2) | copy-start | bytes 100
  158.9 39.9 %copy-start.6 = (pred[768]{0:T(1024)(128)(4,1)S(1)}, pred[768]{0:T(1024)(128)(4,1)}, u32[]{:S(2)}) copy-start(pred[768]{0:T(1024)(128)(4,1)} %copy-done.5) | copy-start | bytes 2308
  (2 other events, 2.8 us)

commit v16 on v15

--- a/solution.py
+++ b/solution.py
@@ -85,7 +85,9 @@
     for rows in (received[: cells // 2], received[cells // 2 :]):
         copies = jnp.broadcast_to(rows[None], (n_z,) + rows.shape)
         part = lax.all_to_all(copies, "mz", split_axis=0, concat_axis=0, tiled=True)
-        halves.append(ring_gather(part, "mx", n_x).reshape(n_mp, cells // 2, shard_width))
+        spread = jnp.broadcast_to(part[None], (n_x,) + part.shape)
+        gathered = lax.all_to_all(spread, "mx", split_axis=0, concat_axis=0, tiled=True)
+        halves.append(gathered.reshape(n_mp, cells // 2, shard_width))
     hidden_halves = {}
     gate_parts = []
     for lower, whole in zip((True, False), halves):
@@ -94,16 +96,16 @@
         features = features.astype(jnp.float32)
         mean_square = jnp.sum(features * features, axis=1) / model_width
         scale = lax.rsqrt(mean_square + norm_eps)
-        normed = (features * scale[:, None] * rows_relative(norm_gain)).astype(jnp.bfloat16)
+        normed = (features * scale[:, None] * norm_gain).astype(jnp.bfloat16)
 
-        logits = jnp.dot(normed, rows_relative(router_weight), preferred_element_type=jnp.float32)
+        logits = jnp.dot(normed, router_weight, preferred_element_type=jnp.float32)
         picked = jnp.sum(
             jnp.where(jnp.arange(experts, dtype=jnp.int32)[None, :] == me, logits, 0.0), axis=1
         )
         gate_parts.append(jax.nn.sigmoid(picked))
 
-        pre_gate = jnp.dot(normed, rows_relative(gate_proj[0]), preferred_element_type=jnp.float32)
-        pre_up = jnp.dot(normed, rows_relative(up_proj[0]), preferred_element_type=jnp.float32)
+        pre_gate = jnp.dot(normed, gate_proj[0], preferred_element_type=jnp.float32)
+        pre_up = jnp.dot(normed, up_proj[0], preferred_element_type=jnp.float32)
         hidden_halves[lower] = (jax.nn.gelu(pre_gate, approximate=True) * pre_up).astype(
             jnp.bfloat16
         )

time: 201 us -> 228 us (1.13)
  blocking collectives: 47.4 us -> 89.5 us
  starting transfers between devices: 62.7 us -> 39.4 us
  waiting for transfers between devices: 55.8 us -> 67.3 us
  matrix products: 14.4 us -> 11.8 us
  local copies, waits for them, and re-layouts: 6.74 us -> 4.38 us
    all_to_all x0 -> x2, blocking collectives: none -> 45.3 us  [the longest x1 25.7 us: shards(): lax.all_to_all(spread, 'mx', split_axis=0, concat_axis=0, tiled=True)]
    ppermute x14 -> x6, starting transfers between devices: 43 us -> 18 us  [shift(): return lax.ppermute(value, axis, [(i, (i + step) % n) for i in range(n)])]
    all_to_all x0 -> x1, waiting for transfers between devices: none -> 18.8 us  [shards(): lax.all_to_all(spread, 'mx', split_axis=0, concat_axis=0, tiled=True)]
    all_to_all x2 -> x1, waiting for transfers between devices: 22.6 us -> 14 us  [shards(): part = lax.all_to_all(copies, 'mz', split_axis=0, concat_axis=0, tiled=True)]
    all_to_all x0 -> x1, starting transfers between devices: none -> 6.48 us  [shards(): lax.all_to_all(spread, 'mx', split_axis=0, concat_axis=0, tiled=True)]
    all_to_all x2 -> x1, starting transfers between devices: 13.8 us -> 9.4 us  [shards(): part = lax.all_to_all(copies, 'mz', split_axis=0, concat_axis=0, tiled=True)]
    slice x4 -> x0, local copies, waits for them, and re-layouts: 3.4 us -> none  [the longest x2 1.71 us: ring_gather(): second = shift(leftward[half:], axis, n, -1)]
    all_to_all x1, blocking collectives: 25.1 us -> 21.9 us  [shards(): lax.all_to_all(gated.reshape(experts, slot_count, shard_width), 'expert',...]
  transfers between devices with their start and end apart: 17 -> 9, of which waited for: 11 -> 9; matrix products, arithmetic and copies ran while one was open for 9% -> 5% of each run, Pallas kernels for 0% -> 0%
where the time goes in v16:
time: 228 us
  blocking collectives  89.5 us (39%)
  waiting for transfers between devices  67.3 us (30%)
  starting transfers between devices  39.4 us (17%)
  other arithmetic  14.8 us (6%)
  matrix products  11.8 us (5%)
  local copies, waits for them, and re-layouts  4.38 us (2%)
    all_to_all x1, blocking collectives, shards(): lax.all_to_all(spread, 'mx', split_axis=0, concat_axis=0, tiled=True)  25.7 us
    ppermute x6, waiting for transfers between devices, shift(): return lax.ppermute(value, axis, [(i, (i + step) % n) for i in range(n)])  23.9 us
    all_to_all x1, blocking collectives, shards(): lax.all_to_all(masked.reshape(experts, slot_count, shard_width), 'expert'...  22.3 us
    all_to_all x1, blocking collectives, shards(): lax.all_to_all(gated.reshape(experts, slot_count, shard_width), 'expert',...  21.9 us
    all_to_all x1, blocking collectives, shards(): part = lax.all_to_all(copies, 'mz', split_axis=0, concat_axis=0, tiled=True)  19.6 us
    all_to_all x1, waiting for transfers between devices, shards(): lax.all_to_all(spread, 'mx', split_axis=0, concat_axis=0, tiled=True)  18.8 us
    ppermute x6, starting transfers between devices, shift(): return lax.ppermute(value, axis, [(i, (i + step) % n) for i in range(n)])  18 us
    all_to_all x1, waiting for transfers between devices, shards(): part = lax.all_to_all(copies, 'mz', split_axis=0, concat_axis=0, tiled=True)  14 us
  transfers between devices with their start and end apart: 9, of which 9 were waited for; matrix products, arithmetic and copies ran while one was open for 5% of the time, Pallas kernels for 0%

profile of v16, /device:TPU:6, one launch (start us, length us, event | category | flops | bytes accessed | tf_op | source)
XLA Modules:
  0.0 227.6 jit_solution(10932896835999829975)
XLA Ops:
  2.3 2.1 fusion.39
  4.5 22.3 %all_to_all.35 = bf16[32,32,128]{2,1,0:T(8,128)(2,1)S(1)} all-to-all(bf16[32,32,128]{2,1,0:T(8,128)(2,1)S(1)} %bitcast.118), channel_id=1, replica_groups=mesh['expert'=32,'mx'=4,'mz'=4] {'expert'}, dimensions={0} | all-to-all | bytes 524288 | tf_op jit(solution)/shard_map/all_to_all | solution.py:69
  27.7 9.4 %all-to-all-start.3 = ((bf16[4,512,128]{1,2,0:T(8,128)(2,1)}), bf16[4,512,128]{1,2,0:T(8,128)(2,1)S(1)}, u32[]{:S(2)}, u32[]{:S(2)}) async-start(bf16[4,512,128]{1,2,0:T(8,128)(2,1)} %broadcast_in_dim.77), calls=%async_computation.3 | async-start | bytes 1048576 | tf_op jit(solution)/shard_map/all_to_all | solution.py:87
  37.3 14.0 %all-to-all-done.3 = bf16[4,512,128]{1,2,0:T(8,128)(2,1)S(1)} async-done(((bf16[4,512,128]{1,2,0:T(8,128)(2,1)}), bf16[4,512,128]{1,2,0:T(8,128)(2,1)S(1)}, u32[]{:S(2)}, u32[]{:S(2)}) %all-to-all-start.3) | async-done | bytes 524320 | tf_op jit(solution)/shard_map/all_to_all | solution.py:87
  51.3 19.6 %all_to_all.36 = bf16[4,512,128]{1,2,0:T(8,128)(2,1)S(1)} all-to-all(bf16[4,512,128]{1,2,0:T(8,128)(2,1)S(1)} %broadcast_in_dim.44), channel_id=1, replica_groups=mesh['expert'=32,'mx'=4,'mz'=4] {'mz'}, dimensions={0} | all-to-all | bytes 1048576 | tf_op jit(solution)/shard_map/all_to_all | solution.py:87
  71.1 25.7 %all_to_all.37 = bf16[4,4,512,128]{2,3,1,0:T(8,128)(2,1)S(1)} all-to-all(bf16[4,4,512,128]{2,3,1,0:T(8,128)(2,1)S(1)} %broadcast_in_dim.78), channel_id=1, replica_groups=mesh['expert'=32,'mx'=4,'mz'=4] {'mx'}, dimensions={0} | all-to-all | bytes 4194304 | tf_op jit(solution)/shard_map/all_to_all | solution.py:89
  98.4 6.5 %all-to-all-start.2 = ((bf16[4,4,512,128]{2,3,1,0:T(8,128)(2,1)}), bf16[4,4,512,128]{2,3,1,0:T(8,128)(2,1)}, u32[]{:S(2)}, u32[]{:S(2)}) async-start(bf16[4,4,512,128]{2,3,1,0:T(8,128)(2,1)} %broadcast_in_dim.74), calls=%async_computation.2 | async-start | bytes 4194304 | tf_op jit(solution)/shard_map/all_to_all | solution.py:89
  106.0 18.8 %all-to-all-done.2 = bf16[4,4,512,128]{2,3,1,0:T(8,128)(2,1)} async-done(((bf16[4,4,512,128]{2,3,1,0:T(8,128)(2,1)}), bf16[4,4,512,128]{2,3,1,0:T(8,128)(2,1)}, u32[]{:S(2)}, u32[]{:S(2)}) %all-to-all-start.2) | async-done | bytes 2097184 | tf_op jit(solution)/shard_map/all_to_all | solution.py:89
  124.9 2.1 multiply_reduce_fusion.1
  127.0 2.4 %multiply_convert_fusion.1 = (bf16[16,512,128]{1,2,0:T(8,128)(2,1)S(1)}, bf16[16,512,128]{1,2,0:T(8,128)(2,1)S(1)}) fusion(bf16[4,4,512,128]{2,3,1,0:T(8,128)(2,1)} %all-to-all-done.2, f32[16,128]{1,0:T(8,128)S(1)} %bitcast.119, f32[512]{0:T(512)S(1)} %add_rsqrt_fusion.1, f32[512]{0:T(512)S(1)} %add_rsqrt_fusion, bf16[4,4,512,128]{2,3,1,0:T(8,128)(2,1)S(1)} %all_to_all.37), kind=kLoop, calls=%fused_computation.7 | loop fusion | flops 8388608 | bytes 8400896 | tf_op jit(solution)/shard_map/convert.11
  132.0 4.0 %collective-permute-start = (bf16[512,512]{1,0:T(8,128)(2,1)S(1)}, bf16[512,512]{1,0:T(8,128)(2,1)S(1)}, u32[]{:S(2)}, u32[]{:S(2)}) collective-permute-start(bf16[512,512]{1,0:T(8,128)(2,1)S(1)} %convolution_convert_fusion.7), channel_id=1, source_target_pairs={{0,4},{4,8},{8,12},{12,0},{1,5},{5,9},{9,13},{13,1},{2,6},{6,10},{... | collective-permute-start | bytes 1572872 | tf_op jit(solution)/shard_map/ppermute | solution.py:10
  138.3 1.9 collective-permute-start.3
  140.7 4.5 %collective-permute-done = bf16[512,512]{1,0:T(8,128)(2,1)S(1)} collective-permute-done((bf16[512,512]{1,0:T(8,128)(2,1)S(1)}, bf16[512,512]{1,0:T(8,128)(2,1)S(1)}, u32[]{:S(2)}, u32[]{:S(2)}) %collective-permute-start) | collective-permute-done | bytes 524320 | tf_op jit(solution)/shard_map/ppermute | solution.py:10
  145.7 4.0 %collective-permute-start.1 = (bf16[512,512]{1,0:T(8,128)(2,1)S(1)}, bf16[512,512]{1,0:T(8,128)(2,1)S(1)}, u32[]{:S(2)}, u32[]{:S(2)}) collective-permute-start(bf16[512,512]{1,0:T(8,128)(2,1)S(1)} %add_convert_fusion.5), channel_id=1, source_target_pairs={{0,4},{4,8},{8,12},{12,0},{1,5},{5,9},{9,13},{13,1},{2,6},{6,10},{... | collective-permute-start | bytes 1572872 | tf_op jit(solution)/shard_map/ppermute | solution.py:10
  152.3 1.9 collective-permute-start.4
  154.7 5.4 %collective-permute-done.1 = bf16[512,512]{1,0:T(8,128)(2,1)S(1)} collective-permute-done((bf16[512,512]{1,0:T(8,128)(2,1)S(1)}, bf16[512,512]{1,0:T(8,128)(2,1)S(1)}, u32[]{:S(2)}, u32[]{:S(2)}) %collective-permute-start.1) | collective-permute-done | bytes 524320 | tf_op jit(solution)/shard_map/ppermute | solution.py:10
  160.2 4.3 %collective-permute-start.2 = (bf16[512,512]{1,0:T(8,128)(2,1)S(1)}, bf16[512,512]{1,0:T(8,128)(2,1)S(1)}, u32[]{:S(2)}, u32[]{:S(2)}) collective-permute-start(bf16[512,512]{1,0:T(8,128)(2,1)S(1)} %add_convert_fusion.4), channel_id=1, source_target_pairs={{0,4},{4,8},{8,12},{12,0},{1,5},{5,9},{9,13},{13,1},{2,6},{6,10},{... | collective-permute-start | bytes 1572872 | tf_op jit(solution)/shard_map/ppermute | solution.py:10
  164.5 2.7 %collective-permute-done.4 = bf16[512,512]{1,0:T(8,128)(2,1)S(1)} collective-permute-done((bf16[512,512]{1,0:T(8,128)(2,1)S(1)}, bf16[512,512]{1,0:T(8,128)(2,1)S(1)}, u32[]{:S(2)}, u32[]{:S(2)}) %collective-permute-start.4) | collective-permute-done | bytes 524320 | tf_op jit(solution)/shard_map/ppermute | solution.py:10
  167.3 1.9 collective-permute-start.5
  171.4 8.2 %collective-permute-done.5 = bf16[512,512]{1,0:T(8,128)(2,1)S(1)} collective-permute-done((bf16[512,512]{1,0:T(8,128)(2,1)S(1)}, bf16[512,512]{1,0:T(8,128)(2,1)S(1)}, u32[]{:S(2)}, u32[]{:S(2)}) %collective-permute-start.5) | collective-permute-done | bytes 524320 | tf_op jit(solution)/shard_map/ppermute | solution.py:10
  180.9 5.5 %all-to-all-start.5 = ((bf16[4,1024,128]{2,1,0:T(8,128)(2,1)}), bf16[4,1024,128]{2,1,0:T(8,128)(2,1)}, u32[]{:S(2)}, u32[]{:S(2)}) async-start(bf16[4,1024,128]{2,1,0:T(8,128)(2,1)} %bitcast_bitcast_fusion), calls=%async_computation.5 | async-start | bytes 2097152 | tf_op jit(solution)/shard_map/all_to_all | solution.py:125
  186.5 3.3 %fusion.3 = (bf16[512,2048]{0,1:T(8,128)(2,1)S(1)}, bf16[512,2048]{0,1:T(8,128)(2,1)}) fusion(bf16[4,4,512,128]{2,3,1,0:T(8,128)(2,1)} %all-to-all-done.2, f32[2048]{0:T(1024)S(1)} %copy-done.3, f32[512]{0:T(512)S(1)} %add_rsqrt_fusion.1, f32[512]{0:T(512)S(1)} %add_rsqrt_fusion, bf16[4,4,512,128]{2,3,1,0:T(8,128)(2,1)S(1)} %all_to_all.37), kind=kLoop, calls=%fused_computation.5 | loop fusion | flops 8388608 | bytes 8400896 | tf_op jit(solution)/shard_map/convert_element_type | solution.py:99
  192.0 10.5 %all-to-all-done.5 = bf16[4,1024,128]{2,1,0:T(8,128)(2,1)} async-done(((bf16[4,1024,128]{2,1,0:T(8,128)(2,1)}), bf16[4,1024,128]{2,1,0:T(8,128)(2,1)}, u32[]{:S(2)}, u32[]{:S(2)}) %all-to-all-start.5) | async-done | bytes 1048608 | tf_op jit(solution)/shard_map/all_to_all | solution.py:125
  204.2 21.9 %all_to_all.38 = bf16[32,32,128]{2,1,0:T(8,128)(2,1)S(1)} all-to-all(bf16[32,32,128]{2,1,0:T(8,128)(2,1)S(1)} %fusion.65), channel_id=1, replica_groups=mesh['expert'=32,'mx'=4,'mz'=4] {'expert'}, dimensions={0} | all-to-all | bytes 524288 | tf_op jit(solution)/shard_map/all_to_all | solution.py:131
  (67 shorter events, 24.3 us)
Async XLA Ops:
  0.0 131.6 %copy-start = (bf16[1,320,2048]{2,1,0:T(8,128)(2,1)S(1)}, bf16[1,320,2048]{2,1,0:T(8,128)(2,1)}, u32[]{:S(2)}) copy-start(bf16[1,320,2048]{2,1,0:T(8,128)(2,1)} %param.14) | copy-start | bytes 3932164
  1.6 2.9 %copy-start.4 = (s32[768]{0:T(1024)}, s32[768]{0:T(1024)S(1)}, u32[]{:S(2)}) copy-start(s32[768]{0:T(1024)S(1)} %multiply_add_fusion) | copy-start | bytes 9220
  2.3 2.2 copy-start.8
  27.7 23.5 %all-to-all-start.3 = ((bf16[4,512,128]{1,2,0:T(8,128)(2,1)}), bf16[4,512,128]{1,2,0:T(8,128)(2,1)S(1)}, u32[]{:S(2)}, u32[]{:S(2)}) async-start(bf16[4,512,128]{1,2,0:T(8,128)(2,1)} %broadcast_in_dim.77), calls=%async_computation.3 | async-start | bytes 1048576 | tf_op jit(solution)/shard_map/all_to_all | solution.py:87
  98.4 26.5 %all-to-all-start.2 = ((bf16[4,4,512,128]{2,3,1,0:T(8,128)(2,1)}), bf16[4,4,512,128]{2,3,1,0:T(8,128)(2,1)}, u32[]{:S(2)}, u32[]{:S(2)}) async-start(bf16[4,4,512,128]{2,3,1,0:T(8,128)(2,1)} %broadcast_in_dim.74), calls=%async_computation.2 | async-start | bytes 4194304 | tf_op jit(solution)/shard_map/all_to_all | solution.py:89
  105.4 21.6 %copy-start.3 = (f32[2048]{0:T(1024)S(1)}, f32[2048]{0:T(1024)}, u32[]{:S(2)}) copy-start(f32[2048]{0:T(1024)} %param.10) | copy-start | bytes 24580
  127.0 2.4 %copy-start.10 = (bf16[1,2048,320]{1,2,0:T(8,128)(2,1)S(1)}, bf16[1,2048,320]{1,2,0:T(8,128)(2,1)}, u32[]{:S(2)}) copy-start(bf16[1,2048,320]{1,2,0:T(8,128)(2,1)} %param.12) | copy-start | bytes 3932164
  129.4 1.3 copy-start.11
  132.0 13.2 %collective-permute-start = (bf16[512,512]{1,0:T(8,128)(2,1)S(1)}, bf16[512,512]{1,0:T(8,128)(2,1)S(1)}, u32[]{:S(2)}, u32[]{:S(2)}) collective-permute-start(bf16[512,512]{1,0:T(8,128)(2,1)S(1)} %convolution_convert_fusion.7), channel_id=1, source_target_pairs={{0,4},{4,8},{8,12},{12,0},{1,5},{5,9},{9,13},{13,1},{2,6},{6,10},{... | collective-permute-start | bytes 1572872 | tf_op jit(solution)/shard_map/ppermute | solution.py:10
  138.3 13.5 %collective-permute-start.3 = (bf16[512,512]{1,0:T(8,128)(2,1)S(1)}, bf16[512,512]{1,0:T(8,128)(2,1)S(1)}, u32[]{:S(2)}, u32[]{:S(2)}) collective-permute-start(bf16[512,512]{1,0:T(8,128)(2,1)S(1)} %convolution_convert_fusion.3), channel_id=1, source_target_pairs={{0,12},{4,0},{8,4},{12,8},{1,13},{5,1},{9,5},{13,9},{2,14},{6,2},{... | collective-permute-start | bytes 1572872 | tf_op jit(solution)/shard_map/ppermute | solution.py:10
  145.7 14.3 %collective-permute-start.1 = (bf16[512,512]{1,0:T(8,128)(2,1)S(1)}, bf16[512,512]{1,0:T(8,128)(2,1)S(1)}, u32[]{:S(2)}, u32[]{:S(2)}) collective-permute-start(bf16[512,512]{1,0:T(8,128)(2,1)S(1)} %add_convert_fusion.5), channel_id=1, source_target_pairs={{0,4},{4,8},{8,12},{12,0},{1,5},{5,9},{9,13},{13,1},{2,6},{6,10},{... | collective-permute-start | bytes 1572872 | tf_op jit(solution)/shard_map/ppermute | solution.py:10
  152.3 14.9 %collective-permute-start.4 = (bf16[512,512]{1,0:T(8,128)(2,1)S(1)}, bf16[512,512]{1,0:T(8,128)(2,1)S(1)}, u32[]{:S(2)}, u32[]{:S(2)}) collective-permute-start(bf16[512,512]{1,0:T(8,128)(2,1)S(1)} %add_convert_fusion.2), channel_id=1, source_target_pairs={{0,12},{4,0},{8,4},{12,8},{1,13},{5,1},{9,5},{13,9},{2,14},{6,2},{... | collective-permute-start | bytes 1572872 | tf_op jit(solution)/shard_map/ppermute | solution.py:10
  160.2 11.1 %collective-permute-start.2 = (bf16[512,512]{1,0:T(8,128)(2,1)S(1)}, bf16[512,512]{1,0:T(8,128)(2,1)S(1)}, u32[]{:S(2)}, u32[]{:S(2)}) collective-permute-start(bf16[512,512]{1,0:T(8,128)(2,1)S(1)} %add_convert_fusion.4), channel_id=1, source_target_pairs={{0,4},{4,8},{8,12},{12,0},{1,5},{5,9},{9,13},{13,1},{2,6},{6,10},{... | collective-permute-start | bytes 1572872 | tf_op jit(solution)/shard_map/ppermute | solution.py:10
  167.3 12.3 %collective-permute-start.5 = (bf16[512,512]{1,0:T(8,128)(2,1)S(1)}, bf16[512,512]{1,0:T(8,128)(2,1)S(1)}, u32[]{:S(2)}, u32[]{:S(2)}) collective-permute-start(bf16[512,512]{1,0:T(8,128)(2,1)S(1)} %add_convert_fusion.1), channel_id=1, source_target_pairs={{0,12},{4,0},{8,4},{12,8},{1,13},{5,1},{9,5},{13,9},{2,14},{6,2},{... | collective-permute-start | bytes 1572872 | tf_op jit(solution)/shard_map/ppermute | solution.py:10
  180.9 21.6 %all-to-all-start.5 = ((bf16[4,1024,128]{2,1,0:T(8,128)(2,1)}), bf16[4,1024,128]{2,1,0:T(8,128)(2,1)}, u32[]{:S(2)}, u32[]{:S(2)}) async-start(bf16[4,1024,128]{2,1,0:T(8,128)(2,1)} %bitcast_bitcast_fusion), calls=%async_computation.5 | async-start | bytes 2097152 | tf_op jit(solution)/shard_map/all_to_all | solution.py:125
  186.5 3.3 %copy-start.2 = (bf16[2048,32]{0,1:T(8,128)(2,1)S(1)}, bf16[2048,32]{0,1:T(8,128)(2,1)}, u32[]{:S(2)}) copy-start(bf16[2048,32]{0,1:T(8,128)(2,1)} %param.11) | copy-start | bytes 393220
  186.5 3.3 %copy-start.6 = (pred[32]{0:T(512)(128)(4,1)S(1)}, pred[32]{0:T(512)(128)(4,1)}, u32[]{:S(2)}) copy-start(pred[32]{0:T(512)(128)(4,1)} %iota_compare_fusion.2) | copy-start | bytes 100
  189.8 1.6 copy-start.1
  189.8 1.6 copy-start.7
  191.4 34.8 %copy-start.5 = (s32[768]{0:T(1024)S(1)}, s32[768]{0:T(1024)}, u32[]{:S(2)}) copy-start(s32[768]{0:T(1024)} %copy-done.4) | copy-start | bytes 9220
  191.8 34.3 %copy-start.9 = (pred[768]{0:T(1024)(128)(4,1)S(1)}, pred[768]{0:T(1024)(128)(4,1)}, u32[]{:S(2)}) copy-start(pred[768]{0:T(1024)(128)(4,1)} %copy-done.8) | copy-start | bytes 2308
